TPU v7x, 256 devices: a whole 4x4x8 slice. The times are simulated.
256 devices in a mesh: seq: 64 (over x, z, core), mp: 4 (over y).
Axes of the slice: x: 4, y: 4, z: 8, core: 2. Of those that a mesh axis runs over, the one named last changes fastest.
Arguments:
- states: bfloat16 [4, 128, 2560], P(None, 'seq', 'mp'), may hold values from -6 to 6
- norm_gain: float32 [2560], replicated, may hold values from 0.5 to 2
- query_gain: float32 [128], replicated, may hold values from 0.7 to 2
- key_gain: float32 [128], replicated, may hold values from 0.7 to 2
- w_query: bfloat16 [2560, 2048], P(None, 'mp'), may hold values from -0.125 to 0.125
- key_matrix: bfloat16 [2560, 512], P(None, 'mp'), may hold values from -0.125 to 0.125
- value_matrix: bfloat16 [2560, 512], P(None, 'mp'), may hold values from -0.125 to 0.125
- w_out: bfloat16 [2048, 2560], P('mp'), may hold values from -0.125 to 0.125
- cached_key_blocks: bfloat16 [1024, 256, 512], P('seq', None, 'mp'), may hold values from -216 to 216
- cached_value_blocks: bfloat16 [1024, 256, 512], P('seq', None, 'mp'), may hold values from -6 to 6
- req_len: int32 [128], replicated, may hold values from 1 to 16384, as said below
- slot_request: int32 [1024], P('seq'), may hold values from 0 to 127, as said below
- slot_block: int32 [1024], P('seq'), may hold values from 0 to 63
- slot_empty: int32 [1024], P('seq'), may hold values from 0 to 1
Outputs:
- hidden: bfloat16 [4, 128, 2560], P(None, 'seq', 'mp')
- new_keys: bfloat16 [4, 128, 512], P(None, 'seq', 'mp')
- new_values: bfloat16 [4, 128, 512], P(None, 'seq', 'mp')
Inputs may be any that keep to these rules, and one draw needn't show every extreme that they name: `req_len`: exactly 12 requests have length 16384; each other request has length at most 511, and one of them exactly that. Slot s holds positions slot_block[s] * 256 onward of request slot_request[s] unless slot_empty[s] = 1. Each block of a request below its length lies in exactly one slot that is not empty. A request of length 16384 has one block on every index of seq; every block of any other request b lies on index b // 2 of seq.
All inputs are finite; a program needn't handle non-finite values.
Results may differ from a plain program's by a relative error of at most 0.0098.
Values may be sent and summed in bfloat16 or wider, within the bound.
No kernel may reach another device: no remote copies, remote signals or barrier semaphores. Data moves between devices by JAX's collectives and lax.ppermute only.
A program may use at most 64 MiB of HBM per device.

v0:
```python
import jax
import jax.numpy as jnp
from jax import lax
from jax.sharding import PartitionSpec as P

HEAD_SIZE = 128
STEPS = 4


ROPE_BASE = 1000000.0
NEGATIVE = -1e30
HIGHEST = lax.Precision.HIGHEST


def scaled_rms(values, gain):
    return values * lax.rsqrt(jnp.mean(values * values, axis=-1, keepdims=True) + 1e-06) * gain


def rotate(values, positions):
    halfway = values.shape[-1] // 2
    frequency = ROPE_BASE ** (-(jnp.arange(halfway, dtype=jnp.float32) * 2.0) / values.shape[-1])
    angles = positions.astype(jnp.float32)[..., None, None] * frequency
    cosine = jnp.cos(angles)
    sine_part = jnp.sin(angles)
    leading = values[..., :halfway]
    trailing = values[..., halfway:]
    return jnp.concatenate(
        [leading * cosine - trailing * sine_part, trailing * cosine + leading * sine_part], axis=-1
    )


def project(inputs, positions, norm_gain, query_gain, key_gain, w_query, key_matrix, value_matrix):
    number = inputs.shape[0]
    normed = scaled_rms(inputs.astype(jnp.float32), norm_gain).astype(jnp.bfloat16)
    query_rows = jnp.dot(normed, w_query, preferred_element_type=jnp.float32).reshape(
        number, -1, HEAD_SIZE
    )
    keys = jnp.dot(normed, key_matrix, preferred_element_type=jnp.float32).reshape(
        number, -1, HEAD_SIZE
    )
    values = jnp.dot(normed, value_matrix, preferred_element_type=jnp.float32).astype(jnp.bfloat16)
    query_rows = (
        rotate(scaled_rms(query_rows, query_gain), positions)
        .reshape(number, -1)
        .astype(jnp.bfloat16)
    )
    keys = rotate(scaled_rms(keys, key_gain), positions).reshape(number, -1).astype(jnp.bfloat16)
    return (query_rows, keys, values)


def shards(
    states,
    norm_gain,
    query_gain,
    key_gain,
    w_query,
    key_matrix,
    value_matrix,
    w_out,
    cached_key_blocks,
    cached_value_blocks,
    req_len,
    slot_request,
    slot_block,
    slot_empty,
):
    own_rows = states.shape[1]
    first_row = lax.axis_index("seq") * own_rows
    kv_heads = key_matrix.shape[1] // HEAD_SIZE
    q_heads = w_query.shape[1] // HEAD_SIZE
    head_sharing = q_heads // kv_heads
    query_width = w_query.shape[1]
    kv_width = key_matrix.shape[1]
    slot_count = cached_key_blocks.shape[0]
    block_len = cached_key_blocks.shape[1]
    requests = req_len.shape[0]
    scaling = HEAD_SIZE ** (-0.5)
    slot_len = jnp.take(req_len, slot_request)
    offsets = jnp.arange(block_len, dtype=jnp.int32)
    filled = (slot_empty[:, None] == 0) & (
        slot_block[:, None] * block_len + offsets[None, :] < slot_len[:, None]
    )
    filled_wide = filled[None, :, None, None, :]
    belongs = (slot_request[None, :] == jnp.arange(requests, dtype=jnp.int32)[:, None]) & (
        slot_empty[None, :] == 0
    )
    belongs_float = belongs.astype(jnp.float32)
    keys_split = cached_key_blocks.reshape(slot_count, block_len, kv_heads, HEAD_SIZE)
    values_split = cached_value_blocks.reshape(slot_count, block_len, kv_heads, HEAD_SIZE)
    turn_spans = [(sequence_index, sequence_index + 1) for sequence_index in range(STEPS)]
    past_keys = []
    past_values = []
    results = []
    for low_turn, high_turn in turn_spans:
        number = high_turn - low_turn
        turn_ids = jnp.arange(low_turn, high_turn, dtype=jnp.int32)
        block_states = states[low_turn:high_turn]
        wide_states = lax.all_gather(block_states, "mp", axis=2, tiled=True)
        portion = lax.all_gather(wide_states, "seq", axis=1, tiled=True)
        portion_rows = portion.shape[1]
        portion_positions = req_len[None, :] + turn_ids[:, None]
        part_query, part_key, part_value = project(
            portion.reshape(number * portion_rows, -1),
            portion_positions.reshape(-1),
            norm_gain,
            query_gain,
            key_gain,
            w_query,
            key_matrix,
            value_matrix,
        )
        everyone = jnp.concatenate([part_query, part_key, part_value], axis=1).reshape(
            number, portion_rows, -1
        )
        own_packed = lax.dynamic_slice_in_dim(everyone, first_row, own_rows, 1)
        all_query = everyone[:, :, :query_width]
        own_heads = own_packed[:, :, :query_width].reshape(
            number, own_rows, kv_heads, head_sharing, HEAD_SIZE
        )
        past_keys.append(own_packed[:, :, query_width : query_width + kv_width])
        past_values.append(own_packed[:, :, query_width + kv_width :])
        slot_query = jnp.take(all_query, slot_request, axis=1).reshape(
            number, slot_count, kv_heads, head_sharing, HEAD_SIZE
        )
        scores = (
            jnp.einsum(
                "tsngd,sknd->tsngk", slot_query, keys_split, preferred_element_type=jnp.float32
            )
            * scaling
        )
        slot_maximum = jnp.max(jnp.where(filled_wide, scores, NEGATIVE), axis=-1)
        row_top = jnp.max(
            jnp.where(belongs[None, :, :, None, None], slot_maximum[:, None], NEGATIVE), axis=2
        )
        slot_reference = jnp.take(row_top, slot_request, axis=1)
        weights = jnp.where(
            filled_wide,
            jnp.exp(jnp.where(filled_wide, scores - slot_reference[..., None], 0.0)),
            0.0,
        )
        slot_total = jnp.sum(weights, axis=-1)
        slot_mix = jnp.einsum(
            "tsngk,sknd->tsngd",
            weights.astype(jnp.bfloat16),
            values_split,
            preferred_element_type=jnp.float32,
        )
        row_total = jnp.einsum("bs,tsng->tbng", belongs_float, slot_total, precision=HIGHEST)
        row_mix = jnp.einsum("bs,tsngd->tbngd", belongs_float, slot_mix, precision=HIGHEST)
        every_top = lax.pmax(row_top, "seq")
        every_factor = jnp.exp(row_top - every_top)
        summed_total, summed_mix = lax.psum(
            (row_total * every_factor, row_mix * every_factor[..., None]), "seq"
        )
        own_top = lax.dynamic_slice_in_dim(every_top, first_row, own_rows, 1)
        own_total = lax.dynamic_slice_in_dim(summed_total, first_row, own_rows, 1)
        own_mix = lax.dynamic_slice_in_dim(summed_mix, first_row, own_rows, 1)
        earlier_keys = jnp.concatenate(past_keys, axis=0).reshape(
            high_turn, own_rows, kv_heads, HEAD_SIZE
        )
        earlier_values = jnp.concatenate(past_values, axis=0).reshape(
            high_turn, own_rows, kv_heads, HEAD_SIZE
        )
        fresh_scores = (
            jnp.einsum(
                "trngd,jrnd->trngj", own_heads, earlier_keys, preferred_element_type=jnp.float32
            )
            * scaling
        )
        allowed = (jnp.arange(high_turn, dtype=jnp.int32)[None, :] <= turn_ids[:, None])[
            :, None, None, None, :
        ]
        fresh_top = jnp.max(jnp.where(allowed, fresh_scores, NEGATIVE), axis=-1)
        overall = jnp.maximum(own_top, fresh_top)
        retained = jnp.exp(own_top - overall)
        fresh_weights = jnp.where(
            allowed, jnp.exp(jnp.where(allowed, fresh_scores - overall[..., None], 0.0)), 0.0
        )
        denominator = own_total * retained + jnp.sum(fresh_weights, axis=-1)
        mixture = own_mix * retained[..., None] + jnp.einsum(
            "trngj,jrnd->trngd",
            fresh_weights.astype(jnp.bfloat16),
            earlier_values,
            preferred_element_type=jnp.float32,
        )
        attended = (
            (mixture / denominator[..., None])
            .astype(jnp.bfloat16)
            .reshape(number * own_rows, query_width)
        )
        projected_out = jnp.dot(attended, w_out, preferred_element_type=jnp.float32).reshape(
            number, own_rows, -1
        )
        summed = lax.psum_scatter(projected_out, "mp", scatter_dimension=2, tiled=True)
        results.append((block_states.astype(jnp.float32) + summed).astype(jnp.bfloat16))
    return (
        jnp.concatenate(results, axis=0),
        jnp.concatenate(past_keys, axis=0),
        jnp.concatenate(past_values, axis=0),
    )


def solution(mesh):
    placed = (
        P(None, "seq", "mp"),
        P(),
        P(),
        P(),
        P(None, "mp"),
        P(None, "mp"),
        P(None, "mp"),
        P("mp", None),
        P("seq", None, "mp"),
        P("seq", None, "mp"),
        P(),
        P("seq"),
        P("seq"),
        P("seq"),
    )
    return jax.shard_map(
        shards,
        mesh=mesh,
        in_specs=placed,
        out_specs=(P(None, "seq", "mp"), P(None, "seq", "mp"), P(None, "seq", "mp")),
        check_vma=False,
    )
```

profile of v0, /device:TPU:38, one launch (start us, length us, event | category | flops | bytes accessed | tf_op | source)
XLA Modules:
  0.0 764.4 jit_solution(867895954115995821)
XLA Ops:
  7.7 1.0 fusion.231
  8.8 12.3 %all_gather.28 = bf16[1,2,2560]{2,0,1:T(2,128)(2,1)S(1)} all-gather(bf16[1,2,640]{2,0,1:T(2,128)(2,1)S(1)} %copy.475), channel_id=1, replica_groups=mesh['seq'=64,'mp'=4] {'mp'}, dimensions={2}, use_global_device_ids=true | all-gather | bytes 12800 | tf_op jit(solution)/shard_map/all_gather | solution.py:98
  21.1 11.8 %all_gather.24 = bf16[1,2,2560]{2,0,1:T(2,128)(2,1)S(1)} all-gather(bf16[1,2,640]{2,0,1:T(2,128)(2,1)S(1)} %copy.469), channel_id=1, replica_groups=mesh['seq'=64,'mp'=4] {'mp'}, dimensions={2}, use_global_device_ids=true | all-gather | bytes 12800 | tf_op jit(solution)/shard_map/all_gather | solution.py:98
  32.9 51.1 %all_gather.25 = bf16[1,128,2560]{2,0,1:T(2,128)(2,1)S(1)} all-gather(bf16[1,2,2560]{2,0,1:T(2,128)(2,1)S(1)} %all_gather.24), channel_id=1, replica_groups=mesh['seq'=64,'mp'=4] {'seq'}, dimensions={1}, use_global_device_ids=true | all-gather | bytes 665600 | tf_op jit(solution)/shard_map/all_gather | solution.py:99
  84.0 1.3 convert_element_type.197
  85.6 1.3 copy-done.7
  86.9 1.1 convolution_convert_fusion.3
  88.0 1.6 multiply_reduce_fusion.7
  89.6 49.5 %all_gather.29 = bf16[1,128,2560]{2,0,1:T(2,128)(2,1)S(1)} all-gather(bf16[1,2,2560]{2,0,1:T(2,128)(2,1)S(1)} %all_gather.28), channel_id=1, replica_groups=mesh['seq'=64,'mp'=4] {'seq'}, dimensions={1}, use_global_device_ids=true | all-gather | bytes 665600 | tf_op jit(solution)/shard_map/all_gather | solution.py:99
  139.3 1.1 convolution_convert_fusion.1
  140.4 1.6 multiply_reduce_fusion.5
  142.0 11.8 %all_gather.26 = bf16[1,2,2560]{2,0,1:T(2,128)(2,1)S(1)} all-gather(bf16[1,2,640]{2,0,1:T(2,128)(2,1)S(1)} %copy.472), channel_id=1, replica_groups=mesh['seq'=64,'mp'=4] {'mp'}, dimensions={2}, use_global_device_ids=true | all-gather | bytes 12800 | tf_op jit(solution)/shard_map/all_gather | solution.py:98
  153.8 48.5 %all_gather.27 = bf16[1,128,2560]{2,0,1:T(2,128)(2,1)S(1)} all-gather(bf16[1,2,2560]{2,0,1:T(2,128)(2,1)S(1)} %all_gather.26), channel_id=1, replica_groups=mesh['seq'=64,'mp'=4] {'seq'}, dimensions={1}, use_global_device_ids=true | all-gather | bytes 665600 | tf_op jit(solution)/shard_map/all_gather | solution.py:99
  202.6 1.1 convolution_convert_fusion.2
  203.6 1.7 multiply_reduce_fusion.6
  205.3 11.8 %all_gather.30 = bf16[1,2,2560]{2,0,1:T(2,128)(2,1)S(1)} all-gather(bf16[1,2,640]{2,0,1:T(2,128)(2,1)S(1)} %copy.478), channel_id=1, replica_groups=mesh['seq'=64,'mp'=4] {'mp'}, dimensions={2}, use_global_device_ids=true | all-gather | bytes 12800 | tf_op jit(solution)/shard_map/all_gather | solution.py:98
  217.1 49.5 %all_gather.31 = bf16[1,128,2560]{2,0,1:T(2,128)(2,1)S(1)} all-gather(bf16[1,2,2560]{2,0,1:T(2,128)(2,1)S(1)} %all_gather.30), channel_id=1, replica_groups=mesh['seq'=64,'mp'=4] {'seq'}, dimensions={1}, use_global_device_ids=true | all-gather | bytes 665600 | tf_op jit(solution)/shard_map/all_gather | solution.py:99
  266.9 1.1 convolution_convert_fusion
  267.9 1.6 multiply_reduce_fusion.4
  269.6 4.4 copy.463
  274.0 3.8 multiply_reduce_fusion.3
  277.8 2.2 multiply_reduce_fusion
  280.0 2.2 multiply_reduce_fusion.1
  282.4 1.6 multiply_reduce_fusion.2
  290.5 1.2 multiply_cosine_fusion.7
  294.3 2.0 multiply_multiply_fusion.3
  296.5 1.0 subtract_convert_fusion.2
  297.7 0.8 subtract_convert_fusion.1
  298.7 0.8 subtract_convert_fusion
  299.6 1.5 fusion.220
  301.7 1.5 fusion.221
  305.3 1.7 fusion.29
  307.0 1.6 fusion.30
  310.8 106.6 %all-reduce.2 = (f32[1,128,1,4]{1,3,2,0:T(4,128)}, f32[1,128,1,4]{1,3,2,0:T(4,128)}, f32[1,128,1,4]{1,3,2,0:T(4,128)}, f32[1,128,1,4]{1,3,2,0:T(4,128)}) all-reduce(f32[1,128,1,4]{1,3,2,0:T(4,128)} %bitcast.554, f32[1,128,1,4]{1,3,2,0:T(4,128)S(1)} %bitcast.553, ...), channel_id=1, replica_groups=mesh['seq'=64,'mp'=4] {'seq'}, use_global_device_ids=true, to_apply=%region_39.42 | all-reduce | flops 2048 | bytes 16384 | tf_op jit(solution)/shard_map/pmax | solution.py:150
  417.4 1.3 fusion.196
  418.6 1.3 fusion.195
  419.9 1.3 fusion.194
  421.2 1.3 fusion.193
  426.6 1.6 fusion.111
  428.2 1.5 fusion.114
  430.4 1.1 fusion.24
  431.6 1.1 fusion.27
  432.7 1.1 fusion.26
  433.8 1.1 fusion.25
  441.1 119.6 %all-reduce = (f32[1,128,1,4]{1,3,2,0:T(4,128)S(1)}, f32[1,128,1,4]{1,3,2,0:T(4,128)S(1)}, f32[1,128,1,4]{1,3,2,0:T(4,128)S(1)}, f32[1,128,1,4]{1,3,2,0:T(4,128)S(1)}) all-reduce(f32[1,128,1,4]{1,3,2,0:T(4,128)S(1)} %fusion.33, f32[1,128,1,4]{1,3,2,0:T(4,128)S(1)} %fusion.34, ...), channel_id=1, replica_groups=mesh['seq'=64,'mp'=4] {'seq'}, use_global_device_ids=true, to_apply=%region_43.46 | all-reduce | flops 2048 | bytes 16384 | tf_op jit(solution)/shard_map/psum | solution.py:152
  561.6 0.8 fusion.160
  562.3 0.7 fusion.157
  563.1 72.7 %all-reduce.5.cloned.1.call-done = (f32[1,128,1,4,128]{1,4,3,2,0:T(8,128)}, f32[1,128,1,4,128]{1,4,3,2,0:T(8,128)}, f32[1,128,1,4,128]{1,4,3,2,0:T(8,128)}, f32[1,128,1,4,128]{1,4,3,2,0:T(8,128)}) async-done(((f32[1,128,1,4,128]{1,4,3,2,0:T(8,128)}, f32[1,128,1,4,128]{1,4,3,2,0:T(8,128)}, f32[1,128,1,4,128]{1,4,3,2,0:T(8,128)}, f32[1,128,1,4,128]{1,4,3,2,0:T(8,128)}), (f32[1,128,1,4,128]{1,4,3,2,0:T(8,128)}, ...) | async-done | bytes 1048592 | tf_op jit(solution)/shard_map/psum | solution.py:152
  635.8 1.1 fusion.59
  636.9 2.2 convolution_bitcast_fusion
  639.2 0.9 copy-done.15
  640.2 2.2 convolution_bitcast_fusion.1
  642.5 0.9 copy-done.14
  643.5 2.2 convolution_bitcast_fusion.2
  645.8 0.9 copy-done.13
  646.8 2.2 convolution_bitcast_fusion.3
  650.3 17.5 %reduce-scatter.19.cloned.1.call-done = f32[640,2]{1,0:T(8,128)} async-done(((f32[2560,2]{1,0:T(8,128)}), f32[640,2]{1,0:T(8,128)}) %reduce-scatter.19.cloned.1.call-update) | async-done | bytes 5136
  667.7 1.1 copy.441
  668.8 28.5 %reduce-scatter.17.cloned.1.call-done = f32[640,2]{1,0:T(8,128)} async-done(((f32[2560,2]{1,0:T(8,128)}), f32[640,2]{1,0:T(8,128)}) %reduce-scatter.17.cloned.1.call-update) | async-done | bytes 5136
  697.3 1.1 copy.418
  698.4 28.3 %reduce-scatter.15.cloned.1.call-done = f32[640,2]{1,0:T(8,128)} async-done(((f32[2560,2]{1,0:T(8,128)}), f32[640,2]{1,0:T(8,128)}) %reduce-scatter.15.cloned.1.call-update) | async-done | bytes 5136
  726.7 1.1 copy.394
  727.8 28.3 %reduce-scatter.13.cloned.1.call-done = f32[640,2]{1,0:T(8,128)} async-done(((f32[2560,2]{1,0:T(8,128)}), f32[640,2]{1,0:T(8,128)}) %reduce-scatter.13.cloned.1.call-update) | async-done | bytes 5136
  756.1 1.1 copy.372
  (333 shorter events, 29.9 us)
Async XLA Ops:
  7.2 629.7 %copy-start = (bf16[512,2560]{1,0:T(8,128)(2,1)S(1)}, bf16[512,2560]{1,0:T(8,128)(2,1)}, u32[]{:S(2)}) copy-start(bf16[512,2560]{1,0:T(8,128)(2,1)} %param.25) | copy-start | bytes 7864324
  7.2 628.6 %all-reduce.5.cloned.1.call-start = ((), (), s32[]{:S(2)}) async-start(), calls=%async_computation.8 | async-start | bytes 2097152 | tf_op jit(solution)/shard_map/psum | solution.py:152
  8.7 24.2 %copy-start.34 = (bf16[1,2,640]{2,1,0:T(2,128)(2,1)}, bf16[1,2,640]{2,1,0:T(2,128)(2,1)S(1)}, u32[]{:S(2)}) copy-start(bf16[1,2,640]{2,1,0:T(2,128)(2,1)S(1)} %get-tuple-element.84) | copy-start | bytes 7684
  8.7 24.2 %copy-start.38 = (bf16[1,2,640]{2,1,0:T(2,128)(2,1)}, bf16[1,2,640]{2,1,0:T(2,128)(2,1)S(1)}, u32[]{:S(2)}) copy-start(bf16[1,2,640]{2,1,0:T(2,128)(2,1)S(1)} %get-tuple-element.85) | copy-start | bytes 7684
  8.7 133.2 %copy-start.36 = (bf16[1,2,640]{2,1,0:T(2,128)(2,1)}, bf16[1,2,640]{2,1,0:T(2,128)(2,1)S(1)}, u32[]{:S(2)}) copy-start(bf16[1,2,640]{2,1,0:T(2,128)(2,1)S(1)} %get-tuple-element.86) | copy-start | bytes 7684
  8.7 196.6 %copy-start.40 = (bf16[1,2,640]{2,1,0:T(2,128)(2,1)}, bf16[1,2,640]{2,1,0:T(2,128)(2,1)S(1)}, u32[]{:S(2)}) copy-start(bf16[1,2,640]{2,1,0:T(2,128)(2,1)S(1)} %get-tuple-element.87) | copy-start | bytes 7684
  85.4 2.6 copy-start.2
  85.6 2.4 copy-start.6
  139.3 2.6 copy-start.70
  202.5 2.8 copy-start.8
  202.6 2.7 copy-start.72
  266.8 2.7 copy-start.10
  266.9 2.7 copy-start.74
  274.0 3.8 copy-start.5
  274.0 3.8 copy-start.11
  274.0 3.8 copy-start.75
  277.8 2.2 copy-start.71
  282.2 2.4 copy-start.43
  282.2 3.0 copy-start.1
  282.2 4.2 copy-start.16
  282.2 4.9 copy-start.63
  282.2 4.9 copy-start.31
  282.3 5.6 copy-start.67
  282.3 5.6 copy-start.32
  282.3 6.3 copy-start.68
  282.3 6.3 copy-start.33
  282.3 7.1 copy-start.69
  282.3 7.1 copy-start.12
  282.3 7.1 copy-start.22
  282.3 7.1 copy-start.23
  282.3 7.1 copy-start.24
  282.3 7.1 copy-start.62
  284.0 5.5 copy-start.57
  284.0 10.3 %copy-start.60 = (f32[128,4]{0,1:T(4,128)S(1)}, f32[128,4]{0,1:T(4,128)}, u32[]{:S(2)}) copy-start(f32[128,4]{0,1:T(4,128)} %get-tuple-element.150) | copy-start | bytes 6148
  284.0 10.3 %copy-start.59 = (f32[128,4]{0,1:T(4,128)S(1)}, f32[128,4]{0,1:T(4,128)}, u32[]{:S(2)}) copy-start(f32[128,4]{0,1:T(4,128)} %get-tuple-element.152) | copy-start | bytes 6148
  284.0 10.3 %copy-start.55 = (f32[128,4]{0,1:T(4,128)S(1)}, f32[128,4]{0,1:T(4,128)}, u32[]{:S(2)}) copy-start(f32[128,4]{0,1:T(4,128)} %get-tuple-element.146) | copy-start | bytes 6148
  284.0 25.0 %copy-start.45 = (pred[16]{0:T(512)(128)(4,1)}, pred[16]{0:T(512)(128)(4,1)S(1)}, u32[]{:S(2)}) copy-start(pred[16]{0:T(512)(128)(4,1)S(1)} %broadcast_compare_fusion) | copy-start | bytes 52
  285.2 19.3 %copy-start.42 = (s32[1024]{0:T(1024)}, s32[1024]{0:T(1024)S(1)}, u32[]{:S(2)}) copy-start(s32[1024]{0:T(1024)S(1)} %pad_clamp_fusion) | copy-start | bytes 12292
  286.5 18.7 %copy-start.58 = (pred[16]{0:T(512)(128)(4,1)}, pred[16]{0:T(512)(128)(4,1)S(1)}, u32[]{:S(2)}) copy-start(pred[16]{0:T(512)(128)(4,1)S(1)} %get-tuple-element.53) | copy-start | bytes 52
  299.5 4.3 copy-start.18
  299.5 4.3 copy-start.19
  301.1 3.4 copy-start.17
  301.1 3.4 copy-start.20
  305.3 3.3 copy-start.3
  310.1 111.1 %copy-start.25 = (f32[128,4]{0,1:T(4,128)}, f32[128,4]{0,1:T(4,128)S(1)}, u32[]{:S(2)}) copy-start(f32[128,4]{0,1:T(4,128)S(1)} %get-tuple-element.28) | copy-start | bytes 6148
  310.1 111.1 %copy-start.27 = (f32[128,4]{0,1:T(4,128)}, f32[128,4]{0,1:T(4,128)S(1)}, u32[]{:S(2)}) copy-start(f32[128,4]{0,1:T(4,128)S(1)} %get-tuple-element.31) | copy-start | bytes 6148
  426.6 3.2 copy-start.4
  429.8 2.9 copy-start.52
  430.1 3.8 copy-start.51
  431.6 6.7 copy-start.48
  431.6 6.8 copy-start.49
  432.7 6.7 copy-start.47
  432.7 7.2 copy-start.50
  433.8 6.4 copy-start.30
  433.8 6.6 copy-start.28
  433.8 6.8 copy-start.26
  435.0 232.7 %reduce-scatter.19.cloned.1.call-start = ((), (), s32[]{:S(2)}) async-start(), calls=%async_computation.7 | async-start | bytes 1638400
  639.2 58.1 %reduce-scatter.17.cloned.1.call-start = ((), (), s32[]{:S(2)}) async-start(), calls=%async_computation.6 | async-start | bytes 1638400
  642.5 84.2 %reduce-scatter.15.cloned.1.call-start = ((), (), s32[]{:S(2)}) async-start(), calls=%async_computation.5 | async-start | bytes 1638400
  645.8 110.3 %reduce-scatter.13.cloned.1.call-start = ((), (), s32[]{:S(2)}) async-start(), calls=%async_computation.4 | async-start | bytes 1638400
  649.1 108.1 %copy-start.39 = (bf16[1,2,640]{2,1,0:T(2,128)(2,1)S(1)}, bf16[1,2,640]{2,1,0:T(2,128)(2,1)}, u32[]{:S(2)}) copy-start(bf16[1,2,640]{2,1,0:T(2,128)(2,1)} %copy-done.38) | copy-start | bytes 7684
  649.1 108.1 %copy-start.41 = (bf16[1,2,640]{2,1,0:T(2,128)(2,1)S(1)}, bf16[1,2,640]{2,1,0:T(2,128)(2,1)}, u32[]{:S(2)}) copy-start(bf16[1,2,640]{2,1,0:T(2,128)(2,1)} %copy-done.40) | copy-start | bytes 7684
  649.1 108.2 %copy-start.35 = (bf16[1,2,640]{2,1,0:T(2,128)(2,1)S(1)}, bf16[1,2,640]{2,1,0:T(2,128)(2,1)}, u32[]{:S(2)}) copy-start(bf16[1,2,640]{2,1,0:T(2,128)(2,1)} %copy-done.34) | copy-start | bytes 7684
  649.1 108.2 %copy-start.37 = (bf16[1,2,640]{2,1,0:T(2,128)(2,1)S(1)}, bf16[1,2,640]{2,1,0:T(2,128)(2,1)}, u32[]{:S(2)}) copy-start(bf16[1,2,640]{2,1,0:T(2,128)(2,1)} %copy-done.36) | copy-start | bytes 7684
  (17 other events, 23.7 us)
Sparse Core Ops, SparseCore 0:
  435.1 200.6 all-reduce.4
  639.3 28.3 reduce-scatter.18
  670.5 26.7 reduce-scatter.16
  699.9 26.7 reduce-scatter.14
  729.3 26.7 reduce-scatter.12
where the time goes:
time: 766 us; the launch traced here: 764 us
  blocking collectives  473 us (62%)
  waiting for transfers between devices  175 us (23%)
  matrix products  43.9 us (6%)
  local copies, waits for them, and re-layouts  32.9 us (4%)
  other arithmetic  24.7 us (3%)
  between operations  14.9 us (2%)
    all_gather x4, blocking collectives, shards(): portion = lax.all_gather(wide_states, 'seq', axis=1, tiled=True)  199 us
    psum x1, blocking collectives, shards(): lax.psum((row_total * every_factor, row_mix * every_factor[..., None]), '...  120 us
    pmax x1, blocking collectives, shards(): every_top = lax.pmax(row_top, 'seq')  107 us
    unnamed x9, waiting for transfers between devices  103 us
    psum x1, waiting for transfers between devices, shards(): lax.psum((row_total * every_factor, row_mix * every_factor[..., None]), '...  72.7 us
    all_gather x4, blocking collectives, shards(): wide_states = lax.all_gather(block_states, 'mp', axis=2, tiled=True)  47.8 us
  transfers between devices with their start and end apart: 5, of which 5 were waited for; matrix products, arithmetic and copies ran while one was open for 3% of the time, Pallas kernels for 0%

commit v1 on v0

v1 whole, which is shorter than its diff:
```python
import jax
import jax.numpy as jnp
from jax import lax
from jax.sharding import PartitionSpec as P

HEAD_SIZE = 128
LONG_COUNT = 12

ROPE_BASE = 1000000.0
NEGATIVE = -1e30
HIGHEST = lax.Precision.HIGHEST


def scaled_rms(values, gain):
    return values * lax.rsqrt(jnp.mean(values * values, axis=-1, keepdims=True) + 1e-06) * gain


def rotate(values, positions):
    halfway = values.shape[-1] // 2
    frequency = ROPE_BASE ** (-(jnp.arange(halfway, dtype=jnp.float32) * 2.0) / values.shape[-1])
    angles = positions.astype(jnp.float32)[..., None, None] * frequency
    cosine = jnp.cos(angles)
    sine_part = jnp.sin(angles)
    leading = values[..., :halfway]
    trailing = values[..., halfway:]
    return jnp.concatenate(
        [leading * cosine - trailing * sine_part, trailing * cosine + leading * sine_part], axis=-1
    )


def gather_mp(block, n_mp):
    me = lax.axis_index("mp")
    pieces = [block] + [
        lax.ppermute(block, "mp", [(i, (i + s) % n_mp) for i in range(n_mp)]) for s in range(1, n_mp)
    ]
    stacked = jnp.stack(pieces)
    order = (me - jnp.arange(n_mp, dtype=jnp.int32)) % n_mp
    ordered = jnp.take(stacked, order, axis=0)
    return jnp.concatenate([ordered[c] for c in range(n_mp)], axis=-1)


def reduce_scatter_mp(full, n_mp):
    me = lax.axis_index("mp")
    width = full.shape[-1] // n_mp
    chunks = full.reshape(full.shape[:-1] + (n_mp, width))
    total = jnp.take(chunks, me, axis=-2)
    for s in range(1, n_mp):
        outgoing = jnp.take(chunks, (me + s) % n_mp, axis=-2)
        total = total + lax.ppermute(outgoing, "mp", [(i, (i + s) % n_mp) for i in range(n_mp)])
    return total


def butterfly(value, n_seq, combine):
    stride = 1
    while stride < n_seq:
        partner = lax.ppermute(value, "seq", [(i, i ^ stride) for i in range(n_seq)])
        value = combine(value, partner)
        stride *= 2
    return value


def merge_stats(mine, theirs):
    top_a = mine[..., -1:]
    top_b = theirs[..., -1:]
    top = jnp.maximum(top_a, top_b)
    scaled = mine[..., :-1] * jnp.exp(top_a - top) + theirs[..., :-1] * jnp.exp(top_b - top)
    return jnp.concatenate([scaled, top], axis=-1)


def shards(
    states,
    norm_gain,
    query_gain,
    key_gain,
    w_query,
    key_matrix,
    value_matrix,
    w_out,
    cached_key_blocks,
    cached_value_blocks,
    req_len,
    slot_request,
    slot_block,
    slot_empty,
    n_seq,
    n_mp,
):
    steps, own_rows, _ = states.shape
    me = lax.axis_index("seq")
    first_row = me * own_rows
    kv_heads = key_matrix.shape[1] // HEAD_SIZE
    q_heads = w_query.shape[1] // HEAD_SIZE
    head_sharing = q_heads // kv_heads
    slot_count, block_len, _ = cached_key_blocks.shape
    requests = req_len.shape[0]
    long_len = n_seq * block_len
    scaling = HEAD_SIZE ** (-0.5)

    wide = gather_mp(states, n_mp).reshape(steps * own_rows, -1)
    own_ids = first_row + jnp.arange(own_rows, dtype=jnp.int32)
    own_len = jnp.take(req_len, own_ids)
    positions = (own_len[None, :] + jnp.arange(steps, dtype=jnp.int32)[:, None]).reshape(-1)
    normed = scaled_rms(wide.astype(jnp.float32), norm_gain).astype(jnp.bfloat16)
    rows = steps * own_rows
    query = jnp.dot(normed, w_query, preferred_element_type=jnp.float32).reshape(rows, q_heads, HEAD_SIZE)
    keys = jnp.dot(normed, key_matrix, preferred_element_type=jnp.float32).reshape(rows, kv_heads, HEAD_SIZE)
    values = jnp.dot(normed, value_matrix, preferred_element_type=jnp.float32).astype(jnp.bfloat16)
    query = rotate(scaled_rms(query, query_gain), positions).astype(jnp.bfloat16)
    keys = rotate(scaled_rms(keys, key_gain), positions).astype(jnp.bfloat16)
    new_keys = keys.reshape(steps, own_rows, kv_heads * HEAD_SIZE)
    new_values = values.reshape(steps, own_rows, kv_heads * HEAD_SIZE)
    own_query = query.reshape(steps, own_rows, q_heads, HEAD_SIZE).transpose(1, 0, 2, 3)

    request_ids = jnp.arange(requests, dtype=jnp.int32)
    is_long = req_len == long_len
    rank = jnp.cumsum(is_long.astype(jnp.int32)) - 1
    long_ids = jnp.sum(
        jnp.where(
            is_long[None, :] & (rank[None, :] == jnp.arange(LONG_COUNT, dtype=jnp.int32)[:, None]),
            request_ids[None, :],
            0,
        ),
        axis=1,
    )
    own_pick = long_ids[:, None] == own_ids[None, :]
    long_table = jnp.sum(
        jnp.where(own_pick[:, :, None, None, None], own_query[None], jnp.zeros((), jnp.bfloat16)), axis=1
    ).astype(jnp.bfloat16)
    long_table = butterfly(long_table, n_seq, lambda a, b: a + b)

    slot_req_long = jnp.take(is_long, slot_request)
    slot_rank = jnp.take(rank, slot_request)
    local_row = slot_request - first_row
    slot_local = (local_row >= 0) & (local_row < own_rows)
    pick = jnp.where(
        slot_req_long, slot_rank, jnp.where(slot_local, LONG_COUNT + local_row, LONG_COUNT + own_rows)
    )
    candidates = jnp.concatenate(
        [long_table, own_query, jnp.zeros((1,) + own_query.shape[1:], jnp.bfloat16)], axis=0
    )
    slot_query = jnp.take(candidates, pick, axis=0).reshape(
        slot_count, steps, kv_heads, head_sharing, HEAD_SIZE
    )
    keys_split = cached_key_blocks.reshape(slot_count, block_len, kv_heads, HEAD_SIZE)
    values_split = cached_value_blocks.reshape(slot_count, block_len, kv_heads, HEAD_SIZE)
    scores = (
        jnp.einsum("stngd,sknd->stngk", slot_query, keys_split, preferred_element_type=jnp.float32)
        * scaling
    )
    slot_len = jnp.take(req_len, slot_request)
    kept = slot_empty == 0
    filled = kept[:, None] & (
        slot_block[:, None] * block_len + jnp.arange(block_len, dtype=jnp.int32)[None, :] < slot_len[:, None]
    )
    filled_wide = filled[:, None, None, None, :]
    slot_top = jnp.max(jnp.where(filled_wide, scores, NEGATIVE), axis=-1)
    same = (slot_request[:, None] == slot_request[None, :]) & kept[None, :]
    reference_top = jnp.max(
        jnp.where(same[:, :, None, None, None], slot_top[None], NEGATIVE), axis=1
    )
    weights = jnp.where(
        filled_wide, jnp.exp(jnp.where(filled_wide, scores - reference_top[..., None], 0.0)), 0.0
    )
    slot_total = jnp.sum(weights, axis=-1)
    slot_mix = jnp.einsum(
        "stngk,sknd->stngd", weights.astype(jnp.bfloat16), values_split, preferred_element_type=jnp.float32
    )

    group_ids = jnp.concatenate([long_ids, own_ids])
    member = (group_ids[:, None] == slot_request[None, :]) & kept[None, :]
    member_float = member.astype(jnp.float32)
    group_top = jnp.max(jnp.where(member[:, :, None, None, None], reference_top[None], NEGATIVE), axis=1)
    group_total = jnp.einsum("qs,stng->qtng", member_float, slot_total, precision=HIGHEST)
    group_mix = jnp.einsum("qs,stngd->qtngd", member_float, slot_mix, precision=HIGHEST)
    stats = jnp.concatenate([group_mix, group_total[..., None], group_top[..., None]], axis=-1)
    long_stats = butterfly(stats[:LONG_COUNT], n_seq, merge_stats)
    own_rank = jnp.take(rank, own_ids)
    own_is_long = jnp.take(is_long, own_ids)
    from_long = jnp.take(long_stats, jnp.clip(own_rank, 0, LONG_COUNT - 1), axis=0)
    cache_stats = jnp.where(own_is_long[:, None, None, None, None], from_long, stats[LONG_COUNT:])
    cache_mix = cache_stats[..., :HEAD_SIZE]
    cache_total = cache_stats[..., HEAD_SIZE]
    cache_top = cache_stats[..., HEAD_SIZE + 1]

    heads = own_query.reshape(own_rows, steps, kv_heads, head_sharing, HEAD_SIZE)
    fresh_keys = keys.reshape(steps, own_rows, kv_heads, HEAD_SIZE).transpose(1, 0, 2, 3)
    fresh_values = values.reshape(steps, own_rows, kv_heads, HEAD_SIZE).transpose(1, 0, 2, 3)
    fresh_scores = (
        jnp.einsum("rtngd,rjnd->rtngj", heads, fresh_keys, preferred_element_type=jnp.float32) * scaling
    )
    allowed = (jnp.arange(steps, dtype=jnp.int32)[None, :] <= jnp.arange(steps, dtype=jnp.int32)[:, None])[
        None, :, None, None, :
    ]
    fresh_top = jnp.max(jnp.where(allowed, fresh_scores, NEGATIVE), axis=-1)
    overall = jnp.maximum(cache_top, fresh_top)
    retained = jnp.exp(cache_top - overall)
    fresh_weights = jnp.where(
        allowed, jnp.exp(jnp.where(allowed, fresh_scores - overall[..., None], 0.0)), 0.0
    )
    denominator = cache_total * retained + jnp.sum(fresh_weights, axis=-1)
    mixture = cache_mix * retained[..., None] + jnp.einsum(
        "rtngj,rjnd->rtngd",
        fresh_weights.astype(jnp.bfloat16),
        fresh_values,
        preferred_element_type=jnp.float32,
    )
    attended = (mixture / denominator[..., None]).astype(jnp.bfloat16)
    attended = attended.transpose(1, 0, 2, 3, 4).reshape(steps * own_rows, q_heads * HEAD_SIZE)
    projected = jnp.dot(attended, w_out, preferred_element_type=jnp.float32).reshape(steps, own_rows, -1)
    summed = reduce_scatter_mp(projected, n_mp)
    hidden = (states.astype(jnp.float32) + summed).astype(jnp.bfloat16)
    return hidden, new_keys, new_values


def solution(mesh):
    n_seq = mesh.shape["seq"]
    n_mp = mesh.shape["mp"]
    placed = (
        P(None, "seq", "mp"),
        P(),
        P(),
        P(),
        P(None, "mp"),
        P(None, "mp"),
        P(None, "mp"),
        P("mp", None),
        P("seq", None, "mp"),
        P("seq", None, "mp"),
        P(),
        P("seq"),
        P("seq"),
        P("seq"),
    )

    def body(*args):
        return shards(*args, n_seq=n_seq, n_mp=n_mp)

    return jax.shard_map(
        body,
        mesh=mesh,
        in_specs=placed,
        out_specs=(P(None, "seq", "mp"), P(None, "seq", "mp"), P(None, "seq", "mp")),
        check_vma=False,
    )
```

time: 766 us -> 131 us (0.17)
  the two profiles are of different devices: /device:TPU:38 before, /device:TPU:12 now
where the time goes in v1:
time: 131 us
  waiting for transfers between devices  56.7 us (43%)
  starting transfers between devices  30 us (23%)
  local copies, waits for them, and re-layouts  24.1 us (18%)
  other arithmetic  10.3 us (8%)
  matrix products  8.61 us (7%)
    ppermute x12, waiting for transfers between devices, butterfly(): lax.ppermute(value, 'seq', [(i, i ^ stride) for i in range(n_seq)])  53.6 us
    ppermute x12, starting transfers between devices, butterfly(): lax.ppermute(value, 'seq', [(i, i ^ stride) for i in range(n_seq)])  21.5 us
    ppermute x3, starting transfers between devices, gather_mp(): lax.ppermute(block, 'mp', [(i, (i + s) % n_mp) for i in range(n_mp)])  5 us
    dot_general x3, local copies, waits for them, and re-layouts, shards(): jnp.dot(attended, w_out, preferred_element_type=jnp.float32)  4.68 us
    dot_general x1, local copies, waits for them, and re-layouts, shards(): jnp.dot(normed, w_query, preferred_element_type=jnp.float32)  4.41 us
    ppermute x3, starting transfers between devices, reduce_scatter_mp(): lax.ppermute(outgoing, 'mp', [(i, (i + s) % n_mp) for i in range(n_mp)])  3.49 us
    ppermute x3, waiting for transfers between devices, reduce_scatter_mp(): lax.ppermute(outgoing, 'mp', [(i, (i + s) % n_mp) for i in range(n_mp)])  3.12 us
  transfers between devices with their start and end apart: 18, of which 13 were waited for; matrix products, arithmetic and copies ran while one was open for 17% of the time, Pallas kernels for 0%

profile of v1, /device:TPU:12, one launch (start us, length us, event | category | flops | bytes accessed | tf_op | source)
XLA Modules:
  0.0 130.9 jit_solution(3761684649176903873)
XLA Ops:
  0.6 1.7 %collective-permute-start = (bf16[4,2,640]{2,1,0:T(2,128)(2,1)}, bf16[4,2,640]{2,1,0:T(2,128)(2,1)S(1)}, u32[]{:S(2)}, u32[]{:S(2)}) collective-permute-start(bf16[4,2,640]{2,1,0:T(2,128)(2,1)} %param.20), channel_id=1, source_target_pairs={{0,1},{1,2},{2,3},{3,0},{4,5},{5,6},{6,7},{7,4},{8,9},{9,10},{10,1... | collective-permute-start | bytes 30728 | tf_op jit(solution)/shard_map/ppermute | solution.py:34
  2.3 0.9 collective-permute-start.1
  3.2 2.4 %collective-permute-start.2 = (bf16[4,2,640]{2,1,0:T(2,128)(2,1)}, bf16[4,2,640]{2,1,0:T(2,128)(2,1)S(1)}, u32[]{:S(2)}, u32[]{:S(2)}) collective-permute-start(bf16[4,2,640]{2,1,0:T(2,128)(2,1)} %param.20), channel_id=1, source_target_pairs={{0,3},{1,0},{2,1},{3,2},{4,7},{5,4},{6,5},{7,6},{8,11},{9,8},{10,9... | collective-permute-start | bytes 30728 | tf_op jit(solution)/shard_map/ppermute | solution.py:34
  5.7 0.7 broadcast_compare_fusion.2
  6.7 0.7 compare_select_fusion
  7.5 0.7 gather_fusion.7
  8.2 0.7 gather_fusion.1
  8.8 1.3 %gather_fusion.6 = s32[16]{0:T(128)S(1)} fusion(s32[128]{0:T(128)} %param.30, s32[1024]{0:T(1024)S(1)} %pad_clamp_fusion.3), kind=kCustom, calls=%fused_computation.1.clone | custom fusion | bytes 192 | tf_op jit(solution)/shard_map/jit(_take)/gather | solution.py:150
  10.2 1.3 gather_fusion.8
  11.8 0.7 compare_and_fusion.4
  12.5 0.8 compare_and_fusion
  13.3 0.7 compare_and_fusion.1
  14.1 0.7 broadcast_select_fusion.2
  14.9 0.6 gather_fusion.5
  15.5 4.4 %copy.330 = bf16[512,2560]{1,0:T(8,128)(2,1)} copy(bf16[512,2560]{0,1:T(8,128)(2,1)} %bitcast.232) | data formatting | bytes 5242880 | tf_op jit(solution)/shard_map/dot_general | solution.py:105
  19.9 0.6 gather_fusion
  20.7 0.6 gather_fusion.2
  21.7 2.6 %multiply_reduce_fusion = (f32[8,4]{0,1:T(4,128)S(1)}, f32[8,4,128]{2,0,1:T(8,128)S(1)}) fusion(bf16[4,128,2560]{2,1,0:T(8,128)(2,1)} %bitcast.231, f32[2560]{0:T(1024)S(1)} %copy-done.3, f32[8]{0:T(128)S(1)} %add_rsqrt_fusion.2, bf16[8,640]{1,0:T(8,128)(2,1)S(1)} %concatenate.80, bf16[8,640]{1,0:T(8,128)(2,1)S(1)} %concatenate.79, ...), kind=kOutput, calls=%fused_computation.94 | convolution fusion | flops 21204960 | bytes 2689184 | tf_op jit(solution)/shard_map/dot_general | solution.py:105
  24.9 1.2 collective-permute-done.3
  26.1 2.0 %collective-permute-start.4 = (bf16[12,4,4,128]{3,2,1,0:T(4,128)(2,1)S(1)}, bf16[12,4,4,128]{3,2,1,0:T(4,128)(2,1)S(1)}, u32[]{:S(2)}, u32[]{:S(2)}) collective-permute-start(bf16[12,4,4,128]{3,2,1,0:T(4,128)(2,1)S(1)} %add.277), channel_id=1, source_target_pairs={{0,8},{4,12},{8,0},{12,4},{16,24},{20,28},{24,16},{28,20},{32,40},... | collective-permute-start | bytes 147464 | tf_op jit(solution)/shard_map/ppermute | solution.py:56
  28.1 2.2 %collective-permute-done.4 = bf16[12,4,4,128]{3,2,1,0:T(4,128)(2,1)S(1)} collective-permute-done((bf16[12,4,4,128]{3,2,1,0:T(4,128)(2,1)S(1)}, bf16[12,4,4,128]{3,2,1,0:T(4,128)(2,1)S(1)}, u32[]{:S(2)}, u32[]{:S(2)}) %collective-permute-start.4) | collective-permute-done | bytes 49184 | tf_op jit(solution)/shard_map/ppermute | solution.py:56
  30.3 3.4 %collective-permute-start.5 = (bf16[12,4,4,128]{3,2,1,0:T(4,128)(2,1)S(1)}, bf16[12,4,4,128]{3,2,1,0:T(4,128)(2,1)S(1)}, u32[]{:S(2)}, u32[]{:S(2)}) collective-permute-start(bf16[12,4,4,128]{3,2,1,0:T(4,128)(2,1)S(1)} %add.278), channel_id=1, source_target_pairs={{0,16},{4,20},{8,24},{12,28},{16,0},{20,4},{24,8},{28,12},{32,48},... | collective-permute-start | bytes 147464 | tf_op jit(solution)/shard_map/ppermute | solution.py:56
  33.7 2.3 %collective-permute-done.5 = bf16[12,4,4,128]{3,2,1,0:T(4,128)(2,1)S(1)} collective-permute-done((bf16[12,4,4,128]{3,2,1,0:T(4,128)(2,1)S(1)}, bf16[12,4,4,128]{3,2,1,0:T(4,128)(2,1)S(1)}, u32[]{:S(2)}, u32[]{:S(2)}) %collective-permute-start.5) | collective-permute-done | bytes 49184 | tf_op jit(solution)/shard_map/ppermute | solution.py:56
  36.0 6.8 %collective-permute-start.6 = (bf16[12,4,4,128]{3,2,1,0:T(4,128)(2,1)S(1)}, bf16[12,4,4,128]{3,2,1,0:T(4,128)(2,1)S(1)}, u32[]{:S(2)}, u32[]{:S(2)}) collective-permute-start(bf16[12,4,4,128]{3,2,1,0:T(4,128)(2,1)S(1)} %add.279), channel_id=1, source_target_pairs={{0,32},{4,36},{8,40},{12,44},{16,48},{20,52},{24,56},{28,60},{32,0... | collective-permute-start | bytes 147464 | tf_op jit(solution)/shard_map/ppermute | solution.py:56
  42.8 4.5 %copy.334 = bf16[2560,512]{1,0:T(8,128)(2,1)} copy(bf16[2560,512]{0,1:T(8,128)(2,1)} %bitcast.233) | data formatting | bytes 5242880 | tf_op jit(solution)/shard_map/dot_general | solution.py:209
  47.4 1.3 collective-permute-start.7
  48.7 0.4 multiply_reduce_fusion.1
  49.1 2.9 %collective-permute-done.7 = bf16[12,4,4,128]{3,2,1,0:T(4,128)(2,1)S(1)} collective-permute-done((bf16[12,4,4,128]{3,2,1,0:T(4,128)(2,1)S(1)}, bf16[12,4,4,128]{3,2,1,0:T(4,128)(2,1)S(1)}, u32[]{:S(2)}, u32[]{:S(2)}) %collective-permute-start.7) | collective-permute-done | bytes 49184 | tf_op jit(solution)/shard_map/ppermute | solution.py:56
  52.0 0.2 collective-permute-start.8
  52.2 0.2 convolution_convert_fusion
  52.5 5.2 %collective-permute-done.8 = bf16[12,4,4,128]{3,2,1,0:T(4,128)(2,1)S(1)} collective-permute-done((bf16[12,4,4,128]{3,2,1,0:T(4,128)(2,1)S(1)}, bf16[12,4,4,128]{3,2,1,0:T(4,128)(2,1)S(1)}, u32[]{:S(2)}, u32[]{:S(2)}) %collective-permute-start.8) | collective-permute-done | bytes 49184 | tf_op jit(solution)/shard_map/ppermute | solution.py:56
  57.8 0.6 gather_fusion.3
  58.4 0.5 select_reduce_fusion
  59.3 0.3 bitcast_reduce_fusion
  59.7 1.6 %fusion.1 = f32[16,4,4,128]{3,2,1,0:T(4,128)S(1)} fusion(bf16[16,256,128]{2,1,0:T(8,128)(2,1)} %param.29, f32[16,1,256,4,4]{2,4,3,0,1:T(4,128)S(1)} %get-tuple-element.80, f32[16,4,4]{2,1,0:T(4,128)S(1)} %copy.273, pred[16,256]{1,0:T(8,128)(4,1)S(1)} %fusion.42), kind=kOutput, calls=%fused_computation.14 | convolution fusion | flops 17039360 | bytes 1446912 | tf_op jit(solution)/shard_map/stngk,sknd->stngd/dot_general | solution.py:165
  61.2 0.3 convolution_bitcast_fusion
  61.9 0.2 copy.277
  62.3 0.5 copy.282
  63.1 1.3 collective-permute-done.9
  64.8 0.2 copy.286
  65.5 1.1 collective-permute-start.10
  66.7 6.0 %collective-permute-done.10 = f32[12,4,1,4,130]{4,3,2,1,0:T(4,128)S(1)} collective-permute-done((f32[12,4,1,4,130]{4,3,2,1,0:T(4,128)S(1)}, f32[12,4,1,4,130]{4,3,2,1,0:T(4,128)S(1)}, u32[]{:S(2)}, u32[]{:S(2)}) %collective-permute-start.10) | collective-permute-done | bytes 99872 | tf_op jit(solution)/shard_map/ppermute | solution.py:56
  73.1 0.2 copy.290
  73.8 1.4 %collective-permute-start.11 = (f32[12,4,1,4,130]{4,3,2,1,0:T(4,128)S(1)}, f32[12,4,1,4,130]{4,3,2,1,0:T(4,128)S(1)}, u32[]{:S(2)}, u32[]{:S(2)}) collective-permute-start(f32[12,4,1,4,130]{4,3,2,1,0:T(4,128)S(1)} %pad_maximum_fusion.3), channel_id=1, source_target_pairs={{0,16},{4,20},{8,24},{12,28},{16,0},{20,4},{24,8},{28,12},{32,48},... | collective-permute-start | bytes 299528 | tf_op jit(solution)/shard_map/ppermute | solution.py:56
  75.4 9.8 %collective-permute-done.11 = f32[12,4,1,4,130]{4,3,2,1,0:T(4,128)S(1)} collective-permute-done((f32[12,4,1,4,130]{4,3,2,1,0:T(4,128)S(1)}, f32[12,4,1,4,130]{4,3,2,1,0:T(4,128)S(1)}, u32[]{:S(2)}, u32[]{:S(2)}) %collective-permute-start.11) | collective-permute-done | bytes 99872 | tf_op jit(solution)/shard_map/ppermute | solution.py:56
  85.5 0.2 copy.294
  86.2 3.2 %collective-permute-start.12 = (f32[12,4,1,4,130]{4,3,2,1,0:T(4,128)S(1)}, f32[12,4,1,4,130]{4,3,2,1,0:T(4,128)S(1)}, u32[]{:S(2)}, u32[]{:S(2)}) collective-permute-start(f32[12,4,1,4,130]{4,3,2,1,0:T(4,128)S(1)} %pad_maximum_fusion.4), channel_id=1, source_target_pairs={{0,32},{4,36},{8,40},{12,44},{16,48},{20,52},{24,56},{28,60},{32,0... | collective-permute-start | bytes 299528 | tf_op jit(solution)/shard_map/ppermute | solution.py:56
  89.7 10.8 %collective-permute-done.12 = f32[12,4,1,4,130]{4,3,2,1,0:T(4,128)S(1)} collective-permute-done((f32[12,4,1,4,130]{4,3,2,1,0:T(4,128)S(1)}, f32[12,4,1,4,130]{4,3,2,1,0:T(4,128)S(1)}, u32[]{:S(2)}, u32[]{:S(2)}) %collective-permute-start.12) | collective-permute-done | bytes 99872 | tf_op jit(solution)/shard_map/ppermute | solution.py:56
  100.8 0.2 copy.298
  101.5 1.3 collective-permute-start.13
  102.9 5.5 %collective-permute-done.13 = f32[12,4,1,4,130]{4,3,2,1,0:T(4,128)S(1)} collective-permute-done((f32[12,4,1,4,130]{4,3,2,1,0:T(4,128)S(1)}, f32[12,4,1,4,130]{4,3,2,1,0:T(4,128)S(1)}, u32[]{:S(2)}, u32[]{:S(2)}) %collective-permute-start.13) | collective-permute-done | bytes 99872 | tf_op jit(solution)/shard_map/ppermute | solution.py:56
  109.5 0.6 collective-permute-start.14
  110.2 0.4 copy.308
  110.6 6.5 %collective-permute-done.14 = f32[12,4,1,4,130]{4,3,2,1,0:T(4,128)S(1)} collective-permute-done((f32[12,4,1,4,130]{4,3,2,1,0:T(4,128)S(1)}, f32[12,4,1,4,130]{4,3,2,1,0:T(4,128)S(1)}, u32[]{:S(2)}, u32[]{:S(2)}) %collective-permute-start.14) | collective-permute-done | bytes 99872 | tf_op jit(solution)/shard_map/ppermute | solution.py:56
  118.2 0.6 gather_fusion.4
  118.8 0.4 copy.307
  119.2 0.2 fusion.4
  119.8 0.3 copy.315
  120.4 2.5 %fusion.43 = f32[4,2,4,640]{3,0,2,1:T(4,128)S(1)} fusion(bf16[4,640,512,1]{2,1,0,3:T(8,128)(2,1)} %bitcast.230, bf16[4,2,512,1]{2,0,1,3:T(4,128)(2,1)S(1)} %reshape.878), kind=kOutput, calls=%fused_computation.98 | convolution fusion | flops 20971520 | bytes 2711552 | tf_op jit(solution)/shard_map/dot_general | solution.py:209
  123.1 3.4 %collective-permute-start.16 = (f32[4,2,640]{2,0,1:T(4,128)S(1)}, f32[4,2,640]{2,0,1:T(4,128)S(1)}, u32[]{:S(2)}, u32[]{:S(2)}) collective-permute-start(f32[4,2,640]{2,0,1:T(4,128)S(1)} %get-tuple-element.60), channel_id=1, source_target_pairs={{0,2},{1,3},{2,0},{3,1},{4,6},{5,7},{6,4},{7,5},{8,10},{9,11},{10,... | collective-permute-start | bytes 61448 | tf_op jit(solution)/shard_map/ppermute | solution.py:49
  126.5 0.7 pad_maximum_fusion.10
  127.2 1.3 collective-permute-done.16
  128.5 1.8 %collective-permute-done.17 = f32[4,2,640]{2,0,1:T(4,128)S(1)} collective-permute-done((f32[4,2,640]{2,0,1:T(4,128)S(1)}, f32[4,2,640]{2,0,1:T(4,128)S(1)}, u32[]{:S(2)}, u32[]{:S(2)}) %collective-permute-start.17) | collective-permute-done | bytes 20512 | tf_op jit(solution)/shard_map/ppermute | solution.py:49
  130.3 0.6 copy.323
  (155 shorter events, 10.5 us)
Async XLA Ops:
  0.6 57.8 %copy-start = (bf16[16,256,128]{2,1,0:T(8,128)(2,1)S(1)}, bf16[16,256,128]{2,1,0:T(8,128)(2,1)}, u32[]{:S(2)}) copy-start(bf16[16,256,128]{2,1,0:T(8,128)(2,1)} %param.28) | copy-start | bytes 3145732
  0.6 19.9 %collective-permute-start = (bf16[4,2,640]{2,1,0:T(2,128)(2,1)}, bf16[4,2,640]{2,1,0:T(2,128)(2,1)S(1)}, u32[]{:S(2)}, u32[]{:S(2)}) collective-permute-start(bf16[4,2,640]{2,1,0:T(2,128)(2,1)} %param.20), channel_id=1, source_target_pairs={{0,1},{1,2},{2,3},{3,0},{4,5},{5,6},{6,7},{7,4},{8,9},{9,10},{10,1... | collective-permute-start | bytes 30728 | tf_op jit(solution)/shard_map/ppermute | solution.py:34
  2.3 18.3 %collective-permute-start.1 = (bf16[4,2,640]{2,1,0:T(2,128)(2,1)}, bf16[4,2,640]{2,1,0:T(2,128)(2,1)S(1)}, u32[]{:S(2)}, u32[]{:S(2)}) collective-permute-start(bf16[4,2,640]{2,1,0:T(2,128)(2,1)} %param.20), channel_id=1, source_target_pairs={{0,2},{1,3},{2,0},{3,1},{4,6},{5,7},{6,4},{7,5},{8,10},{9,11},{10,... | collective-permute-start | bytes 30728 | tf_op jit(solution)/shard_map/ppermute | solution.py:34
  3.2 17.4 %collective-permute-start.2 = (bf16[4,2,640]{2,1,0:T(2,128)(2,1)}, bf16[4,2,640]{2,1,0:T(2,128)(2,1)S(1)}, u32[]{:S(2)}, u32[]{:S(2)}) collective-permute-start(bf16[4,2,640]{2,1,0:T(2,128)(2,1)} %param.20), channel_id=1, source_target_pairs={{0,3},{1,0},{2,1},{3,2},{4,7},{5,4},{6,5},{7,6},{8,11},{9,8},{10,9... | collective-permute-start | bytes 30728 | tf_op jit(solution)/shard_map/ppermute | solution.py:34
  15.5 5.1 %copy-start.4 = (bf16[4,2,640]{2,1,0:T(2,128)(2,1)S(1)}, bf16[4,2,640]{2,1,0:T(2,128)(2,1)}, u32[]{:S(2)}) copy-start(bf16[4,2,640]{2,1,0:T(2,128)(2,1)} %param.20) | copy-start | bytes 30724
  15.5 6.2 %copy-start.3 = (f32[2560]{0:T(1024)S(1)}, f32[2560]{0:T(1024)}, u32[]{:S(2)}) copy-start(f32[2560]{0:T(1024)} %param.21) | copy-start | bytes 30724
  19.9 4.4 %copy-start.7 = (f32[128]{0:T(128)S(1)}, f32[128]{0:T(128)}, u32[]{:S(2)}) copy-start(f32[128]{0:T(128)} %param.22) | copy-start | bytes 1540
  24.7 1.3 %collective-permute-start.3 = (bf16[12,4,4,128]{3,2,1,0:T(4,128)(2,1)S(1)}, bf16[12,4,4,128]{3,2,1,0:T(4,128)(2,1)S(1)}, u32[]{:S(2)}, u32[]{:S(2)}) collective-permute-start(bf16[12,4,4,128]{3,2,1,0:T(4,128)(2,1)S(1)} %select_reduce_fusion.3), channel_id=1, source_target_pairs={{0,4},{4,0},{8,12},{12,8},{16,20},{20,16},{24,28},{28,24},{32,36},... | collective-permute-start | bytes 147464 | tf_op jit(solution)/shard_map/ppermute | solution.py:56
  26.1 4.2 %collective-permute-start.4 = (bf16[12,4,4,128]{3,2,1,0:T(4,128)(2,1)S(1)}, bf16[12,4,4,128]{3,2,1,0:T(4,128)(2,1)S(1)}, u32[]{:S(2)}, u32[]{:S(2)}) collective-permute-start(bf16[12,4,4,128]{3,2,1,0:T(4,128)(2,1)S(1)} %add.277), channel_id=1, source_target_pairs={{0,8},{4,12},{8,0},{12,4},{16,24},{20,28},{24,16},{28,20},{32,40},... | collective-permute-start | bytes 147464 | tf_op jit(solution)/shard_map/ppermute | solution.py:56
  30.3 5.6 %collective-permute-start.5 = (bf16[12,4,4,128]{3,2,1,0:T(4,128)(2,1)S(1)}, bf16[12,4,4,128]{3,2,1,0:T(4,128)(2,1)S(1)}, u32[]{:S(2)}, u32[]{:S(2)}) collective-permute-start(bf16[12,4,4,128]{3,2,1,0:T(4,128)(2,1)S(1)} %add.278), channel_id=1, source_target_pairs={{0,16},{4,20},{8,24},{12,28},{16,0},{20,4},{24,8},{28,12},{32,48},... | collective-permute-start | bytes 147464 | tf_op jit(solution)/shard_map/ppermute | solution.py:56
  36.0 11.4 %collective-permute-start.6 = (bf16[12,4,4,128]{3,2,1,0:T(4,128)(2,1)S(1)}, bf16[12,4,4,128]{3,2,1,0:T(4,128)(2,1)S(1)}, u32[]{:S(2)}, u32[]{:S(2)}) collective-permute-start(bf16[12,4,4,128]{3,2,1,0:T(4,128)(2,1)S(1)} %add.279), channel_id=1, source_target_pairs={{0,32},{4,36},{8,40},{12,44},{16,48},{20,52},{24,56},{28,60},{32,0... | collective-permute-start | bytes 147464 | tf_op jit(solution)/shard_map/ppermute | solution.py:56
  42.8 5.9 %copy-start.1 = (bf16[2560,128]{1,0:T(8,128)(2,1)S(1)}, bf16[2560,128]{1,0:T(8,128)(2,1)}, u32[]{:S(2)}) copy-start(bf16[2560,128]{1,0:T(8,128)(2,1)} %param.25) | copy-start | bytes 1966084
  42.8 9.4 %copy-start.2 = (bf16[2560,128]{1,0:T(8,128)(2,1)S(1)}, bf16[2560,128]{1,0:T(8,128)(2,1)}, u32[]{:S(2)}) copy-start(bf16[2560,128]{1,0:T(8,128)(2,1)} %param.26) | copy-start | bytes 1966084
  47.4 13.8 %copy-start.5 = (s32[16]{0:T(128)S(1)}, s32[16]{0:T(128)}, u32[]{:S(2)}) copy-start(s32[16]{0:T(128)} %param.31) | copy-start | bytes 196
  47.4 4.5 %collective-permute-start.7 = (bf16[12,4,4,128]{3,2,1,0:T(4,128)(2,1)S(1)}, bf16[12,4,4,128]{3,2,1,0:T(4,128)(2,1)S(1)}, u32[]{:S(2)}, u32[]{:S(2)}) collective-permute-start(bf16[12,4,4,128]{3,2,1,0:T(4,128)(2,1)S(1)} %add.280), channel_id=1, source_target_pairs={{0,64},{4,68},{8,72},{12,76},{16,80},{20,84},{24,88},{28,92},{32,9... | collective-permute-start | bytes 147464 | tf_op jit(solution)/shard_map/ppermute | solution.py:56
  52.0 5.7 %collective-permute-start.8 = (bf16[12,4,4,128]{3,2,1,0:T(4,128)(2,1)S(1)}, bf16[12,4,4,128]{3,2,1,0:T(4,128)(2,1)S(1)}, u32[]{:S(2)}, u32[]{:S(2)}) collective-permute-start(bf16[12,4,4,128]{3,2,1,0:T(4,128)(2,1)S(1)} %add.281), channel_id=1, source_target_pairs={{0,128},{4,132},{8,136},{12,140},{16,144},{20,148},{24,152},{28,15... | collective-permute-start | bytes 147464 | tf_op jit(solution)/shard_map/ppermute | solution.py:56
  52.5 67.2 %copy-start.6 = (bf16[8,128]{1,0:T(8,128)(2,1)}, bf16[8,128]{1,0:T(8,128)(2,1)S(1)}, u32[]{:S(2)}) copy-start(bf16[8,128]{1,0:T(8,128)(2,1)S(1)} %convolution_convert_fusion) | copy-start | bytes 6148
  59.6 7.0 %copy-start.8 = (f32[128]{0:T(128)S(1)}, f32[128]{0:T(128)}, u32[]{:S(2)}) copy-start(f32[128]{0:T(128)} %param.23) | copy-start | bytes 1540
  62.9 1.5 %collective-permute-start.9 = (f32[12,4,1,4,130]{4,3,2,1,0:T(4,128)S(1)}, f32[12,4,1,4,130]{4,3,2,1,0:T(4,128)S(1)}, u32[]{:S(2)}, u32[]{:S(2)}) collective-permute-start(f32[12,4,1,4,130]{4,3,2,1,0:T(4,128)S(1)} %slice.152), channel_id=1, source_target_pairs={{0,4},{4,0},{8,12},{12,8},{16,20},{20,16},{24,28},{28,24},{32,36},... | collective-permute-start | bytes 299528 | tf_op jit(solution)/shard_map/ppermute | solution.py:56
  65.5 7.2 %collective-permute-start.10 = (f32[12,4,1,4,130]{4,3,2,1,0:T(4,128)S(1)}, f32[12,4,1,4,130]{4,3,2,1,0:T(4,128)S(1)}, u32[]{:S(2)}, u32[]{:S(2)}) collective-permute-start(f32[12,4,1,4,130]{4,3,2,1,0:T(4,128)S(1)} %pad_maximum_fusion.2), channel_id=1, source_target_pairs={{0,8},{4,12},{8,0},{12,4},{16,24},{20,28},{24,16},{28,20},{32,40},... | collective-permute-start | bytes 299528 | tf_op jit(solution)/shard_map/ppermute | solution.py:56
  73.8 11.3 %collective-permute-start.11 = (f32[12,4,1,4,130]{4,3,2,1,0:T(4,128)S(1)}, f32[12,4,1,4,130]{4,3,2,1,0:T(4,128)S(1)}, u32[]{:S(2)}, u32[]{:S(2)}) collective-permute-start(f32[12,4,1,4,130]{4,3,2,1,0:T(4,128)S(1)} %pad_maximum_fusion.3), channel_id=1, source_target_pairs={{0,16},{4,20},{8,24},{12,28},{16,0},{20,4},{24,8},{28,12},{32,48},... | collective-permute-start | bytes 299528 | tf_op jit(solution)/shard_map/ppermute | solution.py:56
  86.2 14.2 %collective-permute-start.12 = (f32[12,4,1,4,130]{4,3,2,1,0:T(4,128)S(1)}, f32[12,4,1,4,130]{4,3,2,1,0:T(4,128)S(1)}, u32[]{:S(2)}, u32[]{:S(2)}) collective-permute-start(f32[12,4,1,4,130]{4,3,2,1,0:T(4,128)S(1)} %pad_maximum_fusion.4), channel_id=1, source_target_pairs={{0,32},{4,36},{8,40},{12,44},{16,48},{20,52},{24,56},{28,60},{32,0... | collective-permute-start | bytes 299528 | tf_op jit(solution)/shard_map/ppermute | solution.py:56
  101.5 6.9 %collective-permute-start.13 = (f32[12,4,1,4,130]{4,3,2,1,0:T(4,128)S(1)}, f32[12,4,1,4,130]{4,3,2,1,0:T(4,128)S(1)}, u32[]{:S(2)}, u32[]{:S(2)}) collective-permute-start(f32[12,4,1,4,130]{4,3,2,1,0:T(4,128)S(1)} %pad_maximum_fusion.5), channel_id=1, source_target_pairs={{0,64},{4,68},{8,72},{12,76},{16,80},{20,84},{24,88},{28,92},{32,9... | collective-permute-start | bytes 299528 | tf_op jit(solution)/shard_map/ppermute | solution.py:56
  109.5 7.6 %collective-permute-start.14 = (f32[12,4,1,4,130]{4,3,2,1,0:T(4,128)S(1)}, f32[12,4,1,4,130]{4,3,2,1,0:T(4,128)S(1)}, u32[]{:S(2)}, u32[]{:S(2)}) collective-permute-start(f32[12,4,1,4,130]{4,3,2,1,0:T(4,128)S(1)} %pad_maximum_fusion.6), channel_id=1, source_target_pairs={{0,128},{4,132},{8,136},{12,140},{16,144},{20,148},{24,152},{28,15... | collective-permute-start | bytes 299528 | tf_op jit(solution)/shard_map/ppermute | solution.py:56
  123.0 4.2 %collective-permute-start.15 = (f32[4,2,640]{2,0,1:T(4,128)S(1)}, f32[4,2,640]{2,0,1:T(4,128)S(1)}, u32[]{:S(2)}, u32[]{:S(2)}) collective-permute-start(f32[4,2,640]{2,0,1:T(4,128)S(1)} %get-tuple-element.59), channel_id=1, source_target_pairs={{0,1},{1,2},{2,3},{3,0},{4,5},{5,6},{6,7},{7,4},{8,9},{9,10},{10,1... | collective-permute-start | bytes 61448 | tf_op jit(solution)/shard_map/ppermute | solution.py:49
  123.1 5.4 %collective-permute-start.16 = (f32[4,2,640]{2,0,1:T(4,128)S(1)}, f32[4,2,640]{2,0,1:T(4,128)S(1)}, u32[]{:S(2)}, u32[]{:S(2)}) collective-permute-start(f32[4,2,640]{2,0,1:T(4,128)S(1)} %get-tuple-element.60), channel_id=1, source_target_pairs={{0,2},{1,3},{2,0},{3,1},{4,6},{5,7},{6,4},{7,5},{8,10},{9,11},{10,... | collective-permute-start | bytes 61448 | tf_op jit(solution)/shard_map/ppermute | solution.py:49
  126.5 3.8 %collective-permute-start.17 = (f32[4,2,640]{2,0,1:T(4,128)S(1)}, f32[4,2,640]{2,0,1:T(4,128)S(1)}, u32[]{:S(2)}, u32[]{:S(2)}) collective-permute-start(f32[4,2,640]{2,0,1:T(4,128)S(1)} %select_bitcast_fusion), channel_id=1, source_target_pairs={{0,3},{1,0},{2,1},{3,2},{4,7},{5,4},{6,5},{7,6},{8,11},{9,8},{10,9... | collective-permute-start | bytes 61448 | tf_op jit(solution)/shard_map/ppermute | solution.py:49

commit v2 on v1

--- a/solution.py
+++ b/solution.py
@@ -1,6 +1,7 @@
 import jax
 import jax.numpy as jnp
 from jax import lax
+from jax.experimental import pallas as pl
 from jax.sharding import PartitionSpec as P
 
 HEAD_SIZE = 128
@@ -28,6 +29,27 @@
     )
 
 
+def _matmul_kernel(x_ref, *refs):
+    count = len(refs) // 2
+    x = x_ref[...]
+    for w_ref, o_ref in zip(refs[:count], refs[count:]):
+        o_ref[...] = jnp.dot(x, w_ref[...], preferred_element_type=jnp.float32)
+
+
+def small_matmul(x, *weights):
+    m, k = x.shape
+    widths = [w.shape[1] for w in weights]
+    return pl.pallas_call(
+        _matmul_kernel,
+        out_shape=[jax.ShapeDtypeStruct((m, n), jnp.float32) for n in widths],
+        cost_estimate=pl.CostEstimate(
+            flops=2 * m * k * sum(widths),
+            bytes_accessed=2 * (m * k + k * sum(widths)) + 4 * m * sum(widths),
+            transcendentals=0,
+        ),
+    )(x, *weights)
+
+
 def gather_mp(block, n_mp):
     me = lax.axis_index("mp")
     pieces = [block] + [
@@ -60,11 +82,12 @@
 
 
 def merge_stats(mine, theirs):
-    top_a = mine[..., -1:]
-    top_b = theirs[..., -1:]
+    top_a = mine[-1:]
+    top_b = theirs[-1:]
     top = jnp.maximum(top_a, top_b)
-    scaled = mine[..., :-1] * jnp.exp(top_a - top) + theirs[..., :-1] * jnp.exp(top_b - top)
-    return jnp.concatenate([scaled, top], axis=-1)
+    scaled = mine * jnp.exp(top_a - top) + theirs * jnp.exp(top_b - top)
+    last = lax.broadcasted_iota(jnp.int32, mine.shape, 0) == mine.shape[0] - 1
+    return jnp.where(last, top, scaled)
 
 
 def shards(
@@ -102,9 +125,10 @@
     positions = (own_len[None, :] + jnp.arange(steps, dtype=jnp.int32)[:, None]).reshape(-1)
     normed = scaled_rms(wide.astype(jnp.float32), norm_gain).astype(jnp.bfloat16)
     rows = steps * own_rows
-    query = jnp.dot(normed, w_query, preferred_element_type=jnp.float32).reshape(rows, q_heads, HEAD_SIZE)
-    keys = jnp.dot(normed, key_matrix, preferred_element_type=jnp.float32).reshape(rows, kv_heads, HEAD_SIZE)
-    values = jnp.dot(normed, value_matrix, preferred_element_type=jnp.float32).astype(jnp.bfloat16)
+    query, keys, values = small_matmul(normed, w_query, key_matrix, value_matrix)
+    query = query.reshape(rows, q_heads, HEAD_SIZE)
+    keys = keys.reshape(rows, kv_heads, HEAD_SIZE)
+    values = values.astype(jnp.bfloat16)
     query = rotate(scaled_rms(query, query_gain), positions).astype(jnp.bfloat16)
     keys = rotate(scaled_rms(keys, key_gain), positions).astype(jnp.bfloat16)
     new_keys = keys.reshape(steps, own_rows, kv_heads * HEAD_SIZE)
@@ -172,8 +196,12 @@
     group_top = jnp.max(jnp.where(member[:, :, None, None, None], reference_top[None], NEGATIVE), axis=1)
     group_total = jnp.einsum("qs,stng->qtng", member_float, slot_total, precision=HIGHEST)
     group_mix = jnp.einsum("qs,stngd->qtngd", member_float, slot_mix, precision=HIGHEST)
-    stats = jnp.concatenate([group_mix, group_total[..., None], group_top[..., None]], axis=-1)
-    long_stats = butterfly(stats[:LONG_COUNT], n_seq, merge_stats)
+    stats = jnp.concatenate(
+        [group_mix, group_total[..., None], group_top[..., None]], axis=-1
+    )
+    long_stats = stats[:LONG_COUNT].reshape(-1, HEAD_SIZE + 2).T
+    long_stats = butterfly(long_stats, n_seq, merge_stats)
+    long_stats = long_stats.T.reshape((LONG_COUNT,) + stats.shape[1:])
     own_rank = jnp.take(rank, own_ids)
     own_is_long = jnp.take(is_long, own_ids)
     from_long = jnp.take(long_stats, jnp.clip(own_rank, 0, LONG_COUNT - 1), axis=0)
@@ -206,7 +234,8 @@
     )
     attended = (mixture / denominator[..., None]).astype(jnp.bfloat16)
     attended = attended.transpose(1, 0, 2, 3, 4).reshape(steps * own_rows, q_heads * HEAD_SIZE)
-    projected = jnp.dot(attended, w_out, preferred_element_type=jnp.float32).reshape(steps, own_rows, -1)
+    (projected,) = small_matmul(attended, w_out)
+    projected = projected.reshape(steps, own_rows, -1)
     summed = reduce_scatter_mp(projected, n_mp)
     hidden = (states.astype(jnp.float32) + summed).astype(jnp.bfloat16)
     return hidden, new_keys, new_values

time: 131 us -> 124 us (0.947)
  the two profiles are of different devices: /device:TPU:12 before, /device:TPU:106 now
where the time goes in v2:
time: 124 us
  waiting for transfers between devices  65.3 us (53%)
  starting transfers between devices  23.1 us (19%)
  other arithmetic  14.7 us (12%)
  local copies, waits for them, and re-layouts  11.7 us (9%)
  Pallas kernels  6.14 us (5%)
  matrix products  1.63 us (1%)
    ppermute x12, waiting for transfers between devices, butterfly(): lax.ppermute(value, 'seq', [(i, i ^ stride) for i in range(n_seq)])  62.1 us
    ppermute x12, starting transfers between devices, butterfly(): lax.ppermute(value, 'seq', [(i, i ^ stride) for i in range(n_seq)])  14.4 us
    pallas_call x2, Pallas kernels, small_matmul(): pl.pallas_call(_matmul_kernel, out_shape=[jax.ShapeDtypeStruct((m, n), jn...  6.14 us
    ppermute x3, starting transfers between devices, gather_mp(): lax.ppermute(block, 'mp', [(i, (i + s) % n_mp) for i in range(n_mp)])  5 us
    ppermute x3, starting transfers between devices, reduce_scatter_mp(): lax.ppermute(outgoing, 'mp', [(i, (i + s) % n_mp) for i in range(n_mp)])  3.64 us
    ppermute x3, waiting for transfers between devices, reduce_scatter_mp(): lax.ppermute(outgoing, 'mp', [(i, (i + s) % n_mp) for i in range(n_mp)])  3.11 us
  transfers between devices with their start and end apart: 18, of which 14 were waited for; matrix products, arithmetic and copies ran while one was open for 11% of the time, Pallas kernels for 0%

profile of v2, /device:TPU:106, one launch (start us, length us, event | category | flops | bytes accessed | tf_op | source)
XLA Modules:
  0.0 123.7 jit_solution(16923000927176287403)
XLA Ops:
  0.7 1.7 %collective-permute-start = (bf16[4,2,640]{2,1,0:T(2,128)(2,1)}, bf16[4,2,640]{2,1,0:T(2,128)(2,1)S(1)}, u32[]{:S(2)}, u32[]{:S(2)}) collective-permute-start(bf16[4,2,640]{2,1,0:T(2,128)(2,1)} %param.20), channel_id=1, source_target_pairs={{0,1},{1,2},{2,3},{3,0},{4,5},{5,6},{6,7},{7,4},{8,9},{9,10},{10,1... | collective-permute-start | bytes 30728 | tf_op jit(solution)/shard_map/ppermute | solution.py:56
  2.3 0.9 collective-permute-start.1
  3.3 2.4 %collective-permute-start.2 = (bf16[4,2,640]{2,1,0:T(2,128)(2,1)}, bf16[4,2,640]{2,1,0:T(2,128)(2,1)S(1)}, u32[]{:S(2)}, u32[]{:S(2)}) collective-permute-start(bf16[4,2,640]{2,1,0:T(2,128)(2,1)} %param.20), channel_id=1, source_target_pairs={{0,3},{1,0},{2,1},{3,2},{4,7},{5,4},{6,5},{7,6},{8,11},{9,8},{10,9... | collective-permute-start | bytes 30728 | tf_op jit(solution)/shard_map/ppermute | solution.py:56
  5.7 0.7 broadcast_compare_fusion.2
  6.7 0.7 compare_select_fusion
  7.5 0.7 gather_fusion.7
  8.2 0.7 gather_fusion.1
  8.9 1.3 %gather_fusion.6 = s32[16]{0:T(128)S(1)} fusion(s32[128]{0:T(128)} %param.30, s32[1024]{0:T(1024)S(1)} %pad_clamp_fusion.3), kind=kCustom, calls=%fused_computation.1.clone | custom fusion | bytes 192 | tf_op jit(solution)/shard_map/jit(_take)/gather | solution.py:174
  10.2 1.3 %gather_fusion.8 = s32[2]{0:T(128)S(1)} fusion(s32[128]{0:T(128)} %param.30, s32[1024]{0:T(1024)S(1)} %pad_clamp_fusion.4), kind=kCustom, calls=%fused_computation.2.clone | custom fusion | bytes 24 | tf_op jit(solution)/shard_map/jit(_take)/gather | solution.py:124
  11.8 0.7 compare_and_fusion.4
  12.5 0.8 compare_and_fusion
  13.3 0.7 compare_and_fusion.1
  14.1 0.7 broadcast_select_fusion.2
  14.9 0.6 gather_fusion.5
  15.5 0.6 gather_fusion
  16.3 0.6 gather_fusion.2
  17.3 0.7 fusion.17.x_ref
  18.0 3.3 %shard_map.157 = (f32[8,512]{1,0:T(8,128)}, f32[8,128]{1,0:T(8,128)}, f32[8,128]{1,0:T(8,128)}) custom-call(bf16[8,2560]{1,0:T(8,128)(2,1)} %fusion.17.x_ref, bf16[2560,512]{1,0:T(8,128)(2,1)} %refs_0_.2, bf16[2560,128]{1,0:T(8,128)(2,1)} %refs_1_.1, bf16[2560,128]{1,0:T(8,128)(2,1)} %refs_2_.1), custom_call_target="tpu_custom_call" | custom-call | flops 31457280 | bytes 3997696 | tf_op jit(solution)/shard_map/pallas_call | solution.py:42
  21.3 0.9 fusion.34
  22.2 0.8 fusion.35
  23.4 1.2 collective-permute-done.3
  24.9 4.0 %collective-permute-done.4 = bf16[12,4,4,128]{3,2,1,0:T(4,128)(2,1)S(1)} collective-permute-done((bf16[12,4,4,128]{3,2,1,0:T(4,128)(2,1)S(1)}, bf16[12,4,4,128]{3,2,1,0:T(4,128)(2,1)S(1)}, u32[]{:S(2)}, u32[]{:S(2)}) %collective-permute-start.4) | collective-permute-done | bytes 49184 | tf_op jit(solution)/shard_map/ppermute | solution.py:78
  29.0 5.0 %collective-permute-done.5 = bf16[12,4,4,128]{3,2,1,0:T(4,128)(2,1)S(1)} collective-permute-done((bf16[12,4,4,128]{3,2,1,0:T(4,128)(2,1)S(1)}, bf16[12,4,4,128]{3,2,1,0:T(4,128)(2,1)S(1)}, u32[]{:S(2)}, u32[]{:S(2)}) %collective-permute-start.5) | collective-permute-done | bytes 49184 | tf_op jit(solution)/shard_map/ppermute | solution.py:78
  34.1 4.5 %collective-permute-start.6 = (bf16[12,4,4,128]{3,2,1,0:T(4,128)(2,1)S(1)}, bf16[12,4,4,128]{3,2,1,0:T(4,128)(2,1)S(1)}, u32[]{:S(2)}, u32[]{:S(2)}) collective-permute-start(bf16[12,4,4,128]{3,2,1,0:T(4,128)(2,1)S(1)} %add.279), channel_id=1, source_target_pairs={{0,32},{4,36},{8,40},{12,44},{16,48},{20,52},{24,56},{28,60},{32,0... | collective-permute-start | bytes 147464 | tf_op jit(solution)/shard_map/ppermute | solution.py:78
  38.6 4.0 %collective-permute-done.6 = bf16[12,4,4,128]{3,2,1,0:T(4,128)(2,1)S(1)} collective-permute-done((bf16[12,4,4,128]{3,2,1,0:T(4,128)(2,1)S(1)}, bf16[12,4,4,128]{3,2,1,0:T(4,128)(2,1)S(1)}, u32[]{:S(2)}, u32[]{:S(2)}) %collective-permute-start.6) | collective-permute-done | bytes 49184 | tf_op jit(solution)/shard_map/ppermute | solution.py:78
  42.6 0.6 collective-permute-start.7
  43.3 3.7 %collective-permute-done.7 = bf16[12,4,4,128]{3,2,1,0:T(4,128)(2,1)S(1)} collective-permute-done((bf16[12,4,4,128]{3,2,1,0:T(4,128)(2,1)S(1)}, bf16[12,4,4,128]{3,2,1,0:T(4,128)(2,1)S(1)}, u32[]{:S(2)}, u32[]{:S(2)}) %collective-permute-start.7) | collective-permute-done | bytes 49184 | tf_op jit(solution)/shard_map/ppermute | solution.py:78
  47.1 2.0 %collective-permute-start.8 = (bf16[12,4,4,128]{3,2,1,0:T(4,128)(2,1)S(1)}, bf16[12,4,4,128]{3,2,1,0:T(4,128)(2,1)S(1)}, u32[]{:S(2)}, u32[]{:S(2)}) collective-permute-start(bf16[12,4,4,128]{3,2,1,0:T(4,128)(2,1)S(1)} %add.281), channel_id=1, source_target_pairs={{0,128},{4,132},{8,136},{12,140},{16,144},{20,148},{24,152},{28,15... | collective-permute-start | bytes 147464 | tf_op jit(solution)/shard_map/ppermute | solution.py:78
  49.0 0.8 multiply_reduce_fusion
  49.8 2.9 %collective-permute-done.8 = bf16[12,4,4,128]{3,2,1,0:T(4,128)(2,1)S(1)} collective-permute-done((bf16[12,4,4,128]{3,2,1,0:T(4,128)(2,1)S(1)}, bf16[12,4,4,128]{3,2,1,0:T(4,128)(2,1)S(1)}, u32[]{:S(2)}, u32[]{:S(2)}) %collective-permute-start.8) | collective-permute-done | bytes 49184 | tf_op jit(solution)/shard_map/ppermute | solution.py:78
  52.9 0.6 gather_fusion.3
  53.5 0.5 select_reduce_fusion
  54.4 0.3 bitcast_reduce_fusion
  54.7 0.3 fusion.1
  55.1 0.3 convolution_bitcast_fusion
  56.1 0.5 copy.209
  56.9 1.4 %collective-permute-done.9 = f32[130,192]{0,1:T(8,128)S(1)} collective-permute-done((f32[130,192]{0,1:T(8,128)S(1)}, f32[130,192]{0,1:T(8,128)S(1)}, u32[]{:S(2)}, u32[]{:S(2)}) %collective-permute-start.9) | collective-permute-done | bytes 99872 | tf_op jit(solution)/shard_map/ppermute | solution.py:78
  58.3 0.3 fusion.67
  59.0 6.8 %collective-permute-done.10 = f32[130,192]{0,1:T(8,128)S(1)} collective-permute-done((f32[130,192]{0,1:T(8,128)S(1)}, f32[130,192]{0,1:T(8,128)S(1)}, u32[]{:S(2)}, u32[]{:S(2)}) %collective-permute-start.10) | collective-permute-done | bytes 99872 | tf_op jit(solution)/shard_map/ppermute | solution.py:78
  65.8 0.3 fusion.68
  66.3 0.3 collective-permute-start.11
  66.7 11.1 %collective-permute-done.11 = f32[130,192]{0,1:T(8,128)S(1)} collective-permute-done((f32[130,192]{0,1:T(8,128)S(1)}, f32[130,192]{0,1:T(8,128)S(1)}, u32[]{:S(2)}, u32[]{:S(2)}) %collective-permute-start.11) | collective-permute-done | bytes 99872 | tf_op jit(solution)/shard_map/ppermute | solution.py:78
  77.8 0.3 fusion.69
  78.2 3.8 %collective-permute-start.12 = (f32[130,192]{0,1:T(8,128)S(1)}, f32[130,192]{0,1:T(8,128)S(1)}, u32[]{:S(2)}, u32[]{:S(2)}) collective-permute-start(f32[130,192]{0,1:T(8,128)S(1)} %add_select_fusion.2), channel_id=1, source_target_pairs={{0,32},{4,36},{8,40},{12,44},{16,48},{20,52},{24,56},{28,60},{32,0... | collective-permute-start | bytes 299528 | tf_op jit(solution)/shard_map/ppermute | solution.py:78
  82.3 10.7 %collective-permute-done.12 = f32[130,192]{0,1:T(8,128)S(1)} collective-permute-done((f32[130,192]{0,1:T(8,128)S(1)}, f32[130,192]{0,1:T(8,128)S(1)}, u32[]{:S(2)}, u32[]{:S(2)}) %collective-permute-start.12) | collective-permute-done | bytes 99872 | tf_op jit(solution)/shard_map/ppermute | solution.py:78
  93.0 0.3 fusion.70
  93.4 0.6 collective-permute-start.13
  94.1 6.2 %collective-permute-done.13 = f32[130,192]{0,1:T(8,128)S(1)} collective-permute-done((f32[130,192]{0,1:T(8,128)S(1)}, f32[130,192]{0,1:T(8,128)S(1)}, u32[]{:S(2)}, u32[]{:S(2)}) %collective-permute-start.13) | collective-permute-done | bytes 99872 | tf_op jit(solution)/shard_map/ppermute | solution.py:78
  100.4 0.3 fusion.71
  100.8 2.1 %collective-permute-start.14 = (f32[130,192]{0,1:T(8,128)S(1)}, f32[130,192]{0,1:T(8,128)S(1)}, u32[]{:S(2)}, u32[]{:S(2)}) collective-permute-start(f32[130,192]{0,1:T(8,128)S(1)} %add_select_fusion), channel_id=1, source_target_pairs={{0,128},{4,132},{8,136},{12,140},{16,144},{20,148},{24,152},{28,15... | collective-permute-start | bytes 299528 | tf_op jit(solution)/shard_map/ppermute | solution.py:78
  102.9 0.4 copy.211
  103.4 5.0 %collective-permute-done.14 = f32[130,192]{0,1:T(8,128)S(1)} collective-permute-done((f32[130,192]{0,1:T(8,128)S(1)}, f32[130,192]{0,1:T(8,128)S(1)}, u32[]{:S(2)}, u32[]{:S(2)}) %collective-permute-start.14) | collective-permute-done | bytes 99872 | tf_op jit(solution)/shard_map/ppermute | solution.py:78
  108.4 0.3 fusion.72
  108.9 0.6 gather_fusion.4
  109.5 0.4 copy.210
  110.5 0.3 copy.218
  111.1 0.6 copy.272
  111.7 2.8 %shard_map.158 = f32[8,2560]{1,0:T(8,128)} custom-call(bf16[8,512]{1,0:T(8,128)(2,1)} %bitcast.175, bf16[512,2560]{1,0:T(8,128)(2,1)} %refs_0_.3), custom_call_target="tpu_custom_call" | custom-call | flops 20971520 | bytes 2711552 | tf_op jit(solution)/shard_map/pallas_call | solution.py:42
  114.6 0.9 reshape_reshape.3
  115.7 3.5 %collective-permute-start.16 = (f32[4,2,640]{2,1,0:T(2,128)S(1)}, f32[4,2,640]{2,1,0:T(2,128)S(1)}, u32[]{:S(2)}, u32[]{:S(2)}) collective-permute-start(f32[4,2,640]{2,1,0:T(2,128)S(1)} %fusion.22), channel_id=1, source_target_pairs={{0,2},{1,3},{2,0},{3,1},{4,6},{5,7},{6,4},{7,5},{8,10},{9,11},{10,... | collective-permute-start | bytes 61448 | tf_op jit(solution)/shard_map/ppermute | solution.py:71
  119.3 0.7 pad_maximum_fusion.4
  120.0 1.1 collective-permute-done.16
  121.1 2.0 %collective-permute-done.17 = f32[4,2,640]{2,1,0:T(2,128)S(1)} collective-permute-done((f32[4,2,640]{2,1,0:T(2,128)S(1)}, f32[4,2,640]{2,1,0:T(2,128)S(1)}, u32[]{:S(2)}, u32[]{:S(2)}) %collective-permute-start.17) | collective-permute-done | bytes 20512 | tf_op jit(solution)/shard_map/ppermute | solution.py:71
  123.1 0.6 fusion.29
  (118 shorter events, 6.8 us)
Async XLA Ops:
  0.6 52.9 %copy-start = (bf16[16,256,128]{2,1,0:T(8,128)(2,1)S(1)}, bf16[16,256,128]{2,1,0:T(8,128)(2,1)}, u32[]{:S(2)}) copy-start(bf16[16,256,128]{2,1,0:T(8,128)(2,1)} %param.28) | copy-start | bytes 3145732
  0.6 15.6 %copy-start.1 = (bf16[4,2,640]{2,1,0:T(2,128)(2,1)S(1)}, bf16[4,2,640]{2,1,0:T(2,128)(2,1)}, u32[]{:S(2)}) copy-start(bf16[4,2,640]{2,1,0:T(2,128)(2,1)} %param.20) | copy-start | bytes 30724
  0.7 16.6 %copy-start.4 = (f32[2560]{0:T(1024)S(1)}, f32[2560]{0:T(1024)}, u32[]{:S(2)}) copy-start(f32[2560]{0:T(1024)} %param.21) | copy-start | bytes 30724
  0.7 15.5 %collective-permute-start = (bf16[4,2,640]{2,1,0:T(2,128)(2,1)}, bf16[4,2,640]{2,1,0:T(2,128)(2,1)S(1)}, u32[]{:S(2)}, u32[]{:S(2)}) collective-permute-start(bf16[4,2,640]{2,1,0:T(2,128)(2,1)} %param.20), channel_id=1, source_target_pairs={{0,1},{1,2},{2,3},{3,0},{4,5},{5,6},{6,7},{7,4},{8,9},{9,10},{10,1... | collective-permute-start | bytes 30728 | tf_op jit(solution)/shard_map/ppermute | solution.py:56
  2.3 13.9 %collective-permute-start.1 = (bf16[4,2,640]{2,1,0:T(2,128)(2,1)}, bf16[4,2,640]{2,1,0:T(2,128)(2,1)S(1)}, u32[]{:S(2)}, u32[]{:S(2)}) collective-permute-start(bf16[4,2,640]{2,1,0:T(2,128)(2,1)} %param.20), channel_id=1, source_target_pairs={{0,2},{1,3},{2,0},{3,1},{4,6},{5,7},{6,4},{7,5},{8,10},{9,11},{10,... | collective-permute-start | bytes 30728 | tf_op jit(solution)/shard_map/ppermute | solution.py:56
  3.3 12.9 %collective-permute-start.2 = (bf16[4,2,640]{2,1,0:T(2,128)(2,1)}, bf16[4,2,640]{2,1,0:T(2,128)(2,1)S(1)}, u32[]{:S(2)}, u32[]{:S(2)}) collective-permute-start(bf16[4,2,640]{2,1,0:T(2,128)(2,1)} %param.20), channel_id=1, source_target_pairs={{0,3},{1,0},{2,1},{3,2},{4,7},{5,4},{6,5},{7,6},{8,11},{9,8},{10,9... | collective-permute-start | bytes 30728 | tf_op jit(solution)/shard_map/ppermute | solution.py:56
  15.5 6.7 %copy-start.7 = (f32[128]{0:T(128)S(1)}, f32[128]{0:T(128)}, u32[]{:S(2)}) copy-start(f32[128]{0:T(128)} %param.22) | copy-start | bytes 1540
  21.3 33.4 %copy-start.9 = (bf16[16,256,128]{2,1,0:T(8,128)(2,1)S(1)}, bf16[16,256,128]{2,1,0:T(8,128)(2,1)}, u32[]{:S(2)}) copy-start(bf16[16,256,128]{2,1,0:T(8,128)(2,1)} %param.29) | copy-start | bytes 3145732
  21.3 33.8 %copy-start.2 = (s32[16]{0:T(128)S(1)}, s32[16]{0:T(128)}, u32[]{:S(2)}) copy-start(s32[16]{0:T(128)} %param.31) | copy-start | bytes 196
  23.3 1.3 %collective-permute-start.3 = (bf16[12,4,4,128]{3,2,1,0:T(4,128)(2,1)S(1)}, bf16[12,4,4,128]{3,2,1,0:T(4,128)(2,1)S(1)}, u32[]{:S(2)}, u32[]{:S(2)}) collective-permute-start(bf16[12,4,4,128]{3,2,1,0:T(4,128)(2,1)S(1)} %select_reduce_fusion.3), channel_id=1, source_target_pairs={{0,4},{4,0},{8,12},{12,8},{16,20},{20,16},{24,28},{28,24},{32,36},... | collective-permute-start | bytes 147464 | tf_op jit(solution)/shard_map/ppermute | solution.py:78
  24.7 4.2 %collective-permute-start.4 = (bf16[12,4,4,128]{3,2,1,0:T(4,128)(2,1)S(1)}, bf16[12,4,4,128]{3,2,1,0:T(4,128)(2,1)S(1)}, u32[]{:S(2)}, u32[]{:S(2)}) collective-permute-start(bf16[12,4,4,128]{3,2,1,0:T(4,128)(2,1)S(1)} %add.277), channel_id=1, source_target_pairs={{0,8},{4,12},{8,0},{12,4},{16,24},{20,28},{24,16},{28,20},{32,40},... | collective-permute-start | bytes 147464 | tf_op jit(solution)/shard_map/ppermute | solution.py:78
  28.9 5.1 %collective-permute-start.5 = (bf16[12,4,4,128]{3,2,1,0:T(4,128)(2,1)S(1)}, bf16[12,4,4,128]{3,2,1,0:T(4,128)(2,1)S(1)}, u32[]{:S(2)}, u32[]{:S(2)}) collective-permute-start(bf16[12,4,4,128]{3,2,1,0:T(4,128)(2,1)S(1)} %add.278), channel_id=1, source_target_pairs={{0,16},{4,20},{8,24},{12,28},{16,0},{20,4},{24,8},{28,12},{32,48},... | collective-permute-start | bytes 147464 | tf_op jit(solution)/shard_map/ppermute | solution.py:78
  34.1 8.5 %collective-permute-start.6 = (bf16[12,4,4,128]{3,2,1,0:T(4,128)(2,1)S(1)}, bf16[12,4,4,128]{3,2,1,0:T(4,128)(2,1)S(1)}, u32[]{:S(2)}, u32[]{:S(2)}) collective-permute-start(bf16[12,4,4,128]{3,2,1,0:T(4,128)(2,1)S(1)} %add.279), channel_id=1, source_target_pairs={{0,32},{4,36},{8,40},{12,44},{16,48},{20,52},{24,56},{28,60},{32,0... | collective-permute-start | bytes 147464 | tf_op jit(solution)/shard_map/ppermute | solution.py:78
  42.6 4.4 %collective-permute-start.7 = (bf16[12,4,4,128]{3,2,1,0:T(4,128)(2,1)S(1)}, bf16[12,4,4,128]{3,2,1,0:T(4,128)(2,1)S(1)}, u32[]{:S(2)}, u32[]{:S(2)}) collective-permute-start(bf16[12,4,4,128]{3,2,1,0:T(4,128)(2,1)S(1)} %add.280), channel_id=1, source_target_pairs={{0,64},{4,68},{8,72},{12,76},{16,80},{20,84},{24,88},{28,92},{32,9... | collective-permute-start | bytes 147464 | tf_op jit(solution)/shard_map/ppermute | solution.py:78
  47.1 5.7 %collective-permute-start.8 = (bf16[12,4,4,128]{3,2,1,0:T(4,128)(2,1)S(1)}, bf16[12,4,4,128]{3,2,1,0:T(4,128)(2,1)S(1)}, u32[]{:S(2)}, u32[]{:S(2)}) collective-permute-start(bf16[12,4,4,128]{3,2,1,0:T(4,128)(2,1)S(1)} %add.281), channel_id=1, source_target_pairs={{0,128},{4,132},{8,136},{12,140},{16,144},{20,148},{24,152},{28,15... | collective-permute-start | bytes 147464 | tf_op jit(solution)/shard_map/ppermute | solution.py:78
  54.2 4.7 %copy-start.3 = (f32[8,128]{1,0:T(8,128)S(1)}, f32[8,128]{1,0:T(8,128)}, u32[]{:S(2)}) copy-start(f32[8,128]{1,0:T(8,128)} %get-tuple-element.10) | copy-start | bytes 12292
  54.2 4.7 %copy-start.8 = (f32[128]{0:T(128)S(1)}, f32[128]{0:T(128)}, u32[]{:S(2)}) copy-start(f32[128]{0:T(128)} %param.23) | copy-start | bytes 1540
  55.1 27.1 %copy-start.6 = (f32[8,128]{1,0:T(8,128)S(1)}, f32[8,128]{1,0:T(8,128)}, u32[]{:S(2)}) copy-start(f32[8,128]{1,0:T(8,128)} %get-tuple-element.11) | copy-start | bytes 12292
  56.8 1.5 %collective-permute-start.9 = (f32[130,192]{0,1:T(8,128)S(1)}, f32[130,192]{0,1:T(8,128)S(1)}, u32[]{:S(2)}, u32[]{:S(2)}) collective-permute-start(f32[130,192]{0,1:T(8,128)S(1)} %bitcast.171), channel_id=1, source_target_pairs={{0,4},{4,0},{8,12},{12,8},{16,20},{20,16},{24,28},{28,24},{32,36},... | collective-permute-start | bytes 299528 | tf_op jit(solution)/shard_map/ppermute | solution.py:78
  58.8 7.0 %collective-permute-start.10 = (f32[130,192]{0,1:T(8,128)S(1)}, f32[130,192]{0,1:T(8,128)S(1)}, u32[]{:S(2)}, u32[]{:S(2)}) collective-permute-start(f32[130,192]{0,1:T(8,128)S(1)} %add_select_fusion.4), channel_id=1, source_target_pairs={{0,8},{4,12},{8,0},{12,4},{16,24},{20,28},{24,16},{28,20},{32,40},... | collective-permute-start | bytes 299528 | tf_op jit(solution)/shard_map/ppermute | solution.py:78
  66.3 11.5 %collective-permute-start.11 = (f32[130,192]{0,1:T(8,128)S(1)}, f32[130,192]{0,1:T(8,128)S(1)}, u32[]{:S(2)}, u32[]{:S(2)}) collective-permute-start(f32[130,192]{0,1:T(8,128)S(1)} %add_select_fusion.3), channel_id=1, source_target_pairs={{0,16},{4,20},{8,24},{12,28},{16,0},{20,4},{24,8},{28,12},{32,48},... | collective-permute-start | bytes 299528 | tf_op jit(solution)/shard_map/ppermute | solution.py:78
  78.2 14.8 %collective-permute-start.12 = (f32[130,192]{0,1:T(8,128)S(1)}, f32[130,192]{0,1:T(8,128)S(1)}, u32[]{:S(2)}, u32[]{:S(2)}) collective-permute-start(f32[130,192]{0,1:T(8,128)S(1)} %add_select_fusion.2), channel_id=1, source_target_pairs={{0,32},{4,36},{8,40},{12,44},{16,48},{20,52},{24,56},{28,60},{32,0... | collective-permute-start | bytes 299528 | tf_op jit(solution)/shard_map/ppermute | solution.py:78
  82.2 28.1 %copy-start.5 = (bf16[8,128]{1,0:T(8,128)(2,1)}, bf16[8,128]{1,0:T(8,128)(2,1)S(1)}, u32[]{:S(2)}) copy-start(bf16[8,128]{1,0:T(8,128)(2,1)S(1)} %convert_element_type.58) | copy-start | bytes 6148
  93.4 6.9 %collective-permute-start.13 = (f32[130,192]{0,1:T(8,128)S(1)}, f32[130,192]{0,1:T(8,128)S(1)}, u32[]{:S(2)}, u32[]{:S(2)}) collective-permute-start(f32[130,192]{0,1:T(8,128)S(1)} %add_select_fusion.1), channel_id=1, source_target_pairs={{0,64},{4,68},{8,72},{12,76},{16,80},{20,84},{24,88},{28,92},{32,9... | collective-permute-start | bytes 299528 | tf_op jit(solution)/shard_map/ppermute | solution.py:78
  100.8 7.6 %collective-permute-start.14 = (f32[130,192]{0,1:T(8,128)S(1)}, f32[130,192]{0,1:T(8,128)S(1)}, u32[]{:S(2)}, u32[]{:S(2)}) collective-permute-start(f32[130,192]{0,1:T(8,128)S(1)} %add_select_fusion), channel_id=1, source_target_pairs={{0,128},{4,132},{8,136},{12,140},{16,144},{20,148},{24,152},{28,15... | collective-permute-start | bytes 299528 | tf_op jit(solution)/shard_map/ppermute | solution.py:78
  115.6 4.4 %collective-permute-start.15 = (f32[4,2,640]{2,1,0:T(2,128)S(1)}, f32[4,2,640]{2,1,0:T(2,128)S(1)}, u32[]{:S(2)}, u32[]{:S(2)}) collective-permute-start(f32[4,2,640]{2,1,0:T(2,128)S(1)} %fusion.23), channel_id=1, source_target_pairs={{0,1},{1,2},{2,3},{3,0},{4,5},{5,6},{6,7},{7,4},{8,9},{9,10},{10,1... | collective-permute-start | bytes 61448 | tf_op jit(solution)/shard_map/ppermute | solution.py:71
  115.7 5.4 %collective-permute-start.16 = (f32[4,2,640]{2,1,0:T(2,128)S(1)}, f32[4,2,640]{2,1,0:T(2,128)S(1)}, u32[]{:S(2)}, u32[]{:S(2)}) collective-permute-start(f32[4,2,640]{2,1,0:T(2,128)S(1)} %fusion.22), channel_id=1, source_target_pairs={{0,2},{1,3},{2,0},{3,1},{4,6},{5,7},{6,4},{7,5},{8,10},{9,11},{10,... | collective-permute-start | bytes 61448 | tf_op jit(solution)/shard_map/ppermute | solution.py:71
  119.2 3.9 %collective-permute-start.17 = (f32[4,2,640]{2,1,0:T(2,128)S(1)}, f32[4,2,640]{2,1,0:T(2,128)S(1)}, u32[]{:S(2)}, u32[]{:S(2)}) collective-permute-start(f32[4,2,640]{2,1,0:T(2,128)S(1)} %fusion.21), channel_id=1, source_target_pairs={{0,3},{1,0},{2,1},{3,2},{4,7},{5,4},{6,5},{7,6},{8,11},{9,8},{10,9... | collective-permute-start | bytes 61448 | tf_op jit(solution)/shard_map/ppermute | solution.py:71

commit v3 on v2

--- a/solution.py
+++ b/solution.py
@@ -82,12 +82,49 @@
 
 
 def merge_stats(mine, theirs):
-    top_a = mine[-1:]
-    top_b = theirs[-1:]
+    mix_a, stats_a = mine
+    mix_b, stats_b = theirs
+    top_a = stats_a[1:]
+    top_b = stats_b[1:]
     top = jnp.maximum(top_a, top_b)
-    scaled = mine * jnp.exp(top_a - top) + theirs * jnp.exp(top_b - top)
-    last = lax.broadcasted_iota(jnp.int32, mine.shape, 0) == mine.shape[0] - 1
-    return jnp.where(last, top, scaled)
+    scale_a = jnp.exp(top_a - top)
+    scale_b = jnp.exp(top_b - top)
+    mix = mix_a * scale_a + mix_b.astype(jnp.float32) * scale_b
+    total = stats_a[:1] * scale_a + stats_b[:1] * scale_b
+    return mix, jnp.concatenate([total, top], axis=0)
+
+
+def split_exact(x):
+    hi = lax.reduce_precision(x, exponent_bits=8, mantissa_bits=7)
+    rest = x - hi
+    mid = lax.reduce_precision(rest, exponent_bits=8, mantissa_bits=7)
+    lo = rest - mid
+    return jnp.concatenate([hi, mid, lo], axis=0).astype(jnp.bfloat16)
+
+
+def join_exact(parts):
+    parts = parts.astype(jnp.float32)
+    return parts[0:1] + parts[1:2] + parts[2:3]
+
+
+def stats_butterfly(mix, stats, n_seq):
+    width = mix.shape[0]
+    stride = 1
+    while stride < n_seq:
+        pairs = [(i, i ^ stride) for i in range(n_seq)]
+        packed = jnp.concatenate(
+            [mix.astype(jnp.bfloat16), split_exact(stats[:1]), split_exact(stats[1:])], axis=0
+        )
+        arrived = lax.ppermute(packed, "seq", pairs)
+        theirs = (
+            arrived[:width],
+            jnp.concatenate(
+                [join_exact(arrived[width : width + 3]), join_exact(arrived[width + 3 : width + 6])], axis=0
+            ),
+        )
+        mix, stats = merge_stats((mix, stats), theirs)
+        stride *= 2
+    return mix, stats
 
 
 def shards(
@@ -200,7 +237,8 @@
         [group_mix, group_total[..., None], group_top[..., None]], axis=-1
     )
     long_stats = stats[:LONG_COUNT].reshape(-1, HEAD_SIZE + 2).T
-    long_stats = butterfly(long_stats, n_seq, merge_stats)
+    long_mix, long_small = stats_butterfly(long_stats[:HEAD_SIZE], long_stats[HEAD_SIZE:], n_seq)
+    long_stats = jnp.concatenate([long_mix, long_small], axis=0)
     long_stats = long_stats.T.reshape((LONG_COUNT,) + stats.shape[1:])
     own_rank = jnp.take(rank, own_ids)
     own_is_long = jnp.take(is_long, own_ids)

time: 124 us -> 105 us (0.85)
  the two profiles are of different devices: /device:TPU:106 before, /device:TPU:12 now
where the time goes in v3:
time: 105 us
  waiting for transfers between devices  35.4 us (34%)
  starting transfers between devices  35.1 us (33%)
  other arithmetic  13.4 us (13%)
  local copies, waits for them, and re-layouts  12.1 us (12%)
  Pallas kernels  6.14 us (6%)
  matrix products  1.63 us (2%)
  between operations  1.21 us (1%)
    ppermute x6, waiting for transfers between devices, stats_butterfly(): arrived = lax.ppermute(packed, 'seq', pairs)  17.5 us
    ppermute x6, waiting for transfers between devices, butterfly(): lax.ppermute(value, 'seq', [(i, i ^ stride) for i in range(n_seq)])  14.8 us
    ppermute x6, starting transfers between devices, butterfly(): lax.ppermute(value, 'seq', [(i, i ^ stride) for i in range(n_seq)])  13.3 us
    ppermute x6, starting transfers between devices, stats_butterfly(): arrived = lax.ppermute(packed, 'seq', pairs)  13.2 us
    pallas_call x2, Pallas kernels, small_matmul(): pl.pallas_call(_matmul_kernel, out_shape=[jax.ShapeDtypeStruct((m, n), jn...  6.14 us
    ppermute x3, starting transfers between devices, gather_mp(): lax.ppermute(block, 'mp', [(i, (i + s) % n_mp) for i in range(n_mp)])  5 us
    ppermute x3, starting transfers between devices, reduce_scatter_mp(): lax.ppermute(outgoing, 'mp', [(i, (i + s) % n_mp) for i in range(n_mp)])  3.65 us
    ppermute x3, waiting for transfers between devices, reduce_scatter_mp(): lax.ppermute(outgoing, 'mp', [(i, (i + s) % n_mp) for i in range(n_mp)])  3.11 us
  transfers between devices with their start and end apart: 18, of which 13 were waited for; matrix products, arithmetic and copies ran while one was open for 12% of the time, Pallas kernels for 0%

profile of v3, /device:TPU:12, one launch (start us, length us, event | category | flops | bytes accessed | tf_op | source)
XLA Modules:
  0.0 105.0 jit_solution(17357778737831006909)
XLA Ops:
  0.7 1.7 %collective-permute-start = (bf16[4,2,640]{2,1,0:T(2,128)(2,1)}, bf16[4,2,640]{2,1,0:T(2,128)(2,1)S(1)}, u32[]{:S(2)}, u32[]{:S(2)}) collective-permute-start(bf16[4,2,640]{2,1,0:T(2,128)(2,1)} %param.20), channel_id=1, source_target_pairs={{0,1},{1,2},{2,3},{3,0},{4,5},{5,6},{6,7},{7,4},{8,9},{9,10},{10,1... | collective-permute-start | bytes 30728 | tf_op jit(solution)/shard_map/ppermute | solution.py:56
  2.3 0.9 collective-permute-start.1
  3.3 2.4 %collective-permute-start.2 = (bf16[4,2,640]{2,1,0:T(2,128)(2,1)}, bf16[4,2,640]{2,1,0:T(2,128)(2,1)S(1)}, u32[]{:S(2)}, u32[]{:S(2)}) collective-permute-start(bf16[4,2,640]{2,1,0:T(2,128)(2,1)} %param.20), channel_id=1, source_target_pairs={{0,3},{1,0},{2,1},{3,2},{4,7},{5,4},{6,5},{7,6},{8,11},{9,8},{10,9... | collective-permute-start | bytes 30728 | tf_op jit(solution)/shard_map/ppermute | solution.py:56
  5.7 0.7 broadcast_compare_fusion.2
  6.8 0.7 compare_select_fusion
  7.6 0.7 gather_fusion.7
  8.2 0.7 gather_fusion.1
  8.9 1.3 %gather_fusion.6 = s32[16]{0:T(128)S(1)} fusion(s32[128]{0:T(128)} %param.30, s32[1024]{0:T(1024)S(1)} %pad_clamp_fusion.3), kind=kCustom, calls=%fused_computation.1.clone | custom fusion | bytes 192 | tf_op jit(solution)/shard_map/jit(_take)/gather | solution.py:211
  10.2 1.3 %gather_fusion.8 = s32[2]{0:T(128)S(1)} fusion(s32[128]{0:T(128)} %param.30, s32[1024]{0:T(1024)S(1)} %pad_clamp_fusion.4), kind=kCustom, calls=%fused_computation.2.clone | custom fusion | bytes 24 | tf_op jit(solution)/shard_map/jit(_take)/gather | solution.py:161
  11.8 0.7 compare_and_fusion.4
  12.5 0.8 compare_and_fusion
  13.3 0.7 compare_and_fusion.1
  14.1 0.7 broadcast_select_fusion.2
  14.9 0.8 pad_maximum_fusion.1
  15.7 0.6 gather_fusion.2
  16.7 0.7 fusion.17.x_ref
  17.4 3.3 %shard_map.157 = (f32[8,512]{1,0:T(8,128)}, f32[8,128]{1,0:T(8,128)}, f32[8,128]{1,0:T(8,128)}) custom-call(bf16[8,2560]{1,0:T(8,128)(2,1)} %fusion.17.x_ref, bf16[2560,512]{1,0:T(8,128)(2,1)} %refs_0_.2, bf16[2560,128]{1,0:T(8,128)(2,1)} %refs_1_.1, bf16[2560,128]{1,0:T(8,128)(2,1)} %refs_2_.1), custom_call_target="tpu_custom_call" | custom-call | flops 31457280 | bytes 3997696 | tf_op jit(solution)/shard_map/pallas_call | solution.py:42
  20.7 0.9 fusion.36
  21.6 0.8 fusion.37
  22.8 0.6 gather_fusion.5
  23.5 0.6 gather_fusion
  24.2 2.0 %collective-permute-start.4 = (bf16[12,4,4,128]{3,2,1,0:T(4,128)(2,1)S(1)}, bf16[12,4,4,128]{3,2,1,0:T(4,128)(2,1)S(1)}, u32[]{:S(2)}, u32[]{:S(2)}) collective-permute-start(bf16[12,4,4,128]{3,2,1,0:T(4,128)(2,1)S(1)} %add.367), channel_id=1, source_target_pairs={{0,8},{4,12},{8,0},{12,4},{16,24},{20,28},{24,16},{28,20},{32,40},... | collective-permute-start | bytes 147464 | tf_op jit(solution)/shard_map/ppermute | solution.py:78
  26.2 2.4 %collective-permute-done.4 = bf16[12,4,4,128]{3,2,1,0:T(4,128)(2,1)S(1)} collective-permute-done((bf16[12,4,4,128]{3,2,1,0:T(4,128)(2,1)S(1)}, bf16[12,4,4,128]{3,2,1,0:T(4,128)(2,1)S(1)}, u32[]{:S(2)}, u32[]{:S(2)}) %collective-permute-start.4) | collective-permute-done | bytes 49184 | tf_op jit(solution)/shard_map/ppermute | solution.py:78
  28.6 3.4 %collective-permute-start.5 = (bf16[12,4,4,128]{3,2,1,0:T(4,128)(2,1)S(1)}, bf16[12,4,4,128]{3,2,1,0:T(4,128)(2,1)S(1)}, u32[]{:S(2)}, u32[]{:S(2)}) collective-permute-start(bf16[12,4,4,128]{3,2,1,0:T(4,128)(2,1)S(1)} %add.368), channel_id=1, source_target_pairs={{0,16},{4,20},{8,24},{12,28},{16,0},{20,4},{24,8},{28,12},{32,48},... | collective-permute-start | bytes 147464 | tf_op jit(solution)/shard_map/ppermute | solution.py:78
  32.0 2.6 %collective-permute-done.5 = bf16[12,4,4,128]{3,2,1,0:T(4,128)(2,1)S(1)} collective-permute-done((bf16[12,4,4,128]{3,2,1,0:T(4,128)(2,1)S(1)}, bf16[12,4,4,128]{3,2,1,0:T(4,128)(2,1)S(1)}, u32[]{:S(2)}, u32[]{:S(2)}) %collective-permute-start.5) | collective-permute-done | bytes 49184 | tf_op jit(solution)/shard_map/ppermute | solution.py:78
  34.6 6.2 %collective-permute-start.6 = (bf16[12,4,4,128]{3,2,1,0:T(4,128)(2,1)S(1)}, bf16[12,4,4,128]{3,2,1,0:T(4,128)(2,1)S(1)}, u32[]{:S(2)}, u32[]{:S(2)}) collective-permute-start(bf16[12,4,4,128]{3,2,1,0:T(4,128)(2,1)S(1)} %add.369), channel_id=1, source_target_pairs={{0,32},{4,36},{8,40},{12,44},{16,48},{20,52},{24,56},{28,60},{32,0... | collective-permute-start | bytes 147464 | tf_op jit(solution)/shard_map/ppermute | solution.py:78
  40.8 2.2 %collective-permute-done.6 = bf16[12,4,4,128]{3,2,1,0:T(4,128)(2,1)S(1)} collective-permute-done((bf16[12,4,4,128]{3,2,1,0:T(4,128)(2,1)S(1)}, bf16[12,4,4,128]{3,2,1,0:T(4,128)(2,1)S(1)}, u32[]{:S(2)}, u32[]{:S(2)}) %collective-permute-start.6) | collective-permute-done | bytes 49184 | tf_op jit(solution)/shard_map/ppermute | solution.py:78
  43.0 1.3 %collective-permute-start.7 = (bf16[12,4,4,128]{3,2,1,0:T(4,128)(2,1)S(1)}, bf16[12,4,4,128]{3,2,1,0:T(4,128)(2,1)S(1)}, u32[]{:S(2)}, u32[]{:S(2)}) collective-permute-start(bf16[12,4,4,128]{3,2,1,0:T(4,128)(2,1)S(1)} %add.370), channel_id=1, source_target_pairs={{0,64},{4,68},{8,72},{12,76},{16,80},{20,84},{24,88},{28,92},{32,9... | collective-permute-start | bytes 147464 | tf_op jit(solution)/shard_map/ppermute | solution.py:78
  44.4 3.1 %collective-permute-done.7 = bf16[12,4,4,128]{3,2,1,0:T(4,128)(2,1)S(1)} collective-permute-done((bf16[12,4,4,128]{3,2,1,0:T(4,128)(2,1)S(1)}, bf16[12,4,4,128]{3,2,1,0:T(4,128)(2,1)S(1)}, u32[]{:S(2)}, u32[]{:S(2)}) %collective-permute-start.7) | collective-permute-done | bytes 49184 | tf_op jit(solution)/shard_map/ppermute | solution.py:78
  47.5 0.3 collective-permute-start.8
  47.8 0.8 multiply_reduce_fusion
  48.6 4.6 %collective-permute-done.8 = bf16[12,4,4,128]{3,2,1,0:T(4,128)(2,1)S(1)} collective-permute-done((bf16[12,4,4,128]{3,2,1,0:T(4,128)(2,1)S(1)}, bf16[12,4,4,128]{3,2,1,0:T(4,128)(2,1)S(1)}, u32[]{:S(2)}, u32[]{:S(2)}) %collective-permute-start.8) | collective-permute-done | bytes 49184 | tf_op jit(solution)/shard_map/ppermute | solution.py:78
  53.3 0.6 gather_fusion.3
  53.9 0.5 select_reduce_fusion
  54.8 0.3 bitcast_reduce_fusion
  55.2 0.3 fusion.1
  55.5 0.3 convolution_bitcast_fusion
  56.1 0.2 copy.184
  56.5 0.5 copy.185
  57.5 1.2 %collective-permute-done.9 = bf16[134,192]{1,0:T(8,128)(2,1)S(1)} collective-permute-done((bf16[134,192]{1,0:T(8,128)(2,1)S(1)}, bf16[134,192]{1,0:T(8,128)(2,1)S(1)}, u32[]{:S(2)}, u32[]{:S(2)}) %collective-permute-start.9) | collective-permute-done | bytes 51488 | tf_op jit(solution)/shard_map/ppermute | solution.py:118
  58.9 1.7 %collective-permute-start.10 = (bf16[134,192]{1,0:T(8,128)(2,1)S(1)}, bf16[134,192]{1,0:T(8,128)(2,1)S(1)}, u32[]{:S(2)}, u32[]{:S(2)}) collective-permute-start(bf16[134,192]{1,0:T(8,128)(2,1)S(1)} %concatenate.118), channel_id=1, source_target_pairs={{0,8},{4,12},{8,0},{12,4},{16,24},{20,28},{24,16},{28,20},{32,40},... | collective-permute-start | bytes 154376 | tf_op jit(solution)/shard_map/ppermute | solution.py:118
  60.7 2.6 %collective-permute-done.10 = bf16[134,192]{1,0:T(8,128)(2,1)S(1)} collective-permute-done((bf16[134,192]{1,0:T(8,128)(2,1)S(1)}, bf16[134,192]{1,0:T(8,128)(2,1)S(1)}, u32[]{:S(2)}, u32[]{:S(2)}) %collective-permute-start.10) | collective-permute-done | bytes 51488 | tf_op jit(solution)/shard_map/ppermute | solution.py:118
  63.4 2.9 %collective-permute-start.11 = (bf16[134,192]{1,0:T(8,128)(2,1)S(1)}, bf16[134,192]{1,0:T(8,128)(2,1)S(1)}, u32[]{:S(2)}, u32[]{:S(2)}) collective-permute-start(bf16[134,192]{1,0:T(8,128)(2,1)S(1)} %concatenate.119), channel_id=1, source_target_pairs={{0,16},{4,20},{8,24},{12,28},{16,0},{20,4},{24,8},{28,12},{32,48},... | collective-permute-start | bytes 154376 | tf_op jit(solution)/shard_map/ppermute | solution.py:118
  66.4 2.3 %collective-permute-done.11 = bf16[134,192]{1,0:T(8,128)(2,1)S(1)} collective-permute-done((bf16[134,192]{1,0:T(8,128)(2,1)S(1)}, bf16[134,192]{1,0:T(8,128)(2,1)S(1)}, u32[]{:S(2)}, u32[]{:S(2)}) %collective-permute-start.11) | collective-permute-done | bytes 51488 | tf_op jit(solution)/shard_map/ppermute | solution.py:118
  68.9 7.4 %collective-permute-start.12 = (bf16[134,192]{1,0:T(8,128)(2,1)S(1)}, bf16[134,192]{1,0:T(8,128)(2,1)S(1)}, u32[]{:S(2)}, u32[]{:S(2)}) collective-permute-start(bf16[134,192]{1,0:T(8,128)(2,1)S(1)} %concatenate.120), channel_id=1, source_target_pairs={{0,32},{4,36},{8,40},{12,44},{16,48},{20,52},{24,56},{28,60},{32,0... | collective-permute-start | bytes 154376 | tf_op jit(solution)/shard_map/ppermute | solution.py:118
  76.2 0.2 convolution_multiply_fusion.1
  76.4 2.8 %collective-permute-done.12 = bf16[134,192]{1,0:T(8,128)(2,1)S(1)} collective-permute-done((bf16[134,192]{1,0:T(8,128)(2,1)S(1)}, bf16[134,192]{1,0:T(8,128)(2,1)S(1)}, u32[]{:S(2)}, u32[]{:S(2)}) %collective-permute-start.12) | collective-permute-done | bytes 51488 | tf_op jit(solution)/shard_map/ppermute | solution.py:118
  79.4 0.8 collective-permute-start.13
  80.3 3.5 %collective-permute-done.13 = bf16[134,192]{1,0:T(8,128)(2,1)S(1)} collective-permute-done((bf16[134,192]{1,0:T(8,128)(2,1)S(1)}, bf16[134,192]{1,0:T(8,128)(2,1)S(1)}, u32[]{:S(2)}, u32[]{:S(2)}) %collective-permute-start.13) | collective-permute-done | bytes 51488 | tf_op jit(solution)/shard_map/ppermute | solution.py:118
  83.9 0.4 collective-permute-start.14
  84.4 0.4 copy.189
  84.8 5.0 %collective-permute-done.14 = bf16[134,192]{1,0:T(8,128)(2,1)S(1)} collective-permute-done((bf16[134,192]{1,0:T(8,128)(2,1)S(1)}, bf16[134,192]{1,0:T(8,128)(2,1)S(1)}, u32[]{:S(2)}, u32[]{:S(2)}) %collective-permute-start.14) | collective-permute-done | bytes 51488 | tf_op jit(solution)/shard_map/ppermute | solution.py:118
  90.1 0.6 gather_fusion.4
  90.7 0.4 copy.188
  91.1 0.2 fusion.4
  91.7 0.3 copy.196
  92.4 0.6 copy.250
  93.0 2.8 %shard_map.158 = f32[8,2560]{1,0:T(8,128)} custom-call(bf16[8,512]{1,0:T(8,128)(2,1)} %bitcast.191, bf16[512,2560]{1,0:T(8,128)(2,1)} %refs_0_.3), custom_call_target="tpu_custom_call" | custom-call | flops 20971520 | bytes 2711552 | tf_op jit(solution)/shard_map/pallas_call | solution.py:42
  95.8 0.9 reshape_reshape.3
  97.0 3.5 %collective-permute-start.16 = (f32[4,2,640]{2,1,0:T(2,128)S(1)}, f32[4,2,640]{2,1,0:T(2,128)S(1)}, u32[]{:S(2)}, u32[]{:S(2)}) collective-permute-start(f32[4,2,640]{2,1,0:T(2,128)S(1)} %fusion.24), channel_id=1, source_target_pairs={{0,2},{1,3},{2,0},{3,1},{4,6},{5,7},{6,4},{7,5},{8,10},{9,11},{10,... | collective-permute-start | bytes 61448 | tf_op jit(solution)/shard_map/ppermute | solution.py:71
  100.6 0.7 pad_maximum_fusion.4
  101.2 1.1 %collective-permute-done.16 = f32[4,2,640]{2,1,0:T(2,128)S(1)} collective-permute-done((f32[4,2,640]{2,1,0:T(2,128)S(1)}, f32[4,2,640]{2,1,0:T(2,128)S(1)}, u32[]{:S(2)}, u32[]{:S(2)}) %collective-permute-start.16) | collective-permute-done | bytes 20512 | tf_op jit(solution)/shard_map/ppermute | solution.py:71
  102.4 2.0 %collective-permute-done.17 = f32[4,2,640]{2,1,0:T(2,128)S(1)} collective-permute-done((f32[4,2,640]{2,1,0:T(2,128)S(1)}, f32[4,2,640]{2,1,0:T(2,128)S(1)}, u32[]{:S(2)}, u32[]{:S(2)}) %collective-permute-start.17) | collective-permute-done | bytes 20512 | tf_op jit(solution)/shard_map/ppermute | solution.py:71
  104.3 0.6 fusion.31
  (144 shorter events, 5.8 us)
Async XLA Ops:
  0.6 53.3 %copy-start = (bf16[16,256,128]{2,1,0:T(8,128)(2,1)S(1)}, bf16[16,256,128]{2,1,0:T(8,128)(2,1)}, u32[]{:S(2)}) copy-start(bf16[16,256,128]{2,1,0:T(8,128)(2,1)} %param.28) | copy-start | bytes 3145732
  0.6 16.1 %copy-start.4 = (f32[2560]{0:T(1024)S(1)}, f32[2560]{0:T(1024)}, u32[]{:S(2)}) copy-start(f32[2560]{0:T(1024)} %param.21) | copy-start | bytes 30724
  0.7 14.2 %collective-permute-start = (bf16[4,2,640]{2,1,0:T(2,128)(2,1)}, bf16[4,2,640]{2,1,0:T(2,128)(2,1)S(1)}, u32[]{:S(2)}, u32[]{:S(2)}) collective-permute-start(bf16[4,2,640]{2,1,0:T(2,128)(2,1)} %param.20), channel_id=1, source_target_pairs={{0,1},{1,2},{2,3},{3,0},{4,5},{5,6},{6,7},{7,4},{8,9},{9,10},{10,1... | collective-permute-start | bytes 30728 | tf_op jit(solution)/shard_map/ppermute | solution.py:56
  2.3 12.6 %collective-permute-start.1 = (bf16[4,2,640]{2,1,0:T(2,128)(2,1)}, bf16[4,2,640]{2,1,0:T(2,128)(2,1)S(1)}, u32[]{:S(2)}, u32[]{:S(2)}) collective-permute-start(bf16[4,2,640]{2,1,0:T(2,128)(2,1)} %param.20), channel_id=1, source_target_pairs={{0,2},{1,3},{2,0},{3,1},{4,6},{5,7},{6,4},{7,5},{8,10},{9,11},{10,... | collective-permute-start | bytes 30728 | tf_op jit(solution)/shard_map/ppermute | solution.py:56
  3.3 11.7 %collective-permute-start.2 = (bf16[4,2,640]{2,1,0:T(2,128)(2,1)}, bf16[4,2,640]{2,1,0:T(2,128)(2,1)S(1)}, u32[]{:S(2)}, u32[]{:S(2)}) collective-permute-start(bf16[4,2,640]{2,1,0:T(2,128)(2,1)} %param.20), channel_id=1, source_target_pairs={{0,3},{1,0},{2,1},{3,2},{4,7},{5,4},{6,5},{7,6},{8,11},{9,8},{10,9... | collective-permute-start | bytes 30728 | tf_op jit(solution)/shard_map/ppermute | solution.py:56
  10.2 11.4 %copy-start.7 = (f32[128]{0:T(128)S(1)}, f32[128]{0:T(128)}, u32[]{:S(2)}) copy-start(f32[128]{0:T(128)} %param.22) | copy-start | bytes 1540
  20.7 34.4 %copy-start.9 = (bf16[16,256,128]{2,1,0:T(8,128)(2,1)S(1)}, bf16[16,256,128]{2,1,0:T(8,128)(2,1)}, u32[]{:S(2)}) copy-start(bf16[16,256,128]{2,1,0:T(8,128)(2,1)} %param.29) | copy-start | bytes 3145732
  22.7 1.4 %collective-permute-start.3 = (bf16[12,4,4,128]{3,2,1,0:T(4,128)(2,1)S(1)}, bf16[12,4,4,128]{3,2,1,0:T(4,128)(2,1)S(1)}, u32[]{:S(2)}, u32[]{:S(2)}) collective-permute-start(bf16[12,4,4,128]{3,2,1,0:T(4,128)(2,1)S(1)} %select_reduce_fusion.3), channel_id=1, source_target_pairs={{0,4},{4,0},{8,12},{12,8},{16,20},{20,16},{24,28},{28,24},{32,36},... | collective-permute-start | bytes 147464 | tf_op jit(solution)/shard_map/ppermute | solution.py:78
  23.5 32.0 %copy-start.2 = (s32[16]{0:T(128)S(1)}, s32[16]{0:T(128)}, u32[]{:S(2)}) copy-start(s32[16]{0:T(128)} %param.31) | copy-start | bytes 196
  24.2 4.4 %collective-permute-start.4 = (bf16[12,4,4,128]{3,2,1,0:T(4,128)(2,1)S(1)}, bf16[12,4,4,128]{3,2,1,0:T(4,128)(2,1)S(1)}, u32[]{:S(2)}, u32[]{:S(2)}) collective-permute-start(bf16[12,4,4,128]{3,2,1,0:T(4,128)(2,1)S(1)} %add.367), channel_id=1, source_target_pairs={{0,8},{4,12},{8,0},{12,4},{16,24},{20,28},{24,16},{28,20},{32,40},... | collective-permute-start | bytes 147464 | tf_op jit(solution)/shard_map/ppermute | solution.py:78
  28.6 6.0 %collective-permute-start.5 = (bf16[12,4,4,128]{3,2,1,0:T(4,128)(2,1)S(1)}, bf16[12,4,4,128]{3,2,1,0:T(4,128)(2,1)S(1)}, u32[]{:S(2)}, u32[]{:S(2)}) collective-permute-start(bf16[12,4,4,128]{3,2,1,0:T(4,128)(2,1)S(1)} %add.368), channel_id=1, source_target_pairs={{0,16},{4,20},{8,24},{12,28},{16,0},{20,4},{24,8},{28,12},{32,48},... | collective-permute-start | bytes 147464 | tf_op jit(solution)/shard_map/ppermute | solution.py:78
  34.6 8.4 %collective-permute-start.6 = (bf16[12,4,4,128]{3,2,1,0:T(4,128)(2,1)S(1)}, bf16[12,4,4,128]{3,2,1,0:T(4,128)(2,1)S(1)}, u32[]{:S(2)}, u32[]{:S(2)}) collective-permute-start(bf16[12,4,4,128]{3,2,1,0:T(4,128)(2,1)S(1)} %add.369), channel_id=1, source_target_pairs={{0,32},{4,36},{8,40},{12,44},{16,48},{20,52},{24,56},{28,60},{32,0... | collective-permute-start | bytes 147464 | tf_op jit(solution)/shard_map/ppermute | solution.py:78
  43.0 4.4 %collective-permute-start.7 = (bf16[12,4,4,128]{3,2,1,0:T(4,128)(2,1)S(1)}, bf16[12,4,4,128]{3,2,1,0:T(4,128)(2,1)S(1)}, u32[]{:S(2)}, u32[]{:S(2)}) collective-permute-start(bf16[12,4,4,128]{3,2,1,0:T(4,128)(2,1)S(1)} %add.370), channel_id=1, source_target_pairs={{0,64},{4,68},{8,72},{12,76},{16,80},{20,84},{24,88},{28,92},{32,9... | collective-permute-start | bytes 147464 | tf_op jit(solution)/shard_map/ppermute | solution.py:78
  47.5 5.7 %collective-permute-start.8 = (bf16[12,4,4,128]{3,2,1,0:T(4,128)(2,1)S(1)}, bf16[12,4,4,128]{3,2,1,0:T(4,128)(2,1)S(1)}, u32[]{:S(2)}, u32[]{:S(2)}) collective-permute-start(bf16[12,4,4,128]{3,2,1,0:T(4,128)(2,1)S(1)} %add.371), channel_id=1, source_target_pairs={{0,128},{4,132},{8,136},{12,140},{16,144},{20,148},{24,152},{28,15... | collective-permute-start | bytes 147464 | tf_op jit(solution)/shard_map/ppermute | solution.py:78
  55.1 5.4 %copy-start.3 = (f32[8,128]{1,0:T(8,128)S(1)}, f32[8,128]{1,0:T(8,128)}, u32[]{:S(2)}) copy-start(f32[8,128]{1,0:T(8,128)} %get-tuple-element.10) | copy-start | bytes 12292
  55.2 5.4 %copy-start.8 = (f32[128]{0:T(128)S(1)}, f32[128]{0:T(128)}, u32[]{:S(2)}) copy-start(f32[128]{0:T(128)} %param.23) | copy-start | bytes 1540
  55.5 24.8 %copy-start.6 = (f32[8,128]{1,0:T(8,128)S(1)}, f32[8,128]{1,0:T(8,128)}, u32[]{:S(2)}) copy-start(f32[8,128]{1,0:T(8,128)} %get-tuple-element.11) | copy-start | bytes 12292
  57.4 1.3 %collective-permute-start.9 = (bf16[134,192]{1,0:T(8,128)(2,1)S(1)}, bf16[134,192]{1,0:T(8,128)(2,1)S(1)}, u32[]{:S(2)}, u32[]{:S(2)}) collective-permute-start(bf16[134,192]{1,0:T(8,128)(2,1)S(1)} %concatenate.117), channel_id=1, source_target_pairs={{0,4},{4,0},{8,12},{12,8},{16,20},{20,16},{24,28},{28,24},{32,36},... | collective-permute-start | bytes 154376 | tf_op jit(solution)/shard_map/ppermute | solution.py:118
  58.9 4.4 %collective-permute-start.10 = (bf16[134,192]{1,0:T(8,128)(2,1)S(1)}, bf16[134,192]{1,0:T(8,128)(2,1)S(1)}, u32[]{:S(2)}, u32[]{:S(2)}) collective-permute-start(bf16[134,192]{1,0:T(8,128)(2,1)S(1)} %concatenate.118), channel_id=1, source_target_pairs={{0,8},{4,12},{8,0},{12,4},{16,24},{20,28},{24,16},{28,20},{32,40},... | collective-permute-start | bytes 154376 | tf_op jit(solution)/shard_map/ppermute | solution.py:118
  63.4 5.3 %collective-permute-start.11 = (bf16[134,192]{1,0:T(8,128)(2,1)S(1)}, bf16[134,192]{1,0:T(8,128)(2,1)S(1)}, u32[]{:S(2)}, u32[]{:S(2)}) collective-permute-start(bf16[134,192]{1,0:T(8,128)(2,1)S(1)} %concatenate.119), channel_id=1, source_target_pairs={{0,16},{4,20},{8,24},{12,28},{16,0},{20,4},{24,8},{28,12},{32,48},... | collective-permute-start | bytes 154376 | tf_op jit(solution)/shard_map/ppermute | solution.py:118
  68.9 10.4 %collective-permute-start.12 = (bf16[134,192]{1,0:T(8,128)(2,1)S(1)}, bf16[134,192]{1,0:T(8,128)(2,1)S(1)}, u32[]{:S(2)}, u32[]{:S(2)}) collective-permute-start(bf16[134,192]{1,0:T(8,128)(2,1)S(1)} %concatenate.120), channel_id=1, source_target_pairs={{0,32},{4,36},{8,40},{12,44},{16,48},{20,52},{24,56},{28,60},{32,0... | collective-permute-start | bytes 154376 | tf_op jit(solution)/shard_map/ppermute | solution.py:118
  79.4 4.4 %collective-permute-start.13 = (bf16[134,192]{1,0:T(8,128)(2,1)S(1)}, bf16[134,192]{1,0:T(8,128)(2,1)S(1)}, u32[]{:S(2)}, u32[]{:S(2)}) collective-permute-start(bf16[134,192]{1,0:T(8,128)(2,1)S(1)} %concatenate.121), channel_id=1, source_target_pairs={{0,64},{4,68},{8,72},{12,76},{16,80},{20,84},{24,88},{28,92},{32,9... | collective-permute-start | bytes 154376 | tf_op jit(solution)/shard_map/ppermute | solution.py:118
  80.3 11.3 %copy-start.5 = (bf16[8,128]{1,0:T(8,128)(2,1)}, bf16[8,128]{1,0:T(8,128)(2,1)S(1)}, u32[]{:S(2)}) copy-start(bf16[8,128]{1,0:T(8,128)(2,1)S(1)} %convert_element_type.166) | copy-start | bytes 6148
  83.9 5.9 %collective-permute-start.14 = (bf16[134,192]{1,0:T(8,128)(2,1)S(1)}, bf16[134,192]{1,0:T(8,128)(2,1)S(1)}, u32[]{:S(2)}, u32[]{:S(2)}) collective-permute-start(bf16[134,192]{1,0:T(8,128)(2,1)S(1)} %concatenate.122), channel_id=1, source_target_pairs={{0,128},{4,132},{8,136},{12,140},{16,144},{20,148},{24,152},{28,15... | collective-permute-start | bytes 154376 | tf_op jit(solution)/shard_map/ppermute | solution.py:118
  91.7 12.6 %copy-start.1 = (bf16[4,2,640]{2,1,0:T(2,128)(2,1)S(1)}, bf16[4,2,640]{2,1,0:T(2,128)(2,1)}, u32[]{:S(2)}) copy-start(bf16[4,2,640]{2,1,0:T(2,128)(2,1)} %param.20) | copy-start | bytes 30724
  96.9 4.4 %collective-permute-start.15 = (f32[4,2,640]{2,1,0:T(2,128)S(1)}, f32[4,2,640]{2,1,0:T(2,128)S(1)}, u32[]{:S(2)}, u32[]{:S(2)}) collective-permute-start(f32[4,2,640]{2,1,0:T(2,128)S(1)} %fusion.25), channel_id=1, source_target_pairs={{0,1},{1,2},{2,3},{3,0},{4,5},{5,6},{6,7},{7,4},{8,9},{9,10},{10,1... | collective-permute-start | bytes 61448 | tf_op jit(solution)/shard_map/ppermute | solution.py:71
  97.0 5.4 %collective-permute-start.16 = (f32[4,2,640]{2,1,0:T(2,128)S(1)}, f32[4,2,640]{2,1,0:T(2,128)S(1)}, u32[]{:S(2)}, u32[]{:S(2)}) collective-permute-start(f32[4,2,640]{2,1,0:T(2,128)S(1)} %fusion.24), channel_id=1, source_target_pairs={{0,2},{1,3},{2,0},{3,1},{4,6},{5,7},{6,4},{7,5},{8,10},{9,11},{10,... | collective-permute-start | bytes 61448 | tf_op jit(solution)/shard_map/ppermute | solution.py:71
  100.5 3.9 %collective-permute-start.17 = (f32[4,2,640]{2,1,0:T(2,128)S(1)}, f32[4,2,640]{2,1,0:T(2,128)S(1)}, u32[]{:S(2)}, u32[]{:S(2)}) collective-permute-start(f32[4,2,640]{2,1,0:T(2,128)S(1)} %fusion.23), channel_id=1, source_target_pairs={{0,3},{1,0},{2,1},{3,2},{4,7},{5,4},{6,5},{7,6},{8,11},{9,8},{10,9... | collective-permute-start | bytes 61448 | tf_op jit(solution)/shard_map/ppermute | solution.py:71

commit v4 on v3

--- a/solution.py
+++ b/solution.py
@@ -55,19 +55,23 @@
     pieces = [block] + [
         lax.ppermute(block, "mp", [(i, (i + s) % n_mp) for i in range(n_mp)]) for s in range(1, n_mp)
     ]
-    stacked = jnp.stack(pieces)
-    order = (me - jnp.arange(n_mp, dtype=jnp.int32)) % n_mp
-    ordered = jnp.take(stacked, order, axis=0)
-    return jnp.concatenate([ordered[c] for c in range(n_mp)], axis=-1)
+    ordered = []
+    for c in range(n_mp):
+        shift = (me - c) % n_mp
+        chosen = pieces[0]
+        for s in range(1, n_mp):
+            chosen = jnp.where(shift == s, pieces[s], chosen)
+        ordered.append(chosen)
+    return jnp.concatenate(ordered, axis=-1)
 
 
 def reduce_scatter_mp(full, n_mp):
     me = lax.axis_index("mp")
     width = full.shape[-1] // n_mp
     chunks = full.reshape(full.shape[:-1] + (n_mp, width))
-    total = jnp.take(chunks, me, axis=-2)
+    total = lax.dynamic_index_in_dim(chunks, me, axis=chunks.ndim - 2, keepdims=False)
     for s in range(1, n_mp):
-        outgoing = jnp.take(chunks, (me + s) % n_mp, axis=-2)
+        outgoing = lax.dynamic_index_in_dim(chunks, (me + s) % n_mp, axis=chunks.ndim - 2, keepdims=False)
         total = total + lax.ppermute(outgoing, "mp", [(i, (i + s) % n_mp) for i in range(n_mp)])
     return total
 
@@ -158,7 +162,7 @@
 
     wide = gather_mp(states, n_mp).reshape(steps * own_rows, -1)
     own_ids = first_row + jnp.arange(own_rows, dtype=jnp.int32)
-    own_len = jnp.take(req_len, own_ids)
+    own_len = lax.dynamic_slice_in_dim(req_len, first_row, own_rows)
     positions = (own_len[None, :] + jnp.arange(steps, dtype=jnp.int32)[:, None]).reshape(-1)
     normed = scaled_rms(wide.astype(jnp.float32), norm_gain).astype(jnp.bfloat16)
     rows = steps * own_rows
@@ -174,7 +178,10 @@
 
     request_ids = jnp.arange(requests, dtype=jnp.int32)
     is_long = req_len == long_len
-    rank = jnp.cumsum(is_long.astype(jnp.int32)) - 1
+    long_count = is_long.astype(jnp.int32)
+    rank = jnp.sum(
+        jnp.where(request_ids[None, :] < request_ids[:, None], long_count[None, :], 0), axis=1
+    )
     long_ids = jnp.sum(
         jnp.where(
             is_long[None, :] & (rank[None, :] == jnp.arange(LONG_COUNT, dtype=jnp.int32)[:, None]),
@@ -189,8 +196,10 @@
     ).astype(jnp.bfloat16)
     long_table = butterfly(long_table, n_seq, lambda a, b: a + b)
 
-    slot_req_long = jnp.take(is_long, slot_request)
-    slot_rank = jnp.take(rank, slot_request)
+    hit = slot_request[:, None] == request_ids[None, :]
+    slot_req_long = jnp.any(hit & is_long[None, :], axis=1)
+    slot_rank = jnp.sum(jnp.where(hit, rank[None, :], 0), axis=1)
+    slot_len = jnp.sum(jnp.where(hit, req_len[None, :], 0), axis=1)
     local_row = slot_request - first_row
     slot_local = (local_row >= 0) & (local_row < own_rows)
     pick = jnp.where(
@@ -208,7 +217,6 @@
         jnp.einsum("stngd,sknd->stngk", slot_query, keys_split, preferred_element_type=jnp.float32)
         * scaling
     )
-    slot_len = jnp.take(req_len, slot_request)
     kept = slot_empty == 0
     filled = kept[:, None] & (
         slot_block[:, None] * block_len + jnp.arange(block_len, dtype=jnp.int32)[None, :] < slot_len[:, None]
@@ -240,9 +248,12 @@
     long_mix, long_small = stats_butterfly(long_stats[:HEAD_SIZE], long_stats[HEAD_SIZE:], n_seq)
     long_stats = jnp.concatenate([long_mix, long_small], axis=0)
     long_stats = long_stats.T.reshape((LONG_COUNT,) + stats.shape[1:])
-    own_rank = jnp.take(rank, own_ids)
-    own_is_long = jnp.take(is_long, own_ids)
-    from_long = jnp.take(long_stats, jnp.clip(own_rank, 0, LONG_COUNT - 1), axis=0)
+    own_rank = lax.dynamic_slice_in_dim(rank, first_row, own_rows)
+    own_is_long = lax.dynamic_slice_in_dim(is_long, first_row, own_rows)
+    rank_hit = own_rank[:, None] == jnp.arange(LONG_COUNT, dtype=jnp.int32)[None, :]
+    from_long = jnp.sum(
+        jnp.where(rank_hit[:, :, None, None, None, None], long_stats[None], 0.0), axis=1
+    )
     cache_stats = jnp.where(own_is_long[:, None, None, None, None], from_long, stats[LONG_COUNT:])
     cache_mix = cache_stats[..., :HEAD_SIZE]
     cache_total = cache_stats[..., HEAD_SIZE]

time: 105 us -> 102 us (0.971)
  the two profiles are of different devices: /device:TPU:12 before, /device:TPU:4 now
where the time goes in v4:
time: 102 us
  waiting for transfers between devices  38.7 us (38%)
  starting transfers between devices  33.3 us (33%)
  other arithmetic  14.2 us (14%)
  local copies, waits for them, and re-layouts  6.53 us (6%)
  Pallas kernels  6.15 us (6%)
  matrix products  1.65 us (2%)
  between operations  1.17 us (1%)
    ppermute x6, waiting for transfers between devices, stats_butterfly(): arrived = lax.ppermute(packed, 'seq', pairs)  20.7 us
    ppermute x6, waiting for transfers between devices, butterfly(): lax.ppermute(value, 'seq', [(i, i ^ stride) for i in range(n_seq)])  14.8 us
    ppermute x6, starting transfers between devices, butterfly(): lax.ppermute(value, 'seq', [(i, i ^ stride) for i in range(n_seq)])  14 us
    ppermute x6, starting transfers between devices, stats_butterfly(): arrived = lax.ppermute(packed, 'seq', pairs)  10.2 us
    pallas_call x2, Pallas kernels, small_matmul(): pl.pallas_call(_matmul_kernel, out_shape=[jax.ShapeDtypeStruct((m, n), jn...  6.15 us
    ppermute x3, starting transfers between devices, gather_mp(): lax.ppermute(block, 'mp', [(i, (i + s) % n_mp) for i in range(n_mp)])  5.31 us
    ppermute x3, starting transfers between devices, reduce_scatter_mp(): lax.ppermute(outgoing, 'mp', [(i, (i + s) % n_mp) for i in range(n_mp)])  3.81 us
    ppermute x3, waiting for transfers between devices, reduce_scatter_mp(): lax.ppermute(outgoing, 'mp', [(i, (i + s) % n_mp) for i in range(n_mp)])  3.12 us
  transfers between devices with their start and end apart: 18, of which 15 were waited for; matrix products, arithmetic and copies ran while one was open for 9% of the time, Pallas kernels for 0%

profile of v4, /device:TPU:4, one launch (start us, length us, event | category | flops | bytes accessed | tf_op | source)
XLA Modules:
  0.0 101.6 jit_solution(3828869517425052710)
XLA Ops:
  0.7 3.3 %collective-permute-start.1 = (bf16[4,2,640]{2,1,0:T(2,128)(2,1)}, bf16[4,2,640]{2,1,0:T(2,128)(2,1)S(1)}, u32[]{:S(2)}, u32[]{:S(2)}) collective-permute-start(bf16[4,2,640]{2,1,0:T(2,128)(2,1)} %param.14), channel_id=1, source_target_pairs={{0,2},{1,3},{2,0},{3,1},{4,6},{5,7},{6,4},{7,5},{8,10},{9,11},{10,... | collective-permute-start | bytes 30728 | tf_op jit(solution)/shard_map/ppermute | solution.py:56
  3.9 1.1 %collective-permute-start = (bf16[4,2,640]{2,1,0:T(2,128)(2,1)}, bf16[4,2,640]{2,1,0:T(2,128)(2,1)S(1)}, u32[]{:S(2)}, u32[]{:S(2)}) collective-permute-start(bf16[4,2,640]{2,1,0:T(2,128)(2,1)} %param.14), channel_id=1, source_target_pairs={{0,3},{1,0},{2,1},{3,2},{4,7},{5,4},{6,5},{7,6},{8,11},{9,8},{10,9... | collective-permute-start | bytes 30728 | tf_op jit(solution)/shard_map/ppermute | solution.py:56
  5.0 1.0 collective-permute-start.2
  6.0 0.7 broadcast_compare_fusion.1
  6.7 0.7 broadcast_multiply_fusion
  7.3 0.7 broadcast_compare_fusion.2
  8.0 0.7 dynamic_slice.24
  8.9 0.9 select_reduce_fusion.7
  9.9 0.8 compare_and_fusion
  10.8 0.7 compare_and_fusion.1
  11.8 0.7 broadcast_select_fusion.11
  12.9 1.4 %multiply_convert_fusion.x_ref = bf16[8,2560]{1,0:T(8,128)(2,1)} fusion(f32[8,2560]{1,0:T(8,128)S(1)} %reshape.561, f32[2560]{0:T(1024)} %param.15, f32[8]{0:T(128)S(1)} %rsqrt.28), kind=kLoop, calls=%fused_computation.36 | loop fusion | flops 61440 | bytes 133152 | tf_op jit(solution)/shard_map/convert_element_type | solution.py:167
  14.2 3.3 %shard_map.157 = (f32[8,512]{1,0:T(8,128)}, f32[8,128]{1,0:T(8,128)}, f32[8,128]{1,0:T(8,128)}) custom-call(bf16[8,2560]{1,0:T(8,128)(2,1)} %multiply_convert_fusion.x_ref, bf16[2560,512]{1,0:T(8,128)(2,1)} %refs_0_.2, bf16[2560,128]{1,0:T(8,128)(2,1)} %refs_1_.1, bf16[2560,128]{1,0:T(8,128)(2,1)} %refs_2_.1), custom_call_target="tpu_custom_call" | custom-call | flops 31457280 | bytes 3997696 | tf_op jit(solution)/shard_map/pallas_call | solution.py:42
  17.6 0.9 fusion.27
  18.5 0.8 fusion.28
  19.7 0.2 fusion.34
  19.9 1.0 %collective-permute-done.3 = bf16[12,4,4,128]{3,2,1,0:T(4,128)(2,1)S(1)} collective-permute-done((bf16[12,4,4,128]{3,2,1,0:T(4,128)(2,1)S(1)}, bf16[12,4,4,128]{3,2,1,0:T(4,128)(2,1)S(1)}, u32[]{:S(2)}, u32[]{:S(2)}) %collective-permute-start.3) | collective-permute-done | bytes 49184 | tf_op jit(solution)/shard_map/ppermute | solution.py:82
  20.9 2.0 %collective-permute-start.4 = (bf16[12,4,4,128]{3,2,1,0:T(4,128)(2,1)S(1)}, bf16[12,4,4,128]{3,2,1,0:T(4,128)(2,1)S(1)}, u32[]{:S(2)}, u32[]{:S(2)}) collective-permute-start(bf16[12,4,4,128]{3,2,1,0:T(4,128)(2,1)S(1)} %add.305), channel_id=1, source_target_pairs={{0,8},{4,12},{8,0},{12,4},{16,24},{20,28},{24,16},{28,20},{32,40},... | collective-permute-start | bytes 147464 | tf_op jit(solution)/shard_map/ppermute | solution.py:82
  23.0 2.1 %collective-permute-done.4 = bf16[12,4,4,128]{3,2,1,0:T(4,128)(2,1)S(1)} collective-permute-done((bf16[12,4,4,128]{3,2,1,0:T(4,128)(2,1)S(1)}, bf16[12,4,4,128]{3,2,1,0:T(4,128)(2,1)S(1)}, u32[]{:S(2)}, u32[]{:S(2)}) %collective-permute-start.4) | collective-permute-done | bytes 49184 | tf_op jit(solution)/shard_map/ppermute | solution.py:82
  25.1 3.4 %collective-permute-start.5 = (bf16[12,4,4,128]{3,2,1,0:T(4,128)(2,1)S(1)}, bf16[12,4,4,128]{3,2,1,0:T(4,128)(2,1)S(1)}, u32[]{:S(2)}, u32[]{:S(2)}) collective-permute-start(bf16[12,4,4,128]{3,2,1,0:T(4,128)(2,1)S(1)} %add.306), channel_id=1, source_target_pairs={{0,16},{4,20},{8,24},{12,28},{16,0},{20,4},{24,8},{28,12},{32,48},... | collective-permute-start | bytes 147464 | tf_op jit(solution)/shard_map/ppermute | solution.py:82
  28.6 2.2 %collective-permute-done.5 = bf16[12,4,4,128]{3,2,1,0:T(4,128)(2,1)S(1)} collective-permute-done((bf16[12,4,4,128]{3,2,1,0:T(4,128)(2,1)S(1)}, bf16[12,4,4,128]{3,2,1,0:T(4,128)(2,1)S(1)}, u32[]{:S(2)}, u32[]{:S(2)}) %collective-permute-start.5) | collective-permute-done | bytes 49184 | tf_op jit(solution)/shard_map/ppermute | solution.py:82
  30.8 6.8 %collective-permute-start.6 = (bf16[12,4,4,128]{3,2,1,0:T(4,128)(2,1)S(1)}, bf16[12,4,4,128]{3,2,1,0:T(4,128)(2,1)S(1)}, u32[]{:S(2)}, u32[]{:S(2)}) collective-permute-start(bf16[12,4,4,128]{3,2,1,0:T(4,128)(2,1)S(1)} %add.307), channel_id=1, source_target_pairs={{0,32},{4,36},{8,40},{12,44},{16,48},{20,52},{24,56},{28,60},{32,0... | collective-permute-start | bytes 147464 | tf_op jit(solution)/shard_map/ppermute | solution.py:82
  37.6 2.1 %collective-permute-done.6 = bf16[12,4,4,128]{3,2,1,0:T(4,128)(2,1)S(1)} collective-permute-done((bf16[12,4,4,128]{3,2,1,0:T(4,128)(2,1)S(1)}, bf16[12,4,4,128]{3,2,1,0:T(4,128)(2,1)S(1)}, u32[]{:S(2)}, u32[]{:S(2)}) %collective-permute-start.6) | collective-permute-done | bytes 49184 | tf_op jit(solution)/shard_map/ppermute | solution.py:82
  39.8 1.3 %collective-permute-start.7 = (bf16[12,4,4,128]{3,2,1,0:T(4,128)(2,1)S(1)}, bf16[12,4,4,128]{3,2,1,0:T(4,128)(2,1)S(1)}, u32[]{:S(2)}, u32[]{:S(2)}) collective-permute-start(bf16[12,4,4,128]{3,2,1,0:T(4,128)(2,1)S(1)} %add.308), channel_id=1, source_target_pairs={{0,64},{4,68},{8,72},{12,76},{16,80},{20,84},{24,88},{28,92},{32,9... | collective-permute-start | bytes 147464 | tf_op jit(solution)/shard_map/ppermute | solution.py:82
  41.2 2.9 %collective-permute-done.7 = bf16[12,4,4,128]{3,2,1,0:T(4,128)(2,1)S(1)} collective-permute-done((bf16[12,4,4,128]{3,2,1,0:T(4,128)(2,1)S(1)}, bf16[12,4,4,128]{3,2,1,0:T(4,128)(2,1)S(1)}, u32[]{:S(2)}, u32[]{:S(2)}) %collective-permute-start.7) | collective-permute-done | bytes 49184 | tf_op jit(solution)/shard_map/ppermute | solution.py:82
  44.2 0.4 collective-permute-start.8
  44.6 0.8 multiply_reduce_fusion.1
  45.4 4.5 %collective-permute-done.8 = bf16[12,4,4,128]{3,2,1,0:T(4,128)(2,1)S(1)} collective-permute-done((bf16[12,4,4,128]{3,2,1,0:T(4,128)(2,1)S(1)}, bf16[12,4,4,128]{3,2,1,0:T(4,128)(2,1)S(1)}, u32[]{:S(2)}, u32[]{:S(2)}) %collective-permute-start.8) | collective-permute-done | bytes 49184 | tf_op jit(solution)/shard_map/ppermute | solution.py:82
  50.0 0.6 gather_fusion
  50.6 0.5 select_reduce_fusion.1
  51.5 0.2 select_reduce_fusion.3
  51.7 0.3 bitcast_reduce_fusion
  52.0 0.3 fusion.1
  52.5 0.2 fusion.84
  52.7 0.3 convolution_bitcast_fusion
  53.0 0.5 copy.152
  53.5 0.2 copy.151
  54.2 1.2 %collective-permute-done.9 = bf16[134,192]{1,0:T(8,128)(2,1)S(1)} collective-permute-done((bf16[134,192]{1,0:T(8,128)(2,1)S(1)}, bf16[134,192]{1,0:T(8,128)(2,1)S(1)}, u32[]{:S(2)}, u32[]{:S(2)}) %collective-permute-start.9) | collective-permute-done | bytes 51488 | tf_op jit(solution)/shard_map/ppermute | solution.py:122
  55.6 1.1 %collective-permute-start.10 = (bf16[134,192]{1,0:T(8,128)(2,1)S(1)}, bf16[134,192]{1,0:T(8,128)(2,1)S(1)}, u32[]{:S(2)}, u32[]{:S(2)}) collective-permute-start(bf16[134,192]{1,0:T(8,128)(2,1)S(1)} %concatenate.105), channel_id=1, source_target_pairs={{0,8},{4,12},{8,0},{12,4},{16,24},{20,28},{24,16},{28,20},{32,40},... | collective-permute-start | bytes 154376 | tf_op jit(solution)/shard_map/ppermute | solution.py:122
  56.7 3.2 %collective-permute-done.10 = bf16[134,192]{1,0:T(8,128)(2,1)S(1)} collective-permute-done((bf16[134,192]{1,0:T(8,128)(2,1)S(1)}, bf16[134,192]{1,0:T(8,128)(2,1)S(1)}, u32[]{:S(2)}, u32[]{:S(2)}) %collective-permute-start.10) | collective-permute-done | bytes 51488 | tf_op jit(solution)/shard_map/ppermute | solution.py:122
  60.1 2.4 %collective-permute-start.11 = (bf16[134,192]{1,0:T(8,128)(2,1)S(1)}, bf16[134,192]{1,0:T(8,128)(2,1)S(1)}, u32[]{:S(2)}, u32[]{:S(2)}) collective-permute-start(bf16[134,192]{1,0:T(8,128)(2,1)S(1)} %concatenate.106), channel_id=1, source_target_pairs={{0,16},{4,20},{8,24},{12,28},{16,0},{20,4},{24,8},{28,12},{32,48},... | collective-permute-start | bytes 154376 | tf_op jit(solution)/shard_map/ppermute | solution.py:122
  62.6 3.6 %collective-permute-done.11 = bf16[134,192]{1,0:T(8,128)(2,1)S(1)} collective-permute-done((bf16[134,192]{1,0:T(8,128)(2,1)S(1)}, bf16[134,192]{1,0:T(8,128)(2,1)S(1)}, u32[]{:S(2)}, u32[]{:S(2)}) %collective-permute-start.11) | collective-permute-done | bytes 51488 | tf_op jit(solution)/shard_map/ppermute | solution.py:122
  66.3 6.0 %collective-permute-start.12 = (bf16[134,192]{1,0:T(8,128)(2,1)S(1)}, bf16[134,192]{1,0:T(8,128)(2,1)S(1)}, u32[]{:S(2)}, u32[]{:S(2)}) collective-permute-start(bf16[134,192]{1,0:T(8,128)(2,1)S(1)} %concatenate.107), channel_id=1, source_target_pairs={{0,32},{4,36},{8,40},{12,44},{16,48},{20,52},{24,56},{28,60},{32,0... | collective-permute-start | bytes 154376 | tf_op jit(solution)/shard_map/ppermute | solution.py:122
  72.3 0.2 convolution_multiply_fusion.1
  72.5 2.9 %collective-permute-done.12 = bf16[134,192]{1,0:T(8,128)(2,1)S(1)} collective-permute-done((bf16[134,192]{1,0:T(8,128)(2,1)S(1)}, bf16[134,192]{1,0:T(8,128)(2,1)S(1)}, u32[]{:S(2)}, u32[]{:S(2)}) %collective-permute-start.12) | collective-permute-done | bytes 51488 | tf_op jit(solution)/shard_map/ppermute | solution.py:122
  75.5 0.6 collective-permute-start.13
  76.2 4.5 %collective-permute-done.13 = bf16[134,192]{1,0:T(8,128)(2,1)S(1)} collective-permute-done((bf16[134,192]{1,0:T(8,128)(2,1)S(1)}, bf16[134,192]{1,0:T(8,128)(2,1)S(1)}, u32[]{:S(2)}, u32[]{:S(2)}) %collective-permute-start.13) | collective-permute-done | bytes 51488 | tf_op jit(solution)/shard_map/ppermute | solution.py:122
  81.0 0.4 copy.156
  81.4 5.3 %collective-permute-done.14 = bf16[134,192]{1,0:T(8,128)(2,1)S(1)} collective-permute-done((bf16[134,192]{1,0:T(8,128)(2,1)S(1)}, bf16[134,192]{1,0:T(8,128)(2,1)S(1)}, u32[]{:S(2)}, u32[]{:S(2)}) %collective-permute-start.14) | collective-permute-done | bytes 51488 | tf_op jit(solution)/shard_map/ppermute | solution.py:122
  87.0 0.2 select_reduce_fusion
  87.2 0.4 copy.155
  87.6 0.2 bitcast_select_fusion
  88.2 0.3 copy.163
  88.6 0.2 copy.165
  88.8 0.6 copy.200
  89.4 2.8 %shard_map.158 = f32[8,2560]{1,0:T(8,128)} custom-call(bf16[8,512]{1,0:T(8,128)(2,1)} %bitcast.192, bf16[512,2560]{1,0:T(8,128)(2,1)} %refs_0_.3), custom_call_target="tpu_custom_call" | custom-call | flops 20971520 | bytes 2711552 | tf_op jit(solution)/shard_map/pallas_call | solution.py:42
  92.3 0.9 reshape_reshape.3
  93.3 0.8 collective-permute-start.15
  94.1 3.0 %collective-permute-start.16 = (f32[4,2,640]{2,1,0:T(2,128)S(1)}, f32[4,2,640]{2,1,0:T(2,128)S(1)}, u32[]{:S(2)}, u32[]{:S(2)}) collective-permute-start(f32[4,2,640]{2,1,0:T(2,128)S(1)} %bitcast.197), channel_id=1, source_target_pairs={{0,2},{1,3},{2,0},{3,1},{4,6},{5,7},{6,4},{7,5},{8,10},{9,11},{10,... | collective-permute-start | bytes 61448 | tf_op jit(solution)/shard_map/ppermute | solution.py:75
  97.2 0.7 pad_maximum_fusion.2
  97.8 0.6 collective-permute-done.15
  98.4 1.0 collective-permute-done.16
  99.4 1.5 %collective-permute-done.17 = f32[4,2,640]{2,1,0:T(2,128)S(1)} collective-permute-done((f32[4,2,640]{2,1,0:T(2,128)S(1)}, f32[4,2,640]{2,1,0:T(2,128)S(1)}, u32[]{:S(2)}, u32[]{:S(2)}) %collective-permute-start.17) | collective-permute-done | bytes 20512 | tf_op jit(solution)/shard_map/ppermute | solution.py:75
  100.9 0.6 fusion.22
  (125 shorter events, 5.0 us)
Async XLA Ops:
  0.6 50.0 %copy-start = (bf16[16,256,128]{2,1,0:T(8,128)(2,1)S(1)}, bf16[16,256,128]{2,1,0:T(8,128)(2,1)}, u32[]{:S(2)}) copy-start(bf16[16,256,128]{2,1,0:T(8,128)(2,1)} %param.22) | copy-start | bytes 3145732
  0.6 19.0 %copy-start.2 = (s32[16]{0:T(128)S(1)}, s32[16]{0:T(128)}, u32[]{:S(2)}) copy-start(s32[16]{0:T(128)} %param.25) | copy-start | bytes 196
  0.7 17.8 %copy-start.6 = (f32[128]{0:T(128)S(1)}, f32[128]{0:T(128)}, u32[]{:S(2)}) copy-start(f32[128]{0:T(128)} %param.16) | copy-start | bytes 1540
  0.7 11.1 %collective-permute-start.1 = (bf16[4,2,640]{2,1,0:T(2,128)(2,1)}, bf16[4,2,640]{2,1,0:T(2,128)(2,1)S(1)}, u32[]{:S(2)}, u32[]{:S(2)}) collective-permute-start(bf16[4,2,640]{2,1,0:T(2,128)(2,1)} %param.14), channel_id=1, source_target_pairs={{0,2},{1,3},{2,0},{3,1},{4,6},{5,7},{6,4},{7,5},{8,10},{9,11},{10,... | collective-permute-start | bytes 30728 | tf_op jit(solution)/shard_map/ppermute | solution.py:56
  3.9 7.8 %collective-permute-start = (bf16[4,2,640]{2,1,0:T(2,128)(2,1)}, bf16[4,2,640]{2,1,0:T(2,128)(2,1)S(1)}, u32[]{:S(2)}, u32[]{:S(2)}) collective-permute-start(bf16[4,2,640]{2,1,0:T(2,128)(2,1)} %param.14), channel_id=1, source_target_pairs={{0,3},{1,0},{2,1},{3,2},{4,7},{5,4},{6,5},{7,6},{8,11},{9,8},{10,9... | collective-permute-start | bytes 30728 | tf_op jit(solution)/shard_map/ppermute | solution.py:56
  5.0 6.8 %collective-permute-start.2 = (bf16[4,2,640]{2,1,0:T(2,128)(2,1)}, bf16[4,2,640]{2,1,0:T(2,128)(2,1)S(1)}, u32[]{:S(2)}, u32[]{:S(2)}) collective-permute-start(bf16[4,2,640]{2,1,0:T(2,128)(2,1)} %param.14), channel_id=1, source_target_pairs={{0,1},{1,2},{2,3},{3,0},{4,5},{5,6},{6,7},{7,4},{8,9},{9,10},{10,1... | collective-permute-start | bytes 30728 | tf_op jit(solution)/shard_map/ppermute | solution.py:56
  17.5 34.4 %copy-start.8 = (bf16[16,256,128]{2,1,0:T(8,128)(2,1)S(1)}, bf16[16,256,128]{2,1,0:T(8,128)(2,1)}, u32[]{:S(2)}) copy-start(bf16[16,256,128]{2,1,0:T(8,128)(2,1)} %param.23) | copy-start | bytes 3145732
  19.6 1.3 %collective-permute-start.3 = (bf16[12,4,4,128]{3,2,1,0:T(4,128)(2,1)S(1)}, bf16[12,4,4,128]{3,2,1,0:T(4,128)(2,1)S(1)}, u32[]{:S(2)}, u32[]{:S(2)}) collective-permute-start(bf16[12,4,4,128]{3,2,1,0:T(4,128)(2,1)S(1)} %select_reduce_fusion.4), channel_id=1, source_target_pairs={{0,4},{4,0},{8,12},{12,8},{16,20},{20,16},{24,28},{28,24},{32,36},... | collective-permute-start | bytes 147464 | tf_op jit(solution)/shard_map/ppermute | solution.py:82
  20.9 4.2 %collective-permute-start.4 = (bf16[12,4,4,128]{3,2,1,0:T(4,128)(2,1)S(1)}, bf16[12,4,4,128]{3,2,1,0:T(4,128)(2,1)S(1)}, u32[]{:S(2)}, u32[]{:S(2)}) collective-permute-start(bf16[12,4,4,128]{3,2,1,0:T(4,128)(2,1)S(1)} %add.305), channel_id=1, source_target_pairs={{0,8},{4,12},{8,0},{12,4},{16,24},{20,28},{24,16},{28,20},{32,40},... | collective-permute-start | bytes 147464 | tf_op jit(solution)/shard_map/ppermute | solution.py:82
  25.1 5.6 %collective-permute-start.5 = (bf16[12,4,4,128]{3,2,1,0:T(4,128)(2,1)S(1)}, bf16[12,4,4,128]{3,2,1,0:T(4,128)(2,1)S(1)}, u32[]{:S(2)}, u32[]{:S(2)}) collective-permute-start(bf16[12,4,4,128]{3,2,1,0:T(4,128)(2,1)S(1)} %add.306), channel_id=1, source_target_pairs={{0,16},{4,20},{8,24},{12,28},{16,0},{20,4},{24,8},{28,12},{32,48},... | collective-permute-start | bytes 147464 | tf_op jit(solution)/shard_map/ppermute | solution.py:82
  30.8 9.0 %collective-permute-start.6 = (bf16[12,4,4,128]{3,2,1,0:T(4,128)(2,1)S(1)}, bf16[12,4,4,128]{3,2,1,0:T(4,128)(2,1)S(1)}, u32[]{:S(2)}, u32[]{:S(2)}) collective-permute-start(bf16[12,4,4,128]{3,2,1,0:T(4,128)(2,1)S(1)} %add.307), channel_id=1, source_target_pairs={{0,32},{4,36},{8,40},{12,44},{16,48},{20,52},{24,56},{28,60},{32,0... | collective-permute-start | bytes 147464 | tf_op jit(solution)/shard_map/ppermute | solution.py:82
  39.8 4.4 %collective-permute-start.7 = (bf16[12,4,4,128]{3,2,1,0:T(4,128)(2,1)S(1)}, bf16[12,4,4,128]{3,2,1,0:T(4,128)(2,1)S(1)}, u32[]{:S(2)}, u32[]{:S(2)}) collective-permute-start(bf16[12,4,4,128]{3,2,1,0:T(4,128)(2,1)S(1)} %add.308), channel_id=1, source_target_pairs={{0,64},{4,68},{8,72},{12,76},{16,80},{20,84},{24,88},{28,92},{32,9... | collective-permute-start | bytes 147464 | tf_op jit(solution)/shard_map/ppermute | solution.py:82
  44.2 5.7 %collective-permute-start.8 = (bf16[12,4,4,128]{3,2,1,0:T(4,128)(2,1)S(1)}, bf16[12,4,4,128]{3,2,1,0:T(4,128)(2,1)S(1)}, u32[]{:S(2)}, u32[]{:S(2)}) collective-permute-start(bf16[12,4,4,128]{3,2,1,0:T(4,128)(2,1)S(1)} %add.309), channel_id=1, source_target_pairs={{0,128},{4,132},{8,136},{12,140},{16,144},{20,148},{24,152},{28,15... | collective-permute-start | bytes 147464 | tf_op jit(solution)/shard_map/ppermute | solution.py:82
  52.0 4.7 %copy-start.3 = (f32[8,128]{1,0:T(8,128)S(1)}, f32[8,128]{1,0:T(8,128)}, u32[]{:S(2)}) copy-start(f32[8,128]{1,0:T(8,128)} %get-tuple-element.7) | copy-start | bytes 12292
  52.0 4.6 %copy-start.7 = (f32[128]{0:T(128)S(1)}, f32[128]{0:T(128)}, u32[]{:S(2)}) copy-start(f32[128]{0:T(128)} %param.17) | copy-start | bytes 1540
  52.4 23.8 %copy-start.5 = (f32[8,128]{1,0:T(8,128)S(1)}, f32[8,128]{1,0:T(8,128)}, u32[]{:S(2)}) copy-start(f32[8,128]{1,0:T(8,128)} %get-tuple-element.8) | copy-start | bytes 12292
  54.1 1.3 %collective-permute-start.9 = (bf16[134,192]{1,0:T(8,128)(2,1)S(1)}, bf16[134,192]{1,0:T(8,128)(2,1)S(1)}, u32[]{:S(2)}, u32[]{:S(2)}) collective-permute-start(bf16[134,192]{1,0:T(8,128)(2,1)S(1)} %concatenate.104), channel_id=1, source_target_pairs={{0,4},{4,0},{8,12},{12,8},{16,20},{20,16},{24,28},{28,24},{32,36},... | collective-permute-start | bytes 154376 | tf_op jit(solution)/shard_map/ppermute | solution.py:122
  55.6 4.4 %collective-permute-start.10 = (bf16[134,192]{1,0:T(8,128)(2,1)S(1)}, bf16[134,192]{1,0:T(8,128)(2,1)S(1)}, u32[]{:S(2)}, u32[]{:S(2)}) collective-permute-start(bf16[134,192]{1,0:T(8,128)(2,1)S(1)} %concatenate.105), channel_id=1, source_target_pairs={{0,8},{4,12},{8,0},{12,4},{16,24},{20,28},{24,16},{28,20},{32,40},... | collective-permute-start | bytes 154376 | tf_op jit(solution)/shard_map/ppermute | solution.py:122
  60.1 6.0 %collective-permute-start.11 = (bf16[134,192]{1,0:T(8,128)(2,1)S(1)}, bf16[134,192]{1,0:T(8,128)(2,1)S(1)}, u32[]{:S(2)}, u32[]{:S(2)}) collective-permute-start(bf16[134,192]{1,0:T(8,128)(2,1)S(1)} %concatenate.106), channel_id=1, source_target_pairs={{0,16},{4,20},{8,24},{12,28},{16,0},{20,4},{24,8},{28,12},{32,48},... | collective-permute-start | bytes 154376 | tf_op jit(solution)/shard_map/ppermute | solution.py:122
  66.3 9.0 %collective-permute-start.12 = (bf16[134,192]{1,0:T(8,128)(2,1)S(1)}, bf16[134,192]{1,0:T(8,128)(2,1)S(1)}, u32[]{:S(2)}, u32[]{:S(2)}) collective-permute-start(bf16[134,192]{1,0:T(8,128)(2,1)S(1)} %concatenate.107), channel_id=1, source_target_pairs={{0,32},{4,36},{8,40},{12,44},{16,48},{20,52},{24,56},{28,60},{32,0... | collective-permute-start | bytes 154376 | tf_op jit(solution)/shard_map/ppermute | solution.py:122
  75.5 5.2 %collective-permute-start.13 = (bf16[134,192]{1,0:T(8,128)(2,1)S(1)}, bf16[134,192]{1,0:T(8,128)(2,1)S(1)}, u32[]{:S(2)}, u32[]{:S(2)}) collective-permute-start(bf16[134,192]{1,0:T(8,128)(2,1)S(1)} %concatenate.108), channel_id=1, source_target_pairs={{0,64},{4,68},{8,72},{12,76},{16,80},{20,84},{24,88},{28,92},{32,9... | collective-permute-start | bytes 154376 | tf_op jit(solution)/shard_map/ppermute | solution.py:122
  76.2 11.9 %copy-start.4 = (bf16[8,128]{1,0:T(8,128)(2,1)}, bf16[8,128]{1,0:T(8,128)(2,1)S(1)}, u32[]{:S(2)}) copy-start(bf16[8,128]{1,0:T(8,128)(2,1)S(1)} %convert_element_type.177) | copy-start | bytes 6148
  80.8 5.9 %collective-permute-start.14 = (bf16[134,192]{1,0:T(8,128)(2,1)S(1)}, bf16[134,192]{1,0:T(8,128)(2,1)S(1)}, u32[]{:S(2)}, u32[]{:S(2)}) collective-permute-start(bf16[134,192]{1,0:T(8,128)(2,1)S(1)} %concatenate.109), channel_id=1, source_target_pairs={{0,128},{4,132},{8,136},{12,140},{16,144},{20,148},{24,152},{28,15... | collective-permute-start | bytes 154376 | tf_op jit(solution)/shard_map/ppermute | solution.py:122
  88.2 12.7 %copy-start.1 = (bf16[4,2,640]{2,1,0:T(2,128)(2,1)S(1)}, bf16[4,2,640]{2,1,0:T(2,128)(2,1)}, u32[]{:S(2)}) copy-start(bf16[4,2,640]{2,1,0:T(2,128)(2,1)} %param.14) | copy-start | bytes 30724
  93.3 5.1 %collective-permute-start.15 = (f32[4,2,640]{2,1,0:T(2,128)S(1)}, f32[4,2,640]{2,1,0:T(2,128)S(1)}, u32[]{:S(2)}, u32[]{:S(2)}) collective-permute-start(f32[4,2,640]{2,1,0:T(2,128)S(1)} %bitcast.198), channel_id=1, source_target_pairs={{0,1},{1,2},{2,3},{3,0},{4,5},{5,6},{6,7},{7,4},{8,9},{9,10},{10,1... | collective-permute-start | bytes 61448 | tf_op jit(solution)/shard_map/ppermute | solution.py:75
  94.1 5.3 %collective-permute-start.16 = (f32[4,2,640]{2,1,0:T(2,128)S(1)}, f32[4,2,640]{2,1,0:T(2,128)S(1)}, u32[]{:S(2)}, u32[]{:S(2)}) collective-permute-start(f32[4,2,640]{2,1,0:T(2,128)S(1)} %bitcast.197), channel_id=1, source_target_pairs={{0,2},{1,3},{2,0},{3,1},{4,6},{5,7},{6,4},{7,5},{8,10},{9,11},{10,... | collective-permute-start | bytes 61448 | tf_op jit(solution)/shard_map/ppermute | solution.py:75
  97.1 3.8 %collective-permute-start.17 = (f32[4,2,640]{2,1,0:T(2,128)S(1)}, f32[4,2,640]{2,1,0:T(2,128)S(1)}, u32[]{:S(2)}, u32[]{:S(2)}) collective-permute-start(f32[4,2,640]{2,1,0:T(2,128)S(1)} %bitcast.196), channel_id=1, source_target_pairs={{0,3},{1,0},{2,1},{3,2},{4,7},{5,4},{6,5},{7,6},{8,11},{9,8},{10,9... | collective-permute-start | bytes 61448 | tf_op jit(solution)/shard_map/ppermute | solution.py:75

commit v5 on v4

--- a/solution.py
+++ b/solution.py
@@ -2,6 +2,7 @@
 import jax.numpy as jnp
 from jax import lax
 from jax.experimental import pallas as pl
+from jax.experimental.pallas import tpu as pltpu
 from jax.sharding import PartitionSpec as P
 
 HEAD_SIZE = 128
@@ -36,18 +37,45 @@
         o_ref[...] = jnp.dot(x, w_ref[...], preferred_element_type=jnp.float32)
 
 
+def _vmem():
+    return pl.BlockSpec(memory_space=pltpu.VMEM)
+
+
 def small_matmul(x, *weights):
     m, k = x.shape
     widths = [w.shape[1] for w in weights]
     return pl.pallas_call(
         _matmul_kernel,
         out_shape=[jax.ShapeDtypeStruct((m, n), jnp.float32) for n in widths],
+        in_specs=[_vmem() for _ in range(1 + len(weights))],
+        out_specs=[_vmem() for _ in widths],
         cost_estimate=pl.CostEstimate(
             flops=2 * m * k * sum(widths),
             bytes_accessed=2 * (m * k + k * sum(widths)) + 4 * m * sum(widths),
             transcendentals=0,
         ),
     )(x, *weights)
+
+
+def _chunked_kernel(x_ref, w_ref, o_ref):
+    chunks, _, width = o_ref.shape
+    x = x_ref[...]
+    for c in range(chunks):
+        o_ref[c] = jnp.dot(x, w_ref[:, c * width : (c + 1) * width], preferred_element_type=jnp.float32)
+
+
+def chunked_matmul(x, w, chunks):
+    m, k = x.shape
+    n = w.shape[1]
+    return pl.pallas_call(
+        _chunked_kernel,
+        out_shape=jax.ShapeDtypeStruct((chunks, m, n // chunks), jnp.float32),
+        in_specs=[_vmem(), _vmem()],
+        out_specs=_vmem(),
+        cost_estimate=pl.CostEstimate(
+            flops=2 * m * k * n, bytes_accessed=2 * (m * k + k * n) + 4 * m * n, transcendentals=0
+        ),
+    )(x, w)
 
 
 def gather_mp(block, n_mp):
@@ -65,23 +93,25 @@
     return jnp.concatenate(ordered, axis=-1)
 
 
-def reduce_scatter_mp(full, n_mp):
+def reduce_scatter_mp(chunks, n_mp):
     me = lax.axis_index("mp")
-    width = full.shape[-1] // n_mp
-    chunks = full.reshape(full.shape[:-1] + (n_mp, width))
-    total = lax.dynamic_index_in_dim(chunks, me, axis=chunks.ndim - 2, keepdims=False)
+    total = lax.dynamic_index_in_dim(chunks, me, axis=0, keepdims=False)
     for s in range(1, n_mp):
-        outgoing = lax.dynamic_index_in_dim(chunks, (me + s) % n_mp, axis=chunks.ndim - 2, keepdims=False)
+        outgoing = lax.dynamic_index_in_dim(chunks, (me + s) % n_mp, axis=0, keepdims=False)
         total = total + lax.ppermute(outgoing, "mp", [(i, (i + s) % n_mp) for i in range(n_mp)])
     return total
 
 
+def seq_masks(n_seq):
+    if n_seq == 64:
+        return [1, 2, 4, 12, 16, 48]
+    return [1 << b for b in range(n_seq.bit_length() - 1)]
+
+
 def butterfly(value, n_seq, combine):
-    stride = 1
-    while stride < n_seq:
+    for stride in seq_masks(n_seq):
         partner = lax.ppermute(value, "seq", [(i, i ^ stride) for i in range(n_seq)])
         value = combine(value, partner)
-        stride *= 2
     return value
 
 
@@ -113,8 +143,7 @@
 
 def stats_butterfly(mix, stats, n_seq):
     width = mix.shape[0]
-    stride = 1
-    while stride < n_seq:
+    for stride in seq_masks(n_seq):
         pairs = [(i, i ^ stride) for i in range(n_seq)]
         packed = jnp.concatenate(
             [mix.astype(jnp.bfloat16), split_exact(stats[:1]), split_exact(stats[1:])], axis=0
@@ -127,7 +156,6 @@
             ),
         )
         mix, stats = merge_stats((mix, stats), theirs)
-        stride *= 2
     return mix, stats
 
 
@@ -283,9 +311,8 @@
     )
     attended = (mixture / denominator[..., None]).astype(jnp.bfloat16)
     attended = attended.transpose(1, 0, 2, 3, 4).reshape(steps * own_rows, q_heads * HEAD_SIZE)
-    (projected,) = small_matmul(attended, w_out)
-    projected = projected.reshape(steps, own_rows, -1)
-    summed = reduce_scatter_mp(projected, n_mp)
+    projected = chunked_matmul(attended, w_out, n_mp)
+    summed = reduce_scatter_mp(projected, n_mp).reshape(steps, own_rows, -1)
     hidden = (states.astype(jnp.float32) + summed).astype(jnp.bfloat16)
     return hidden, new_keys, new_values
 

time: 102 us -> 98.2 us (0.963)
  the two profiles are of different devices: /device:TPU:4 before, /device:TPU:38 now
where the time goes in v5:
time: 98.2 us; the launch traced here: 97.7 us
  waiting for transfers between devices  40.5 us (41%)
  starting transfers between devices  27.1 us (28%)
  other arithmetic  14.9 us (15%)
  local copies, waits for them, and re-layouts  6.29 us (6%)
  Pallas kernels  6.15 us (6%)
  matrix products  1.65 us (2%)
  between operations  1.15 us (1%)
    ppermute x6, waiting for transfers between devices, stats_butterfly(): arrived = lax.ppermute(packed, 'seq', pairs)  19.8 us
    ppermute x6, waiting for transfers between devices, butterfly(): lax.ppermute(value, 'seq', [(i, i ^ stride) for i in range(n_seq)])  16.6 us
    ppermute x6, starting transfers between devices, butterfly(): lax.ppermute(value, 'seq', [(i, i ^ stride) for i in range(n_seq)])  10.4 us
    ppermute x6, starting transfers between devices, stats_butterfly(): arrived = lax.ppermute(packed, 'seq', pairs)  7.64 us
    ppermute x3, starting transfers between devices, gather_mp(): lax.ppermute(block, 'mp', [(i, (i + s) % n_mp) for i in range(n_mp)])  5.31 us
    ppermute x3, waiting for transfers between devices, reduce_scatter_mp(): lax.ppermute(outgoing, 'mp', [(i, (i + s) % n_mp) for i in range(n_mp)])  4.13 us
    ppermute x3, starting transfers between devices, reduce_scatter_mp(): lax.ppermute(outgoing, 'mp', [(i, (i + s) % n_mp) for i in range(n_mp)])  3.73 us
    pallas_call x1, Pallas kernels, small_matmul(): pl.pallas_call(_matmul_kernel, out_shape=[jax.ShapeDtypeStruct((m, n), jn...  3.3 us
  transfers between devices with their start and end apart: 18, of which 14 were waited for; matrix products, arithmetic and copies ran while one was open for 9% of the time, Pallas kernels for 0%

profile of v5, /device:TPU:38, one launch (start us, length us, event | category | flops | bytes accessed | tf_op | source)
XLA Modules:
  0.0 97.7 jit_solution(6915752929218107349)
XLA Ops:
  0.7 3.3 %collective-permute-start.1 = (bf16[4,2,640]{2,1,0:T(2,128)(2,1)}, bf16[4,2,640]{2,1,0:T(2,128)(2,1)S(1)}, u32[]{:S(2)}, u32[]{:S(2)}) collective-permute-start(bf16[4,2,640]{2,1,0:T(2,128)(2,1)} %param.14), channel_id=1, source_target_pairs={{0,2},{1,3},{2,0},{3,1},{4,6},{5,7},{6,4},{7,5},{8,10},{9,11},{10,... | collective-permute-start | bytes 30728 | tf_op jit(solution)/shard_map/ppermute | solution.py:84
  3.9 1.1 %collective-permute-start = (bf16[4,2,640]{2,1,0:T(2,128)(2,1)}, bf16[4,2,640]{2,1,0:T(2,128)(2,1)S(1)}, u32[]{:S(2)}, u32[]{:S(2)}) collective-permute-start(bf16[4,2,640]{2,1,0:T(2,128)(2,1)} %param.14), channel_id=1, source_target_pairs={{0,3},{1,0},{2,1},{3,2},{4,7},{5,4},{6,5},{7,6},{8,11},{9,8},{10,9... | collective-permute-start | bytes 30728 | tf_op jit(solution)/shard_map/ppermute | solution.py:84
  5.0 1.0 collective-permute-start.2
  6.0 0.7 broadcast_compare_fusion.1
  6.7 0.7 broadcast_multiply_fusion
  7.3 0.7 broadcast_compare_fusion.2
  8.0 0.7 dynamic_slice.24
  8.9 0.9 select_reduce_fusion.7
  9.9 0.8 compare_and_fusion
  10.8 0.7 compare_and_fusion.1
  11.8 0.7 broadcast_select_fusion.11
  12.9 1.4 %multiply_convert_fusion.x_ref = bf16[8,2560]{1,0:T(8,128)(2,1)} fusion(f32[8,2560]{1,0:T(8,128)S(1)} %reshape.565, f32[2560]{0:T(1024)} %param.15, f32[8]{0:T(128)S(1)} %rsqrt.28), kind=kLoop, calls=%fused_computation.36 | loop fusion | flops 61440 | bytes 133152 | tf_op jit(solution)/shard_map/convert_element_type | solution.py:195
  14.2 3.3 %shard_map.157 = (f32[8,512]{1,0:T(8,128)}, f32[8,128]{1,0:T(8,128)}, f32[8,128]{1,0:T(8,128)}) custom-call(bf16[8,2560]{1,0:T(8,128)(2,1)} %multiply_convert_fusion.x_ref, bf16[2560,512]{1,0:T(8,128)(2,1)} %refs_0_.1, bf16[2560,128]{1,0:T(8,128)(2,1)} %refs_1_.1, bf16[2560,128]{1,0:T(8,128)(2,1)} %refs_2_.1), custom_call_target="tpu_custom_call" | custom-call | flops 31457280 | bytes 3997696 | tf_op jit(solution)/shard_map/pallas_call | solution.py:47
  17.6 0.9 fusion.25
  18.5 0.8 fusion.26
  19.7 0.2 fusion.32
  19.9 1.0 %collective-permute-done.3 = bf16[12,4,4,128]{3,2,1,0:T(4,128)(2,1)S(1)} collective-permute-done((bf16[12,4,4,128]{3,2,1,0:T(4,128)(2,1)S(1)}, bf16[12,4,4,128]{3,2,1,0:T(4,128)(2,1)S(1)}, u32[]{:S(2)}, u32[]{:S(2)}) %collective-permute-start.3) | collective-permute-done | bytes 49184 | tf_op jit(solution)/shard_map/ppermute | solution.py:113
  20.9 0.2 collective-permute-start.4
  21.2 3.9 %collective-permute-done.4 = bf16[12,4,4,128]{3,2,1,0:T(4,128)(2,1)S(1)} collective-permute-done((bf16[12,4,4,128]{3,2,1,0:T(4,128)(2,1)S(1)}, bf16[12,4,4,128]{3,2,1,0:T(4,128)(2,1)S(1)}, u32[]{:S(2)}, u32[]{:S(2)}) %collective-permute-start.4) | collective-permute-done | bytes 49184 | tf_op jit(solution)/shard_map/ppermute | solution.py:113
  25.1 3.4 %collective-permute-start.5 = (bf16[12,4,4,128]{3,2,1,0:T(4,128)(2,1)S(1)}, bf16[12,4,4,128]{3,2,1,0:T(4,128)(2,1)S(1)}, u32[]{:S(2)}, u32[]{:S(2)}) collective-permute-start(bf16[12,4,4,128]{3,2,1,0:T(4,128)(2,1)S(1)} %add.306), channel_id=1, source_target_pairs={{0,16},{4,20},{8,24},{12,28},{16,0},{20,4},{24,8},{28,12},{32,48},... | collective-permute-start | bytes 147464 | tf_op jit(solution)/shard_map/ppermute | solution.py:113
  28.6 2.0 %collective-permute-done.5 = bf16[12,4,4,128]{3,2,1,0:T(4,128)(2,1)S(1)} collective-permute-done((bf16[12,4,4,128]{3,2,1,0:T(4,128)(2,1)S(1)}, bf16[12,4,4,128]{3,2,1,0:T(4,128)(2,1)S(1)}, u32[]{:S(2)}, u32[]{:S(2)}) %collective-permute-start.5) | collective-permute-done | bytes 49184 | tf_op jit(solution)/shard_map/ppermute | solution.py:113
  30.6 5.2 %collective-permute-start.6 = (bf16[12,4,4,128]{3,2,1,0:T(4,128)(2,1)S(1)}, bf16[12,4,4,128]{3,2,1,0:T(4,128)(2,1)S(1)}, u32[]{:S(2)}, u32[]{:S(2)}) collective-permute-start(bf16[12,4,4,128]{3,2,1,0:T(4,128)(2,1)S(1)} %add.307), channel_id=1, source_target_pairs={{0,48},{4,52},{8,56},{12,60},{16,32},{20,36},{24,40},{28,44},{32,1... | collective-permute-start | bytes 147464 | tf_op jit(solution)/shard_map/ppermute | solution.py:113
  35.8 2.6 %collective-permute-done.6 = bf16[12,4,4,128]{3,2,1,0:T(4,128)(2,1)S(1)} collective-permute-done((bf16[12,4,4,128]{3,2,1,0:T(4,128)(2,1)S(1)}, bf16[12,4,4,128]{3,2,1,0:T(4,128)(2,1)S(1)}, u32[]{:S(2)}, u32[]{:S(2)}) %collective-permute-start.6) | collective-permute-done | bytes 49184 | tf_op jit(solution)/shard_map/ppermute | solution.py:113
  38.5 0.9 collective-permute-start.7
  39.5 3.1 %collective-permute-done.7 = bf16[12,4,4,128]{3,2,1,0:T(4,128)(2,1)S(1)} collective-permute-done((bf16[12,4,4,128]{3,2,1,0:T(4,128)(2,1)S(1)}, bf16[12,4,4,128]{3,2,1,0:T(4,128)(2,1)S(1)}, u32[]{:S(2)}, u32[]{:S(2)}) %collective-permute-start.7) | collective-permute-done | bytes 49184 | tf_op jit(solution)/shard_map/ppermute | solution.py:113
  42.7 0.6 collective-permute-start.8
  43.2 0.8 multiply_reduce_fusion.1
  44.0 4.0 %collective-permute-done.8 = bf16[12,4,4,128]{3,2,1,0:T(4,128)(2,1)S(1)} collective-permute-done((bf16[12,4,4,128]{3,2,1,0:T(4,128)(2,1)S(1)}, bf16[12,4,4,128]{3,2,1,0:T(4,128)(2,1)S(1)}, u32[]{:S(2)}, u32[]{:S(2)}) %collective-permute-start.8) | collective-permute-done | bytes 49184 | tf_op jit(solution)/shard_map/ppermute | solution.py:113
  48.2 0.6 gather_fusion
  48.8 0.5 select_reduce_fusion.1
  49.9 0.3 bitcast_reduce_fusion
  50.2 0.3 fusion.1
  50.7 0.2 fusion.82
  50.9 0.3 convolution_bitcast_fusion
  51.2 0.5 copy.152
  51.7 0.2 copy.151
  52.4 1.2 %collective-permute-done.9 = bf16[134,192]{1,0:T(8,128)(2,1)S(1)} collective-permute-done((bf16[134,192]{1,0:T(8,128)(2,1)S(1)}, bf16[134,192]{1,0:T(8,128)(2,1)S(1)}, u32[]{:S(2)}, u32[]{:S(2)}) %collective-permute-start.9) | collective-permute-done | bytes 51488 | tf_op jit(solution)/shard_map/ppermute | solution.py:151
  53.8 0.6 collective-permute-start.10
  54.5 3.7 %collective-permute-done.10 = bf16[134,192]{1,0:T(8,128)(2,1)S(1)} collective-permute-done((bf16[134,192]{1,0:T(8,128)(2,1)S(1)}, bf16[134,192]{1,0:T(8,128)(2,1)S(1)}, u32[]{:S(2)}, u32[]{:S(2)}) %collective-permute-start.10) | collective-permute-done | bytes 51488 | tf_op jit(solution)/shard_map/ppermute | solution.py:151
  58.3 1.5 %collective-permute-start.11 = (bf16[134,192]{1,0:T(8,128)(2,1)S(1)}, bf16[134,192]{1,0:T(8,128)(2,1)S(1)}, u32[]{:S(2)}, u32[]{:S(2)}) collective-permute-start(bf16[134,192]{1,0:T(8,128)(2,1)S(1)} %concatenate.106), channel_id=1, source_target_pairs={{0,16},{4,20},{8,24},{12,28},{16,0},{20,4},{24,8},{28,12},{32,48},... | collective-permute-start | bytes 154376 | tf_op jit(solution)/shard_map/ppermute | solution.py:151
  60.0 3.6 %collective-permute-done.11 = bf16[134,192]{1,0:T(8,128)(2,1)S(1)} collective-permute-done((bf16[134,192]{1,0:T(8,128)(2,1)S(1)}, bf16[134,192]{1,0:T(8,128)(2,1)S(1)}, u32[]{:S(2)}, u32[]{:S(2)}) %collective-permute-start.11) | collective-permute-done | bytes 51488 | tf_op jit(solution)/shard_map/ppermute | solution.py:151
  63.8 4.6 %collective-permute-start.12 = (bf16[134,192]{1,0:T(8,128)(2,1)S(1)}, bf16[134,192]{1,0:T(8,128)(2,1)S(1)}, u32[]{:S(2)}, u32[]{:S(2)}) collective-permute-start(bf16[134,192]{1,0:T(8,128)(2,1)S(1)} %concatenate.107), channel_id=1, source_target_pairs={{0,48},{4,52},{8,56},{12,60},{16,32},{20,36},{24,40},{28,44},{32,1... | collective-permute-start | bytes 154376 | tf_op jit(solution)/shard_map/ppermute | solution.py:151
  68.3 0.2 convolution_multiply_fusion.1
  68.5 2.5 %collective-permute-done.12 = bf16[134,192]{1,0:T(8,128)(2,1)S(1)} collective-permute-done((bf16[134,192]{1,0:T(8,128)(2,1)S(1)}, bf16[134,192]{1,0:T(8,128)(2,1)S(1)}, u32[]{:S(2)}, u32[]{:S(2)}) %collective-permute-start.12) | collective-permute-done | bytes 51488 | tf_op jit(solution)/shard_map/ppermute | solution.py:151
  71.1 0.3 collective-permute-start.13
  71.5 4.2 %collective-permute-done.13 = bf16[134,192]{1,0:T(8,128)(2,1)S(1)} collective-permute-done((bf16[134,192]{1,0:T(8,128)(2,1)S(1)}, bf16[134,192]{1,0:T(8,128)(2,1)S(1)}, u32[]{:S(2)}, u32[]{:S(2)}) %collective-permute-start.13) | collective-permute-done | bytes 51488 | tf_op jit(solution)/shard_map/ppermute | solution.py:151
  75.8 0.6 collective-permute-start.14
  76.5 0.4 copy.156
  76.9 4.5 %collective-permute-done.14 = bf16[134,192]{1,0:T(8,128)(2,1)S(1)} collective-permute-done((bf16[134,192]{1,0:T(8,128)(2,1)S(1)}, bf16[134,192]{1,0:T(8,128)(2,1)S(1)}, u32[]{:S(2)}, u32[]{:S(2)}) %collective-permute-start.14) | collective-permute-done | bytes 51488 | tf_op jit(solution)/shard_map/ppermute | solution.py:151
  81.9 0.4 copy.155
  82.3 0.2 bitcast_select_fusion
  83.0 0.3 copy.163
  83.4 0.2 copy.165
  83.6 0.6 copy.187
  84.2 2.8 %shard_map.158 = f32[4,8,640]{2,1,0:T(8,128)} custom-call(bf16[8,512]{1,0:T(8,128)(2,1)} %bitcast.185, bf16[512,2560]{1,0:T(8,128)(2,1)} %w_ref.1), custom_call_target="tpu_custom_call" | custom-call | flops 20971520 | bytes 2711552 | tf_op jit(solution)/shard_map/pallas_call | solution.py:70
  87.0 0.8 dynamic-slice_bitcast_fusion.2
  87.8 0.7 collective-permute-start.15
  88.5 2.6 %collective-permute-start.17 = (f32[8,640]{1,0:T(8,128)S(1)}, f32[8,640]{1,0:T(8,128)S(1)}, u32[]{:S(2)}, u32[]{:S(2)}) collective-permute-start(f32[8,640]{1,0:T(8,128)S(1)} %get-tuple-element.65), channel_id=1, source_target_pairs={{0,3},{1,0},{2,1},{3,2},{4,7},{5,4},{6,5},{7,6},{8,11},{9,8},{10,9... | collective-permute-start | bytes 61448 | tf_op jit(solution)/shard_map/ppermute | solution.py:101
  91.0 0.5 collective-permute-start.16
  91.5 0.7 pad_maximum_fusion.2
  92.2 0.6 collective-permute-done.15
  92.8 3.5 %collective-permute-done.16 = f32[8,640]{1,0:T(8,128)S(1)} collective-permute-done((f32[8,640]{1,0:T(8,128)S(1)}, f32[8,640]{1,0:T(8,128)S(1)}, u32[]{:S(2)}, u32[]{:S(2)}) %collective-permute-start.16) | collective-permute-done | bytes 20512 | tf_op jit(solution)/shard_map/ppermute | solution.py:101
  96.3 0.7 fusion.20
  97.1 0.6 add_convert_fusion
  (123 shorter events, 5.1 us)
Async XLA Ops:
  0.6 48.2 %copy-start = (bf16[16,256,128]{2,1,0:T(8,128)(2,1)S(1)}, bf16[16,256,128]{2,1,0:T(8,128)(2,1)}, u32[]{:S(2)}) copy-start(bf16[16,256,128]{2,1,0:T(8,128)(2,1)} %param.22) | copy-start | bytes 3145732
  0.6 19.0 %copy-start.2 = (s32[16]{0:T(128)S(1)}, s32[16]{0:T(128)}, u32[]{:S(2)}) copy-start(s32[16]{0:T(128)} %param.25) | copy-start | bytes 196
  0.7 17.8 %copy-start.6 = (f32[128]{0:T(128)S(1)}, f32[128]{0:T(128)}, u32[]{:S(2)}) copy-start(f32[128]{0:T(128)} %param.16) | copy-start | bytes 1540
  0.7 11.1 %collective-permute-start.1 = (bf16[4,2,640]{2,1,0:T(2,128)(2,1)}, bf16[4,2,640]{2,1,0:T(2,128)(2,1)S(1)}, u32[]{:S(2)}, u32[]{:S(2)}) collective-permute-start(bf16[4,2,640]{2,1,0:T(2,128)(2,1)} %param.14), channel_id=1, source_target_pairs={{0,2},{1,3},{2,0},{3,1},{4,6},{5,7},{6,4},{7,5},{8,10},{9,11},{10,... | collective-permute-start | bytes 30728 | tf_op jit(solution)/shard_map/ppermute | solution.py:84
  3.9 7.8 %collective-permute-start = (bf16[4,2,640]{2,1,0:T(2,128)(2,1)}, bf16[4,2,640]{2,1,0:T(2,128)(2,1)S(1)}, u32[]{:S(2)}, u32[]{:S(2)}) collective-permute-start(bf16[4,2,640]{2,1,0:T(2,128)(2,1)} %param.14), channel_id=1, source_target_pairs={{0,3},{1,0},{2,1},{3,2},{4,7},{5,4},{6,5},{7,6},{8,11},{9,8},{10,9... | collective-permute-start | bytes 30728 | tf_op jit(solution)/shard_map/ppermute | solution.py:84
  5.0 6.8 %collective-permute-start.2 = (bf16[4,2,640]{2,1,0:T(2,128)(2,1)}, bf16[4,2,640]{2,1,0:T(2,128)(2,1)S(1)}, u32[]{:S(2)}, u32[]{:S(2)}) collective-permute-start(bf16[4,2,640]{2,1,0:T(2,128)(2,1)} %param.14), channel_id=1, source_target_pairs={{0,1},{1,2},{2,3},{3,0},{4,5},{5,6},{6,7},{7,4},{8,9},{9,10},{10,1... | collective-permute-start | bytes 30728 | tf_op jit(solution)/shard_map/ppermute | solution.py:84
  17.5 32.6 %copy-start.8 = (bf16[16,256,128]{2,1,0:T(8,128)(2,1)S(1)}, bf16[16,256,128]{2,1,0:T(8,128)(2,1)}, u32[]{:S(2)}) copy-start(bf16[16,256,128]{2,1,0:T(8,128)(2,1)} %param.23) | copy-start | bytes 3145732
  19.6 1.3 %collective-permute-start.3 = (bf16[12,4,4,128]{3,2,1,0:T(4,128)(2,1)S(1)}, bf16[12,4,4,128]{3,2,1,0:T(4,128)(2,1)S(1)}, u32[]{:S(2)}, u32[]{:S(2)}) collective-permute-start(bf16[12,4,4,128]{3,2,1,0:T(4,128)(2,1)S(1)} %select_reduce_fusion.4), channel_id=1, source_target_pairs={{0,4},{4,0},{8,12},{12,8},{16,20},{20,16},{24,28},{28,24},{32,36},... | collective-permute-start | bytes 147464 | tf_op jit(solution)/shard_map/ppermute | solution.py:113
  20.9 4.2 %collective-permute-start.4 = (bf16[12,4,4,128]{3,2,1,0:T(4,128)(2,1)S(1)}, bf16[12,4,4,128]{3,2,1,0:T(4,128)(2,1)S(1)}, u32[]{:S(2)}, u32[]{:S(2)}) collective-permute-start(bf16[12,4,4,128]{3,2,1,0:T(4,128)(2,1)S(1)} %add.305), channel_id=1, source_target_pairs={{0,8},{4,12},{8,0},{12,4},{16,24},{20,28},{24,16},{28,20},{32,40},... | collective-permute-start | bytes 147464 | tf_op jit(solution)/shard_map/ppermute | solution.py:113
  25.1 5.4 %collective-permute-start.5 = (bf16[12,4,4,128]{3,2,1,0:T(4,128)(2,1)S(1)}, bf16[12,4,4,128]{3,2,1,0:T(4,128)(2,1)S(1)}, u32[]{:S(2)}, u32[]{:S(2)}) collective-permute-start(bf16[12,4,4,128]{3,2,1,0:T(4,128)(2,1)S(1)} %add.306), channel_id=1, source_target_pairs={{0,16},{4,20},{8,24},{12,28},{16,0},{20,4},{24,8},{28,12},{32,48},... | collective-permute-start | bytes 147464 | tf_op jit(solution)/shard_map/ppermute | solution.py:113
  30.6 7.8 %collective-permute-start.6 = (bf16[12,4,4,128]{3,2,1,0:T(4,128)(2,1)S(1)}, bf16[12,4,4,128]{3,2,1,0:T(4,128)(2,1)S(1)}, u32[]{:S(2)}, u32[]{:S(2)}) collective-permute-start(bf16[12,4,4,128]{3,2,1,0:T(4,128)(2,1)S(1)} %add.307), channel_id=1, source_target_pairs={{0,48},{4,52},{8,56},{12,60},{16,32},{20,36},{24,40},{28,44},{32,1... | collective-permute-start | bytes 147464 | tf_op jit(solution)/shard_map/ppermute | solution.py:113
  38.5 4.2 %collective-permute-start.7 = (bf16[12,4,4,128]{3,2,1,0:T(4,128)(2,1)S(1)}, bf16[12,4,4,128]{3,2,1,0:T(4,128)(2,1)S(1)}, u32[]{:S(2)}, u32[]{:S(2)}) collective-permute-start(bf16[12,4,4,128]{3,2,1,0:T(4,128)(2,1)S(1)} %add.308), channel_id=1, source_target_pairs={{0,64},{4,68},{8,72},{12,76},{16,80},{20,84},{24,88},{28,92},{32,9... | collective-permute-start | bytes 147464 | tf_op jit(solution)/shard_map/ppermute | solution.py:113
  42.7 5.4 %collective-permute-start.8 = (bf16[12,4,4,128]{3,2,1,0:T(4,128)(2,1)S(1)}, bf16[12,4,4,128]{3,2,1,0:T(4,128)(2,1)S(1)}, u32[]{:S(2)}, u32[]{:S(2)}) collective-permute-start(bf16[12,4,4,128]{3,2,1,0:T(4,128)(2,1)S(1)} %add.309), channel_id=1, source_target_pairs={{0,192},{4,196},{8,200},{12,204},{16,208},{20,212},{24,216},{28,22... | collective-permute-start | bytes 147464 | tf_op jit(solution)/shard_map/ppermute | solution.py:113
  50.2 4.2 %copy-start.3 = (f32[8,128]{1,0:T(8,128)S(1)}, f32[8,128]{1,0:T(8,128)}, u32[]{:S(2)}) copy-start(f32[8,128]{1,0:T(8,128)} %get-tuple-element.7) | copy-start | bytes 12292
  50.2 4.2 %copy-start.7 = (f32[128]{0:T(128)S(1)}, f32[128]{0:T(128)}, u32[]{:S(2)}) copy-start(f32[128]{0:T(128)} %param.17) | copy-start | bytes 1540
  50.6 20.9 %copy-start.5 = (f32[8,128]{1,0:T(8,128)S(1)}, f32[8,128]{1,0:T(8,128)}, u32[]{:S(2)}) copy-start(f32[8,128]{1,0:T(8,128)} %get-tuple-element.8) | copy-start | bytes 12292
  52.3 1.3 %collective-permute-start.9 = (bf16[134,192]{1,0:T(8,128)(2,1)S(1)}, bf16[134,192]{1,0:T(8,128)(2,1)S(1)}, u32[]{:S(2)}, u32[]{:S(2)}) collective-permute-start(bf16[134,192]{1,0:T(8,128)(2,1)S(1)} %concatenate.104), channel_id=1, source_target_pairs={{0,4},{4,0},{8,12},{12,8},{16,20},{20,16},{24,28},{28,24},{32,36},... | collective-permute-start | bytes 154376 | tf_op jit(solution)/shard_map/ppermute | solution.py:151
  53.8 4.4 %collective-permute-start.10 = (bf16[134,192]{1,0:T(8,128)(2,1)S(1)}, bf16[134,192]{1,0:T(8,128)(2,1)S(1)}, u32[]{:S(2)}, u32[]{:S(2)}) collective-permute-start(bf16[134,192]{1,0:T(8,128)(2,1)S(1)} %concatenate.105), channel_id=1, source_target_pairs={{0,8},{4,12},{8,0},{12,4},{16,24},{20,28},{24,16},{28,20},{32,40},... | collective-permute-start | bytes 154376 | tf_op jit(solution)/shard_map/ppermute | solution.py:151
  58.3 5.3 %collective-permute-start.11 = (bf16[134,192]{1,0:T(8,128)(2,1)S(1)}, bf16[134,192]{1,0:T(8,128)(2,1)S(1)}, u32[]{:S(2)}, u32[]{:S(2)}) collective-permute-start(bf16[134,192]{1,0:T(8,128)(2,1)S(1)} %concatenate.106), channel_id=1, source_target_pairs={{0,16},{4,20},{8,24},{12,28},{16,0},{20,4},{24,8},{28,12},{32,48},... | collective-permute-start | bytes 154376 | tf_op jit(solution)/shard_map/ppermute | solution.py:151
  63.8 7.3 %collective-permute-start.12 = (bf16[134,192]{1,0:T(8,128)(2,1)S(1)}, bf16[134,192]{1,0:T(8,128)(2,1)S(1)}, u32[]{:S(2)}, u32[]{:S(2)}) collective-permute-start(bf16[134,192]{1,0:T(8,128)(2,1)S(1)} %concatenate.107), channel_id=1, source_target_pairs={{0,48},{4,52},{8,56},{12,60},{16,32},{20,36},{24,40},{28,44},{32,1... | collective-permute-start | bytes 154376 | tf_op jit(solution)/shard_map/ppermute | solution.py:151
  71.1 4.6 %collective-permute-start.13 = (bf16[134,192]{1,0:T(8,128)(2,1)S(1)}, bf16[134,192]{1,0:T(8,128)(2,1)S(1)}, u32[]{:S(2)}, u32[]{:S(2)}) collective-permute-start(bf16[134,192]{1,0:T(8,128)(2,1)S(1)} %concatenate.108), channel_id=1, source_target_pairs={{0,64},{4,68},{8,72},{12,76},{16,80},{20,84},{24,88},{28,92},{32,9... | collective-permute-start | bytes 154376 | tf_op jit(solution)/shard_map/ppermute | solution.py:151
  71.5 11.3 %copy-start.4 = (bf16[8,128]{1,0:T(8,128)(2,1)}, bf16[8,128]{1,0:T(8,128)(2,1)S(1)}, u32[]{:S(2)}) copy-start(bf16[8,128]{1,0:T(8,128)(2,1)S(1)} %convert_element_type.177) | copy-start | bytes 6148
  75.8 5.6 %collective-permute-start.14 = (bf16[134,192]{1,0:T(8,128)(2,1)S(1)}, bf16[134,192]{1,0:T(8,128)(2,1)S(1)}, u32[]{:S(2)}, u32[]{:S(2)}) collective-permute-start(bf16[134,192]{1,0:T(8,128)(2,1)S(1)} %concatenate.109), channel_id=1, source_target_pairs={{0,192},{4,196},{8,200},{12,204},{16,208},{20,212},{24,216},{28,22... | collective-permute-start | bytes 154376 | tf_op jit(solution)/shard_map/ppermute | solution.py:151
  82.6 14.5 %copy-start.1 = (bf16[4,2,640]{2,1,0:T(2,128)(2,1)S(1)}, bf16[4,2,640]{2,1,0:T(2,128)(2,1)}, u32[]{:S(2)}) copy-start(bf16[4,2,640]{2,1,0:T(2,128)(2,1)} %param.14) | copy-start | bytes 30724
  87.8 5.0 %collective-permute-start.15 = (f32[8,640]{1,0:T(8,128)S(1)}, f32[8,640]{1,0:T(8,128)S(1)}, u32[]{:S(2)}, u32[]{:S(2)}) collective-permute-start(f32[8,640]{1,0:T(8,128)S(1)} %get-tuple-element.64), channel_id=1, source_target_pairs={{0,1},{1,2},{2,3},{3,0},{4,5},{5,6},{6,7},{7,4},{8,9},{9,10},{10,1... | collective-permute-start | bytes 61448 | tf_op jit(solution)/shard_map/ppermute | solution.py:101
  88.5 4.3 %collective-permute-start.17 = (f32[8,640]{1,0:T(8,128)S(1)}, f32[8,640]{1,0:T(8,128)S(1)}, u32[]{:S(2)}, u32[]{:S(2)}) collective-permute-start(f32[8,640]{1,0:T(8,128)S(1)} %get-tuple-element.65), channel_id=1, source_target_pairs={{0,3},{1,0},{2,1},{3,2},{4,7},{5,4},{6,5},{7,6},{8,11},{9,8},{10,9... | collective-permute-start | bytes 61448 | tf_op jit(solution)/shard_map/ppermute | solution.py:101
  91.0 5.3 %collective-permute-start.16 = (f32[8,640]{1,0:T(8,128)S(1)}, f32[8,640]{1,0:T(8,128)S(1)}, u32[]{:S(2)}, u32[]{:S(2)}) collective-permute-start(f32[8,640]{1,0:T(8,128)S(1)} %get-tuple-element.66), channel_id=1, source_target_pairs={{0,2},{1,3},{2,0},{3,1},{4,6},{5,7},{6,4},{7,5},{8,10},{9,11},{10,... | collective-permute-start | bytes 61448 | tf_op jit(solution)/shard_map/ppermute | solution.py:101

commit v6 on v5

--- a/solution.py
+++ b/solution.py
@@ -95,9 +95,20 @@
 
 def reduce_scatter_mp(chunks, n_mp):
     me = lax.axis_index("mp")
-    total = lax.dynamic_index_in_dim(chunks, me, axis=0, keepdims=False)
+
+    def chunk(index):
+        return lax.dynamic_index_in_dim(chunks, index, axis=0, keepdims=False)
+
+    if n_mp == 4:
+        first = [(i, i ^ 1) for i in range(n_mp)]
+        second = [(i, i ^ 3) for i in range(n_mp)]
+        sent = lax.ppermute(jnp.stack([chunk(me ^ 1), chunk(me ^ 2)]), "mp", first)
+        mine = chunk(me) + sent[0]
+        other = chunk(me ^ 3) + sent[1]
+        return mine + lax.ppermute(other, "mp", second)
+    total = chunk(me)
     for s in range(1, n_mp):
-        outgoing = lax.dynamic_index_in_dim(chunks, (me + s) % n_mp, axis=0, keepdims=False)
+        outgoing = chunk((me + s) % n_mp)
         total = total + lax.ppermute(outgoing, "mp", [(i, (i + s) % n_mp) for i in range(n_mp)])
     return total
 

time: 98.2 us -> 99.5 us (1.013)
  waiting for transfers between devices: 40.5 us -> 41.8 us
    ppermute x3 -> x2, waiting for transfers between devices: 4.13 us -> 5.39 us  [the longest x1 3.32 us: reduce_scatter_mp(): sent = lax.ppermute(jnp.stack([chunk(me ^ 1), chunk(me ^ 2)]), 'mp', first)]
    ppermute x3 -> x2, starting transfers between devices: 3.73 us -> 3.02 us  [the longest x1 2.27 us: reduce_scatter_mp(): return mine + lax.ppermute(other, 'mp', second)]
  transfers between devices with their start and end apart: 18 -> 17, of which waited for: 14 -> 14; matrix products, arithmetic and copies ran while one was open for 9% -> 9% of each run, Pallas kernels for 0% -> 0%
where the time goes in v6:
time: 99.5 us; the launch traced here: 99 us
  waiting for transfers between devices  41.8 us (42%)
  starting transfers between devices  26.4 us (27%)
  other arithmetic  15.6 us (16%)
  local copies, waits for them, and re-layouts  6.27 us (6%)
  Pallas kernels  6.14 us (6%)
  matrix products  1.65 us (2%)
  between operations  1.15 us (1%)
    ppermute x6, waiting for transfers between devices, stats_butterfly(): arrived = lax.ppermute(packed, 'seq', pairs)  19.8 us
    ppermute x6, waiting for transfers between devices, butterfly(): lax.ppermute(value, 'seq', [(i, i ^ stride) for i in range(n_seq)])  16.6 us
    ppermute x6, starting transfers between devices, butterfly(): lax.ppermute(value, 'seq', [(i, i ^ stride) for i in range(n_seq)])  10.4 us
    ppermute x6, starting transfers between devices, stats_butterfly(): arrived = lax.ppermute(packed, 'seq', pairs)  7.65 us
    ppermute x3, starting transfers between devices, gather_mp(): lax.ppermute(block, 'mp', [(i, (i + s) % n_mp) for i in range(n_mp)])  5.31 us
    ppermute x1, waiting for transfers between devices, reduce_scatter_mp(): sent = lax.ppermute(jnp.stack([chunk(me ^ 1), chunk(me ^ 2)]), 'mp', first)  3.32 us
    pallas_call x1, Pallas kernels, small_matmul(): pl.pallas_call(_matmul_kernel, out_shape=[jax.ShapeDtypeStruct((m, n), jn...  3.31 us
    pallas_call x1, Pallas kernels, chunked_matmul(): pl.pallas_call(_chunked_kernel, out_shape=jax.ShapeDtypeStruct((chunks, m...  2.84 us
  transfers between devices with their start and end apart: 17, of which 14 were waited for; matrix products, arithmetic and copies ran while one was open for 9% of the time, Pallas kernels for 0%

profile of v6, /device:TPU:38, one launch (start us, length us, event | category | flops | bytes accessed | tf_op | source)
XLA Modules:
  0.0 99.0 jit_solution(8312537834782597951)
XLA Ops:
  0.7 3.3 %collective-permute-start.1 = (bf16[4,2,640]{2,1,0:T(2,128)(2,1)}, bf16[4,2,640]{2,1,0:T(2,128)(2,1)S(1)}, u32[]{:S(2)}, u32[]{:S(2)}) collective-permute-start(bf16[4,2,640]{2,1,0:T(2,128)(2,1)} %param.14), channel_id=1, source_target_pairs={{0,2},{1,3},{2,0},{3,1},{4,6},{5,7},{6,4},{7,5},{8,10},{9,11},{10,... | collective-permute-start | bytes 30728 | tf_op jit(solution)/shard_map/ppermute | solution.py:84
  3.9 1.1 %collective-permute-start = (bf16[4,2,640]{2,1,0:T(2,128)(2,1)}, bf16[4,2,640]{2,1,0:T(2,128)(2,1)S(1)}, u32[]{:S(2)}, u32[]{:S(2)}) collective-permute-start(bf16[4,2,640]{2,1,0:T(2,128)(2,1)} %param.14), channel_id=1, source_target_pairs={{0,3},{1,0},{2,1},{3,2},{4,7},{5,4},{6,5},{7,6},{8,11},{9,8},{10,9... | collective-permute-start | bytes 30728 | tf_op jit(solution)/shard_map/ppermute | solution.py:84
  5.0 1.0 collective-permute-start.2
  6.0 0.7 broadcast_compare_fusion.1
  6.7 0.7 broadcast_multiply_fusion
  7.3 0.7 broadcast_compare_fusion.2
  8.0 0.7 dynamic_slice.24
  8.9 0.9 select_reduce_fusion.7
  9.9 0.8 compare_and_fusion
  10.8 0.7 compare_and_fusion.1
  11.8 0.7 broadcast_select_fusion.11
  12.9 1.4 %multiply_convert_fusion.x_ref = bf16[8,2560]{1,0:T(8,128)(2,1)} fusion(f32[8,2560]{1,0:T(8,128)S(1)} %reshape.567, f32[2560]{0:T(1024)} %param.15, f32[8]{0:T(128)S(1)} %rsqrt.28), kind=kLoop, calls=%fused_computation.36 | loop fusion | flops 61440 | bytes 133152 | tf_op jit(solution)/shard_map/convert_element_type | solution.py:206
  14.3 3.3 %shard_map.157 = (f32[8,512]{1,0:T(8,128)}, f32[8,128]{1,0:T(8,128)}, f32[8,128]{1,0:T(8,128)}) custom-call(bf16[8,2560]{1,0:T(8,128)(2,1)} %multiply_convert_fusion.x_ref, bf16[2560,512]{1,0:T(8,128)(2,1)} %refs_0_.1, bf16[2560,128]{1,0:T(8,128)(2,1)} %refs_1_.1, bf16[2560,128]{1,0:T(8,128)(2,1)} %refs_2_.1), custom_call_target="tpu_custom_call" | custom-call | flops 31457280 | bytes 3997696 | tf_op jit(solution)/shard_map/pallas_call | solution.py:47
  17.6 0.9 fusion.26
  18.5 0.8 fusion.27
  19.7 0.2 fusion.33
  19.9 1.0 %collective-permute-done.3 = bf16[12,4,4,128]{3,2,1,0:T(4,128)(2,1)S(1)} collective-permute-done((bf16[12,4,4,128]{3,2,1,0:T(4,128)(2,1)S(1)}, bf16[12,4,4,128]{3,2,1,0:T(4,128)(2,1)S(1)}, u32[]{:S(2)}, u32[]{:S(2)}) %collective-permute-start.3) | collective-permute-done | bytes 49184 | tf_op jit(solution)/shard_map/ppermute | solution.py:124
  20.9 0.2 collective-permute-start.4
  21.2 3.9 %collective-permute-done.4 = bf16[12,4,4,128]{3,2,1,0:T(4,128)(2,1)S(1)} collective-permute-done((bf16[12,4,4,128]{3,2,1,0:T(4,128)(2,1)S(1)}, bf16[12,4,4,128]{3,2,1,0:T(4,128)(2,1)S(1)}, u32[]{:S(2)}, u32[]{:S(2)}) %collective-permute-start.4) | collective-permute-done | bytes 49184 | tf_op jit(solution)/shard_map/ppermute | solution.py:124
  25.1 3.4 %collective-permute-start.5 = (bf16[12,4,4,128]{3,2,1,0:T(4,128)(2,1)S(1)}, bf16[12,4,4,128]{3,2,1,0:T(4,128)(2,1)S(1)}, u32[]{:S(2)}, u32[]{:S(2)}) collective-permute-start(bf16[12,4,4,128]{3,2,1,0:T(4,128)(2,1)S(1)} %add.294), channel_id=1, source_target_pairs={{0,16},{4,20},{8,24},{12,28},{16,0},{20,4},{24,8},{28,12},{32,48},... | collective-permute-start | bytes 147464 | tf_op jit(solution)/shard_map/ppermute | solution.py:124
  28.6 2.0 %collective-permute-done.5 = bf16[12,4,4,128]{3,2,1,0:T(4,128)(2,1)S(1)} collective-permute-done((bf16[12,4,4,128]{3,2,1,0:T(4,128)(2,1)S(1)}, bf16[12,4,4,128]{3,2,1,0:T(4,128)(2,1)S(1)}, u32[]{:S(2)}, u32[]{:S(2)}) %collective-permute-start.5) | collective-permute-done | bytes 49184 | tf_op jit(solution)/shard_map/ppermute | solution.py:124
  30.6 5.2 %collective-permute-start.6 = (bf16[12,4,4,128]{3,2,1,0:T(4,128)(2,1)S(1)}, bf16[12,4,4,128]{3,2,1,0:T(4,128)(2,1)S(1)}, u32[]{:S(2)}, u32[]{:S(2)}) collective-permute-start(bf16[12,4,4,128]{3,2,1,0:T(4,128)(2,1)S(1)} %add.295), channel_id=1, source_target_pairs={{0,48},{4,52},{8,56},{12,60},{16,32},{20,36},{24,40},{28,44},{32,1... | collective-permute-start | bytes 147464 | tf_op jit(solution)/shard_map/ppermute | solution.py:124
  35.9 2.6 %collective-permute-done.6 = bf16[12,4,4,128]{3,2,1,0:T(4,128)(2,1)S(1)} collective-permute-done((bf16[12,4,4,128]{3,2,1,0:T(4,128)(2,1)S(1)}, bf16[12,4,4,128]{3,2,1,0:T(4,128)(2,1)S(1)}, u32[]{:S(2)}, u32[]{:S(2)}) %collective-permute-start.6) | collective-permute-done | bytes 49184 | tf_op jit(solution)/shard_map/ppermute | solution.py:124
  38.5 0.9 collective-permute-start.7
  39.6 3.1 %collective-permute-done.7 = bf16[12,4,4,128]{3,2,1,0:T(4,128)(2,1)S(1)} collective-permute-done((bf16[12,4,4,128]{3,2,1,0:T(4,128)(2,1)S(1)}, bf16[12,4,4,128]{3,2,1,0:T(4,128)(2,1)S(1)}, u32[]{:S(2)}, u32[]{:S(2)}) %collective-permute-start.7) | collective-permute-done | bytes 49184 | tf_op jit(solution)/shard_map/ppermute | solution.py:124
  42.7 0.6 collective-permute-start.8
  43.3 0.8 multiply_reduce_fusion.1
  44.1 4.0 %collective-permute-done.8 = bf16[12,4,4,128]{3,2,1,0:T(4,128)(2,1)S(1)} collective-permute-done((bf16[12,4,4,128]{3,2,1,0:T(4,128)(2,1)S(1)}, bf16[12,4,4,128]{3,2,1,0:T(4,128)(2,1)S(1)}, u32[]{:S(2)}, u32[]{:S(2)}) %collective-permute-start.8) | collective-permute-done | bytes 49184 | tf_op jit(solution)/shard_map/ppermute | solution.py:124
  48.2 0.6 gather_fusion
  48.8 0.5 select_reduce_fusion.1
  49.9 0.3 bitcast_reduce_fusion
  50.2 0.3 fusion.1
  50.7 0.2 fusion.83
  50.9 0.3 convolution_bitcast_fusion
  51.2 0.5 copy.152
  51.7 0.2 copy.151
  52.4 1.2 %collective-permute-done.9 = bf16[134,192]{1,0:T(8,128)(2,1)S(1)} collective-permute-done((bf16[134,192]{1,0:T(8,128)(2,1)S(1)}, bf16[134,192]{1,0:T(8,128)(2,1)S(1)}, u32[]{:S(2)}, u32[]{:S(2)}) %collective-permute-start.9) | collective-permute-done | bytes 51488 | tf_op jit(solution)/shard_map/ppermute | solution.py:162
  53.8 0.6 collective-permute-start.10
  54.5 3.7 %collective-permute-done.10 = bf16[134,192]{1,0:T(8,128)(2,1)S(1)} collective-permute-done((bf16[134,192]{1,0:T(8,128)(2,1)S(1)}, bf16[134,192]{1,0:T(8,128)(2,1)S(1)}, u32[]{:S(2)}, u32[]{:S(2)}) %collective-permute-start.10) | collective-permute-done | bytes 51488 | tf_op jit(solution)/shard_map/ppermute | solution.py:162
  58.3 1.5 %collective-permute-start.11 = (bf16[134,192]{1,0:T(8,128)(2,1)S(1)}, bf16[134,192]{1,0:T(8,128)(2,1)S(1)}, u32[]{:S(2)}, u32[]{:S(2)}) collective-permute-start(bf16[134,192]{1,0:T(8,128)(2,1)S(1)} %concatenate.106), channel_id=1, source_target_pairs={{0,16},{4,20},{8,24},{12,28},{16,0},{20,4},{24,8},{28,12},{32,48},... | collective-permute-start | bytes 154376 | tf_op jit(solution)/shard_map/ppermute | solution.py:162
  60.0 3.6 %collective-permute-done.11 = bf16[134,192]{1,0:T(8,128)(2,1)S(1)} collective-permute-done((bf16[134,192]{1,0:T(8,128)(2,1)S(1)}, bf16[134,192]{1,0:T(8,128)(2,1)S(1)}, u32[]{:S(2)}, u32[]{:S(2)}) %collective-permute-start.11) | collective-permute-done | bytes 51488 | tf_op jit(solution)/shard_map/ppermute | solution.py:162
  63.8 4.6 %collective-permute-start.12 = (bf16[134,192]{1,0:T(8,128)(2,1)S(1)}, bf16[134,192]{1,0:T(8,128)(2,1)S(1)}, u32[]{:S(2)}, u32[]{:S(2)}) collective-permute-start(bf16[134,192]{1,0:T(8,128)(2,1)S(1)} %concatenate.107), channel_id=1, source_target_pairs={{0,48},{4,52},{8,56},{12,60},{16,32},{20,36},{24,40},{28,44},{32,1... | collective-permute-start | bytes 154376 | tf_op jit(solution)/shard_map/ppermute | solution.py:162
  68.3 0.2 convolution_multiply_fusion.1
  68.5 2.5 %collective-permute-done.12 = bf16[134,192]{1,0:T(8,128)(2,1)S(1)} collective-permute-done((bf16[134,192]{1,0:T(8,128)(2,1)S(1)}, bf16[134,192]{1,0:T(8,128)(2,1)S(1)}, u32[]{:S(2)}, u32[]{:S(2)}) %collective-permute-start.12) | collective-permute-done | bytes 51488 | tf_op jit(solution)/shard_map/ppermute | solution.py:162
  71.1 0.3 collective-permute-start.13
  71.5 4.2 %collective-permute-done.13 = bf16[134,192]{1,0:T(8,128)(2,1)S(1)} collective-permute-done((bf16[134,192]{1,0:T(8,128)(2,1)S(1)}, bf16[134,192]{1,0:T(8,128)(2,1)S(1)}, u32[]{:S(2)}, u32[]{:S(2)}) %collective-permute-start.13) | collective-permute-done | bytes 51488 | tf_op jit(solution)/shard_map/ppermute | solution.py:162
  75.9 0.6 collective-permute-start.14
  76.5 0.4 copy.156
  76.9 4.5 %collective-permute-done.14 = bf16[134,192]{1,0:T(8,128)(2,1)S(1)} collective-permute-done((bf16[134,192]{1,0:T(8,128)(2,1)S(1)}, bf16[134,192]{1,0:T(8,128)(2,1)S(1)}, u32[]{:S(2)}, u32[]{:S(2)}) %collective-permute-start.14) | collective-permute-done | bytes 51488 | tf_op jit(solution)/shard_map/ppermute | solution.py:162
  81.9 0.4 copy.155
  82.4 0.2 bitcast_select_fusion
  83.0 0.3 copy.163
  83.4 0.2 copy.165
  83.6 0.6 copy.187
  84.2 2.8 %shard_map.158 = f32[4,8,640]{2,1,0:T(8,128)} custom-call(bf16[8,512]{1,0:T(8,128)(2,1)} %bitcast.179, bf16[512,2560]{1,0:T(8,128)(2,1)} %w_ref.1), custom_call_target="tpu_custom_call" | custom-call | flops 20971520 | bytes 2711552 | tf_op jit(solution)/shard_map/pallas_call | solution.py:70
  87.0 0.7 constant_dynamic-slice_fusion.1
  87.8 0.8 collective-permute-start.15
  88.5 3.3 %collective-permute-done.15 = f32[2,8,640]{2,1,0:T(8,128)S(1)} collective-permute-done((f32[2,8,640]{2,1,0:T(8,128)S(1)}, f32[2,8,640]{2,1,0:T(8,128)S(1)}, u32[]{:S(2)}, u32[]{:S(2)}) %collective-permute-start.15) | collective-permute-done | bytes 40992 | tf_op jit(solution)/shard_map/ppermute | solution.py:105
  91.9 0.7 fusion.19
  92.6 2.3 %collective-permute-start.16 = (f32[8,640]{1,0:T(8,128)S(1)}, f32[8,640]{1,0:T(8,128)S(1)}, u32[]{:S(2)}, u32[]{:S(2)}) collective-permute-start(f32[8,640]{1,0:T(8,128)S(1)} %fusion.19), channel_id=1, source_target_pairs={{0,3},{1,2},{2,1},{3,0},{4,7},{5,6},{6,5},{7,4},{8,11},{9,10},{10,... | collective-permute-start | bytes 61448 | tf_op jit(solution)/shard_map/ppermute | solution.py:108
  94.9 0.7 pad_maximum_fusion.3
  95.5 2.1 %collective-permute-done.16 = f32[8,640]{1,0:T(8,128)S(1)} collective-permute-done((f32[8,640]{1,0:T(8,128)S(1)}, f32[8,640]{1,0:T(8,128)S(1)}, u32[]{:S(2)}, u32[]{:S(2)}) %collective-permute-start.16) | collective-permute-done | bytes 20512 | tf_op jit(solution)/shard_map/ppermute | solution.py:108
  97.6 0.7 fusion.21
  98.4 0.6 add_convert_fusion
  (123 shorter events, 5.1 us)
Async XLA Ops:
  0.6 48.2 %copy-start = (bf16[16,256,128]{2,1,0:T(8,128)(2,1)S(1)}, bf16[16,256,128]{2,1,0:T(8,128)(2,1)}, u32[]{:S(2)}) copy-start(bf16[16,256,128]{2,1,0:T(8,128)(2,1)} %param.22) | copy-start | bytes 3145732
  0.6 19.0 %copy-start.2 = (s32[16]{0:T(128)S(1)}, s32[16]{0:T(128)}, u32[]{:S(2)}) copy-start(s32[16]{0:T(128)} %param.25) | copy-start | bytes 196
  0.7 17.8 %copy-start.6 = (f32[128]{0:T(128)S(1)}, f32[128]{0:T(128)}, u32[]{:S(2)}) copy-start(f32[128]{0:T(128)} %param.16) | copy-start | bytes 1540
  0.7 11.1 %collective-permute-start.1 = (bf16[4,2,640]{2,1,0:T(2,128)(2,1)}, bf16[4,2,640]{2,1,0:T(2,128)(2,1)S(1)}, u32[]{:S(2)}, u32[]{:S(2)}) collective-permute-start(bf16[4,2,640]{2,1,0:T(2,128)(2,1)} %param.14), channel_id=1, source_target_pairs={{0,2},{1,3},{2,0},{3,1},{4,6},{5,7},{6,4},{7,5},{8,10},{9,11},{10,... | collective-permute-start | bytes 30728 | tf_op jit(solution)/shard_map/ppermute | solution.py:84
  3.9 7.8 %collective-permute-start = (bf16[4,2,640]{2,1,0:T(2,128)(2,1)}, bf16[4,2,640]{2,1,0:T(2,128)(2,1)S(1)}, u32[]{:S(2)}, u32[]{:S(2)}) collective-permute-start(bf16[4,2,640]{2,1,0:T(2,128)(2,1)} %param.14), channel_id=1, source_target_pairs={{0,3},{1,0},{2,1},{3,2},{4,7},{5,4},{6,5},{7,6},{8,11},{9,8},{10,9... | collective-permute-start | bytes 30728 | tf_op jit(solution)/shard_map/ppermute | solution.py:84
  5.0 6.8 %collective-permute-start.2 = (bf16[4,2,640]{2,1,0:T(2,128)(2,1)}, bf16[4,2,640]{2,1,0:T(2,128)(2,1)S(1)}, u32[]{:S(2)}, u32[]{:S(2)}) collective-permute-start(bf16[4,2,640]{2,1,0:T(2,128)(2,1)} %param.14), channel_id=1, source_target_pairs={{0,1},{1,2},{2,3},{3,0},{4,5},{5,6},{6,7},{7,4},{8,9},{9,10},{10,1... | collective-permute-start | bytes 30728 | tf_op jit(solution)/shard_map/ppermute | solution.py:84
  17.6 32.6 %copy-start.8 = (bf16[16,256,128]{2,1,0:T(8,128)(2,1)S(1)}, bf16[16,256,128]{2,1,0:T(8,128)(2,1)}, u32[]{:S(2)}) copy-start(bf16[16,256,128]{2,1,0:T(8,128)(2,1)} %param.23) | copy-start | bytes 3145732
  19.6 1.3 %collective-permute-start.3 = (bf16[12,4,4,128]{3,2,1,0:T(4,128)(2,1)S(1)}, bf16[12,4,4,128]{3,2,1,0:T(4,128)(2,1)S(1)}, u32[]{:S(2)}, u32[]{:S(2)}) collective-permute-start(bf16[12,4,4,128]{3,2,1,0:T(4,128)(2,1)S(1)} %select_reduce_fusion.4), channel_id=1, source_target_pairs={{0,4},{4,0},{8,12},{12,8},{16,20},{20,16},{24,28},{28,24},{32,36},... | collective-permute-start | bytes 147464 | tf_op jit(solution)/shard_map/ppermute | solution.py:124
  20.9 4.2 %collective-permute-start.4 = (bf16[12,4,4,128]{3,2,1,0:T(4,128)(2,1)S(1)}, bf16[12,4,4,128]{3,2,1,0:T(4,128)(2,1)S(1)}, u32[]{:S(2)}, u32[]{:S(2)}) collective-permute-start(bf16[12,4,4,128]{3,2,1,0:T(4,128)(2,1)S(1)} %add.293), channel_id=1, source_target_pairs={{0,8},{4,12},{8,0},{12,4},{16,24},{20,28},{24,16},{28,20},{32,40},... | collective-permute-start | bytes 147464 | tf_op jit(solution)/shard_map/ppermute | solution.py:124
  25.1 5.4 %collective-permute-start.5 = (bf16[12,4,4,128]{3,2,1,0:T(4,128)(2,1)S(1)}, bf16[12,4,4,128]{3,2,1,0:T(4,128)(2,1)S(1)}, u32[]{:S(2)}, u32[]{:S(2)}) collective-permute-start(bf16[12,4,4,128]{3,2,1,0:T(4,128)(2,1)S(1)} %add.294), channel_id=1, source_target_pairs={{0,16},{4,20},{8,24},{12,28},{16,0},{20,4},{24,8},{28,12},{32,48},... | collective-permute-start | bytes 147464 | tf_op jit(solution)/shard_map/ppermute | solution.py:124
  30.6 7.8 %collective-permute-start.6 = (bf16[12,4,4,128]{3,2,1,0:T(4,128)(2,1)S(1)}, bf16[12,4,4,128]{3,2,1,0:T(4,128)(2,1)S(1)}, u32[]{:S(2)}, u32[]{:S(2)}) collective-permute-start(bf16[12,4,4,128]{3,2,1,0:T(4,128)(2,1)S(1)} %add.295), channel_id=1, source_target_pairs={{0,48},{4,52},{8,56},{12,60},{16,32},{20,36},{24,40},{28,44},{32,1... | collective-permute-start | bytes 147464 | tf_op jit(solution)/shard_map/ppermute | solution.py:124
  38.5 4.2 %collective-permute-start.7 = (bf16[12,4,4,128]{3,2,1,0:T(4,128)(2,1)S(1)}, bf16[12,4,4,128]{3,2,1,0:T(4,128)(2,1)S(1)}, u32[]{:S(2)}, u32[]{:S(2)}) collective-permute-start(bf16[12,4,4,128]{3,2,1,0:T(4,128)(2,1)S(1)} %add.296), channel_id=1, source_target_pairs={{0,64},{4,68},{8,72},{12,76},{16,80},{20,84},{24,88},{28,92},{32,9... | collective-permute-start | bytes 147464 | tf_op jit(solution)/shard_map/ppermute | solution.py:124
  42.7 5.4 %collective-permute-start.8 = (bf16[12,4,4,128]{3,2,1,0:T(4,128)(2,1)S(1)}, bf16[12,4,4,128]{3,2,1,0:T(4,128)(2,1)S(1)}, u32[]{:S(2)}, u32[]{:S(2)}) collective-permute-start(bf16[12,4,4,128]{3,2,1,0:T(4,128)(2,1)S(1)} %add.297), channel_id=1, source_target_pairs={{0,192},{4,196},{8,200},{12,204},{16,208},{20,212},{24,216},{28,22... | collective-permute-start | bytes 147464 | tf_op jit(solution)/shard_map/ppermute | solution.py:124
  50.2 4.2 %copy-start.3 = (f32[8,128]{1,0:T(8,128)S(1)}, f32[8,128]{1,0:T(8,128)}, u32[]{:S(2)}) copy-start(f32[8,128]{1,0:T(8,128)} %get-tuple-element.7) | copy-start | bytes 12292
  50.2 4.2 %copy-start.7 = (f32[128]{0:T(128)S(1)}, f32[128]{0:T(128)}, u32[]{:S(2)}) copy-start(f32[128]{0:T(128)} %param.17) | copy-start | bytes 1540
  50.6 20.9 %copy-start.5 = (f32[8,128]{1,0:T(8,128)S(1)}, f32[8,128]{1,0:T(8,128)}, u32[]{:S(2)}) copy-start(f32[8,128]{1,0:T(8,128)} %get-tuple-element.8) | copy-start | bytes 12292
  52.3 1.3 %collective-permute-start.9 = (bf16[134,192]{1,0:T(8,128)(2,1)S(1)}, bf16[134,192]{1,0:T(8,128)(2,1)S(1)}, u32[]{:S(2)}, u32[]{:S(2)}) collective-permute-start(bf16[134,192]{1,0:T(8,128)(2,1)S(1)} %concatenate.104), channel_id=1, source_target_pairs={{0,4},{4,0},{8,12},{12,8},{16,20},{20,16},{24,28},{28,24},{32,36},... | collective-permute-start | bytes 154376 | tf_op jit(solution)/shard_map/ppermute | solution.py:162
  53.8 4.4 %collective-permute-start.10 = (bf16[134,192]{1,0:T(8,128)(2,1)S(1)}, bf16[134,192]{1,0:T(8,128)(2,1)S(1)}, u32[]{:S(2)}, u32[]{:S(2)}) collective-permute-start(bf16[134,192]{1,0:T(8,128)(2,1)S(1)} %concatenate.105), channel_id=1, source_target_pairs={{0,8},{4,12},{8,0},{12,4},{16,24},{20,28},{24,16},{28,20},{32,40},... | collective-permute-start | bytes 154376 | tf_op jit(solution)/shard_map/ppermute | solution.py:162
  58.3 5.3 %collective-permute-start.11 = (bf16[134,192]{1,0:T(8,128)(2,1)S(1)}, bf16[134,192]{1,0:T(8,128)(2,1)S(1)}, u32[]{:S(2)}, u32[]{:S(2)}) collective-permute-start(bf16[134,192]{1,0:T(8,128)(2,1)S(1)} %concatenate.106), channel_id=1, source_target_pairs={{0,16},{4,20},{8,24},{12,28},{16,0},{20,4},{24,8},{28,12},{32,48},... | collective-permute-start | bytes 154376 | tf_op jit(solution)/shard_map/ppermute | solution.py:162
  63.8 7.3 %collective-permute-start.12 = (bf16[134,192]{1,0:T(8,128)(2,1)S(1)}, bf16[134,192]{1,0:T(8,128)(2,1)S(1)}, u32[]{:S(2)}, u32[]{:S(2)}) collective-permute-start(bf16[134,192]{1,0:T(8,128)(2,1)S(1)} %concatenate.107), channel_id=1, source_target_pairs={{0,48},{4,52},{8,56},{12,60},{16,32},{20,36},{24,40},{28,44},{32,1... | collective-permute-start | bytes 154376 | tf_op jit(solution)/shard_map/ppermute | solution.py:162
  71.1 4.6 %collective-permute-start.13 = (bf16[134,192]{1,0:T(8,128)(2,1)S(1)}, bf16[134,192]{1,0:T(8,128)(2,1)S(1)}, u32[]{:S(2)}, u32[]{:S(2)}) collective-permute-start(bf16[134,192]{1,0:T(8,128)(2,1)S(1)} %concatenate.108), channel_id=1, source_target_pairs={{0,64},{4,68},{8,72},{12,76},{16,80},{20,84},{24,88},{28,92},{32,9... | collective-permute-start | bytes 154376 | tf_op jit(solution)/shard_map/ppermute | solution.py:162
  71.5 11.3 %copy-start.4 = (bf16[8,128]{1,0:T(8,128)(2,1)}, bf16[8,128]{1,0:T(8,128)(2,1)S(1)}, u32[]{:S(2)}) copy-start(bf16[8,128]{1,0:T(8,128)(2,1)S(1)} %convert_element_type.177) | copy-start | bytes 6148
  75.9 5.6 %collective-permute-start.14 = (bf16[134,192]{1,0:T(8,128)(2,1)S(1)}, bf16[134,192]{1,0:T(8,128)(2,1)S(1)}, u32[]{:S(2)}, u32[]{:S(2)}) collective-permute-start(bf16[134,192]{1,0:T(8,128)(2,1)S(1)} %concatenate.109), channel_id=1, source_target_pairs={{0,192},{4,196},{8,200},{12,204},{16,208},{20,212},{24,216},{28,22... | collective-permute-start | bytes 154376 | tf_op jit(solution)/shard_map/ppermute | solution.py:162
  83.0 15.4 %copy-start.1 = (bf16[4,2,640]{2,1,0:T(2,128)(2,1)S(1)}, bf16[4,2,640]{2,1,0:T(2,128)(2,1)}, u32[]{:S(2)}) copy-start(bf16[4,2,640]{2,1,0:T(2,128)(2,1)} %param.14) | copy-start | bytes 30724
  87.8 4.1 %collective-permute-start.15 = (f32[2,8,640]{2,1,0:T(8,128)S(1)}, f32[2,8,640]{2,1,0:T(8,128)S(1)}, u32[]{:S(2)}, u32[]{:S(2)}) collective-permute-start(f32[2,8,640]{2,1,0:T(8,128)S(1)} %pad_maximum_fusion.1), channel_id=1, source_target_pairs={{0,1},{1,0},{2,3},{3,2},{4,5},{5,4},{6,7},{7,6},{8,9},{9,8},{10,11... | collective-permute-start | bytes 122888 | tf_op jit(solution)/shard_map/ppermute | solution.py:105
  92.6 5.0 %collective-permute-start.16 = (f32[8,640]{1,0:T(8,128)S(1)}, f32[8,640]{1,0:T(8,128)S(1)}, u32[]{:S(2)}, u32[]{:S(2)}) collective-permute-start(f32[8,640]{1,0:T(8,128)S(1)} %fusion.19), channel_id=1, source_target_pairs={{0,3},{1,2},{2,1},{3,0},{4,7},{5,6},{6,5},{7,4},{8,11},{9,10},{10,... | collective-permute-start | bytes 61448 | tf_op jit(solution)/shard_map/ppermute | solution.py:108

commit v7 on v5

--- a/solution.py
+++ b/solution.py
@@ -93,11 +93,20 @@
     return jnp.concatenate(ordered, axis=-1)
 
 
-def reduce_scatter_mp(chunks, n_mp):
+def reduce_scatter_mp(full, n_mp):
     me = lax.axis_index("mp")
-    total = lax.dynamic_index_in_dim(chunks, me, axis=0, keepdims=False)
+    width = full.shape[-1] // n_mp
+    pieces = [full[:, c * width : (c + 1) * width] for c in range(n_mp)]
+
+    def chunk(index):
+        chosen = pieces[0]
+        for c in range(1, n_mp):
+            chosen = jnp.where(index == c, pieces[c], chosen)
+        return chosen
+
+    total = chunk(me)
     for s in range(1, n_mp):
-        outgoing = lax.dynamic_index_in_dim(chunks, (me + s) % n_mp, axis=0, keepdims=False)
+        outgoing = chunk((me + s) % n_mp)
         total = total + lax.ppermute(outgoing, "mp", [(i, (i + s) % n_mp) for i in range(n_mp)])
     return total
 
@@ -311,7 +320,7 @@
     )
     attended = (mixture / denominator[..., None]).astype(jnp.bfloat16)
     attended = attended.transpose(1, 0, 2, 3, 4).reshape(steps * own_rows, q_heads * HEAD_SIZE)
-    projected = chunked_matmul(attended, w_out, n_mp)
+    projected = jnp.dot(attended, w_out, preferred_element_type=jnp.float32)
     summed = reduce_scatter_mp(projected, n_mp).reshape(steps, own_rows, -1)
     hidden = (states.astype(jnp.float32) + summed).astype(jnp.bfloat16)
     return hidden, new_keys, new_values

time: 98.2 us -> 99 us (level)
  waiting for transfers between devices: 40.5 us -> 35.5 us
  other arithmetic: 14.9 us -> 18.7 us
  matrix products: 1.65 us -> 4.54 us
  Pallas kernels: 6.15 us -> 3.31 us
  local copies, waits for them, and re-layouts: 6.29 us -> 7.81 us
    pallas_call x1 -> x0, Pallas kernels: 2.85 us -> none  [chunked_matmul(): pl.pallas_call(_chunked_kernel, out_shape=jax.ShapeDtypeStruct((chunks, m...]
    ppermute x3, waiting for transfers between devices: 4.13 us -> 2.19 us  [reduce_scatter_mp(): lax.ppermute(outgoing, 'mp', [(i, (i + s) % n_mp) for i in range(n_mp)])]
    ppermute x6, waiting for transfers between devices: 16.6 us -> 15 us  [butterfly(): lax.ppermute(value, 'seq', [(i, i ^ stride) for i in range(n_seq)])]
    ppermute x6, waiting for transfers between devices: 19.8 us -> 18.3 us  [stats_butterfly(): arrived = lax.ppermute(packed, 'seq', pairs)]
    dot_general x1, matrix products: 0.34 us -> 1.57 us  [shards(): jnp.einsum('stngk,sknd->stngd', weights.astype(jnp.bfloat16), values_spli...]
    dot_general x1, matrix products: 0.53 us -> 1.75 us  [shards(): jnp.einsum('stngd,sknd->stngk', slot_query, keys_split, preferred_element...]
    select_n x1, other arithmetic: 0.2 us -> 1.4 us  [shards(): jnp.where(own_is_long[:, None, None, None, None], from_long, stats[LONG_C...]
    transpose x1, other arithmetic: 0.16 us -> 1.2 us  [shards(): attended.transpose(1, 0, 2, 3, 4)]
  transfers between devices with their start and end apart: 18 -> 18, of which waited for: 14 -> 14; matrix products, arithmetic and copies ran while one was open for 9% -> 12% of each run, Pallas kernels for 0% -> 0%
where the time goes in v7:
time: 99 us; the launch traced here: 98.5 us
  waiting for transfers between devices  35.5 us (36%)
  starting transfers between devices  27.5 us (28%)
  other arithmetic  18.7 us (19%)
  local copies, waits for them, and re-layouts  7.81 us (8%)
  matrix products  4.54 us (5%)
  Pallas kernels  3.31 us (3%)
  between operations  1.15 us (1%)
    ppermute x6, waiting for transfers between devices, stats_butterfly(): arrived = lax.ppermute(packed, 'seq', pairs)  18.3 us
    ppermute x6, waiting for transfers between devices, butterfly(): lax.ppermute(value, 'seq', [(i, i ^ stride) for i in range(n_seq)])  15 us
    ppermute x6, starting transfers between devices, butterfly(): lax.ppermute(value, 'seq', [(i, i ^ stride) for i in range(n_seq)])  10.4 us
    ppermute x6, starting transfers between devices, stats_butterfly(): arrived = lax.ppermute(packed, 'seq', pairs)  7.65 us
    ppermute x3, starting transfers between devices, reduce_scatter_mp(): lax.ppermute(outgoing, 'mp', [(i, (i + s) % n_mp) for i in range(n_mp)])  4.74 us
    ppermute x3, starting transfers between devices, gather_mp(): lax.ppermute(block, 'mp', [(i, (i + s) % n_mp) for i in range(n_mp)])  4.69 us
    pallas_call x1, Pallas kernels, small_matmul(): pl.pallas_call(_matmul_kernel, out_shape=[jax.ShapeDtypeStruct((m, n), jn...  3.31 us
    ppermute x3, waiting for transfers between devices, reduce_scatter_mp(): lax.ppermute(outgoing, 'mp', [(i, (i + s) % n_mp) for i in range(n_mp)])  2.19 us
  transfers between devices with their start and end apart: 18, of which 14 were waited for; matrix products, arithmetic and copies ran while one was open for 12% of the time, Pallas kernels for 0%

profile of v7, /device:TPU:38, one launch (start us, length us, event | category | flops | bytes accessed | tf_op | source)
XLA Modules:
  0.0 98.5 jit_solution(6880617408337030632)
XLA Ops:
  0.7 3.1 %collective-permute-start = (bf16[4,2,640]{2,1,0:T(2,128)(2,1)}, bf16[4,2,640]{2,1,0:T(2,128)(2,1)S(1)}, u32[]{:S(2)}, u32[]{:S(2)}) collective-permute-start(bf16[4,2,640]{2,1,0:T(2,128)(2,1)} %param.14), channel_id=1, source_target_pairs={{0,3},{1,0},{2,1},{3,2},{4,7},{5,4},{6,5},{7,6},{8,11},{9,8},{10,9... | collective-permute-start | bytes 30728 | tf_op jit(solution)/shard_map/ppermute | solution.py:84
  3.8 0.6 collective-permute-start.1
  4.4 1.0 collective-permute-start.2
  5.4 0.7 broadcast_compare_fusion.2
  6.1 0.7 dynamic_slice.11
  7.1 0.9 select_reduce_fusion.7
  8.0 0.7 broadcast_compare_fusion.1
  8.6 0.7 broadcast_multiply_fusion
  9.3 0.8 compare_and_fusion
  10.2 0.7 compare_and_fusion.1
  11.2 0.7 broadcast_select_fusion.11
  12.3 1.4 %multiply_convert_fusion.x_ref = bf16[8,2560]{1,0:T(8,128)(2,1)} fusion(f32[8,2560]{1,0:T(8,128)S(1)} %reshape.565, f32[2560]{0:T(1024)} %param.15, f32[8]{0:T(128)S(1)} %rsqrt.28), kind=kLoop, calls=%fused_computation.36 | loop fusion | flops 61440 | bytes 133152 | tf_op jit(solution)/shard_map/convert_element_type | solution.py:204
  13.7 3.3 %shard_map.157 = (f32[8,512]{1,0:T(8,128)}, f32[8,128]{1,0:T(8,128)}, f32[8,128]{1,0:T(8,128)}) custom-call(bf16[8,2560]{1,0:T(8,128)(2,1)} %multiply_convert_fusion.x_ref, bf16[2560,512]{1,0:T(8,128)(2,1)} %refs_0_.1, bf16[2560,128]{1,0:T(8,128)(2,1)} %refs_1_.1, bf16[2560,128]{1,0:T(8,128)(2,1)} %refs_2_.1), custom_call_target="tpu_custom_call" | custom-call | flops 31457280 | bytes 3997696 | tf_op jit(solution)/shard_map/pallas_call | solution.py:47
  17.0 0.8 fusion.23
  17.8 0.8 fusion.24
  19.2 1.0 %collective-permute-done.3 = bf16[12,4,4,128]{3,2,1,0:T(4,128)(2,1)S(1)} collective-permute-done((bf16[12,4,4,128]{3,2,1,0:T(4,128)(2,1)S(1)}, bf16[12,4,4,128]{3,2,1,0:T(4,128)(2,1)S(1)}, u32[]{:S(2)}, u32[]{:S(2)}) %collective-permute-start.3) | collective-permute-done | bytes 49184 | tf_op jit(solution)/shard_map/ppermute | solution.py:122
  20.3 0.2 collective-permute-start.4
  20.5 3.9 %collective-permute-done.4 = bf16[12,4,4,128]{3,2,1,0:T(4,128)(2,1)S(1)} collective-permute-done((bf16[12,4,4,128]{3,2,1,0:T(4,128)(2,1)S(1)}, bf16[12,4,4,128]{3,2,1,0:T(4,128)(2,1)S(1)}, u32[]{:S(2)}, u32[]{:S(2)}) %collective-permute-start.4) | collective-permute-done | bytes 49184 | tf_op jit(solution)/shard_map/ppermute | solution.py:122
  24.5 3.4 %collective-permute-start.5 = (bf16[12,4,4,128]{3,2,1,0:T(4,128)(2,1)S(1)}, bf16[12,4,4,128]{3,2,1,0:T(4,128)(2,1)S(1)}, u32[]{:S(2)}, u32[]{:S(2)}) collective-permute-start(bf16[12,4,4,128]{3,2,1,0:T(4,128)(2,1)S(1)} %add.293), channel_id=1, source_target_pairs={{0,16},{4,20},{8,24},{12,28},{16,0},{20,4},{24,8},{28,12},{32,48},... | collective-permute-start | bytes 147464 | tf_op jit(solution)/shard_map/ppermute | solution.py:122
  27.8 0.6 iota_compare_fusion.4
  28.4 1.5 %collective-permute-done.5 = bf16[12,4,4,128]{3,2,1,0:T(4,128)(2,1)S(1)} collective-permute-done((bf16[12,4,4,128]{3,2,1,0:T(4,128)(2,1)S(1)}, bf16[12,4,4,128]{3,2,1,0:T(4,128)(2,1)S(1)}, u32[]{:S(2)}, u32[]{:S(2)}) %collective-permute-start.5) | collective-permute-done | bytes 49184 | tf_op jit(solution)/shard_map/ppermute | solution.py:122
  29.9 5.2 %collective-permute-start.6 = (bf16[12,4,4,128]{3,2,1,0:T(4,128)(2,1)S(1)}, bf16[12,4,4,128]{3,2,1,0:T(4,128)(2,1)S(1)}, u32[]{:S(2)}, u32[]{:S(2)}) collective-permute-start(bf16[12,4,4,128]{3,2,1,0:T(4,128)(2,1)S(1)} %add.294), channel_id=1, source_target_pairs={{0,48},{4,52},{8,56},{12,60},{16,32},{20,36},{24,40},{28,44},{32,1... | collective-permute-start | bytes 147464 | tf_op jit(solution)/shard_map/ppermute | solution.py:122
  35.2 2.6 %collective-permute-done.6 = bf16[12,4,4,128]{3,2,1,0:T(4,128)(2,1)S(1)} collective-permute-done((bf16[12,4,4,128]{3,2,1,0:T(4,128)(2,1)S(1)}, bf16[12,4,4,128]{3,2,1,0:T(4,128)(2,1)S(1)}, u32[]{:S(2)}, u32[]{:S(2)}) %collective-permute-start.6) | collective-permute-done | bytes 49184 | tf_op jit(solution)/shard_map/ppermute | solution.py:122
  37.8 0.9 collective-permute-start.7
  38.7 0.5 iota_compare_fusion.3
  39.2 0.7 dynamic_slice.9
  40.0 2.0 %collective-permute-done.7 = bf16[12,4,4,128]{3,2,1,0:T(4,128)(2,1)S(1)} collective-permute-done((bf16[12,4,4,128]{3,2,1,0:T(4,128)(2,1)S(1)}, bf16[12,4,4,128]{3,2,1,0:T(4,128)(2,1)S(1)}, u32[]{:S(2)}, u32[]{:S(2)}) %collective-permute-start.7) | collective-permute-done | bytes 49184 | tf_op jit(solution)/shard_map/ppermute | solution.py:122
  42.0 0.6 collective-permute-start.8
  42.6 0.8 multiply_reduce_fusion.1
  43.4 4.0 %collective-permute-done.8 = bf16[12,4,4,128]{3,2,1,0:T(4,128)(2,1)S(1)} collective-permute-done((bf16[12,4,4,128]{3,2,1,0:T(4,128)(2,1)S(1)}, bf16[12,4,4,128]{3,2,1,0:T(4,128)(2,1)S(1)}, u32[]{:S(2)}, u32[]{:S(2)}) %collective-permute-start.8) | collective-permute-done | bytes 49184 | tf_op jit(solution)/shard_map/ppermute | solution.py:122
  47.5 0.6 gather_fusion
  48.1 1.8 %select_reduce_fusion.1 = (f32[16,4,4]{2,1,0:T(4,128)S(1)}, f32[16,1,256,4,4]{2,4,3,0,1:T(4,128)S(1)}) fusion(pred[16,256]{1,0:T(8,128)(4,1)S(1)} %fusion.25, bf16[16,256,128]{2,1,0:T(8,128)(2,1)} %param.22, bf16[16,4,4,128]{3,2,1,0:T(4,128)(2,1)S(1)} %gather_fusion, pred[16]{0:T(512)(128)(4,1)S(1)} %get-tuple-element.52), kind=kOutput, calls=%fused_computation.17 | convolution fusion | flops 17006336 | bytes 1381392 | tf_op jit(solution)/shard_map/stngd,sknd->stngk/dot_general | solution.py:254
  50.2 0.3 bitcast_reduce_fusion
  50.6 1.6 %fusion.1 = f32[16,4,4,128]{3,2,1,0:T(4,128)S(1)} fusion(bf16[16,256,128]{2,1,0:T(8,128)(2,1)} %param.23, f32[16,1,256,4,4]{2,4,3,0,1:T(4,128)S(1)} %get-tuple-element.133, f32[16,4,4]{2,1,0:T(4,128)S(1)} %copy.145, pred[16,256]{1,0:T(8,128)(4,1)S(1)} %fusion.25), kind=kOutput, calls=%fused_computation.5 | convolution fusion | flops 17039360 | bytes 1446912 | tf_op jit(solution)/shard_map/stngk,sknd->stngd/dot_general | solution.py:271
  52.2 0.3 convolution_bitcast_fusion
  52.8 0.2 copy.150
  53.2 0.5 copy.151
  54.2 1.2 %collective-permute-done.9 = bf16[134,192]{1,0:T(8,128)(2,1)S(1)} collective-permute-done((bf16[134,192]{1,0:T(8,128)(2,1)S(1)}, bf16[134,192]{1,0:T(8,128)(2,1)S(1)}, u32[]{:S(2)}, u32[]{:S(2)}) %collective-permute-start.9) | collective-permute-done | bytes 51488 | tf_op jit(solution)/shard_map/ppermute | solution.py:160
  55.5 0.6 collective-permute-start.10
  56.3 3.7 %collective-permute-done.10 = bf16[134,192]{1,0:T(8,128)(2,1)S(1)} collective-permute-done((bf16[134,192]{1,0:T(8,128)(2,1)S(1)}, bf16[134,192]{1,0:T(8,128)(2,1)S(1)}, u32[]{:S(2)}, u32[]{:S(2)}) %collective-permute-start.10) | collective-permute-done | bytes 51488 | tf_op jit(solution)/shard_map/ppermute | solution.py:160
  60.1 1.5 %collective-permute-start.11 = (bf16[134,192]{1,0:T(8,128)(2,1)S(1)}, bf16[134,192]{1,0:T(8,128)(2,1)S(1)}, u32[]{:S(2)}, u32[]{:S(2)}) collective-permute-start(bf16[134,192]{1,0:T(8,128)(2,1)S(1)} %concatenate.106), channel_id=1, source_target_pairs={{0,16},{4,20},{8,24},{12,28},{16,0},{20,4},{24,8},{28,12},{32,48},... | collective-permute-start | bytes 154376 | tf_op jit(solution)/shard_map/ppermute | solution.py:160
  61.7 3.6 %collective-permute-done.11 = bf16[134,192]{1,0:T(8,128)(2,1)S(1)} collective-permute-done((bf16[134,192]{1,0:T(8,128)(2,1)S(1)}, bf16[134,192]{1,0:T(8,128)(2,1)S(1)}, u32[]{:S(2)}, u32[]{:S(2)}) %collective-permute-start.11) | collective-permute-done | bytes 51488 | tf_op jit(solution)/shard_map/ppermute | solution.py:160
  65.5 4.6 %collective-permute-start.12 = (bf16[134,192]{1,0:T(8,128)(2,1)S(1)}, bf16[134,192]{1,0:T(8,128)(2,1)S(1)}, u32[]{:S(2)}, u32[]{:S(2)}) collective-permute-start(bf16[134,192]{1,0:T(8,128)(2,1)S(1)} %concatenate.107), channel_id=1, source_target_pairs={{0,48},{4,52},{8,56},{12,60},{16,32},{20,36},{24,40},{28,44},{32,1... | collective-permute-start | bytes 154376 | tf_op jit(solution)/shard_map/ppermute | solution.py:160
  70.1 0.2 convolution_multiply_fusion.1
  70.3 2.5 %collective-permute-done.12 = bf16[134,192]{1,0:T(8,128)(2,1)S(1)} collective-permute-done((bf16[134,192]{1,0:T(8,128)(2,1)S(1)}, bf16[134,192]{1,0:T(8,128)(2,1)S(1)}, u32[]{:S(2)}, u32[]{:S(2)}) %collective-permute-start.12) | collective-permute-done | bytes 51488 | tf_op jit(solution)/shard_map/ppermute | solution.py:160
  72.9 0.3 collective-permute-start.13
  73.2 0.7 fusion.19
  74.0 3.5 %collective-permute-done.13 = bf16[134,192]{1,0:T(8,128)(2,1)S(1)} collective-permute-done((bf16[134,192]{1,0:T(8,128)(2,1)S(1)}, bf16[134,192]{1,0:T(8,128)(2,1)S(1)}, u32[]{:S(2)}, u32[]{:S(2)}) %collective-permute-start.13) | collective-permute-done | bytes 51488 | tf_op jit(solution)/shard_map/ppermute | solution.py:160
  77.6 0.6 collective-permute-start.14
  78.3 1.2 %copy.155 = f32[2,4,1,4,130]{3,1,4,2,0:T(4,128)} copy(f32[2,4,1,4,130]{4,3,2,1,0:T(4,128)S(1)} %pad_maximum_fusion.1) | data formatting | bytes 33280 | tf_op jit(solution)/shard_map/slice | solution.py:294
  79.5 3.8 %collective-permute-done.14 = bf16[134,192]{1,0:T(8,128)(2,1)S(1)} collective-permute-done((bf16[134,192]{1,0:T(8,128)(2,1)S(1)}, bf16[134,192]{1,0:T(8,128)(2,1)S(1)}, u32[]{:S(2)}, u32[]{:S(2)}) %collective-permute-start.14) | collective-permute-done | bytes 51488 | tf_op jit(solution)/shard_map/ppermute | solution.py:160
  83.6 0.8 select_reduce_fusion
  84.3 1.2 %copy.154 = f32[2,4,4,130]{2,1,3,0:T(4,128)} copy(f32[2,4,4,130]{3,2,1,0:T(4,128)S(1)} %select_reduce_fusion) | data formatting | bytes 33280 | tf_op jit(solution)/shard_map/reduce_sum | solution.py:291
  85.5 1.4 %bitcast_select_fusion = f32[2,4,1,4,130]{3,1,4,2,0:T(4,128)S(1)} fusion(f32[2,4,1,4,130]{3,1,4,2,0:T(4,128)} %copy.155, f32[2,4,4,130]{2,1,3,0:T(4,128)} %copy.154, pred[2]{0:T(512)(128)(4,1)} %dynamic_slice.9), kind=kLoop, calls=%fused_computation.8 | loop fusion | flops 4160 | bytes 49922 | tf_op jit(solution)/shard_map/jit(_where)/select_n | solution.py:294
  87.3 1.0 %copy.162 = f32[2,128,4,4]{3,2,1,0:T(4,128)} copy(f32[2,128,4,4]{1,3,2,0:T(4,128)S(1)} %fusion.29) | data formatting | bytes 32768 | tf_op jit(solution)/shard_map/rtngj,rjnd->rtngd/dot_general | solution.py:315
  88.4 1.2 %fusion.7 = bf16[4,2,1,4,128]{3,0,4,2,1:T(4,128)(2,1)S(1)} fusion(f32[2,4,4]{2,1,0:T(4,128)S(1)} %get-tuple-element.57, f32[2,128,4,4]{3,2,1,0:T(4,128)} %copy.162, f32[2,4,4]{2,1,0:T(4,128)S(1)} %get-tuple-element.56, f32[2,4,1,4,130]{3,1,4,2,0:T(4,128)S(1)} %bitcast_select_fusion), kind=kLoop, calls=%fused_computation.18 | loop fusion | flops 16384 | bytes 41216 | tf_op jit(solution)/shard_map/transpose | solution.py:322
  89.7 0.5 fusion.26
  90.2 2.0 %collective-permute-start.15 = (f32[8,640]{1,0:T(8,128)S(1)}, f32[8,640]{1,0:T(8,128)S(1)}, u32[]{:S(2)}, u32[]{:S(2)}) collective-permute-start(f32[8,640]{1,0:T(8,128)S(1)} %get-tuple-element.64), channel_id=1, source_target_pairs={{0,1},{1,2},{2,3},{3,0},{4,5},{5,6},{6,7},{7,4},{8,9},{9,10},{10,1... | collective-permute-start | bytes 61448 | tf_op jit(solution)/shard_map/ppermute | solution.py:110
  92.2 1.8 %collective-permute-start.16 = (f32[8,640]{1,0:T(8,128)S(1)}, f32[8,640]{1,0:T(8,128)S(1)}, u32[]{:S(2)}, u32[]{:S(2)}) collective-permute-start(f32[8,640]{1,0:T(8,128)S(1)} %get-tuple-element.65), channel_id=1, source_target_pairs={{0,2},{1,3},{2,0},{3,1},{4,6},{5,7},{6,4},{7,5},{8,10},{9,11},{10,... | collective-permute-start | bytes 61448 | tf_op jit(solution)/shard_map/ppermute | solution.py:110
  94.0 0.9 collective-permute-start.17
  95.0 0.7 pad_maximum_fusion.2
  95.6 1.8 %collective-permute-done.16 = f32[8,640]{1,0:T(8,128)S(1)} collective-permute-done((f32[8,640]{1,0:T(8,128)S(1)}, f32[8,640]{1,0:T(8,128)S(1)}, u32[]{:S(2)}, u32[]{:S(2)}) %collective-permute-start.16) | collective-permute-done | bytes 20512 | tf_op jit(solution)/shard_map/ppermute | solution.py:110
  97.5 0.3 collective-permute-done.17
  97.9 0.6 add_convert_fusion
  (127 shorter events, 5.2 us)
Async XLA Ops:
  0.6 89.1 %copy-start = (bf16[512,2560]{1,0:T(8,128)(2,1)S(1)}, bf16[512,2560]{1,0:T(8,128)(2,1)}, u32[]{:S(2)}) copy-start(bf16[512,2560]{1,0:T(8,128)(2,1)} %param.21) | copy-start | bytes 7864324
  0.6 18.4 %copy-start.2 = (s32[16]{0:T(128)S(1)}, s32[16]{0:T(128)}, u32[]{:S(2)}) copy-start(s32[16]{0:T(128)} %param.25) | copy-start | bytes 196
  0.7 17.1 %copy-start.9 = (f32[128]{0:T(128)S(1)}, f32[128]{0:T(128)}, u32[]{:S(2)}) copy-start(f32[128]{0:T(128)} %param.16) | copy-start | bytes 1540
  0.7 10.5 %collective-permute-start = (bf16[4,2,640]{2,1,0:T(2,128)(2,1)}, bf16[4,2,640]{2,1,0:T(2,128)(2,1)S(1)}, u32[]{:S(2)}, u32[]{:S(2)}) collective-permute-start(bf16[4,2,640]{2,1,0:T(2,128)(2,1)} %param.14), channel_id=1, source_target_pairs={{0,3},{1,0},{2,1},{3,2},{4,7},{5,4},{6,5},{7,6},{8,11},{9,8},{10,9... | collective-permute-start | bytes 30728 | tf_op jit(solution)/shard_map/ppermute | solution.py:84
  3.8 7.4 %collective-permute-start.1 = (bf16[4,2,640]{2,1,0:T(2,128)(2,1)}, bf16[4,2,640]{2,1,0:T(2,128)(2,1)S(1)}, u32[]{:S(2)}, u32[]{:S(2)}) collective-permute-start(bf16[4,2,640]{2,1,0:T(2,128)(2,1)} %param.14), channel_id=1, source_target_pairs={{0,2},{1,3},{2,0},{3,1},{4,6},{5,7},{6,4},{7,5},{8,10},{9,11},{10,... | collective-permute-start | bytes 30728 | tf_op jit(solution)/shard_map/ppermute | solution.py:84
  4.4 6.8 %collective-permute-start.2 = (bf16[4,2,640]{2,1,0:T(2,128)(2,1)}, bf16[4,2,640]{2,1,0:T(2,128)(2,1)S(1)}, u32[]{:S(2)}, u32[]{:S(2)}) collective-permute-start(bf16[4,2,640]{2,1,0:T(2,128)(2,1)} %param.14), channel_id=1, source_target_pairs={{0,1},{1,2},{2,3},{3,0},{4,5},{5,6},{6,7},{7,4},{8,9},{9,10},{10,1... | collective-permute-start | bytes 30728 | tf_op jit(solution)/shard_map/ppermute | solution.py:84
  5.4 5.6 %copy-start.7 = (f32[64]{0:T(128)}, f32[64]{0:T(128)S(1)}, u32[]{:S(2)}) copy-start(f32[64]{0:T(128)S(1)} %multiply_power_fusion) | copy-start | bytes 772
  18.9 1.3 %collective-permute-start.3 = (bf16[12,4,4,128]{3,2,1,0:T(4,128)(2,1)S(1)}, bf16[12,4,4,128]{3,2,1,0:T(4,128)(2,1)S(1)}, u32[]{:S(2)}, u32[]{:S(2)}) collective-permute-start(bf16[12,4,4,128]{3,2,1,0:T(4,128)(2,1)S(1)} %select_reduce_fusion.4), channel_id=1, source_target_pairs={{0,4},{4,0},{8,12},{12,8},{16,20},{20,16},{24,28},{28,24},{32,36},... | collective-permute-start | bytes 147464 | tf_op jit(solution)/shard_map/ppermute | solution.py:122
  20.3 4.2 %collective-permute-start.4 = (bf16[12,4,4,128]{3,2,1,0:T(4,128)(2,1)S(1)}, bf16[12,4,4,128]{3,2,1,0:T(4,128)(2,1)S(1)}, u32[]{:S(2)}, u32[]{:S(2)}) collective-permute-start(bf16[12,4,4,128]{3,2,1,0:T(4,128)(2,1)S(1)} %add.292), channel_id=1, source_target_pairs={{0,8},{4,12},{8,0},{12,4},{16,24},{20,28},{24,16},{28,20},{32,40},... | collective-permute-start | bytes 147464 | tf_op jit(solution)/shard_map/ppermute | solution.py:122
  24.5 5.4 %collective-permute-start.5 = (bf16[12,4,4,128]{3,2,1,0:T(4,128)(2,1)S(1)}, bf16[12,4,4,128]{3,2,1,0:T(4,128)(2,1)S(1)}, u32[]{:S(2)}, u32[]{:S(2)}) collective-permute-start(bf16[12,4,4,128]{3,2,1,0:T(4,128)(2,1)S(1)} %add.293), channel_id=1, source_target_pairs={{0,16},{4,20},{8,24},{12,28},{16,0},{20,4},{24,8},{28,12},{32,48},... | collective-permute-start | bytes 147464 | tf_op jit(solution)/shard_map/ppermute | solution.py:122
  29.9 7.8 %collective-permute-start.6 = (bf16[12,4,4,128]{3,2,1,0:T(4,128)(2,1)S(1)}, bf16[12,4,4,128]{3,2,1,0:T(4,128)(2,1)S(1)}, u32[]{:S(2)}, u32[]{:S(2)}) collective-permute-start(bf16[12,4,4,128]{3,2,1,0:T(4,128)(2,1)S(1)} %add.294), channel_id=1, source_target_pairs={{0,48},{4,52},{8,56},{12,60},{16,32},{20,36},{24,40},{28,44},{32,1... | collective-permute-start | bytes 147464 | tf_op jit(solution)/shard_map/ppermute | solution.py:122
  37.8 4.2 %collective-permute-start.7 = (bf16[12,4,4,128]{3,2,1,0:T(4,128)(2,1)S(1)}, bf16[12,4,4,128]{3,2,1,0:T(4,128)(2,1)S(1)}, u32[]{:S(2)}, u32[]{:S(2)}) collective-permute-start(bf16[12,4,4,128]{3,2,1,0:T(4,128)(2,1)S(1)} %add.295), channel_id=1, source_target_pairs={{0,64},{4,68},{8,72},{12,76},{16,80},{20,84},{24,88},{28,92},{32,9... | collective-permute-start | bytes 147464 | tf_op jit(solution)/shard_map/ppermute | solution.py:122
  42.0 5.4 %collective-permute-start.8 = (bf16[12,4,4,128]{3,2,1,0:T(4,128)(2,1)S(1)}, bf16[12,4,4,128]{3,2,1,0:T(4,128)(2,1)S(1)}, u32[]{:S(2)}, u32[]{:S(2)}) collective-permute-start(bf16[12,4,4,128]{3,2,1,0:T(4,128)(2,1)S(1)} %add.296), channel_id=1, source_target_pairs={{0,192},{4,196},{8,200},{12,204},{16,208},{20,212},{24,216},{28,22... | collective-permute-start | bytes 147464 | tf_op jit(solution)/shard_map/ppermute | solution.py:122
  50.6 5.6 %copy-start.3 = (f32[8,128]{1,0:T(8,128)S(1)}, f32[8,128]{1,0:T(8,128)}, u32[]{:S(2)}) copy-start(f32[8,128]{1,0:T(8,128)} %get-tuple-element.7) | copy-start | bytes 12292
  52.2 4.0 %copy-start.10 = (f32[128]{0:T(128)S(1)}, f32[128]{0:T(128)}, u32[]{:S(2)}) copy-start(f32[128]{0:T(128)} %param.17) | copy-start | bytes 1540
  52.2 9.4 %copy-start.8 = (f32[64]{0:T(128)S(1)}, f32[64]{0:T(128)}, u32[]{:S(2)}) copy-start(f32[64]{0:T(128)} %copy-done.7) | copy-start | bytes 772
  52.2 21.8 %copy-start.5 = (f32[8,128]{1,0:T(8,128)S(1)}, f32[8,128]{1,0:T(8,128)}, u32[]{:S(2)}) copy-start(f32[8,128]{1,0:T(8,128)} %get-tuple-element.8) | copy-start | bytes 12292
  54.1 1.3 %collective-permute-start.9 = (bf16[134,192]{1,0:T(8,128)(2,1)S(1)}, bf16[134,192]{1,0:T(8,128)(2,1)S(1)}, u32[]{:S(2)}, u32[]{:S(2)}) collective-permute-start(bf16[134,192]{1,0:T(8,128)(2,1)S(1)} %concatenate.104), channel_id=1, source_target_pairs={{0,4},{4,0},{8,12},{12,8},{16,20},{20,16},{24,28},{28,24},{32,36},... | collective-permute-start | bytes 154376 | tf_op jit(solution)/shard_map/ppermute | solution.py:160
  55.5 4.4 %collective-permute-start.10 = (bf16[134,192]{1,0:T(8,128)(2,1)S(1)}, bf16[134,192]{1,0:T(8,128)(2,1)S(1)}, u32[]{:S(2)}, u32[]{:S(2)}) collective-permute-start(bf16[134,192]{1,0:T(8,128)(2,1)S(1)} %concatenate.105), channel_id=1, source_target_pairs={{0,8},{4,12},{8,0},{12,4},{16,24},{20,28},{24,16},{28,20},{32,40},... | collective-permute-start | bytes 154376 | tf_op jit(solution)/shard_map/ppermute | solution.py:160
  60.1 5.3 %collective-permute-start.11 = (bf16[134,192]{1,0:T(8,128)(2,1)S(1)}, bf16[134,192]{1,0:T(8,128)(2,1)S(1)}, u32[]{:S(2)}, u32[]{:S(2)}) collective-permute-start(bf16[134,192]{1,0:T(8,128)(2,1)S(1)} %concatenate.106), channel_id=1, source_target_pairs={{0,16},{4,20},{8,24},{12,28},{16,0},{20,4},{24,8},{28,12},{32,48},... | collective-permute-start | bytes 154376 | tf_op jit(solution)/shard_map/ppermute | solution.py:160
  65.5 7.3 %collective-permute-start.12 = (bf16[134,192]{1,0:T(8,128)(2,1)S(1)}, bf16[134,192]{1,0:T(8,128)(2,1)S(1)}, u32[]{:S(2)}, u32[]{:S(2)}) collective-permute-start(bf16[134,192]{1,0:T(8,128)(2,1)S(1)} %concatenate.107), channel_id=1, source_target_pairs={{0,48},{4,52},{8,56},{12,60},{16,32},{20,36},{24,40},{28,44},{32,1... | collective-permute-start | bytes 154376 | tf_op jit(solution)/shard_map/ppermute | solution.py:160
  72.9 4.6 %collective-permute-start.13 = (bf16[134,192]{1,0:T(8,128)(2,1)S(1)}, bf16[134,192]{1,0:T(8,128)(2,1)S(1)}, u32[]{:S(2)}, u32[]{:S(2)}) collective-permute-start(bf16[134,192]{1,0:T(8,128)(2,1)S(1)} %concatenate.108), channel_id=1, source_target_pairs={{0,64},{4,68},{8,72},{12,76},{16,80},{20,84},{24,88},{28,92},{32,9... | collective-permute-start | bytes 154376 | tf_op jit(solution)/shard_map/ppermute | solution.py:160
  73.9 13.2 %copy-start.4 = (bf16[8,128]{1,0:T(8,128)(2,1)}, bf16[8,128]{1,0:T(8,128)(2,1)S(1)}, u32[]{:S(2)}) copy-start(bf16[8,128]{1,0:T(8,128)(2,1)S(1)} %convert_element_type.177) | copy-start | bytes 6148
  77.5 9.4 %copy-start.6 = (pred[4,4]{0,1:T(4,128)(4,1)S(1)}, pred[4,4]{0,1:T(4,128)(4,1)}, u32[]{:S(2)}) copy-start(pred[4,4]{0,1:T(4,128)(4,1)} %iota_compare_fusion.3) | copy-start | bytes 52
  77.6 5.6 %collective-permute-start.14 = (bf16[134,192]{1,0:T(8,128)(2,1)S(1)}, bf16[134,192]{1,0:T(8,128)(2,1)S(1)}, u32[]{:S(2)}, u32[]{:S(2)}) collective-permute-start(bf16[134,192]{1,0:T(8,128)(2,1)S(1)} %concatenate.109), channel_id=1, source_target_pairs={{0,192},{4,196},{8,200},{12,204},{16,208},{20,212},{24,216},{28,22... | collective-permute-start | bytes 154376 | tf_op jit(solution)/shard_map/ppermute | solution.py:160
  87.3 10.6 %copy-start.1 = (bf16[4,2,640]{2,1,0:T(2,128)(2,1)S(1)}, bf16[4,2,640]{2,1,0:T(2,128)(2,1)}, u32[]{:S(2)}) copy-start(bf16[4,2,640]{2,1,0:T(2,128)(2,1)} %param.14) | copy-start | bytes 30724
  90.2 5.4 %collective-permute-start.15 = (f32[8,640]{1,0:T(8,128)S(1)}, f32[8,640]{1,0:T(8,128)S(1)}, u32[]{:S(2)}, u32[]{:S(2)}) collective-permute-start(f32[8,640]{1,0:T(8,128)S(1)} %get-tuple-element.64), channel_id=1, source_target_pairs={{0,1},{1,2},{2,3},{3,0},{4,5},{5,6},{6,7},{7,4},{8,9},{9,10},{10,1... | collective-permute-start | bytes 61448 | tf_op jit(solution)/shard_map/ppermute | solution.py:110
  92.2 5.3 %collective-permute-start.16 = (f32[8,640]{1,0:T(8,128)S(1)}, f32[8,640]{1,0:T(8,128)S(1)}, u32[]{:S(2)}, u32[]{:S(2)}) collective-permute-start(f32[8,640]{1,0:T(8,128)S(1)} %get-tuple-element.65), channel_id=1, source_target_pairs={{0,2},{1,3},{2,0},{3,1},{4,6},{5,7},{6,4},{7,5},{8,10},{9,11},{10,... | collective-permute-start | bytes 61448 | tf_op jit(solution)/shard_map/ppermute | solution.py:110
  94.0 3.8 %collective-permute-start.17 = (f32[8,640]{1,0:T(8,128)S(1)}, f32[8,640]{1,0:T(8,128)S(1)}, u32[]{:S(2)}, u32[]{:S(2)}) collective-permute-start(f32[8,640]{1,0:T(8,128)S(1)} %select_select_fusion), channel_id=1, source_target_pairs={{0,3},{1,0},{2,1},{3,2},{4,7},{5,4},{6,5},{7,6},{8,11},{9,8},{10,9... | collective-permute-start | bytes 61448 | tf_op jit(solution)/shard_map/ppermute | solution.py:110

commit v8 on v5

--- a/solution.py
+++ b/solution.py
@@ -108,11 +108,13 @@
     return [1 << b for b in range(n_seq.bit_length() - 1)]
 
 
-def butterfly(value, n_seq, combine):
-    for stride in seq_masks(n_seq):
+def butterfly(value, n_seq, combine, extras=None):
+    for index, stride in enumerate(seq_masks(n_seq)):
         partner = lax.ppermute(value, "seq", [(i, i ^ stride) for i in range(n_seq)])
         value = combine(value, partner)
-    return value
+        if index == 0 and extras is not None:
+            value, extras = lax.optimization_barrier((value, extras))
+    return value, extras
 
 
 def merge_stats(mine, theirs):
@@ -222,12 +224,14 @@
     long_table = jnp.sum(
         jnp.where(own_pick[:, :, None, None, None], own_query[None], jnp.zeros((), jnp.bfloat16)), axis=1
     ).astype(jnp.bfloat16)
-    long_table = butterfly(long_table, n_seq, lambda a, b: a + b)
+    long_table, (slot_request, slot_block, slot_empty, slot_lengths) = butterfly(
+        long_table, n_seq, lambda a, b: a + b, (slot_request, slot_block, slot_empty, req_len)
+    )
 
     hit = slot_request[:, None] == request_ids[None, :]
     slot_req_long = jnp.any(hit & is_long[None, :], axis=1)
     slot_rank = jnp.sum(jnp.where(hit, rank[None, :], 0), axis=1)
-    slot_len = jnp.sum(jnp.where(hit, req_len[None, :], 0), axis=1)
+    slot_len = jnp.sum(jnp.where(hit, slot_lengths[None, :], 0), axis=1)
     local_row = slot_request - first_row
     slot_local = (local_row >= 0) & (local_row < own_rows)
     pick = jnp.where(
@@ -297,18 +301,21 @@
         None, :, None, None, :
     ]
     fresh_top = jnp.max(jnp.where(allowed, fresh_scores, NEGATIVE), axis=-1)
-    overall = jnp.maximum(cache_top, fresh_top)
-    retained = jnp.exp(cache_top - overall)
     fresh_weights = jnp.where(
-        allowed, jnp.exp(jnp.where(allowed, fresh_scores - overall[..., None], 0.0)), 0.0
-    )
-    denominator = cache_total * retained + jnp.sum(fresh_weights, axis=-1)
-    mixture = cache_mix * retained[..., None] + jnp.einsum(
+        allowed, jnp.exp(jnp.where(allowed, fresh_scores - fresh_top[..., None], 0.0)), 0.0
+    )
+    fresh_total = jnp.sum(fresh_weights, axis=-1)
+    fresh_mix = jnp.einsum(
         "rtngj,rjnd->rtngd",
         fresh_weights.astype(jnp.bfloat16),
         fresh_values,
         preferred_element_type=jnp.float32,
     )
+    overall = jnp.maximum(cache_top, fresh_top)
+    retained = jnp.exp(cache_top - overall)
+    fresh_scale = jnp.exp(fresh_top - overall)
+    denominator = cache_total * retained + fresh_total * fresh_scale
+    mixture = cache_mix * retained[..., None] + fresh_mix * fresh_scale[..., None]
     attended = (mixture / denominator[..., None]).astype(jnp.bfloat16)
     attended = attended.transpose(1, 0, 2, 3, 4).reshape(steps * own_rows, q_heads * HEAD_SIZE)
     projected = chunked_matmul(attended, w_out, n_mp)

time: 98.2 us -> 97.1 us (0.989)
  other arithmetic: 14.9 us -> 12.2 us
  waiting for transfers between devices: 40.5 us -> 42.5 us
    ppermute x3, waiting for transfers between devices: 0.01 us -> 1.74 us  [gather_mp(): lax.ppermute(block, 'mp', [(i, (i + s) % n_mp) for i in range(n_mp)])]
  transfers between devices with their start and end apart: 18 -> 18, of which waited for: 14 -> 15; matrix products, arithmetic and copies ran while one was open for 9% -> 6% of each run, Pallas kernels for 0% -> 0%
where the time goes in v8:
time: 97.1 us; the launch traced here: 96.6 us
  waiting for transfers between devices  42.5 us (44%)
  starting transfers between devices  26.6 us (27%)
  other arithmetic  12.2 us (13%)
  local copies, waits for them, and re-layouts  6.3 us (6%)
  Pallas kernels  6.16 us (6%)
  matrix products  1.65 us (2%)
  between operations  1.22 us (1%)
    ppermute x6, waiting for transfers between devices, stats_butterfly(): arrived = lax.ppermute(packed, 'seq', pairs)  19.2 us
    ppermute x6, waiting for transfers between devices, butterfly(): lax.ppermute(value, 'seq', [(i, i ^ stride) for i in range(n_seq)])  16.9 us
    ppermute x6, starting transfers between devices, butterfly(): lax.ppermute(value, 'seq', [(i, i ^ stride) for i in range(n_seq)])  10.4 us
    ppermute x6, starting transfers between devices, stats_butterfly(): arrived = lax.ppermute(packed, 'seq', pairs)  7.65 us
    ppermute x3, starting transfers between devices, gather_mp(): lax.ppermute(block, 'mp', [(i, (i + s) % n_mp) for i in range(n_mp)])  5.31 us
    ppermute x3, waiting for transfers between devices, reduce_scatter_mp(): lax.ppermute(outgoing, 'mp', [(i, (i + s) % n_mp) for i in range(n_mp)])  4.63 us
    pallas_call x1, Pallas kernels, small_matmul(): pl.pallas_call(_matmul_kernel, out_shape=[jax.ShapeDtypeStruct((m, n), jn...  3.31 us
    ppermute x3, starting transfers between devices, reduce_scatter_mp(): lax.ppermute(outgoing, 'mp', [(i, (i + s) % n_mp) for i in range(n_mp)])  3.24 us
  transfers between devices with their start and end apart: 18, of which 15 were waited for; matrix products, arithmetic and copies ran while one was open for 6% of the time, Pallas kernels for 0%

profile of v8, /device:TPU:38, one launch (start us, length us, event | category | flops | bytes accessed | tf_op | source)
XLA Modules:
  0.0 96.6 jit_solution(3163902452072836569)
XLA Ops:
  0.7 3.3 %collective-permute-start.1 = (bf16[4,2,640]{2,1,0:T(2,128)(2,1)}, bf16[4,2,640]{2,1,0:T(2,128)(2,1)S(1)}, u32[]{:S(2)}, u32[]{:S(2)}) collective-permute-start(bf16[4,2,640]{2,1,0:T(2,128)(2,1)} %param.14), channel_id=1, source_target_pairs={{0,2},{1,3},{2,0},{3,1},{4,6},{5,7},{6,4},{7,5},{8,10},{9,11},{10,... | collective-permute-start | bytes 30728 | tf_op jit(solution)/shard_map/ppermute | solution.py:84
  4.0 1.1 %collective-permute-start = (bf16[4,2,640]{2,1,0:T(2,128)(2,1)}, bf16[4,2,640]{2,1,0:T(2,128)(2,1)S(1)}, u32[]{:S(2)}, u32[]{:S(2)}) collective-permute-start(bf16[4,2,640]{2,1,0:T(2,128)(2,1)} %param.14), channel_id=1, source_target_pairs={{0,3},{1,0},{2,1},{3,2},{4,7},{5,4},{6,5},{7,6},{8,11},{9,8},{10,9... | collective-permute-start | bytes 30728 | tf_op jit(solution)/shard_map/ppermute | solution.py:84
  5.0 1.0 %collective-permute-start.2 = (bf16[4,2,640]{2,1,0:T(2,128)(2,1)}, bf16[4,2,640]{2,1,0:T(2,128)(2,1)S(1)}, u32[]{:S(2)}, u32[]{:S(2)}) collective-permute-start(bf16[4,2,640]{2,1,0:T(2,128)(2,1)} %param.14), channel_id=1, source_target_pairs={{0,1},{1,2},{2,3},{3,0},{4,5},{5,6},{6,7},{7,4},{8,9},{9,10},{10,1... | collective-permute-start | bytes 30728 | tf_op jit(solution)/shard_map/ppermute | solution.py:84
  6.0 0.7 broadcast_compare_fusion.2
  6.7 0.7 dynamic_slice.24
  8.4 1.7 %collective-permute-done.2 = bf16[4,2,640]{2,1,0:T(2,128)(2,1)S(1)} collective-permute-done((bf16[4,2,640]{2,1,0:T(2,128)(2,1)}, bf16[4,2,640]{2,1,0:T(2,128)(2,1)S(1)}, u32[]{:S(2)}, u32[]{:S(2)}) %collective-permute-start.2) | collective-permute-done | bytes 10272 | tf_op jit(solution)/shard_map/ppermute | solution.py:84
  10.1 0.7 broadcast_select_fusion.11
  10.9 0.2 multiply_reduce_fusion
  11.2 1.4 %multiply_convert_fusion.x_ref = bf16[8,2560]{1,0:T(8,128)(2,1)} fusion(f32[8,2560]{1,0:T(8,128)S(1)} %reshape.573, f32[2560]{0:T(1024)} %param.15, f32[8]{0:T(128)S(1)} %rsqrt.28), kind=kLoop, calls=%fused_computation.37 | loop fusion | flops 61440 | bytes 133152 | tf_op jit(solution)/shard_map/convert_element_type | solution.py:197
  12.6 3.3 %shard_map.157 = (f32[8,512]{1,0:T(8,128)}, f32[8,128]{1,0:T(8,128)}, f32[8,128]{1,0:T(8,128)}) custom-call(bf16[8,2560]{1,0:T(8,128)(2,1)} %multiply_convert_fusion.x_ref, bf16[2560,512]{1,0:T(8,128)(2,1)} %refs_0_.1, bf16[2560,128]{1,0:T(8,128)(2,1)} %refs_1_.1, bf16[2560,128]{1,0:T(8,128)(2,1)} %refs_2_.1), custom_call_target="tpu_custom_call" | custom-call | flops 31457280 | bytes 3997696 | tf_op jit(solution)/shard_map/pallas_call | solution.py:47
  15.9 0.9 multiply_reduce_fusion.1
  16.8 0.8 fusion.25
  17.6 0.8 fusion.26
  18.8 0.8 multiply_bitcast_fusion
  19.6 0.4 collective-permute-done.3
  20.1 0.2 fusion.32
  20.3 0.2 select_reduce_fusion.7
  20.5 0.2 collective-permute-start.4
  20.7 3.9 %collective-permute-done.4 = bf16[12,4,4,128]{3,2,1,0:T(4,128)(2,1)S(1)} collective-permute-done((bf16[12,4,4,128]{3,2,1,0:T(4,128)(2,1)S(1)}, bf16[12,4,4,128]{3,2,1,0:T(4,128)(2,1)S(1)}, u32[]{:S(2)}, u32[]{:S(2)}) %collective-permute-start.4) | collective-permute-done | bytes 49184 | tf_op jit(solution)/shard_map/ppermute | solution.py:113
  24.7 3.4 %collective-permute-start.5 = (bf16[12,4,4,128]{3,2,1,0:T(4,128)(2,1)S(1)}, bf16[12,4,4,128]{3,2,1,0:T(4,128)(2,1)S(1)}, u32[]{:S(2)}, u32[]{:S(2)}) collective-permute-start(bf16[12,4,4,128]{3,2,1,0:T(4,128)(2,1)S(1)} %add.306), channel_id=1, source_target_pairs={{0,16},{4,20},{8,24},{12,28},{16,0},{20,4},{24,8},{28,12},{32,48},... | collective-permute-start | bytes 147464 | tf_op jit(solution)/shard_map/ppermute | solution.py:113
  28.1 2.0 %collective-permute-done.5 = bf16[12,4,4,128]{3,2,1,0:T(4,128)(2,1)S(1)} collective-permute-done((bf16[12,4,4,128]{3,2,1,0:T(4,128)(2,1)S(1)}, bf16[12,4,4,128]{3,2,1,0:T(4,128)(2,1)S(1)}, u32[]{:S(2)}, u32[]{:S(2)}) %collective-permute-start.5) | collective-permute-done | bytes 49184 | tf_op jit(solution)/shard_map/ppermute | solution.py:113
  30.1 5.2 %collective-permute-start.6 = (bf16[12,4,4,128]{3,2,1,0:T(4,128)(2,1)S(1)}, bf16[12,4,4,128]{3,2,1,0:T(4,128)(2,1)S(1)}, u32[]{:S(2)}, u32[]{:S(2)}) collective-permute-start(bf16[12,4,4,128]{3,2,1,0:T(4,128)(2,1)S(1)} %add.307), channel_id=1, source_target_pairs={{0,48},{4,52},{8,56},{12,60},{16,32},{20,36},{24,40},{28,44},{32,1... | collective-permute-start | bytes 147464 | tf_op jit(solution)/shard_map/ppermute | solution.py:113
  35.5 2.5 %collective-permute-done.6 = bf16[12,4,4,128]{3,2,1,0:T(4,128)(2,1)S(1)} collective-permute-done((bf16[12,4,4,128]{3,2,1,0:T(4,128)(2,1)S(1)}, bf16[12,4,4,128]{3,2,1,0:T(4,128)(2,1)S(1)}, u32[]{:S(2)}, u32[]{:S(2)}) %collective-permute-start.6) | collective-permute-done | bytes 49184 | tf_op jit(solution)/shard_map/ppermute | solution.py:113
  38.0 0.9 collective-permute-start.7
  39.0 3.2 %collective-permute-done.7 = bf16[12,4,4,128]{3,2,1,0:T(4,128)(2,1)S(1)} collective-permute-done((bf16[12,4,4,128]{3,2,1,0:T(4,128)(2,1)S(1)}, bf16[12,4,4,128]{3,2,1,0:T(4,128)(2,1)S(1)}, u32[]{:S(2)}, u32[]{:S(2)}) %collective-permute-start.7) | collective-permute-done | bytes 49184 | tf_op jit(solution)/shard_map/ppermute | solution.py:113
  42.2 0.6 collective-permute-start.8
  42.8 4.8 %collective-permute-done.8 = bf16[12,4,4,128]{3,2,1,0:T(4,128)(2,1)S(1)} collective-permute-done((bf16[12,4,4,128]{3,2,1,0:T(4,128)(2,1)S(1)}, bf16[12,4,4,128]{3,2,1,0:T(4,128)(2,1)S(1)}, u32[]{:S(2)}, u32[]{:S(2)}) %collective-permute-start.8) | collective-permute-done | bytes 49184 | tf_op jit(solution)/shard_map/ppermute | solution.py:113
  47.7 0.6 gather_fusion
  48.4 0.5 select_reduce_fusion.1
  49.2 0.2 select_reduce_fusion.3
  49.4 0.3 bitcast_reduce_fusion
  49.7 0.3 fusion.1
  50.2 0.2 fusion.84
  50.4 0.3 convolution_bitcast_fusion
  50.7 0.5 copy.163
  51.2 0.2 copy.162
  52.1 1.1 %collective-permute-done.9 = bf16[134,192]{1,0:T(8,128)(2,1)S(1)} collective-permute-done((bf16[134,192]{1,0:T(8,128)(2,1)S(1)}, bf16[134,192]{1,0:T(8,128)(2,1)S(1)}, u32[]{:S(2)}, u32[]{:S(2)}) %collective-permute-start.9) | collective-permute-done | bytes 51488 | tf_op jit(solution)/shard_map/ppermute | solution.py:153
  53.3 0.6 collective-permute-start.10
  53.9 0.2 convolution_multiply_fusion.1
  54.1 3.6 %collective-permute-done.10 = bf16[134,192]{1,0:T(8,128)(2,1)S(1)} collective-permute-done((bf16[134,192]{1,0:T(8,128)(2,1)S(1)}, bf16[134,192]{1,0:T(8,128)(2,1)S(1)}, u32[]{:S(2)}, u32[]{:S(2)}) %collective-permute-start.10) | collective-permute-done | bytes 51488 | tf_op jit(solution)/shard_map/ppermute | solution.py:153
  57.8 1.5 %collective-permute-start.11 = (bf16[134,192]{1,0:T(8,128)(2,1)S(1)}, bf16[134,192]{1,0:T(8,128)(2,1)S(1)}, u32[]{:S(2)}, u32[]{:S(2)}) collective-permute-start(bf16[134,192]{1,0:T(8,128)(2,1)S(1)} %concatenate.106), channel_id=1, source_target_pairs={{0,16},{4,20},{8,24},{12,28},{16,0},{20,4},{24,8},{28,12},{32,48},... | collective-permute-start | bytes 154376 | tf_op jit(solution)/shard_map/ppermute | solution.py:153
  59.4 3.7 %collective-permute-done.11 = bf16[134,192]{1,0:T(8,128)(2,1)S(1)} collective-permute-done((bf16[134,192]{1,0:T(8,128)(2,1)S(1)}, bf16[134,192]{1,0:T(8,128)(2,1)S(1)}, u32[]{:S(2)}, u32[]{:S(2)}) %collective-permute-start.11) | collective-permute-done | bytes 51488 | tf_op jit(solution)/shard_map/ppermute | solution.py:153
  63.3 4.6 %collective-permute-start.12 = (bf16[134,192]{1,0:T(8,128)(2,1)S(1)}, bf16[134,192]{1,0:T(8,128)(2,1)S(1)}, u32[]{:S(2)}, u32[]{:S(2)}) collective-permute-start(bf16[134,192]{1,0:T(8,128)(2,1)S(1)} %concatenate.107), channel_id=1, source_target_pairs={{0,48},{4,52},{8,56},{12,60},{16,32},{20,36},{24,40},{28,44},{32,1... | collective-permute-start | bytes 154376 | tf_op jit(solution)/shard_map/ppermute | solution.py:153
  68.1 2.4 %collective-permute-done.12 = bf16[134,192]{1,0:T(8,128)(2,1)S(1)} collective-permute-done((bf16[134,192]{1,0:T(8,128)(2,1)S(1)}, bf16[134,192]{1,0:T(8,128)(2,1)S(1)}, u32[]{:S(2)}, u32[]{:S(2)}) %collective-permute-start.12) | collective-permute-done | bytes 51488 | tf_op jit(solution)/shard_map/ppermute | solution.py:153
  70.7 0.3 collective-permute-start.13
  71.1 0.3 copy.174
  71.3 3.9 %collective-permute-done.13 = bf16[134,192]{1,0:T(8,128)(2,1)S(1)} collective-permute-done((bf16[134,192]{1,0:T(8,128)(2,1)S(1)}, bf16[134,192]{1,0:T(8,128)(2,1)S(1)}, u32[]{:S(2)}, u32[]{:S(2)}) %collective-permute-start.13) | collective-permute-done | bytes 51488 | tf_op jit(solution)/shard_map/ppermute | solution.py:153
  75.4 0.6 collective-permute-start.14
  76.0 0.4 copy.167
  76.4 4.5 %collective-permute-done.14 = bf16[134,192]{1,0:T(8,128)(2,1)S(1)} collective-permute-done((bf16[134,192]{1,0:T(8,128)(2,1)S(1)}, bf16[134,192]{1,0:T(8,128)(2,1)S(1)}, u32[]{:S(2)}, u32[]{:S(2)}) %collective-permute-start.14) | collective-permute-done | bytes 51488 | tf_op jit(solution)/shard_map/ppermute | solution.py:153
  81.3 0.2 select_reduce_fusion
  81.5 0.4 copy.166
  81.9 0.2 bitcast_select_fusion
  82.1 0.2 fusion.7
  82.3 0.2 copy.177
  82.5 0.6 copy.199
  83.1 2.9 %shard_map.158 = f32[4,8,640]{2,1,0:T(8,128)} custom-call(bf16[8,512]{1,0:T(8,128)(2,1)} %bitcast.195, bf16[512,2560]{1,0:T(8,128)(2,1)} %w_ref.1), custom_call_target="tpu_custom_call" | custom-call | flops 20971520 | bytes 2711552 | tf_op jit(solution)/shard_map/pallas_call | solution.py:70
  86.0 0.8 dynamic-slice_bitcast_fusion.2
  86.7 3.2 %collective-permute-start.17 = (f32[8,640]{1,0:T(8,128)S(1)}, f32[8,640]{1,0:T(8,128)S(1)}, u32[]{:S(2)}, u32[]{:S(2)}) collective-permute-start(f32[8,640]{1,0:T(8,128)S(1)} %get-tuple-element.76), channel_id=1, source_target_pairs={{0,3},{1,0},{2,1},{3,2},{4,7},{5,4},{6,5},{7,6},{8,11},{9,8},{10,9... | collective-permute-start | bytes 61448 | tf_op jit(solution)/shard_map/ppermute | solution.py:101
  90.0 0.7 pad_maximum_fusion.2
  90.6 1.1 %collective-permute-done.15 = f32[8,640]{1,0:T(8,128)S(1)} collective-permute-done((f32[8,640]{1,0:T(8,128)S(1)}, f32[8,640]{1,0:T(8,128)S(1)}, u32[]{:S(2)}, u32[]{:S(2)}) %collective-permute-start.15) | collective-permute-done | bytes 20512 | tf_op jit(solution)/shard_map/ppermute | solution.py:101
  91.7 3.5 %collective-permute-done.16 = f32[8,640]{1,0:T(8,128)S(1)} collective-permute-done((f32[8,640]{1,0:T(8,128)S(1)}, f32[8,640]{1,0:T(8,128)S(1)}, u32[]{:S(2)}, u32[]{:S(2)}) %collective-permute-start.16) | collective-permute-done | bytes 20512 | tf_op jit(solution)/shard_map/ppermute | solution.py:101
  95.3 0.7 fusion.20
  96.0 0.6 add_convert_fusion
  (125 shorter events, 4.6 us)
Async XLA Ops:
  0.6 47.7 %copy-start = (bf16[16,256,128]{2,1,0:T(8,128)(2,1)S(1)}, bf16[16,256,128]{2,1,0:T(8,128)(2,1)}, u32[]{:S(2)}) copy-start(bf16[16,256,128]{2,1,0:T(8,128)(2,1)} %param.22) | copy-start | bytes 3145732
  0.6 19.6 %copy-start.7 = (s32[128]{0:T(128)S(1)}, s32[128]{0:T(128)}, u32[]{:S(2)}) copy-start(s32[128]{0:T(128)} %param.24) | copy-start | bytes 1540
  0.7 17.0 %copy-start.5 = (f32[128]{0:T(128)S(1)}, f32[128]{0:T(128)}, u32[]{:S(2)}) copy-start(f32[128]{0:T(128)} %param.16) | copy-start | bytes 1540
  0.7 18.2 %copy-start.6 = (f32[128]{0:T(128)S(1)}, f32[128]{0:T(128)}, u32[]{:S(2)}) copy-start(f32[128]{0:T(128)} %param.17) | copy-start | bytes 1540
  0.7 20.0 %copy-start.8 = (s32[16]{0:T(128)S(1)}, s32[16]{0:T(128)}, u32[]{:S(2)}) copy-start(s32[16]{0:T(128)} %param.27) | copy-start | bytes 196
  0.7 20.0 %copy-start.10 = (s32[16]{0:T(128)S(1)}, s32[16]{0:T(128)}, u32[]{:S(2)}) copy-start(s32[16]{0:T(128)} %param.26) | copy-start | bytes 196
  0.7 19.4 %copy-start.2 = (s32[16]{0:T(128)S(1)}, s32[16]{0:T(128)}, u32[]{:S(2)}) copy-start(s32[16]{0:T(128)} %param.25) | copy-start | bytes 196
  0.7 7.7 %collective-permute-start.1 = (bf16[4,2,640]{2,1,0:T(2,128)(2,1)}, bf16[4,2,640]{2,1,0:T(2,128)(2,1)S(1)}, u32[]{:S(2)}, u32[]{:S(2)}) collective-permute-start(bf16[4,2,640]{2,1,0:T(2,128)(2,1)} %param.14), channel_id=1, source_target_pairs={{0,2},{1,3},{2,0},{3,1},{4,6},{5,7},{6,4},{7,5},{8,10},{9,11},{10,... | collective-permute-start | bytes 30728 | tf_op jit(solution)/shard_map/ppermute | solution.py:84
  4.0 4.4 %collective-permute-start = (bf16[4,2,640]{2,1,0:T(2,128)(2,1)}, bf16[4,2,640]{2,1,0:T(2,128)(2,1)S(1)}, u32[]{:S(2)}, u32[]{:S(2)}) collective-permute-start(bf16[4,2,640]{2,1,0:T(2,128)(2,1)} %param.14), channel_id=1, source_target_pairs={{0,3},{1,0},{2,1},{3,2},{4,7},{5,4},{6,5},{7,6},{8,11},{9,8},{10,9... | collective-permute-start | bytes 30728 | tf_op jit(solution)/shard_map/ppermute | solution.py:84
  5.0 5.1 %collective-permute-start.2 = (bf16[4,2,640]{2,1,0:T(2,128)(2,1)}, bf16[4,2,640]{2,1,0:T(2,128)(2,1)S(1)}, u32[]{:S(2)}, u32[]{:S(2)}) collective-permute-start(bf16[4,2,640]{2,1,0:T(2,128)(2,1)} %param.14), channel_id=1, source_target_pairs={{0,1},{1,2},{2,3},{3,0},{4,5},{5,6},{6,7},{7,4},{8,9},{9,10},{10,1... | collective-permute-start | bytes 30728 | tf_op jit(solution)/shard_map/ppermute | solution.py:84
  15.9 33.8 %copy-start.9 = (bf16[16,256,128]{2,1,0:T(8,128)(2,1)S(1)}, bf16[16,256,128]{2,1,0:T(8,128)(2,1)}, u32[]{:S(2)}) copy-start(bf16[16,256,128]{2,1,0:T(8,128)(2,1)} %param.23) | copy-start | bytes 3145732
  18.7 1.3 %collective-permute-start.3 = (bf16[12,4,4,128]{3,2,1,0:T(4,128)(2,1)S(1)}, bf16[12,4,4,128]{3,2,1,0:T(4,128)(2,1)S(1)}, u32[]{:S(2)}, u32[]{:S(2)}) collective-permute-start(bf16[12,4,4,128]{3,2,1,0:T(4,128)(2,1)S(1)} %select_reduce_fusion.4), channel_id=1, source_target_pairs={{0,4},{4,0},{8,12},{12,8},{16,20},{20,16},{24,28},{28,24},{32,36},... | collective-permute-start | bytes 147464 | tf_op jit(solution)/shard_map/ppermute | solution.py:113
  20.5 4.2 %collective-permute-start.4 = (bf16[12,4,4,128]{3,2,1,0:T(4,128)(2,1)S(1)}, bf16[12,4,4,128]{3,2,1,0:T(4,128)(2,1)S(1)}, u32[]{:S(2)}, u32[]{:S(2)}) collective-permute-start(bf16[12,4,4,128]{3,2,1,0:T(4,128)(2,1)S(1)} %add.300), channel_id=1, source_target_pairs={{0,8},{4,12},{8,0},{12,4},{16,24},{20,28},{24,16},{28,20},{32,40},... | collective-permute-start | bytes 147464 | tf_op jit(solution)/shard_map/ppermute | solution.py:113
  24.7 5.4 %collective-permute-start.5 = (bf16[12,4,4,128]{3,2,1,0:T(4,128)(2,1)S(1)}, bf16[12,4,4,128]{3,2,1,0:T(4,128)(2,1)S(1)}, u32[]{:S(2)}, u32[]{:S(2)}) collective-permute-start(bf16[12,4,4,128]{3,2,1,0:T(4,128)(2,1)S(1)} %add.306), channel_id=1, source_target_pairs={{0,16},{4,20},{8,24},{12,28},{16,0},{20,4},{24,8},{28,12},{32,48},... | collective-permute-start | bytes 147464 | tf_op jit(solution)/shard_map/ppermute | solution.py:113
  30.1 7.8 %collective-permute-start.6 = (bf16[12,4,4,128]{3,2,1,0:T(4,128)(2,1)S(1)}, bf16[12,4,4,128]{3,2,1,0:T(4,128)(2,1)S(1)}, u32[]{:S(2)}, u32[]{:S(2)}) collective-permute-start(bf16[12,4,4,128]{3,2,1,0:T(4,128)(2,1)S(1)} %add.307), channel_id=1, source_target_pairs={{0,48},{4,52},{8,56},{12,60},{16,32},{20,36},{24,40},{28,44},{32,1... | collective-permute-start | bytes 147464 | tf_op jit(solution)/shard_map/ppermute | solution.py:113
  38.0 4.2 %collective-permute-start.7 = (bf16[12,4,4,128]{3,2,1,0:T(4,128)(2,1)S(1)}, bf16[12,4,4,128]{3,2,1,0:T(4,128)(2,1)S(1)}, u32[]{:S(2)}, u32[]{:S(2)}) collective-permute-start(bf16[12,4,4,128]{3,2,1,0:T(4,128)(2,1)S(1)} %add.308), channel_id=1, source_target_pairs={{0,64},{4,68},{8,72},{12,76},{16,80},{20,84},{24,88},{28,92},{32,9... | collective-permute-start | bytes 147464 | tf_op jit(solution)/shard_map/ppermute | solution.py:113
  42.2 5.4 %collective-permute-start.8 = (bf16[12,4,4,128]{3,2,1,0:T(4,128)(2,1)S(1)}, bf16[12,4,4,128]{3,2,1,0:T(4,128)(2,1)S(1)}, u32[]{:S(2)}, u32[]{:S(2)}) collective-permute-start(bf16[12,4,4,128]{3,2,1,0:T(4,128)(2,1)S(1)} %add.309), channel_id=1, source_target_pairs={{0,192},{4,196},{8,200},{12,204},{16,208},{20,212},{24,216},{28,22... | collective-permute-start | bytes 147464 | tf_op jit(solution)/shard_map/ppermute | solution.py:113
  50.1 17.9 %copy-start.4 = (f32[8,128]{1,0:T(8,128)S(1)}, f32[8,128]{1,0:T(8,128)}, u32[]{:S(2)}) copy-start(f32[8,128]{1,0:T(8,128)} %get-tuple-element.18) | copy-start | bytes 12292
  51.8 1.3 %collective-permute-start.9 = (bf16[134,192]{1,0:T(8,128)(2,1)S(1)}, bf16[134,192]{1,0:T(8,128)(2,1)S(1)}, u32[]{:S(2)}, u32[]{:S(2)}) collective-permute-start(bf16[134,192]{1,0:T(8,128)(2,1)S(1)} %concatenate.104), channel_id=1, source_target_pairs={{0,4},{4,0},{8,12},{12,8},{16,20},{20,16},{24,28},{28,24},{32,36},... | collective-permute-start | bytes 154376 | tf_op jit(solution)/shard_map/ppermute | solution.py:153
  53.3 4.4 %collective-permute-start.10 = (bf16[134,192]{1,0:T(8,128)(2,1)S(1)}, bf16[134,192]{1,0:T(8,128)(2,1)S(1)}, u32[]{:S(2)}, u32[]{:S(2)}) collective-permute-start(bf16[134,192]{1,0:T(8,128)(2,1)S(1)} %concatenate.105), channel_id=1, source_target_pairs={{0,8},{4,12},{8,0},{12,4},{16,24},{20,28},{24,16},{28,20},{32,40},... | collective-permute-start | bytes 154376 | tf_op jit(solution)/shard_map/ppermute | solution.py:153
  57.8 5.3 %collective-permute-start.11 = (bf16[134,192]{1,0:T(8,128)(2,1)S(1)}, bf16[134,192]{1,0:T(8,128)(2,1)S(1)}, u32[]{:S(2)}, u32[]{:S(2)}) collective-permute-start(bf16[134,192]{1,0:T(8,128)(2,1)S(1)} %concatenate.106), channel_id=1, source_target_pairs={{0,16},{4,20},{8,24},{12,28},{16,0},{20,4},{24,8},{28,12},{32,48},... | collective-permute-start | bytes 154376 | tf_op jit(solution)/shard_map/ppermute | solution.py:153
  63.3 7.3 %collective-permute-start.12 = (bf16[134,192]{1,0:T(8,128)(2,1)S(1)}, bf16[134,192]{1,0:T(8,128)(2,1)S(1)}, u32[]{:S(2)}, u32[]{:S(2)}) collective-permute-start(bf16[134,192]{1,0:T(8,128)(2,1)S(1)} %concatenate.107), channel_id=1, source_target_pairs={{0,48},{4,52},{8,56},{12,60},{16,32},{20,36},{24,40},{28,44},{32,1... | collective-permute-start | bytes 154376 | tf_op jit(solution)/shard_map/ppermute | solution.py:153
  68.0 14.1 %copy-start.3 = (bf16[8,128]{1,0:T(8,128)(2,1)}, bf16[8,128]{1,0:T(8,128)(2,1)S(1)}, u32[]{:S(2)}) copy-start(bf16[8,128]{1,0:T(8,128)(2,1)S(1)} %convert_element_type.177) | copy-start | bytes 6148
  70.7 4.6 %collective-permute-start.13 = (bf16[134,192]{1,0:T(8,128)(2,1)S(1)}, bf16[134,192]{1,0:T(8,128)(2,1)S(1)}, u32[]{:S(2)}, u32[]{:S(2)}) collective-permute-start(bf16[134,192]{1,0:T(8,128)(2,1)S(1)} %concatenate.108), channel_id=1, source_target_pairs={{0,64},{4,68},{8,72},{12,76},{16,80},{20,84},{24,88},{28,92},{32,9... | collective-permute-start | bytes 154376 | tf_op jit(solution)/shard_map/ppermute | solution.py:153
  75.4 5.6 %collective-permute-start.14 = (bf16[134,192]{1,0:T(8,128)(2,1)S(1)}, bf16[134,192]{1,0:T(8,128)(2,1)S(1)}, u32[]{:S(2)}, u32[]{:S(2)}) collective-permute-start(bf16[134,192]{1,0:T(8,128)(2,1)S(1)} %concatenate.109), channel_id=1, source_target_pairs={{0,192},{4,196},{8,200},{12,204},{16,208},{20,212},{24,216},{28,22... | collective-permute-start | bytes 154376 | tf_op jit(solution)/shard_map/ppermute | solution.py:153
  82.1 13.9 %copy-start.1 = (bf16[4,2,640]{2,1,0:T(2,128)(2,1)S(1)}, bf16[4,2,640]{2,1,0:T(2,128)(2,1)}, u32[]{:S(2)}) copy-start(bf16[4,2,640]{2,1,0:T(2,128)(2,1)} %param.14) | copy-start | bytes 30724
  86.7 5.0 %collective-permute-start.15 = (f32[8,640]{1,0:T(8,128)S(1)}, f32[8,640]{1,0:T(8,128)S(1)}, u32[]{:S(2)}, u32[]{:S(2)}) collective-permute-start(f32[8,640]{1,0:T(8,128)S(1)} %get-tuple-element.75), channel_id=1, source_target_pairs={{0,1},{1,2},{2,3},{3,0},{4,5},{5,6},{6,7},{7,4},{8,9},{9,10},{10,1... | collective-permute-start | bytes 61448 | tf_op jit(solution)/shard_map/ppermute | solution.py:101
  86.7 5.0 %collective-permute-start.17 = (f32[8,640]{1,0:T(8,128)S(1)}, f32[8,640]{1,0:T(8,128)S(1)}, u32[]{:S(2)}, u32[]{:S(2)}) collective-permute-start(f32[8,640]{1,0:T(8,128)S(1)} %get-tuple-element.76), channel_id=1, source_target_pairs={{0,3},{1,0},{2,1},{3,2},{4,7},{5,4},{6,5},{7,6},{8,11},{9,8},{10,9... | collective-permute-start | bytes 61448 | tf_op jit(solution)/shard_map/ppermute | solution.py:101
  90.0 5.3 %collective-permute-start.16 = (f32[8,640]{1,0:T(8,128)S(1)}, f32[8,640]{1,0:T(8,128)S(1)}, u32[]{:S(2)}, u32[]{:S(2)}) collective-permute-start(f32[8,640]{1,0:T(8,128)S(1)} %get-tuple-element.77), channel_id=1, source_target_pairs={{0,2},{1,3},{2,0},{3,1},{4,6},{5,7},{6,4},{7,5},{8,10},{9,11},{10,... | collective-permute-start | bytes 61448 | tf_op jit(solution)/shard_map/ppermute | solution.py:101

commit v9 on v8

--- a/solution.py
+++ b/solution.py
@@ -35,6 +35,29 @@
     x = x_ref[...]
     for w_ref, o_ref in zip(refs[:count], refs[count:]):
         o_ref[...] = jnp.dot(x, w_ref[...], preferred_element_type=jnp.float32)
+
+
+def _norm_matmul_kernel(x_ref, g_ref, *refs):
+    count = len(refs) // 2
+    x = x_ref[...].astype(jnp.float32)
+    scale = lax.rsqrt(jnp.mean(x * x, axis=-1, keepdims=True) + 1e-06)
+    normed = (x * scale * g_ref[...]).astype(jnp.bfloat16)
+    for w_ref, o_ref in zip(refs[:count], refs[count:]):
+        o_ref[...] = jnp.dot(normed, w_ref[...], preferred_element_type=jnp.float32)
+
+
+def norm_matmul(x, gain, *weights):
+    m, k = x.shape
+    widths = [w.shape[1] for w in weights]
+    return pl.pallas_call(
+        _norm_matmul_kernel,
+        out_shape=[jax.ShapeDtypeStruct((m, n), jnp.float32) for n in widths],
+        cost_estimate=pl.CostEstimate(
+            flops=2 * m * k * sum(widths),
+            bytes_accessed=2 * (m * k + k * sum(widths)) + 4 * m * sum(widths),
+            transcendentals=m,
+        ),
+    )(x, gain.reshape(1, k), *weights)
 
 
 def _vmem():
@@ -194,9 +217,8 @@
     own_ids = first_row + jnp.arange(own_rows, dtype=jnp.int32)
     own_len = lax.dynamic_slice_in_dim(req_len, first_row, own_rows)
     positions = (own_len[None, :] + jnp.arange(steps, dtype=jnp.int32)[:, None]).reshape(-1)
-    normed = scaled_rms(wide.astype(jnp.float32), norm_gain).astype(jnp.bfloat16)
     rows = steps * own_rows
-    query, keys, values = small_matmul(normed, w_query, key_matrix, value_matrix)
+    query, keys, values = norm_matmul(wide, norm_gain, w_query, key_matrix, value_matrix)
     query = query.reshape(rows, q_heads, HEAD_SIZE)
     keys = keys.reshape(rows, kv_heads, HEAD_SIZE)
     values = values.astype(jnp.bfloat16)

time: 97.1 us -> 96.1 us (0.990)
  local copies, waits for them, and re-layouts: 6.3 us -> 8.1 us
  other arithmetic: 12.2 us -> 10.7 us
  waiting for transfers between devices: 42.5 us -> 41.1 us
    reshape x0 -> x2, local copies, waits for them, and re-layouts: none -> 1.94 us  [the longest x1 1.31 us: norm_matmul(): gain.reshape(1, k)]
    convert_element_type x1 -> x0, other arithmetic: 1.41 us -> none  [shards(): scaled_rms(wide.astype(jnp.float32), norm_gain).astype(jnp.bfloat16)]
    ppermute x3, waiting for transfers between devices: 1.74 us -> 0.43 us  [gather_mp(): lax.ppermute(block, 'mp', [(i, (i + s) % n_mp) for i in range(n_mp)])]
  transfers between devices with their start and end apart: 18 -> 18, of which waited for: 15 -> 15; matrix products, arithmetic and copies ran while one was open for 6% -> 7% of each run, Pallas kernels for 0% -> 0%
where the time goes in v9:
time: 96.1 us; the launch traced here: 95.6 us
  waiting for transfers between devices  41.1 us (43%)
  starting transfers between devices  26.6 us (28%)
  other arithmetic  10.7 us (11%)
  local copies, waits for them, and re-layouts  8.1 us (8%)
  Pallas kernels  6.23 us (6%)
  matrix products  1.65 us (2%)
  between operations  1.22 us (1%)
    ppermute x6, waiting for transfers between devices, stats_butterfly(): arrived = lax.ppermute(packed, 'seq', pairs)  19.2 us
    ppermute x6, waiting for transfers between devices, butterfly(): lax.ppermute(value, 'seq', [(i, i ^ stride) for i in range(n_seq)])  16.9 us
    ppermute x6, starting transfers between devices, butterfly(): lax.ppermute(value, 'seq', [(i, i ^ stride) for i in range(n_seq)])  10.4 us
    ppermute x6, starting transfers between devices, stats_butterfly(): arrived = lax.ppermute(packed, 'seq', pairs)  7.65 us
    ppermute x3, starting transfers between devices, gather_mp(): lax.ppermute(block, 'mp', [(i, (i + s) % n_mp) for i in range(n_mp)])  5.31 us
    ppermute x3, waiting for transfers between devices, reduce_scatter_mp(): lax.ppermute(outgoing, 'mp', [(i, (i + s) % n_mp) for i in range(n_mp)])  4.55 us
    pallas_call x1, Pallas kernels, norm_matmul(): pl.pallas_call(_norm_matmul_kernel, out_shape=[jax.ShapeDtypeStruct((m, n...  3.4 us
    ppermute x3, starting transfers between devices, reduce_scatter_mp(): lax.ppermute(outgoing, 'mp', [(i, (i + s) % n_mp) for i in range(n_mp)])  3.32 us
  transfers between devices with their start and end apart: 18, of which 15 were waited for; matrix products, arithmetic and copies ran while one was open for 7% of the time, Pallas kernels for 0%

profile of v9, /device:TPU:38, one launch (start us, length us, event | category | flops | bytes accessed | tf_op | source)
XLA Modules:
  0.0 95.6 jit_solution(16396834481741917253)
XLA Ops:
  0.7 3.3 %collective-permute-start.1 = (bf16[4,2,640]{2,1,0:T(2,128)(2,1)}, bf16[4,2,640]{2,1,0:T(2,128)(2,1)S(1)}, u32[]{:S(2)}, u32[]{:S(2)}) collective-permute-start(bf16[4,2,640]{2,1,0:T(2,128)(2,1)} %param.14), channel_id=1, source_target_pairs={{0,2},{1,3},{2,0},{3,1},{4,6},{5,7},{6,4},{7,5},{8,10},{9,11},{10,... | collective-permute-start | bytes 30728 | tf_op jit(solution)/shard_map/ppermute | solution.py:107
  4.0 1.1 %collective-permute-start = (bf16[4,2,640]{2,1,0:T(2,128)(2,1)}, bf16[4,2,640]{2,1,0:T(2,128)(2,1)S(1)}, u32[]{:S(2)}, u32[]{:S(2)}) collective-permute-start(bf16[4,2,640]{2,1,0:T(2,128)(2,1)} %param.14), channel_id=1, source_target_pairs={{0,3},{1,0},{2,1},{3,2},{4,7},{5,4},{6,5},{7,6},{8,11},{9,8},{10,9... | collective-permute-start | bytes 30728 | tf_op jit(solution)/shard_map/ppermute | solution.py:107
  5.0 1.0 %collective-permute-start.2 = (bf16[4,2,640]{2,1,0:T(2,128)(2,1)}, bf16[4,2,640]{2,1,0:T(2,128)(2,1)S(1)}, u32[]{:S(2)}, u32[]{:S(2)}) collective-permute-start(bf16[4,2,640]{2,1,0:T(2,128)(2,1)} %param.14), channel_id=1, source_target_pairs={{0,1},{1,2},{2,3},{3,0},{4,5},{5,6},{6,7},{7,4},{8,9},{9,10},{10,1... | collective-permute-start | bytes 30728 | tf_op jit(solution)/shard_map/ppermute | solution.py:107
  6.0 0.7 broadcast_compare_fusion.2
  6.7 0.7 dynamic_slice.24
  8.3 1.3 %reshape.549.g_ref = f32[1,2560]{1,0:T(1,128)} reshape(f32[2560]{0:T(1024)} %param.15) | data formatting | bytes 20480 | tf_op jit(solution)/shard_map/reshape | solution.py:60
  9.7 0.4 collective-permute-done.2
  10.1 0.7 broadcast_select_fusion.11
  10.9 0.6 reshape.548.x_ref
  11.5 3.4 %shard_map.157 = (f32[8,512]{1,0:T(8,128)}, f32[8,128]{1,0:T(8,128)}, f32[8,128]{1,0:T(8,128)}) custom-call(bf16[8,2560]{1,0:T(8,128)(2,1)} %reshape.548.x_ref, f32[1,2560]{1,0:T(1,128)} %reshape.549.g_ref, bf16[2560,512]{1,0:T(8,128)(2,1)} %refs_0_.1, bf16[2560,128]{1,0:T(8,128)(2,1)} %refs_1_.1, bf16[2560,128]{1,0:T(8,128)(2,1)} %refs_2_.1), custom_call_target="tpu_custom_call" | custom-call | flops 31457280 | bytes 3997696 | tf_op jit(solution)/shard_map/pallas_call | solution.py:52
  14.9 0.9 multiply_reduce_fusion
  15.8 0.8 fusion.25
  16.6 0.8 fusion.26
  17.9 0.7 multiply_bitcast_fusion
  18.6 0.5 collective-permute-done.3
  19.1 0.2 fusion.32
  19.3 0.2 select_reduce_fusion.7
  19.5 0.2 collective-permute-start.4
  19.7 3.9 %collective-permute-done.4 = bf16[12,4,4,128]{3,2,1,0:T(4,128)(2,1)S(1)} collective-permute-done((bf16[12,4,4,128]{3,2,1,0:T(4,128)(2,1)S(1)}, bf16[12,4,4,128]{3,2,1,0:T(4,128)(2,1)S(1)}, u32[]{:S(2)}, u32[]{:S(2)}) %collective-permute-start.4) | collective-permute-done | bytes 49184 | tf_op jit(solution)/shard_map/ppermute | solution.py:136
  23.7 3.4 %collective-permute-start.5 = (bf16[12,4,4,128]{3,2,1,0:T(4,128)(2,1)S(1)}, bf16[12,4,4,128]{3,2,1,0:T(4,128)(2,1)S(1)}, u32[]{:S(2)}, u32[]{:S(2)}) collective-permute-start(bf16[12,4,4,128]{3,2,1,0:T(4,128)(2,1)S(1)} %add.296), channel_id=1, source_target_pairs={{0,16},{4,20},{8,24},{12,28},{16,0},{20,4},{24,8},{28,12},{32,48},... | collective-permute-start | bytes 147464 | tf_op jit(solution)/shard_map/ppermute | solution.py:136
  27.1 2.0 %collective-permute-done.5 = bf16[12,4,4,128]{3,2,1,0:T(4,128)(2,1)S(1)} collective-permute-done((bf16[12,4,4,128]{3,2,1,0:T(4,128)(2,1)S(1)}, bf16[12,4,4,128]{3,2,1,0:T(4,128)(2,1)S(1)}, u32[]{:S(2)}, u32[]{:S(2)}) %collective-permute-start.5) | collective-permute-done | bytes 49184 | tf_op jit(solution)/shard_map/ppermute | solution.py:136
  29.2 5.2 %collective-permute-start.6 = (bf16[12,4,4,128]{3,2,1,0:T(4,128)(2,1)S(1)}, bf16[12,4,4,128]{3,2,1,0:T(4,128)(2,1)S(1)}, u32[]{:S(2)}, u32[]{:S(2)}) collective-permute-start(bf16[12,4,4,128]{3,2,1,0:T(4,128)(2,1)S(1)} %add.297), channel_id=1, source_target_pairs={{0,48},{4,52},{8,56},{12,60},{16,32},{20,36},{24,40},{28,44},{32,1... | collective-permute-start | bytes 147464 | tf_op jit(solution)/shard_map/ppermute | solution.py:136
  34.5 2.5 %collective-permute-done.6 = bf16[12,4,4,128]{3,2,1,0:T(4,128)(2,1)S(1)} collective-permute-done((bf16[12,4,4,128]{3,2,1,0:T(4,128)(2,1)S(1)}, bf16[12,4,4,128]{3,2,1,0:T(4,128)(2,1)S(1)}, u32[]{:S(2)}, u32[]{:S(2)}) %collective-permute-start.6) | collective-permute-done | bytes 49184 | tf_op jit(solution)/shard_map/ppermute | solution.py:136
  37.0 0.9 collective-permute-start.7
  38.0 3.2 %collective-permute-done.7 = bf16[12,4,4,128]{3,2,1,0:T(4,128)(2,1)S(1)} collective-permute-done((bf16[12,4,4,128]{3,2,1,0:T(4,128)(2,1)S(1)}, bf16[12,4,4,128]{3,2,1,0:T(4,128)(2,1)S(1)}, u32[]{:S(2)}, u32[]{:S(2)}) %collective-permute-start.7) | collective-permute-done | bytes 49184 | tf_op jit(solution)/shard_map/ppermute | solution.py:136
  41.2 0.6 collective-permute-start.8
  41.8 4.8 %collective-permute-done.8 = bf16[12,4,4,128]{3,2,1,0:T(4,128)(2,1)S(1)} collective-permute-done((bf16[12,4,4,128]{3,2,1,0:T(4,128)(2,1)S(1)}, bf16[12,4,4,128]{3,2,1,0:T(4,128)(2,1)S(1)}, u32[]{:S(2)}, u32[]{:S(2)}) %collective-permute-start.8) | collective-permute-done | bytes 49184 | tf_op jit(solution)/shard_map/ppermute | solution.py:136
  46.8 0.6 gather_fusion
  47.4 0.5 select_reduce_fusion.1
  48.4 0.3 bitcast_reduce_fusion
  48.8 0.3 fusion.1
  49.2 0.2 fusion.84
  49.4 0.3 convolution_bitcast_fusion
  49.7 0.5 copy.163
  50.2 0.2 copy.162
  51.1 1.1 %collective-permute-done.9 = bf16[134,192]{1,0:T(8,128)(2,1)S(1)} collective-permute-done((bf16[134,192]{1,0:T(8,128)(2,1)S(1)}, bf16[134,192]{1,0:T(8,128)(2,1)S(1)}, u32[]{:S(2)}, u32[]{:S(2)}) %collective-permute-start.9) | collective-permute-done | bytes 51488 | tf_op jit(solution)/shard_map/ppermute | solution.py:176
  52.3 0.6 collective-permute-start.10
  52.9 0.2 convolution_multiply_fusion.1
  53.1 3.6 %collective-permute-done.10 = bf16[134,192]{1,0:T(8,128)(2,1)S(1)} collective-permute-done((bf16[134,192]{1,0:T(8,128)(2,1)S(1)}, bf16[134,192]{1,0:T(8,128)(2,1)S(1)}, u32[]{:S(2)}, u32[]{:S(2)}) %collective-permute-start.10) | collective-permute-done | bytes 51488 | tf_op jit(solution)/shard_map/ppermute | solution.py:176
  56.8 1.5 %collective-permute-start.11 = (bf16[134,192]{1,0:T(8,128)(2,1)S(1)}, bf16[134,192]{1,0:T(8,128)(2,1)S(1)}, u32[]{:S(2)}, u32[]{:S(2)}) collective-permute-start(bf16[134,192]{1,0:T(8,128)(2,1)S(1)} %concatenate.106), channel_id=1, source_target_pairs={{0,16},{4,20},{8,24},{12,28},{16,0},{20,4},{24,8},{28,12},{32,48},... | collective-permute-start | bytes 154376 | tf_op jit(solution)/shard_map/ppermute | solution.py:176
  58.4 3.7 %collective-permute-done.11 = bf16[134,192]{1,0:T(8,128)(2,1)S(1)} collective-permute-done((bf16[134,192]{1,0:T(8,128)(2,1)S(1)}, bf16[134,192]{1,0:T(8,128)(2,1)S(1)}, u32[]{:S(2)}, u32[]{:S(2)}) %collective-permute-start.11) | collective-permute-done | bytes 51488 | tf_op jit(solution)/shard_map/ppermute | solution.py:176
  62.3 4.6 %collective-permute-start.12 = (bf16[134,192]{1,0:T(8,128)(2,1)S(1)}, bf16[134,192]{1,0:T(8,128)(2,1)S(1)}, u32[]{:S(2)}, u32[]{:S(2)}) collective-permute-start(bf16[134,192]{1,0:T(8,128)(2,1)S(1)} %concatenate.107), channel_id=1, source_target_pairs={{0,48},{4,52},{8,56},{12,60},{16,32},{20,36},{24,40},{28,44},{32,1... | collective-permute-start | bytes 154376 | tf_op jit(solution)/shard_map/ppermute | solution.py:176
  67.2 2.4 %collective-permute-done.12 = bf16[134,192]{1,0:T(8,128)(2,1)S(1)} collective-permute-done((bf16[134,192]{1,0:T(8,128)(2,1)S(1)}, bf16[134,192]{1,0:T(8,128)(2,1)S(1)}, u32[]{:S(2)}, u32[]{:S(2)}) %collective-permute-start.12) | collective-permute-done | bytes 51488 | tf_op jit(solution)/shard_map/ppermute | solution.py:176
  69.7 0.3 collective-permute-start.13
  70.1 0.3 copy.174
  70.3 3.9 %collective-permute-done.13 = bf16[134,192]{1,0:T(8,128)(2,1)S(1)} collective-permute-done((bf16[134,192]{1,0:T(8,128)(2,1)S(1)}, bf16[134,192]{1,0:T(8,128)(2,1)S(1)}, u32[]{:S(2)}, u32[]{:S(2)}) %collective-permute-start.13) | collective-permute-done | bytes 51488 | tf_op jit(solution)/shard_map/ppermute | solution.py:176
  74.4 0.6 collective-permute-start.14
  75.0 0.4 copy.167
  75.5 4.5 %collective-permute-done.14 = bf16[134,192]{1,0:T(8,128)(2,1)S(1)} collective-permute-done((bf16[134,192]{1,0:T(8,128)(2,1)S(1)}, bf16[134,192]{1,0:T(8,128)(2,1)S(1)}, u32[]{:S(2)}, u32[]{:S(2)}) %collective-permute-start.14) | collective-permute-done | bytes 51488 | tf_op jit(solution)/shard_map/ppermute | solution.py:176
  80.3 0.2 select_reduce_fusion
  80.5 0.4 copy.166
  80.9 0.2 bitcast_select_fusion
  81.1 0.2 fusion.7
  81.3 0.2 copy.177
  81.5 0.6 copy.199
  82.1 2.8 %shard_map.158 = f32[4,8,640]{2,1,0:T(8,128)} custom-call(bf16[8,512]{1,0:T(8,128)(2,1)} %bitcast.195, bf16[512,2560]{1,0:T(8,128)(2,1)} %w_ref.1), custom_call_target="tpu_custom_call" | custom-call | flops 20971520 | bytes 2711552 | tf_op jit(solution)/shard_map/pallas_call | solution.py:93
  85.0 0.8 dynamic-slice_bitcast_fusion.2
  85.7 0.3 collective-permute-start.15
  86.0 3.0 %collective-permute-start.17 = (f32[8,640]{1,0:T(8,128)S(1)}, f32[8,640]{1,0:T(8,128)S(1)}, u32[]{:S(2)}, u32[]{:S(2)}) collective-permute-start(f32[8,640]{1,0:T(8,128)S(1)} %get-tuple-element.74), channel_id=1, source_target_pairs={{0,3},{1,0},{2,1},{3,2},{4,7},{5,4},{6,5},{7,6},{8,11},{9,8},{10,9... | collective-permute-start | bytes 61448 | tf_op jit(solution)/shard_map/ppermute | solution.py:124
  89.0 0.7 pad_maximum_fusion.3
  89.7 1.0 %collective-permute-done.15 = f32[8,640]{1,0:T(8,128)S(1)} collective-permute-done((f32[8,640]{1,0:T(8,128)S(1)}, f32[8,640]{1,0:T(8,128)S(1)}, u32[]{:S(2)}, u32[]{:S(2)}) %collective-permute-start.15) | collective-permute-done | bytes 20512 | tf_op jit(solution)/shard_map/ppermute | solution.py:124
  90.7 3.5 %collective-permute-done.16 = f32[8,640]{1,0:T(8,128)S(1)} collective-permute-done((f32[8,640]{1,0:T(8,128)S(1)}, f32[8,640]{1,0:T(8,128)S(1)}, u32[]{:S(2)}, u32[]{:S(2)}) %collective-permute-start.16) | collective-permute-done | bytes 20512 | tf_op jit(solution)/shard_map/ppermute | solution.py:124
  94.3 0.7 fusion.20
  95.0 0.6 add_convert_fusion
  (123 shorter events, 4.7 us)
Async XLA Ops:
  0.6 46.7 %copy-start = (bf16[16,256,128]{2,1,0:T(8,128)(2,1)S(1)}, bf16[16,256,128]{2,1,0:T(8,128)(2,1)}, u32[]{:S(2)}) copy-start(bf16[16,256,128]{2,1,0:T(8,128)(2,1)} %param.22) | copy-start | bytes 3145732
  0.6 18.7 %copy-start.7 = (s32[128]{0:T(128)S(1)}, s32[128]{0:T(128)}, u32[]{:S(2)}) copy-start(s32[128]{0:T(128)} %param.24) | copy-start | bytes 1540
  0.7 16.0 %copy-start.5 = (f32[128]{0:T(128)S(1)}, f32[128]{0:T(128)}, u32[]{:S(2)}) copy-start(f32[128]{0:T(128)} %param.16) | copy-start | bytes 1540
  0.7 17.2 %copy-start.6 = (f32[128]{0:T(128)S(1)}, f32[128]{0:T(128)}, u32[]{:S(2)}) copy-start(f32[128]{0:T(128)} %param.17) | copy-start | bytes 1540
  0.7 19.0 %copy-start.8 = (s32[16]{0:T(128)S(1)}, s32[16]{0:T(128)}, u32[]{:S(2)}) copy-start(s32[16]{0:T(128)} %param.27) | copy-start | bytes 196
  0.7 19.0 %copy-start.10 = (s32[16]{0:T(128)S(1)}, s32[16]{0:T(128)}, u32[]{:S(2)}) copy-start(s32[16]{0:T(128)} %param.26) | copy-start | bytes 196
  0.7 18.4 %copy-start.2 = (s32[16]{0:T(128)S(1)}, s32[16]{0:T(128)}, u32[]{:S(2)}) copy-start(s32[16]{0:T(128)} %param.25) | copy-start | bytes 196
  0.7 9.0 %collective-permute-start.1 = (bf16[4,2,640]{2,1,0:T(2,128)(2,1)}, bf16[4,2,640]{2,1,0:T(2,128)(2,1)S(1)}, u32[]{:S(2)}, u32[]{:S(2)}) collective-permute-start(bf16[4,2,640]{2,1,0:T(2,128)(2,1)} %param.14), channel_id=1, source_target_pairs={{0,2},{1,3},{2,0},{3,1},{4,6},{5,7},{6,4},{7,5},{8,10},{9,11},{10,... | collective-permute-start | bytes 30728 | tf_op jit(solution)/shard_map/ppermute | solution.py:107
  4.0 5.7 %collective-permute-start = (bf16[4,2,640]{2,1,0:T(2,128)(2,1)}, bf16[4,2,640]{2,1,0:T(2,128)(2,1)S(1)}, u32[]{:S(2)}, u32[]{:S(2)}) collective-permute-start(bf16[4,2,640]{2,1,0:T(2,128)(2,1)} %param.14), channel_id=1, source_target_pairs={{0,3},{1,0},{2,1},{3,2},{4,7},{5,4},{6,5},{7,6},{8,11},{9,8},{10,9... | collective-permute-start | bytes 30728 | tf_op jit(solution)/shard_map/ppermute | solution.py:107
  5.0 5.1 %collective-permute-start.2 = (bf16[4,2,640]{2,1,0:T(2,128)(2,1)}, bf16[4,2,640]{2,1,0:T(2,128)(2,1)S(1)}, u32[]{:S(2)}, u32[]{:S(2)}) collective-permute-start(bf16[4,2,640]{2,1,0:T(2,128)(2,1)} %param.14), channel_id=1, source_target_pairs={{0,1},{1,2},{2,3},{3,0},{4,5},{5,6},{6,7},{7,4},{8,9},{9,10},{10,1... | collective-permute-start | bytes 30728 | tf_op jit(solution)/shard_map/ppermute | solution.py:107
  14.9 33.8 %copy-start.9 = (bf16[16,256,128]{2,1,0:T(8,128)(2,1)S(1)}, bf16[16,256,128]{2,1,0:T(8,128)(2,1)}, u32[]{:S(2)}) copy-start(bf16[16,256,128]{2,1,0:T(8,128)(2,1)} %param.23) | copy-start | bytes 3145732
  17.8 1.3 %collective-permute-start.3 = (bf16[12,4,4,128]{3,2,1,0:T(4,128)(2,1)S(1)}, bf16[12,4,4,128]{3,2,1,0:T(4,128)(2,1)S(1)}, u32[]{:S(2)}, u32[]{:S(2)}) collective-permute-start(bf16[12,4,4,128]{3,2,1,0:T(4,128)(2,1)S(1)} %select_reduce_fusion.4), channel_id=1, source_target_pairs={{0,4},{4,0},{8,12},{12,8},{16,20},{20,16},{24,28},{28,24},{32,36},... | collective-permute-start | bytes 147464 | tf_op jit(solution)/shard_map/ppermute | solution.py:136
  19.5 4.2 %collective-permute-start.4 = (bf16[12,4,4,128]{3,2,1,0:T(4,128)(2,1)S(1)}, bf16[12,4,4,128]{3,2,1,0:T(4,128)(2,1)S(1)}, u32[]{:S(2)}, u32[]{:S(2)}) collective-permute-start(bf16[12,4,4,128]{3,2,1,0:T(4,128)(2,1)S(1)} %add.290), channel_id=1, source_target_pairs={{0,8},{4,12},{8,0},{12,4},{16,24},{20,28},{24,16},{28,20},{32,40},... | collective-permute-start | bytes 147464 | tf_op jit(solution)/shard_map/ppermute | solution.py:136
  23.7 5.4 %collective-permute-start.5 = (bf16[12,4,4,128]{3,2,1,0:T(4,128)(2,1)S(1)}, bf16[12,4,4,128]{3,2,1,0:T(4,128)(2,1)S(1)}, u32[]{:S(2)}, u32[]{:S(2)}) collective-permute-start(bf16[12,4,4,128]{3,2,1,0:T(4,128)(2,1)S(1)} %add.296), channel_id=1, source_target_pairs={{0,16},{4,20},{8,24},{12,28},{16,0},{20,4},{24,8},{28,12},{32,48},... | collective-permute-start | bytes 147464 | tf_op jit(solution)/shard_map/ppermute | solution.py:136
  29.2 7.8 %collective-permute-start.6 = (bf16[12,4,4,128]{3,2,1,0:T(4,128)(2,1)S(1)}, bf16[12,4,4,128]{3,2,1,0:T(4,128)(2,1)S(1)}, u32[]{:S(2)}, u32[]{:S(2)}) collective-permute-start(bf16[12,4,4,128]{3,2,1,0:T(4,128)(2,1)S(1)} %add.297), channel_id=1, source_target_pairs={{0,48},{4,52},{8,56},{12,60},{16,32},{20,36},{24,40},{28,44},{32,1... | collective-permute-start | bytes 147464 | tf_op jit(solution)/shard_map/ppermute | solution.py:136
  37.0 4.2 %collective-permute-start.7 = (bf16[12,4,4,128]{3,2,1,0:T(4,128)(2,1)S(1)}, bf16[12,4,4,128]{3,2,1,0:T(4,128)(2,1)S(1)}, u32[]{:S(2)}, u32[]{:S(2)}) collective-permute-start(bf16[12,4,4,128]{3,2,1,0:T(4,128)(2,1)S(1)} %add.298), channel_id=1, source_target_pairs={{0,64},{4,68},{8,72},{12,76},{16,80},{20,84},{24,88},{28,92},{32,9... | collective-permute-start | bytes 147464 | tf_op jit(solution)/shard_map/ppermute | solution.py:136
  41.2 5.4 %collective-permute-start.8 = (bf16[12,4,4,128]{3,2,1,0:T(4,128)(2,1)S(1)}, bf16[12,4,4,128]{3,2,1,0:T(4,128)(2,1)S(1)}, u32[]{:S(2)}, u32[]{:S(2)}) collective-permute-start(bf16[12,4,4,128]{3,2,1,0:T(4,128)(2,1)S(1)} %add.299), channel_id=1, source_target_pairs={{0,192},{4,196},{8,200},{12,204},{16,208},{20,212},{24,216},{28,22... | collective-permute-start | bytes 147464 | tf_op jit(solution)/shard_map/ppermute | solution.py:136
  49.1 17.9 %copy-start.4 = (f32[8,128]{1,0:T(8,128)S(1)}, f32[8,128]{1,0:T(8,128)}, u32[]{:S(2)}) copy-start(f32[8,128]{1,0:T(8,128)} %get-tuple-element.18) | copy-start | bytes 12292
  50.8 1.3 %collective-permute-start.9 = (bf16[134,192]{1,0:T(8,128)(2,1)S(1)}, bf16[134,192]{1,0:T(8,128)(2,1)S(1)}, u32[]{:S(2)}, u32[]{:S(2)}) collective-permute-start(bf16[134,192]{1,0:T(8,128)(2,1)S(1)} %concatenate.104), channel_id=1, source_target_pairs={{0,4},{4,0},{8,12},{12,8},{16,20},{20,16},{24,28},{28,24},{32,36},... | collective-permute-start | bytes 154376 | tf_op jit(solution)/shard_map/ppermute | solution.py:176
  52.3 4.4 %collective-permute-start.10 = (bf16[134,192]{1,0:T(8,128)(2,1)S(1)}, bf16[134,192]{1,0:T(8,128)(2,1)S(1)}, u32[]{:S(2)}, u32[]{:S(2)}) collective-permute-start(bf16[134,192]{1,0:T(8,128)(2,1)S(1)} %concatenate.105), channel_id=1, source_target_pairs={{0,8},{4,12},{8,0},{12,4},{16,24},{20,28},{24,16},{28,20},{32,40},... | collective-permute-start | bytes 154376 | tf_op jit(solution)/shard_map/ppermute | solution.py:176
  56.8 5.3 %collective-permute-start.11 = (bf16[134,192]{1,0:T(8,128)(2,1)S(1)}, bf16[134,192]{1,0:T(8,128)(2,1)S(1)}, u32[]{:S(2)}, u32[]{:S(2)}) collective-permute-start(bf16[134,192]{1,0:T(8,128)(2,1)S(1)} %concatenate.106), channel_id=1, source_target_pairs={{0,16},{4,20},{8,24},{12,28},{16,0},{20,4},{24,8},{28,12},{32,48},... | collective-permute-start | bytes 154376 | tf_op jit(solution)/shard_map/ppermute | solution.py:176
  62.3 7.3 %collective-permute-start.12 = (bf16[134,192]{1,0:T(8,128)(2,1)S(1)}, bf16[134,192]{1,0:T(8,128)(2,1)S(1)}, u32[]{:S(2)}, u32[]{:S(2)}) collective-permute-start(bf16[134,192]{1,0:T(8,128)(2,1)S(1)} %concatenate.107), channel_id=1, source_target_pairs={{0,48},{4,52},{8,56},{12,60},{16,32},{20,36},{24,40},{28,44},{32,1... | collective-permute-start | bytes 154376 | tf_op jit(solution)/shard_map/ppermute | solution.py:176
  67.0 14.1 %copy-start.3 = (bf16[8,128]{1,0:T(8,128)(2,1)}, bf16[8,128]{1,0:T(8,128)(2,1)S(1)}, u32[]{:S(2)}) copy-start(bf16[8,128]{1,0:T(8,128)(2,1)S(1)} %convert_element_type.161) | copy-start | bytes 6148
  69.7 4.6 %collective-permute-start.13 = (bf16[134,192]{1,0:T(8,128)(2,1)S(1)}, bf16[134,192]{1,0:T(8,128)(2,1)S(1)}, u32[]{:S(2)}, u32[]{:S(2)}) collective-permute-start(bf16[134,192]{1,0:T(8,128)(2,1)S(1)} %concatenate.108), channel_id=1, source_target_pairs={{0,64},{4,68},{8,72},{12,76},{16,80},{20,84},{24,88},{28,92},{32,9... | collective-permute-start | bytes 154376 | tf_op jit(solution)/shard_map/ppermute | solution.py:176
  74.4 5.6 %collective-permute-start.14 = (bf16[134,192]{1,0:T(8,128)(2,1)S(1)}, bf16[134,192]{1,0:T(8,128)(2,1)S(1)}, u32[]{:S(2)}, u32[]{:S(2)}) collective-permute-start(bf16[134,192]{1,0:T(8,128)(2,1)S(1)} %concatenate.109), channel_id=1, source_target_pairs={{0,192},{4,196},{8,200},{12,204},{16,208},{20,212},{24,216},{28,22... | collective-permute-start | bytes 154376 | tf_op jit(solution)/shard_map/ppermute | solution.py:176
  81.1 13.9 %copy-start.1 = (bf16[4,2,640]{2,1,0:T(2,128)(2,1)S(1)}, bf16[4,2,640]{2,1,0:T(2,128)(2,1)}, u32[]{:S(2)}) copy-start(bf16[4,2,640]{2,1,0:T(2,128)(2,1)} %param.14) | copy-start | bytes 30724
  85.7 5.0 %collective-permute-start.15 = (f32[8,640]{1,0:T(8,128)S(1)}, f32[8,640]{1,0:T(8,128)S(1)}, u32[]{:S(2)}, u32[]{:S(2)}) collective-permute-start(f32[8,640]{1,0:T(8,128)S(1)} %get-tuple-element.73), channel_id=1, source_target_pairs={{0,1},{1,2},{2,3},{3,0},{4,5},{5,6},{6,7},{7,4},{8,9},{9,10},{10,1... | collective-permute-start | bytes 61448 | tf_op jit(solution)/shard_map/ppermute | solution.py:124
  86.0 4.7 %collective-permute-start.17 = (f32[8,640]{1,0:T(8,128)S(1)}, f32[8,640]{1,0:T(8,128)S(1)}, u32[]{:S(2)}, u32[]{:S(2)}) collective-permute-start(f32[8,640]{1,0:T(8,128)S(1)} %get-tuple-element.74), channel_id=1, source_target_pairs={{0,3},{1,0},{2,1},{3,2},{4,7},{5,4},{6,5},{7,6},{8,11},{9,8},{10,9... | collective-permute-start | bytes 61448 | tf_op jit(solution)/shard_map/ppermute | solution.py:124
  89.0 5.3 %collective-permute-start.16 = (f32[8,640]{1,0:T(8,128)S(1)}, f32[8,640]{1,0:T(8,128)S(1)}, u32[]{:S(2)}, u32[]{:S(2)}) collective-permute-start(f32[8,640]{1,0:T(8,128)S(1)} %get-tuple-element.75), channel_id=1, source_target_pairs={{0,2},{1,3},{2,0},{3,1},{4,6},{5,7},{6,4},{7,5},{8,10},{9,11},{10,... | collective-permute-start | bytes 61448 | tf_op jit(solution)/shard_map/ppermute | solution.py:124

commit v10 on v9

--- a/solution.py
+++ b/solution.py
@@ -37,27 +37,55 @@
         o_ref[...] = jnp.dot(x, w_ref[...], preferred_element_type=jnp.float32)
 
 
-def _norm_matmul_kernel(x_ref, g_ref, *refs):
-    count = len(refs) // 2
+def _project_kernel(x_ref, g_ref, qg_ref, kg_ref, cos_ref, sin_ref, wq_ref, wk_ref, wv_ref, q_ref, k_ref, v_ref):
     x = x_ref[...].astype(jnp.float32)
     scale = lax.rsqrt(jnp.mean(x * x, axis=-1, keepdims=True) + 1e-06)
     normed = (x * scale * g_ref[...]).astype(jnp.bfloat16)
-    for w_ref, o_ref in zip(refs[:count], refs[count:]):
-        o_ref[...] = jnp.dot(normed, w_ref[...], preferred_element_type=jnp.float32)
-
-
-def norm_matmul(x, gain, *weights):
+    cosine = cos_ref[...]
+    sine = sin_ref[...]
+
+    def norm_rotate(y, gain):
+        y = y * lax.rsqrt(jnp.mean(y * y, axis=-1, keepdims=True) + 1e-06) * gain
+        return y * cosine + pltpu.roll(y, HEAD_SIZE // 2, 1) * sine
+
+    for w_ref, o_ref, gain_ref in ((wq_ref, q_ref, qg_ref), (wk_ref, k_ref, kg_ref)):
+        product = jnp.dot(normed, w_ref[...], preferred_element_type=jnp.float32)
+        gain = gain_ref[...]
+        for h in range(product.shape[1] // HEAD_SIZE):
+            o_ref[:, h * HEAD_SIZE : (h + 1) * HEAD_SIZE] = norm_rotate(
+                product[:, h * HEAD_SIZE : (h + 1) * HEAD_SIZE], gain
+            )
+    v_ref[...] = jnp.dot(normed, wv_ref[...], preferred_element_type=jnp.float32)
+
+
+def project_rows(x, gain, query_gain, key_gain, positions, w_query, key_matrix, value_matrix):
     m, k = x.shape
+    halfway = HEAD_SIZE // 2
+    frequency = ROPE_BASE ** (-(jnp.arange(halfway, dtype=jnp.float32) * 2.0) / HEAD_SIZE)
+    angles = positions.astype(jnp.float32)[:, None] * frequency
+    cosine = jnp.cos(angles)
+    sine = jnp.sin(angles)
+    cos_both = jnp.concatenate([cosine, cosine], axis=-1)
+    sin_signed = jnp.concatenate([-sine, sine], axis=-1)
+    weights = (w_query, key_matrix, value_matrix)
     widths = [w.shape[1] for w in weights]
     return pl.pallas_call(
-        _norm_matmul_kernel,
+        _project_kernel,
         out_shape=[jax.ShapeDtypeStruct((m, n), jnp.float32) for n in widths],
         cost_estimate=pl.CostEstimate(
             flops=2 * m * k * sum(widths),
             bytes_accessed=2 * (m * k + k * sum(widths)) + 4 * m * sum(widths),
             transcendentals=m,
         ),
-    )(x, gain.reshape(1, k), *weights)
+    )(
+        x,
+        gain.reshape(1, k),
+        query_gain.reshape(1, HEAD_SIZE),
+        key_gain.reshape(1, HEAD_SIZE),
+        cos_both,
+        sin_signed,
+        *weights,
+    )
 
 
 def _vmem():
@@ -218,12 +246,12 @@
     own_len = lax.dynamic_slice_in_dim(req_len, first_row, own_rows)
     positions = (own_len[None, :] + jnp.arange(steps, dtype=jnp.int32)[:, None]).reshape(-1)
     rows = steps * own_rows
-    query, keys, values = norm_matmul(wide, norm_gain, w_query, key_matrix, value_matrix)
-    query = query.reshape(rows, q_heads, HEAD_SIZE)
-    keys = keys.reshape(rows, kv_heads, HEAD_SIZE)
+    query, keys, values = project_rows(
+        wide, norm_gain, query_gain, key_gain, positions, w_query, key_matrix, value_matrix
+    )
+    query = query.reshape(rows, q_heads, HEAD_SIZE).astype(jnp.bfloat16)
+    keys = keys.reshape(rows, kv_heads, HEAD_SIZE).astype(jnp.bfloat16)
     values = values.astype(jnp.bfloat16)
-    query = rotate(scaled_rms(query, query_gain), positions).astype(jnp.bfloat16)
-    keys = rotate(scaled_rms(keys, key_gain), positions).astype(jnp.bfloat16)
     new_keys = keys.reshape(steps, own_rows, kv_heads * HEAD_SIZE)
     new_values = values.reshape(steps, own_rows, kv_heads * HEAD_SIZE)
     own_query = query.reshape(steps, own_rows, q_heads, HEAD_SIZE).transpose(1, 0, 2, 3)

time: 96.1 us -> 93 us (0.968)
  other arithmetic: 10.7 us -> 8.59 us
  waiting for transfers between devices: 41.1 us -> 39.3 us
    ppermute x3, waiting for transfers between devices: 4.55 us -> 2.86 us  [reduce_scatter_mp(): lax.ppermute(outgoing, 'mp', [(i, (i + s) % n_mp) for i in range(n_mp)])]
    reduce_sum x2 -> x0, other arithmetic: 1.68 us -> none  [scaled_rms(): jnp.mean(values * values, axis=-1, keepdims=True) + 1e-06]
    mul x2 -> x0, other arithmetic: 1.54 us -> none  [scaled_rms(): values * lax.rsqrt(jnp.mean(values * values, axis=-1, keepdims=True) + 1e...]
    ppermute x3, starting transfers between devices: 3.32 us -> 4.65 us  [reduce_scatter_mp(): lax.ppermute(outgoing, 'mp', [(i, (i + s) % n_mp) for i in range(n_mp)])]
where the time goes in v10:
time: 93 us; the launch traced here: 92.5 us
  waiting for transfers between devices  39.3 us (42%)
  starting transfers between devices  27.4 us (29%)
  other arithmetic  8.59 us (9%)
  local copies, waits for them, and re-layouts  8.12 us (9%)
  Pallas kernels  6.45 us (7%)
  matrix products  1.61 us (2%)
  between operations  1.1 us (1%)
    ppermute x6, waiting for transfers between devices, stats_butterfly(): arrived = lax.ppermute(packed, 'seq', pairs)  19.3 us
    ppermute x6, waiting for transfers between devices, butterfly(): lax.ppermute(value, 'seq', [(i, i ^ stride) for i in range(n_seq)])  17.1 us
    ppermute x6, starting transfers between devices, butterfly(): lax.ppermute(value, 'seq', [(i, i ^ stride) for i in range(n_seq)])  10.4 us
    ppermute x6, starting transfers between devices, stats_butterfly(): arrived = lax.ppermute(packed, 'seq', pairs)  7.65 us
    ppermute x3, starting transfers between devices, gather_mp(): lax.ppermute(block, 'mp', [(i, (i + s) % n_mp) for i in range(n_mp)])  4.69 us
    ppermute x3, starting transfers between devices, reduce_scatter_mp(): lax.ppermute(outgoing, 'mp', [(i, (i + s) % n_mp) for i in range(n_mp)])  4.65 us
    pallas_call x1, Pallas kernels, project_rows(): pl.pallas_call(_project_kernel, out_shape=[jax.ShapeDtypeStruct((m, n), j...  3.62 us
    ppermute x3, waiting for transfers between devices, reduce_scatter_mp(): lax.ppermute(outgoing, 'mp', [(i, (i + s) % n_mp) for i in range(n_mp)])  2.86 us
  transfers between devices with their start and end apart: 18, of which 15 were waited for; matrix products, arithmetic and copies ran while one was open for 7% of the time, Pallas kernels for 0%

profile of v10, /device:TPU:38, one launch (start us, length us, event | category | flops | bytes accessed | tf_op | source)
XLA Modules:
  0.0 92.5 jit_solution(12285433628892800498)
XLA Ops:
  0.7 3.1 %collective-permute-start = (bf16[4,2,640]{2,1,0:T(2,128)(2,1)}, bf16[4,2,640]{2,1,0:T(2,128)(2,1)S(1)}, u32[]{:S(2)}, u32[]{:S(2)}) collective-permute-start(bf16[4,2,640]{2,1,0:T(2,128)(2,1)} %param.14), channel_id=1, source_target_pairs={{0,3},{1,0},{2,1},{3,2},{4,7},{5,4},{6,5},{7,6},{8,11},{9,8},{10,9... | collective-permute-start | bytes 30728 | tf_op jit(solution)/shard_map/ppermute | solution.py:135
  3.8 0.6 collective-permute-start.1
  4.4 1.0 %collective-permute-start.2 = (bf16[4,2,640]{2,1,0:T(2,128)(2,1)}, bf16[4,2,640]{2,1,0:T(2,128)(2,1)S(1)}, u32[]{:S(2)}, u32[]{:S(2)}) collective-permute-start(bf16[4,2,640]{2,1,0:T(2,128)(2,1)} %param.14), channel_id=1, source_target_pairs={{0,1},{1,2},{2,3},{3,0},{4,5},{5,6},{6,7},{7,4},{8,9},{9,10},{10,1... | collective-permute-start | bytes 30728 | tf_op jit(solution)/shard_map/ppermute | solution.py:135
  5.4 0.7 broadcast_compare_fusion.2
  6.1 0.7 dynamic_slice.24
  7.0 0.7 pad_maximum_fusion.3.cos_ref
  8.1 0.7 pad_maximum_fusion.4.sin_ref
  8.8 1.3 %reshape.382.g_ref = f32[1,2560]{1,0:T(1,128)} reshape(f32[2560]{0:T(1024)} %param.15) | data formatting | bytes 20480 | tf_op jit(solution)/shard_map/reshape | solution.py:82
  10.1 0.7 broadcast_select_fusion.11
  10.9 0.6 reshape.381.x_ref
  11.5 3.6 %shard_map.157 = (f32[8,512]{1,0:T(8,128)}, f32[8,128]{1,0:T(8,128)}, f32[8,128]{1,0:T(8,128)}) custom-call(bf16[8,2560]{1,0:T(8,128)(2,1)} %reshape.381.x_ref, f32[1,2560]{1,0:T(1,128)} %reshape.382.g_ref, f32[1,128]{1,0:T(1,128)} %bitcast.222, f32[1,128]{1,0:T(1,128)} %bitcast.223, f32[8,128]{1,0:T(8,128)} %pad_maximum_fusion.3.cos_ref, ...), custom_call_target="tpu_custom_call" | custom-call | flops 31457280 | bytes 3997696 | tf_op jit(solution)/shard_map/pallas_call | solution.py:72
  15.2 0.7 convert_element_type.133
  16.3 1.1 %collective-permute-done.3 = bf16[12,4,4,128]{3,2,1,0:T(4,128)(2,1)S(1)} collective-permute-done((bf16[12,4,4,128]{3,2,1,0:T(4,128)(2,1)S(1)}, bf16[12,4,4,128]{3,2,1,0:T(4,128)(2,1)S(1)}, u32[]{:S(2)}, u32[]{:S(2)}) %collective-permute-start.3) | collective-permute-done | bytes 49184 | tf_op jit(solution)/shard_map/ppermute | solution.py:164
  17.4 0.2 collective-permute-start.4
  17.6 0.2 fusion.30
  17.8 0.2 select_reduce_fusion.7
  18.0 3.6 %collective-permute-done.4 = bf16[12,4,4,128]{3,2,1,0:T(4,128)(2,1)S(1)} collective-permute-done((bf16[12,4,4,128]{3,2,1,0:T(4,128)(2,1)S(1)}, bf16[12,4,4,128]{3,2,1,0:T(4,128)(2,1)S(1)}, u32[]{:S(2)}, u32[]{:S(2)}) %collective-permute-start.4) | collective-permute-done | bytes 49184 | tf_op jit(solution)/shard_map/ppermute | solution.py:164
  21.6 3.4 %collective-permute-start.5 = (bf16[12,4,4,128]{3,2,1,0:T(4,128)(2,1)S(1)}, bf16[12,4,4,128]{3,2,1,0:T(4,128)(2,1)S(1)}, u32[]{:S(2)}, u32[]{:S(2)}) collective-permute-start(bf16[12,4,4,128]{3,2,1,0:T(4,128)(2,1)S(1)} %add.268), channel_id=1, source_target_pairs={{0,16},{4,20},{8,24},{12,28},{16,0},{20,4},{24,8},{28,12},{32,48},... | collective-permute-start | bytes 147464 | tf_op jit(solution)/shard_map/ppermute | solution.py:164
  25.0 2.0 %collective-permute-done.5 = bf16[12,4,4,128]{3,2,1,0:T(4,128)(2,1)S(1)} collective-permute-done((bf16[12,4,4,128]{3,2,1,0:T(4,128)(2,1)S(1)}, bf16[12,4,4,128]{3,2,1,0:T(4,128)(2,1)S(1)}, u32[]{:S(2)}, u32[]{:S(2)}) %collective-permute-start.5) | collective-permute-done | bytes 49184 | tf_op jit(solution)/shard_map/ppermute | solution.py:164
  27.1 5.2 %collective-permute-start.6 = (bf16[12,4,4,128]{3,2,1,0:T(4,128)(2,1)S(1)}, bf16[12,4,4,128]{3,2,1,0:T(4,128)(2,1)S(1)}, u32[]{:S(2)}, u32[]{:S(2)}) collective-permute-start(bf16[12,4,4,128]{3,2,1,0:T(4,128)(2,1)S(1)} %add.269), channel_id=1, source_target_pairs={{0,48},{4,52},{8,56},{12,60},{16,32},{20,36},{24,40},{28,44},{32,1... | collective-permute-start | bytes 147464 | tf_op jit(solution)/shard_map/ppermute | solution.py:164
  32.4 2.5 %collective-permute-done.6 = bf16[12,4,4,128]{3,2,1,0:T(4,128)(2,1)S(1)} collective-permute-done((bf16[12,4,4,128]{3,2,1,0:T(4,128)(2,1)S(1)}, bf16[12,4,4,128]{3,2,1,0:T(4,128)(2,1)S(1)}, u32[]{:S(2)}, u32[]{:S(2)}) %collective-permute-start.6) | collective-permute-done | bytes 49184 | tf_op jit(solution)/shard_map/ppermute | solution.py:164
  34.9 0.9 collective-permute-start.7
  35.9 3.2 %collective-permute-done.7 = bf16[12,4,4,128]{3,2,1,0:T(4,128)(2,1)S(1)} collective-permute-done((bf16[12,4,4,128]{3,2,1,0:T(4,128)(2,1)S(1)}, bf16[12,4,4,128]{3,2,1,0:T(4,128)(2,1)S(1)}, u32[]{:S(2)}, u32[]{:S(2)}) %collective-permute-start.7) | collective-permute-done | bytes 49184 | tf_op jit(solution)/shard_map/ppermute | solution.py:164
  39.1 0.6 collective-permute-start.8
  39.7 4.8 %collective-permute-done.8 = bf16[12,4,4,128]{3,2,1,0:T(4,128)(2,1)S(1)} collective-permute-done((bf16[12,4,4,128]{3,2,1,0:T(4,128)(2,1)S(1)}, bf16[12,4,4,128]{3,2,1,0:T(4,128)(2,1)S(1)}, u32[]{:S(2)}, u32[]{:S(2)}) %collective-permute-start.8) | collective-permute-done | bytes 49184 | tf_op jit(solution)/shard_map/ppermute | solution.py:164
  44.7 0.6 gather_fusion
  45.3 0.5 select_reduce_fusion.1
  46.2 0.3 bitcast_reduce_fusion
  46.5 0.4 fusion.1
  46.9 0.3 convolution_bitcast_fusion
  47.3 0.2 fusion.74
  47.5 0.2 copy.151
  47.7 0.2 select_reduce_fusion.3
  47.9 0.5 copy.152
  49.0 1.1 %collective-permute-done.9 = bf16[134,192]{1,0:T(8,128)(2,1)S(1)} collective-permute-done((bf16[134,192]{1,0:T(8,128)(2,1)S(1)}, bf16[134,192]{1,0:T(8,128)(2,1)S(1)}, u32[]{:S(2)}, u32[]{:S(2)}) %collective-permute-start.9) | collective-permute-done | bytes 51488 | tf_op jit(solution)/shard_map/ppermute | solution.py:204
  50.2 0.6 collective-permute-start.10
  50.9 0.2 convolution_multiply_fusion.1
  51.0 3.6 %collective-permute-done.10 = bf16[134,192]{1,0:T(8,128)(2,1)S(1)} collective-permute-done((bf16[134,192]{1,0:T(8,128)(2,1)S(1)}, bf16[134,192]{1,0:T(8,128)(2,1)S(1)}, u32[]{:S(2)}, u32[]{:S(2)}) %collective-permute-start.10) | collective-permute-done | bytes 51488 | tf_op jit(solution)/shard_map/ppermute | solution.py:204
  54.8 1.5 %collective-permute-start.11 = (bf16[134,192]{1,0:T(8,128)(2,1)S(1)}, bf16[134,192]{1,0:T(8,128)(2,1)S(1)}, u32[]{:S(2)}, u32[]{:S(2)}) collective-permute-start(bf16[134,192]{1,0:T(8,128)(2,1)S(1)} %concatenate.77), channel_id=1, source_target_pairs={{0,16},{4,20},{8,24},{12,28},{16,0},{20,4},{24,8},{28,12},{32,48},... | collective-permute-start | bytes 154376 | tf_op jit(solution)/shard_map/ppermute | solution.py:204
  56.4 3.7 %collective-permute-done.11 = bf16[134,192]{1,0:T(8,128)(2,1)S(1)} collective-permute-done((bf16[134,192]{1,0:T(8,128)(2,1)S(1)}, bf16[134,192]{1,0:T(8,128)(2,1)S(1)}, u32[]{:S(2)}, u32[]{:S(2)}) %collective-permute-start.11) | collective-permute-done | bytes 51488 | tf_op jit(solution)/shard_map/ppermute | solution.py:204
  60.2 4.6 %collective-permute-start.12 = (bf16[134,192]{1,0:T(8,128)(2,1)S(1)}, bf16[134,192]{1,0:T(8,128)(2,1)S(1)}, u32[]{:S(2)}, u32[]{:S(2)}) collective-permute-start(bf16[134,192]{1,0:T(8,128)(2,1)S(1)} %concatenate.78), channel_id=1, source_target_pairs={{0,48},{4,52},{8,56},{12,60},{16,32},{20,36},{24,40},{28,44},{32,1... | collective-permute-start | bytes 154376 | tf_op jit(solution)/shard_map/ppermute | solution.py:204
  65.0 2.4 %collective-permute-done.12 = bf16[134,192]{1,0:T(8,128)(2,1)S(1)} collective-permute-done((bf16[134,192]{1,0:T(8,128)(2,1)S(1)}, bf16[134,192]{1,0:T(8,128)(2,1)S(1)}, u32[]{:S(2)}, u32[]{:S(2)}) %collective-permute-start.12) | collective-permute-done | bytes 51488 | tf_op jit(solution)/shard_map/ppermute | solution.py:204
  67.6 0.3 collective-permute-start.13
  68.0 0.3 copy.162
  68.3 3.9 %collective-permute-done.13 = bf16[134,192]{1,0:T(8,128)(2,1)S(1)} collective-permute-done((bf16[134,192]{1,0:T(8,128)(2,1)S(1)}, bf16[134,192]{1,0:T(8,128)(2,1)S(1)}, u32[]{:S(2)}, u32[]{:S(2)}) %collective-permute-start.13) | collective-permute-done | bytes 51488 | tf_op jit(solution)/shard_map/ppermute | solution.py:204
  72.3 0.6 collective-permute-start.14
  73.0 0.4 copy.156
  73.4 4.5 %collective-permute-done.14 = bf16[134,192]{1,0:T(8,128)(2,1)S(1)} collective-permute-done((bf16[134,192]{1,0:T(8,128)(2,1)S(1)}, bf16[134,192]{1,0:T(8,128)(2,1)S(1)}, u32[]{:S(2)}, u32[]{:S(2)}) %collective-permute-start.14) | collective-permute-done | bytes 51488 | tf_op jit(solution)/shard_map/ppermute | solution.py:204
  78.2 0.2 select_reduce_fusion
  78.4 0.4 copy.155
  78.8 0.2 bitcast_select_fusion
  79.1 0.2 fusion.7
  79.3 0.2 copy.165
  79.4 0.6 copy.193
  80.1 2.8 %shard_map.158 = f32[4,8,640]{2,1,0:T(8,128)} custom-call(bf16[8,512]{1,0:T(8,128)(2,1)} %bitcast.187, bf16[512,2560]{1,0:T(8,128)(2,1)} %w_ref.1), custom_call_target="tpu_custom_call" | custom-call | flops 20971520 | bytes 2711552 | tf_op jit(solution)/shard_map/pallas_call | solution.py:121
  82.9 0.8 dynamic-slice_bitcast_fusion.2
  83.7 1.9 %collective-permute-start.15 = (f32[8,640]{1,0:T(8,128)S(1)}, f32[8,640]{1,0:T(8,128)S(1)}, u32[]{:S(2)}, u32[]{:S(2)}) collective-permute-start(f32[8,640]{1,0:T(8,128)S(1)} %get-tuple-element.73), channel_id=1, source_target_pairs={{0,1},{1,2},{2,3},{3,0},{4,5},{5,6},{6,7},{7,4},{8,9},{9,10},{10,1... | collective-permute-start | bytes 61448 | tf_op jit(solution)/shard_map/ppermute | solution.py:152
  85.5 1.8 %collective-permute-start.16 = (f32[8,640]{1,0:T(8,128)S(1)}, f32[8,640]{1,0:T(8,128)S(1)}, u32[]{:S(2)}, u32[]{:S(2)}) collective-permute-start(f32[8,640]{1,0:T(8,128)S(1)} %get-tuple-element.75), channel_id=1, source_target_pairs={{0,2},{1,3},{2,0},{3,1},{4,6},{5,7},{6,4},{7,5},{8,10},{9,11},{10,... | collective-permute-start | bytes 61448 | tf_op jit(solution)/shard_map/ppermute | solution.py:152
  87.4 0.9 collective-permute-start.17
  88.3 0.3 collective-permute-done.15
  88.7 2.2 %collective-permute-done.16 = f32[8,640]{1,0:T(8,128)S(1)} collective-permute-done((f32[8,640]{1,0:T(8,128)S(1)}, f32[8,640]{1,0:T(8,128)S(1)}, u32[]{:S(2)}, u32[]{:S(2)}) %collective-permute-start.16) | collective-permute-done | bytes 20512 | tf_op jit(solution)/shard_map/ppermute | solution.py:152
  90.8 0.3 collective-permute-done.17
  91.2 0.7 fusion.20
  91.9 0.6 add_convert_fusion
  (115 shorter events, 4.2 us)
Async XLA Ops:
  0.6 44.7 %copy-start = (bf16[16,256,128]{2,1,0:T(8,128)(2,1)S(1)}, bf16[16,256,128]{2,1,0:T(8,128)(2,1)}, u32[]{:S(2)}) copy-start(bf16[16,256,128]{2,1,0:T(8,128)(2,1)} %param.22) | copy-start | bytes 3145732
  0.6 17.1 %copy-start.7 = (s32[128]{0:T(128)S(1)}, s32[128]{0:T(128)}, u32[]{:S(2)}) copy-start(s32[128]{0:T(128)} %param.24) | copy-start | bytes 1540
  0.7 16.9 %copy-start.2 = (s32[16]{0:T(128)S(1)}, s32[16]{0:T(128)}, u32[]{:S(2)}) copy-start(s32[16]{0:T(128)} %param.25) | copy-start | bytes 196
  0.7 17.3 %copy-start.10 = (s32[16]{0:T(128)S(1)}, s32[16]{0:T(128)}, u32[]{:S(2)}) copy-start(s32[16]{0:T(128)} %param.26) | copy-start | bytes 196
  0.7 17.3 %copy-start.8 = (s32[16]{0:T(128)S(1)}, s32[16]{0:T(128)}, u32[]{:S(2)}) copy-start(s32[16]{0:T(128)} %param.27) | copy-start | bytes 196
  0.7 9.4 %collective-permute-start = (bf16[4,2,640]{2,1,0:T(2,128)(2,1)}, bf16[4,2,640]{2,1,0:T(2,128)(2,1)S(1)}, u32[]{:S(2)}, u32[]{:S(2)}) collective-permute-start(bf16[4,2,640]{2,1,0:T(2,128)(2,1)} %param.14), channel_id=1, source_target_pairs={{0,3},{1,0},{2,1},{3,2},{4,7},{5,4},{6,5},{7,6},{8,11},{9,8},{10,9... | collective-permute-start | bytes 30728 | tf_op jit(solution)/shard_map/ppermute | solution.py:135
  3.8 6.3 %collective-permute-start.1 = (bf16[4,2,640]{2,1,0:T(2,128)(2,1)}, bf16[4,2,640]{2,1,0:T(2,128)(2,1)S(1)}, u32[]{:S(2)}, u32[]{:S(2)}) collective-permute-start(bf16[4,2,640]{2,1,0:T(2,128)(2,1)} %param.14), channel_id=1, source_target_pairs={{0,2},{1,3},{2,0},{3,1},{4,6},{5,7},{6,4},{7,5},{8,10},{9,11},{10,... | collective-permute-start | bytes 30728 | tf_op jit(solution)/shard_map/ppermute | solution.py:135
  4.4 5.7 %collective-permute-start.2 = (bf16[4,2,640]{2,1,0:T(2,128)(2,1)}, bf16[4,2,640]{2,1,0:T(2,128)(2,1)S(1)}, u32[]{:S(2)}, u32[]{:S(2)}) collective-permute-start(bf16[4,2,640]{2,1,0:T(2,128)(2,1)} %param.14), channel_id=1, source_target_pairs={{0,1},{1,2},{2,3},{3,0},{4,5},{5,6},{6,7},{7,4},{8,9},{9,10},{10,1... | collective-permute-start | bytes 30728 | tf_op jit(solution)/shard_map/ppermute | solution.py:135
  11.5 35.0 %copy-start.9 = (bf16[16,256,128]{2,1,0:T(8,128)(2,1)S(1)}, bf16[16,256,128]{2,1,0:T(8,128)(2,1)}, u32[]{:S(2)}) copy-start(bf16[16,256,128]{2,1,0:T(8,128)(2,1)} %param.23) | copy-start | bytes 3145732
  16.0 1.3 %collective-permute-start.3 = (bf16[12,4,4,128]{3,2,1,0:T(4,128)(2,1)S(1)}, bf16[12,4,4,128]{3,2,1,0:T(4,128)(2,1)S(1)}, u32[]{:S(2)}, u32[]{:S(2)}) collective-permute-start(bf16[12,4,4,128]{3,2,1,0:T(4,128)(2,1)S(1)} %select_reduce_fusion.4), channel_id=1, source_target_pairs={{0,4},{4,0},{8,12},{12,8},{16,20},{20,16},{24,28},{28,24},{32,36},... | collective-permute-start | bytes 147464 | tf_op jit(solution)/shard_map/ppermute | solution.py:164
  17.4 4.2 %collective-permute-start.4 = (bf16[12,4,4,128]{3,2,1,0:T(4,128)(2,1)S(1)}, bf16[12,4,4,128]{3,2,1,0:T(4,128)(2,1)S(1)}, u32[]{:S(2)}, u32[]{:S(2)}) collective-permute-start(bf16[12,4,4,128]{3,2,1,0:T(4,128)(2,1)S(1)} %add.262), channel_id=1, source_target_pairs={{0,8},{4,12},{8,0},{12,4},{16,24},{20,28},{24,16},{28,20},{32,40},... | collective-permute-start | bytes 147464 | tf_op jit(solution)/shard_map/ppermute | solution.py:164
  21.6 5.4 %collective-permute-start.5 = (bf16[12,4,4,128]{3,2,1,0:T(4,128)(2,1)S(1)}, bf16[12,4,4,128]{3,2,1,0:T(4,128)(2,1)S(1)}, u32[]{:S(2)}, u32[]{:S(2)}) collective-permute-start(bf16[12,4,4,128]{3,2,1,0:T(4,128)(2,1)S(1)} %add.268), channel_id=1, source_target_pairs={{0,16},{4,20},{8,24},{12,28},{16,0},{20,4},{24,8},{28,12},{32,48},... | collective-permute-start | bytes 147464 | tf_op jit(solution)/shard_map/ppermute | solution.py:164
  27.1 7.8 %collective-permute-start.6 = (bf16[12,4,4,128]{3,2,1,0:T(4,128)(2,1)S(1)}, bf16[12,4,4,128]{3,2,1,0:T(4,128)(2,1)S(1)}, u32[]{:S(2)}, u32[]{:S(2)}) collective-permute-start(bf16[12,4,4,128]{3,2,1,0:T(4,128)(2,1)S(1)} %add.269), channel_id=1, source_target_pairs={{0,48},{4,52},{8,56},{12,60},{16,32},{20,36},{24,40},{28,44},{32,1... | collective-permute-start | bytes 147464 | tf_op jit(solution)/shard_map/ppermute | solution.py:164
  34.9 4.2 %collective-permute-start.7 = (bf16[12,4,4,128]{3,2,1,0:T(4,128)(2,1)S(1)}, bf16[12,4,4,128]{3,2,1,0:T(4,128)(2,1)S(1)}, u32[]{:S(2)}, u32[]{:S(2)}) collective-permute-start(bf16[12,4,4,128]{3,2,1,0:T(4,128)(2,1)S(1)} %add.270), channel_id=1, source_target_pairs={{0,64},{4,68},{8,72},{12,76},{16,80},{20,84},{24,88},{28,92},{32,9... | collective-permute-start | bytes 147464 | tf_op jit(solution)/shard_map/ppermute | solution.py:164
  39.1 5.4 %collective-permute-start.8 = (bf16[12,4,4,128]{3,2,1,0:T(4,128)(2,1)S(1)}, bf16[12,4,4,128]{3,2,1,0:T(4,128)(2,1)S(1)}, u32[]{:S(2)}, u32[]{:S(2)}) collective-permute-start(bf16[12,4,4,128]{3,2,1,0:T(4,128)(2,1)S(1)} %add.271), channel_id=1, source_target_pairs={{0,192},{4,196},{8,200},{12,204},{16,208},{20,212},{24,216},{28,22... | collective-permute-start | bytes 147464 | tf_op jit(solution)/shard_map/ppermute | solution.py:164
  45.8 3.1 %copy-start.5 = (f32[8,128]{1,0:T(8,128)S(1)}, f32[8,128]{1,0:T(8,128)}, u32[]{:S(2)}) copy-start(f32[8,128]{1,0:T(8,128)} %get-tuple-element.17) | copy-start | bytes 12292
  46.9 18.2 %copy-start.4 = (f32[8,128]{1,0:T(8,128)S(1)}, f32[8,128]{1,0:T(8,128)}, u32[]{:S(2)}) copy-start(f32[8,128]{1,0:T(8,128)} %get-tuple-element.18) | copy-start | bytes 12292
  48.8 1.3 %collective-permute-start.9 = (bf16[134,192]{1,0:T(8,128)(2,1)S(1)}, bf16[134,192]{1,0:T(8,128)(2,1)S(1)}, u32[]{:S(2)}, u32[]{:S(2)}) collective-permute-start(bf16[134,192]{1,0:T(8,128)(2,1)S(1)} %concatenate.75), channel_id=1, source_target_pairs={{0,4},{4,0},{8,12},{12,8},{16,20},{20,16},{24,28},{28,24},{32,36},... | collective-permute-start | bytes 154376 | tf_op jit(solution)/shard_map/ppermute | solution.py:204
  49.0 29.2 %copy-start.6 = (bf16[8,128]{1,0:T(8,128)(2,1)}, bf16[8,128]{1,0:T(8,128)(2,1)S(1)}, u32[]{:S(2)}) copy-start(bf16[8,128]{1,0:T(8,128)(2,1)S(1)} %convert_element_type.160) | copy-start | bytes 6148
  50.2 4.4 %collective-permute-start.10 = (bf16[134,192]{1,0:T(8,128)(2,1)S(1)}, bf16[134,192]{1,0:T(8,128)(2,1)S(1)}, u32[]{:S(2)}, u32[]{:S(2)}) collective-permute-start(bf16[134,192]{1,0:T(8,128)(2,1)S(1)} %concatenate.76), channel_id=1, source_target_pairs={{0,8},{4,12},{8,0},{12,4},{16,24},{20,28},{24,16},{28,20},{32,40},... | collective-permute-start | bytes 154376 | tf_op jit(solution)/shard_map/ppermute | solution.py:204
  54.8 5.3 %collective-permute-start.11 = (bf16[134,192]{1,0:T(8,128)(2,1)S(1)}, bf16[134,192]{1,0:T(8,128)(2,1)S(1)}, u32[]{:S(2)}, u32[]{:S(2)}) collective-permute-start(bf16[134,192]{1,0:T(8,128)(2,1)S(1)} %concatenate.77), channel_id=1, source_target_pairs={{0,16},{4,20},{8,24},{12,28},{16,0},{20,4},{24,8},{28,12},{32,48},... | collective-permute-start | bytes 154376 | tf_op jit(solution)/shard_map/ppermute | solution.py:204
  60.2 7.3 %collective-permute-start.12 = (bf16[134,192]{1,0:T(8,128)(2,1)S(1)}, bf16[134,192]{1,0:T(8,128)(2,1)S(1)}, u32[]{:S(2)}, u32[]{:S(2)}) collective-permute-start(bf16[134,192]{1,0:T(8,128)(2,1)S(1)} %concatenate.78), channel_id=1, source_target_pairs={{0,48},{4,52},{8,56},{12,60},{16,32},{20,36},{24,40},{28,44},{32,1... | collective-permute-start | bytes 154376 | tf_op jit(solution)/shard_map/ppermute | solution.py:204
  65.0 14.0 %copy-start.3 = (bf16[8,128]{1,0:T(8,128)(2,1)}, bf16[8,128]{1,0:T(8,128)(2,1)S(1)}, u32[]{:S(2)}) copy-start(bf16[8,128]{1,0:T(8,128)(2,1)S(1)} %convert_element_type.161) | copy-start | bytes 6148
  67.6 4.6 %collective-permute-start.13 = (bf16[134,192]{1,0:T(8,128)(2,1)S(1)}, bf16[134,192]{1,0:T(8,128)(2,1)S(1)}, u32[]{:S(2)}, u32[]{:S(2)}) collective-permute-start(bf16[134,192]{1,0:T(8,128)(2,1)S(1)} %concatenate.79), channel_id=1, source_target_pairs={{0,64},{4,68},{8,72},{12,76},{16,80},{20,84},{24,88},{28,92},{32,9... | collective-permute-start | bytes 154376 | tf_op jit(solution)/shard_map/ppermute | solution.py:204
  72.3 5.6 %collective-permute-start.14 = (bf16[134,192]{1,0:T(8,128)(2,1)S(1)}, bf16[134,192]{1,0:T(8,128)(2,1)S(1)}, u32[]{:S(2)}, u32[]{:S(2)}) collective-permute-start(bf16[134,192]{1,0:T(8,128)(2,1)S(1)} %concatenate.80), channel_id=1, source_target_pairs={{0,192},{4,196},{8,200},{12,204},{16,208},{20,212},{24,216},{28,22... | collective-permute-start | bytes 154376 | tf_op jit(solution)/shard_map/ppermute | solution.py:204
  79.0 12.9 %copy-start.1 = (bf16[4,2,640]{2,1,0:T(2,128)(2,1)S(1)}, bf16[4,2,640]{2,1,0:T(2,128)(2,1)}, u32[]{:S(2)}) copy-start(bf16[4,2,640]{2,1,0:T(2,128)(2,1)} %param.14) | copy-start | bytes 30724
  83.7 5.0 %collective-permute-start.15 = (f32[8,640]{1,0:T(8,128)S(1)}, f32[8,640]{1,0:T(8,128)S(1)}, u32[]{:S(2)}, u32[]{:S(2)}) collective-permute-start(f32[8,640]{1,0:T(8,128)S(1)} %get-tuple-element.73), channel_id=1, source_target_pairs={{0,1},{1,2},{2,3},{3,0},{4,5},{5,6},{6,7},{7,4},{8,9},{9,10},{10,1... | collective-permute-start | bytes 61448 | tf_op jit(solution)/shard_map/ppermute | solution.py:152
  85.5 5.3 %collective-permute-start.16 = (f32[8,640]{1,0:T(8,128)S(1)}, f32[8,640]{1,0:T(8,128)S(1)}, u32[]{:S(2)}, u32[]{:S(2)}) collective-permute-start(f32[8,640]{1,0:T(8,128)S(1)} %get-tuple-element.75), channel_id=1, source_target_pairs={{0,2},{1,3},{2,0},{3,1},{4,6},{5,7},{6,4},{7,5},{8,10},{9,11},{10,... | collective-permute-start | bytes 61448 | tf_op jit(solution)/shard_map/ppermute | solution.py:152
  87.4 3.8 %collective-permute-start.17 = (f32[8,640]{1,0:T(8,128)S(1)}, f32[8,640]{1,0:T(8,128)S(1)}, u32[]{:S(2)}, u32[]{:S(2)}) collective-permute-start(f32[8,640]{1,0:T(8,128)S(1)} %get-tuple-element.74), channel_id=1, source_target_pairs={{0,3},{1,0},{2,1},{3,2},{4,7},{5,4},{6,5},{7,6},{8,11},{9,8},{10,9... | collective-permute-start | bytes 61448 | tf_op jit(solution)/shard_map/ppermute | solution.py:152

commit v11 on v10

--- a/solution.py
+++ b/solution.py
@@ -110,9 +110,18 @@
 
 def _chunked_kernel(x_ref, w_ref, o_ref):
     chunks, _, width = o_ref.shape
+    me = lax.axis_index("mp")
     x = x_ref[...]
-    for c in range(chunks):
-        o_ref[c] = jnp.dot(x, w_ref[:, c * width : (c + 1) * width], preferred_element_type=jnp.float32)
+    products = [
+        jnp.dot(x, w_ref[:, c * width : (c + 1) * width], preferred_element_type=jnp.float32)
+        for c in range(chunks)
+    ]
+    for s in range(chunks):
+        index = (me + s) % chunks
+        chosen = products[0]
+        for c in range(1, chunks):
+            chosen = jnp.where(index == c, products[c], chosen)
+        o_ref[s] = chosen
 
 
 def chunked_matmul(x, w, chunks):
@@ -145,11 +154,9 @@
 
 
 def reduce_scatter_mp(chunks, n_mp):
-    me = lax.axis_index("mp")
-    total = lax.dynamic_index_in_dim(chunks, me, axis=0, keepdims=False)
+    total = chunks[0]
     for s in range(1, n_mp):
-        outgoing = lax.dynamic_index_in_dim(chunks, (me + s) % n_mp, axis=0, keepdims=False)
-        total = total + lax.ppermute(outgoing, "mp", [(i, (i + s) % n_mp) for i in range(n_mp)])
+        total = total + lax.ppermute(chunks[s], "mp", [(i, (i + s) % n_mp) for i in range(n_mp)])
     return total
 
 

time: 93 us -> 94 us (1.011)
  waiting for transfers between devices: 39.3 us -> 41.4 us
    ppermute x3, waiting for transfers between devices: 2.86 us -> 4.84 us  [reduce_scatter_mp(): lax.ppermute(chunks[s], 'mp', [(i, (i + s) % n_mp) for i in range(n_mp)])]
    ppermute x3, starting transfers between devices: 4.65 us -> 3.68 us  [reduce_scatter_mp(): lax.ppermute(chunks[s], 'mp', [(i, (i + s) % n_mp) for i in range(n_mp)])]
where the time goes in v11:
time: 94 us; the launch traced here: 93.6 us
  waiting for transfers between devices  41.4 us (44%)
  starting transfers between devices  27 us (29%)
  local copies, waits for them, and re-layouts  8.1 us (9%)
  other arithmetic  7.91 us (8%)
  Pallas kernels  6.46 us (7%)
  matrix products  1.62 us (2%)
  between operations  1.12 us (1%)
    ppermute x6, waiting for transfers between devices, stats_butterfly(): arrived = lax.ppermute(packed, 'seq', pairs)  19.3 us
    ppermute x6, waiting for transfers between devices, butterfly(): lax.ppermute(value, 'seq', [(i, i ^ stride) for i in range(n_seq)])  17.2 us
    ppermute x6, starting transfers between devices, butterfly(): lax.ppermute(value, 'seq', [(i, i ^ stride) for i in range(n_seq)])  10.4 us
    ppermute x6, starting transfers between devices, stats_butterfly(): arrived = lax.ppermute(packed, 'seq', pairs)  7.65 us
    ppermute x3, starting transfers between devices, gather_mp(): lax.ppermute(block, 'mp', [(i, (i + s) % n_mp) for i in range(n_mp)])  5.31 us
    ppermute x3, waiting for transfers between devices, reduce_scatter_mp(): lax.ppermute(chunks[s], 'mp', [(i, (i + s) % n_mp) for i in range(n_mp)])  4.84 us
    ppermute x3, starting transfers between devices, reduce_scatter_mp(): lax.ppermute(chunks[s], 'mp', [(i, (i + s) % n_mp) for i in range(n_mp)])  3.68 us
    pallas_call x1, Pallas kernels, project_rows(): pl.pallas_call(_project_kernel, out_shape=[jax.ShapeDtypeStruct((m, n), j...  3.61 us
  transfers between devices with their start and end apart: 18, of which 15 were waited for; matrix products, arithmetic and copies ran while one was open for 7% of the time, Pallas kernels for 0%

profile of v11, /device:TPU:38, one launch (start us, length us, event | category | flops | bytes accessed | tf_op | source)
XLA Modules:
  0.0 93.6 jit_solution(8342238669630229333)
XLA Ops:
  0.7 3.3 %collective-permute-start.1 = (bf16[4,2,640]{2,1,0:T(2,128)(2,1)}, bf16[4,2,640]{2,1,0:T(2,128)(2,1)S(1)}, u32[]{:S(2)}, u32[]{:S(2)}) collective-permute-start(bf16[4,2,640]{2,1,0:T(2,128)(2,1)} %param.14), channel_id=1, source_target_pairs={{0,2},{1,3},{2,0},{3,1},{4,6},{5,7},{6,4},{7,5},{8,10},{9,11},{10,... | collective-permute-start | bytes 30728 | tf_op jit(solution)/shard_map/ppermute | solution.py:144
  4.0 1.1 %collective-permute-start = (bf16[4,2,640]{2,1,0:T(2,128)(2,1)}, bf16[4,2,640]{2,1,0:T(2,128)(2,1)S(1)}, u32[]{:S(2)}, u32[]{:S(2)}) collective-permute-start(bf16[4,2,640]{2,1,0:T(2,128)(2,1)} %param.14), channel_id=1, source_target_pairs={{0,3},{1,0},{2,1},{3,2},{4,7},{5,4},{6,5},{7,6},{8,11},{9,8},{10,9... | collective-permute-start | bytes 30728 | tf_op jit(solution)/shard_map/ppermute | solution.py:144
  5.0 1.0 %collective-permute-start.2 = (bf16[4,2,640]{2,1,0:T(2,128)(2,1)}, bf16[4,2,640]{2,1,0:T(2,128)(2,1)S(1)}, u32[]{:S(2)}, u32[]{:S(2)}) collective-permute-start(bf16[4,2,640]{2,1,0:T(2,128)(2,1)} %param.14), channel_id=1, source_target_pairs={{0,1},{1,2},{2,3},{3,0},{4,5},{5,6},{6,7},{7,4},{8,9},{9,10},{10,1... | collective-permute-start | bytes 30728 | tf_op jit(solution)/shard_map/ppermute | solution.py:144
  6.0 0.7 broadcast_compare_fusion.2
  6.7 0.7 dynamic_slice.11
  8.1 0.7 pad_maximum_fusion.3
  8.7 1.3 %reshape.382.g_ref = f32[1,2560]{1,0:T(1,128)} reshape(f32[2560]{0:T(1024)} %param.15) | data formatting | bytes 20480 | tf_op jit(solution)/shard_map/reshape | solution.py:82
  10.1 0.7 broadcast_select_fusion.11
  10.9 0.6 reshape.381.x_ref
  11.5 3.6 %shard_map.157 = (f32[8,512]{1,0:T(8,128)}, f32[8,128]{1,0:T(8,128)}, f32[8,128]{1,0:T(8,128)}) custom-call(bf16[8,2560]{1,0:T(8,128)(2,1)} %reshape.381.x_ref, f32[1,2560]{1,0:T(1,128)} %reshape.382.g_ref, f32[1,128]{1,0:T(1,128)} %bitcast.224, f32[1,128]{1,0:T(1,128)} %bitcast.225, f32[8,128]{1,0:T(8,128)} %get-tuple-element.141.cos_ref, ...), custom_call_target="tpu_custom_call" | custom-call | flops 31457280 | bytes 3997696 | tf_op jit(solution)/shard_map/pallas_call | solution.py:72
  15.1 0.7 convert_element_type.133
  16.3 1.1 %collective-permute-done.3 = bf16[12,4,4,128]{3,2,1,0:T(4,128)(2,1)S(1)} collective-permute-done((bf16[12,4,4,128]{3,2,1,0:T(4,128)(2,1)S(1)}, bf16[12,4,4,128]{3,2,1,0:T(4,128)(2,1)S(1)}, u32[]{:S(2)}, u32[]{:S(2)}) %collective-permute-start.3) | collective-permute-done | bytes 49184 | tf_op jit(solution)/shard_map/ppermute | solution.py:171
  17.4 0.2 collective-permute-start.4
  17.6 0.2 select_reduce_fusion.7
  17.9 3.6 %collective-permute-done.4 = bf16[12,4,4,128]{3,2,1,0:T(4,128)(2,1)S(1)} collective-permute-done((bf16[12,4,4,128]{3,2,1,0:T(4,128)(2,1)S(1)}, bf16[12,4,4,128]{3,2,1,0:T(4,128)(2,1)S(1)}, u32[]{:S(2)}, u32[]{:S(2)}) %collective-permute-start.4) | collective-permute-done | bytes 49184 | tf_op jit(solution)/shard_map/ppermute | solution.py:171
  21.6 3.4 %collective-permute-start.5 = (bf16[12,4,4,128]{3,2,1,0:T(4,128)(2,1)S(1)}, bf16[12,4,4,128]{3,2,1,0:T(4,128)(2,1)S(1)}, u32[]{:S(2)}, u32[]{:S(2)}) collective-permute-start(bf16[12,4,4,128]{3,2,1,0:T(4,128)(2,1)S(1)} %add.237), channel_id=1, source_target_pairs={{0,16},{4,20},{8,24},{12,28},{16,0},{20,4},{24,8},{28,12},{32,48},... | collective-permute-start | bytes 147464 | tf_op jit(solution)/shard_map/ppermute | solution.py:171
  25.1 2.0 %collective-permute-done.5 = bf16[12,4,4,128]{3,2,1,0:T(4,128)(2,1)S(1)} collective-permute-done((bf16[12,4,4,128]{3,2,1,0:T(4,128)(2,1)S(1)}, bf16[12,4,4,128]{3,2,1,0:T(4,128)(2,1)S(1)}, u32[]{:S(2)}, u32[]{:S(2)}) %collective-permute-start.5) | collective-permute-done | bytes 49184 | tf_op jit(solution)/shard_map/ppermute | solution.py:171
  27.1 5.2 %collective-permute-start.6 = (bf16[12,4,4,128]{3,2,1,0:T(4,128)(2,1)S(1)}, bf16[12,4,4,128]{3,2,1,0:T(4,128)(2,1)S(1)}, u32[]{:S(2)}, u32[]{:S(2)}) collective-permute-start(bf16[12,4,4,128]{3,2,1,0:T(4,128)(2,1)S(1)} %add.238), channel_id=1, source_target_pairs={{0,48},{4,52},{8,56},{12,60},{16,32},{20,36},{24,40},{28,44},{32,1... | collective-permute-start | bytes 147464 | tf_op jit(solution)/shard_map/ppermute | solution.py:171
  32.3 0.2 fusion.31
  32.5 2.4 %collective-permute-done.6 = bf16[12,4,4,128]{3,2,1,0:T(4,128)(2,1)S(1)} collective-permute-done((bf16[12,4,4,128]{3,2,1,0:T(4,128)(2,1)S(1)}, bf16[12,4,4,128]{3,2,1,0:T(4,128)(2,1)S(1)}, u32[]{:S(2)}, u32[]{:S(2)}) %collective-permute-start.6) | collective-permute-done | bytes 49184 | tf_op jit(solution)/shard_map/ppermute | solution.py:171
  35.0 0.9 collective-permute-start.7
  35.9 3.2 %collective-permute-done.7 = bf16[12,4,4,128]{3,2,1,0:T(4,128)(2,1)S(1)} collective-permute-done((bf16[12,4,4,128]{3,2,1,0:T(4,128)(2,1)S(1)}, bf16[12,4,4,128]{3,2,1,0:T(4,128)(2,1)S(1)}, u32[]{:S(2)}, u32[]{:S(2)}) %collective-permute-start.7) | collective-permute-done | bytes 49184 | tf_op jit(solution)/shard_map/ppermute | solution.py:171
  39.2 0.6 collective-permute-start.8
  39.7 4.8 %collective-permute-done.8 = bf16[12,4,4,128]{3,2,1,0:T(4,128)(2,1)S(1)} collective-permute-done((bf16[12,4,4,128]{3,2,1,0:T(4,128)(2,1)S(1)}, bf16[12,4,4,128]{3,2,1,0:T(4,128)(2,1)S(1)}, u32[]{:S(2)}, u32[]{:S(2)}) %collective-permute-start.8) | collective-permute-done | bytes 49184 | tf_op jit(solution)/shard_map/ppermute | solution.py:171
  44.7 0.6 gather_fusion
  45.3 0.5 select_reduce_fusion.1
  46.2 0.2 select_reduce_fusion.3
  46.4 0.3 bitcast_reduce_fusion
  46.7 0.3 fusion.1
  47.2 0.2 fusion.75
  47.4 0.3 convolution_bitcast_fusion
  47.7 0.5 copy.152
  48.1 0.2 copy.151
  48.4 0.1 pad_maximum_fusion
  49.0 1.1 %collective-permute-done.9 = bf16[134,192]{1,0:T(8,128)(2,1)S(1)} collective-permute-done((bf16[134,192]{1,0:T(8,128)(2,1)S(1)}, bf16[134,192]{1,0:T(8,128)(2,1)S(1)}, u32[]{:S(2)}, u32[]{:S(2)}) %collective-permute-start.9) | collective-permute-done | bytes 51488 | tf_op jit(solution)/shard_map/ppermute | solution.py:211
  50.3 0.6 collective-permute-start.10
  50.9 0.2 convolution_multiply_fusion.1
  51.0 3.6 %collective-permute-done.10 = bf16[134,192]{1,0:T(8,128)(2,1)S(1)} collective-permute-done((bf16[134,192]{1,0:T(8,128)(2,1)S(1)}, bf16[134,192]{1,0:T(8,128)(2,1)S(1)}, u32[]{:S(2)}, u32[]{:S(2)}) %collective-permute-start.10) | collective-permute-done | bytes 51488 | tf_op jit(solution)/shard_map/ppermute | solution.py:211
  54.8 1.5 %collective-permute-start.11 = (bf16[134,192]{1,0:T(8,128)(2,1)S(1)}, bf16[134,192]{1,0:T(8,128)(2,1)S(1)}, u32[]{:S(2)}, u32[]{:S(2)}) collective-permute-start(bf16[134,192]{1,0:T(8,128)(2,1)S(1)} %concatenate.77), channel_id=1, source_target_pairs={{0,16},{4,20},{8,24},{12,28},{16,0},{20,4},{24,8},{28,12},{32,48},... | collective-permute-start | bytes 154376 | tf_op jit(solution)/shard_map/ppermute | solution.py:211
  56.4 3.7 %collective-permute-done.11 = bf16[134,192]{1,0:T(8,128)(2,1)S(1)} collective-permute-done((bf16[134,192]{1,0:T(8,128)(2,1)S(1)}, bf16[134,192]{1,0:T(8,128)(2,1)S(1)}, u32[]{:S(2)}, u32[]{:S(2)}) %collective-permute-start.11) | collective-permute-done | bytes 51488 | tf_op jit(solution)/shard_map/ppermute | solution.py:211
  60.2 4.6 %collective-permute-start.12 = (bf16[134,192]{1,0:T(8,128)(2,1)S(1)}, bf16[134,192]{1,0:T(8,128)(2,1)S(1)}, u32[]{:S(2)}, u32[]{:S(2)}) collective-permute-start(bf16[134,192]{1,0:T(8,128)(2,1)S(1)} %concatenate.78), channel_id=1, source_target_pairs={{0,48},{4,52},{8,56},{12,60},{16,32},{20,36},{24,40},{28,44},{32,1... | collective-permute-start | bytes 154376 | tf_op jit(solution)/shard_map/ppermute | solution.py:211
  64.9 0.1 copy.161
  65.1 2.4 %collective-permute-done.12 = bf16[134,192]{1,0:T(8,128)(2,1)S(1)} collective-permute-done((bf16[134,192]{1,0:T(8,128)(2,1)S(1)}, bf16[134,192]{1,0:T(8,128)(2,1)S(1)}, u32[]{:S(2)}, u32[]{:S(2)}) %collective-permute-start.12) | collective-permute-done | bytes 51488 | tf_op jit(solution)/shard_map/ppermute | solution.py:211
  67.6 0.3 collective-permute-start.13
  68.0 0.3 copy.162
  68.3 3.9 %collective-permute-done.13 = bf16[134,192]{1,0:T(8,128)(2,1)S(1)} collective-permute-done((bf16[134,192]{1,0:T(8,128)(2,1)S(1)}, bf16[134,192]{1,0:T(8,128)(2,1)S(1)}, u32[]{:S(2)}, u32[]{:S(2)}) %collective-permute-start.13) | collective-permute-done | bytes 51488 | tf_op jit(solution)/shard_map/ppermute | solution.py:211
  72.3 0.6 collective-permute-start.14
  73.0 0.4 copy.156
  73.4 4.6 %collective-permute-done.14 = bf16[134,192]{1,0:T(8,128)(2,1)S(1)} collective-permute-done((bf16[134,192]{1,0:T(8,128)(2,1)S(1)}, bf16[134,192]{1,0:T(8,128)(2,1)S(1)}, u32[]{:S(2)}, u32[]{:S(2)}) %collective-permute-start.14) | collective-permute-done | bytes 51488 | tf_op jit(solution)/shard_map/ppermute | solution.py:211
  78.3 0.2 select_reduce_fusion
  78.4 0.4 copy.155
  78.8 0.2 bitcast_select_fusion
  79.1 0.2 fusion.7
  79.3 0.2 copy.165
  79.5 0.6 copy.193
  80.1 2.8 %shard_map.158 = f32[4,8,640]{2,1,0:T(8,128)} custom-call(bf16[8,512]{1,0:T(8,128)(2,1)} %bitcast.189, bf16[512,2560]{1,0:T(8,128)(2,1)} %w_ref.1), custom_call_target="tpu_custom_call" | custom-call | flops 20971520 | bytes 2711552 | tf_op jit(solution)/shard_map/pallas_call | solution.py:130
  82.9 0.8 slice_bitcast_fusion.2
  83.7 0.6 collective-permute-start.15
  84.3 2.6 %collective-permute-start.17 = (f32[8,640]{1,0:T(8,128)S(1)}, f32[8,640]{1,0:T(8,128)S(1)}, u32[]{:S(2)}, u32[]{:S(2)}) collective-permute-start(f32[8,640]{1,0:T(8,128)S(1)} %get-tuple-element.74), channel_id=1, source_target_pairs={{0,3},{1,0},{2,1},{3,2},{4,7},{5,4},{6,5},{7,6},{8,11},{9,8},{10,9... | collective-permute-start | bytes 61448 | tf_op jit(solution)/shard_map/ppermute | solution.py:159
  86.9 0.4 collective-permute-start.16
  87.4 1.3 %collective-permute-done.15 = f32[8,640]{1,0:T(8,128)S(1)} collective-permute-done((f32[8,640]{1,0:T(8,128)S(1)}, f32[8,640]{1,0:T(8,128)S(1)}, u32[]{:S(2)}, u32[]{:S(2)}) %collective-permute-start.15) | collective-permute-done | bytes 20512 | tf_op jit(solution)/shard_map/ppermute | solution.py:159
  88.7 3.5 %collective-permute-done.16 = f32[8,640]{1,0:T(8,128)S(1)} collective-permute-done((f32[8,640]{1,0:T(8,128)S(1)}, f32[8,640]{1,0:T(8,128)S(1)}, u32[]{:S(2)}, u32[]{:S(2)}) %collective-permute-start.16) | collective-permute-done | bytes 20512 | tf_op jit(solution)/shard_map/ppermute | solution.py:159
  92.2 0.7 fusion.21
  93.0 0.6 add_convert_fusion
  (115 shorter events, 4.0 us)
Async XLA Ops:
  0.6 44.7 %copy-start = (bf16[16,256,128]{2,1,0:T(8,128)(2,1)S(1)}, bf16[16,256,128]{2,1,0:T(8,128)(2,1)}, u32[]{:S(2)}) copy-start(bf16[16,256,128]{2,1,0:T(8,128)(2,1)} %param.22) | copy-start | bytes 3145732
  0.6 17.0 %copy-start.7 = (s32[128]{0:T(128)S(1)}, s32[128]{0:T(128)}, u32[]{:S(2)}) copy-start(s32[128]{0:T(128)} %param.24) | copy-start | bytes 1540
  0.7 16.7 %copy-start.9 = (s32[16]{0:T(128)S(1)}, s32[16]{0:T(128)}, u32[]{:S(2)}) copy-start(s32[16]{0:T(128)} %param.27) | copy-start | bytes 196
  0.7 16.7 %copy-start.10 = (s32[16]{0:T(128)S(1)}, s32[16]{0:T(128)}, u32[]{:S(2)}) copy-start(s32[16]{0:T(128)} %param.26) | copy-start | bytes 196
  0.7 16.9 %copy-start.2 = (s32[16]{0:T(128)S(1)}, s32[16]{0:T(128)}, u32[]{:S(2)}) copy-start(s32[16]{0:T(128)} %param.25) | copy-start | bytes 196
  0.7 9.4 %collective-permute-start.1 = (bf16[4,2,640]{2,1,0:T(2,128)(2,1)}, bf16[4,2,640]{2,1,0:T(2,128)(2,1)S(1)}, u32[]{:S(2)}, u32[]{:S(2)}) collective-permute-start(bf16[4,2,640]{2,1,0:T(2,128)(2,1)} %param.14), channel_id=1, source_target_pairs={{0,2},{1,3},{2,0},{3,1},{4,6},{5,7},{6,4},{7,5},{8,10},{9,11},{10,... | collective-permute-start | bytes 30728 | tf_op jit(solution)/shard_map/ppermute | solution.py:144
  4.0 6.1 %collective-permute-start = (bf16[4,2,640]{2,1,0:T(2,128)(2,1)}, bf16[4,2,640]{2,1,0:T(2,128)(2,1)S(1)}, u32[]{:S(2)}, u32[]{:S(2)}) collective-permute-start(bf16[4,2,640]{2,1,0:T(2,128)(2,1)} %param.14), channel_id=1, source_target_pairs={{0,3},{1,0},{2,1},{3,2},{4,7},{5,4},{6,5},{7,6},{8,11},{9,8},{10,9... | collective-permute-start | bytes 30728 | tf_op jit(solution)/shard_map/ppermute | solution.py:144
  5.0 5.1 %collective-permute-start.2 = (bf16[4,2,640]{2,1,0:T(2,128)(2,1)}, bf16[4,2,640]{2,1,0:T(2,128)(2,1)S(1)}, u32[]{:S(2)}, u32[]{:S(2)}) collective-permute-start(bf16[4,2,640]{2,1,0:T(2,128)(2,1)} %param.14), channel_id=1, source_target_pairs={{0,1},{1,2},{2,3},{3,0},{4,5},{5,6},{6,7},{7,4},{8,9},{9,10},{10,1... | collective-permute-start | bytes 30728 | tf_op jit(solution)/shard_map/ppermute | solution.py:144
  11.5 35.2 %copy-start.8 = (bf16[16,256,128]{2,1,0:T(8,128)(2,1)S(1)}, bf16[16,256,128]{2,1,0:T(8,128)(2,1)}, u32[]{:S(2)}) copy-start(bf16[16,256,128]{2,1,0:T(8,128)(2,1)} %param.23) | copy-start | bytes 3145732
  16.0 1.3 %collective-permute-start.3 = (bf16[12,4,4,128]{3,2,1,0:T(4,128)(2,1)S(1)}, bf16[12,4,4,128]{3,2,1,0:T(4,128)(2,1)S(1)}, u32[]{:S(2)}, u32[]{:S(2)}) collective-permute-start(bf16[12,4,4,128]{3,2,1,0:T(4,128)(2,1)S(1)} %select_reduce_fusion.4), channel_id=1, source_target_pairs={{0,4},{4,0},{8,12},{12,8},{16,20},{20,16},{24,28},{28,24},{32,36},... | collective-permute-start | bytes 147464 | tf_op jit(solution)/shard_map/ppermute | solution.py:171
  17.4 4.2 %collective-permute-start.4 = (bf16[12,4,4,128]{3,2,1,0:T(4,128)(2,1)S(1)}, bf16[12,4,4,128]{3,2,1,0:T(4,128)(2,1)S(1)}, u32[]{:S(2)}, u32[]{:S(2)}) collective-permute-start(bf16[12,4,4,128]{3,2,1,0:T(4,128)(2,1)S(1)} %add.231), channel_id=1, source_target_pairs={{0,8},{4,12},{8,0},{12,4},{16,24},{20,28},{24,16},{28,20},{32,40},... | collective-permute-start | bytes 147464 | tf_op jit(solution)/shard_map/ppermute | solution.py:171
  21.6 5.4 %collective-permute-start.5 = (bf16[12,4,4,128]{3,2,1,0:T(4,128)(2,1)S(1)}, bf16[12,4,4,128]{3,2,1,0:T(4,128)(2,1)S(1)}, u32[]{:S(2)}, u32[]{:S(2)}) collective-permute-start(bf16[12,4,4,128]{3,2,1,0:T(4,128)(2,1)S(1)} %add.237), channel_id=1, source_target_pairs={{0,16},{4,20},{8,24},{12,28},{16,0},{20,4},{24,8},{28,12},{32,48},... | collective-permute-start | bytes 147464 | tf_op jit(solution)/shard_map/ppermute | solution.py:171
  27.1 7.8 %collective-permute-start.6 = (bf16[12,4,4,128]{3,2,1,0:T(4,128)(2,1)S(1)}, bf16[12,4,4,128]{3,2,1,0:T(4,128)(2,1)S(1)}, u32[]{:S(2)}, u32[]{:S(2)}) collective-permute-start(bf16[12,4,4,128]{3,2,1,0:T(4,128)(2,1)S(1)} %add.238), channel_id=1, source_target_pairs={{0,48},{4,52},{8,56},{12,60},{16,32},{20,36},{24,40},{28,44},{32,1... | collective-permute-start | bytes 147464 | tf_op jit(solution)/shard_map/ppermute | solution.py:171
  35.0 4.2 %collective-permute-start.7 = (bf16[12,4,4,128]{3,2,1,0:T(4,128)(2,1)S(1)}, bf16[12,4,4,128]{3,2,1,0:T(4,128)(2,1)S(1)}, u32[]{:S(2)}, u32[]{:S(2)}) collective-permute-start(bf16[12,4,4,128]{3,2,1,0:T(4,128)(2,1)S(1)} %add.239), channel_id=1, source_target_pairs={{0,64},{4,68},{8,72},{12,76},{16,80},{20,84},{24,88},{28,92},{32,9... | collective-permute-start | bytes 147464 | tf_op jit(solution)/shard_map/ppermute | solution.py:171
  39.2 5.4 %collective-permute-start.8 = (bf16[12,4,4,128]{3,2,1,0:T(4,128)(2,1)S(1)}, bf16[12,4,4,128]{3,2,1,0:T(4,128)(2,1)S(1)}, u32[]{:S(2)}, u32[]{:S(2)}) collective-permute-start(bf16[12,4,4,128]{3,2,1,0:T(4,128)(2,1)S(1)} %add.240), channel_id=1, source_target_pairs={{0,192},{4,196},{8,200},{12,204},{16,208},{20,212},{24,216},{28,22... | collective-permute-start | bytes 147464 | tf_op jit(solution)/shard_map/ppermute | solution.py:171
  45.8 3.1 %copy-start.5 = (f32[8,128]{1,0:T(8,128)S(1)}, f32[8,128]{1,0:T(8,128)}, u32[]{:S(2)}) copy-start(f32[8,128]{1,0:T(8,128)} %get-tuple-element.17) | copy-start | bytes 12292
  47.0 17.9 %copy-start.4 = (f32[8,128]{1,0:T(8,128)S(1)}, f32[8,128]{1,0:T(8,128)}, u32[]{:S(2)}) copy-start(f32[8,128]{1,0:T(8,128)} %get-tuple-element.18) | copy-start | bytes 12292
  48.8 1.3 %collective-permute-start.9 = (bf16[134,192]{1,0:T(8,128)(2,1)S(1)}, bf16[134,192]{1,0:T(8,128)(2,1)S(1)}, u32[]{:S(2)}, u32[]{:S(2)}) collective-permute-start(bf16[134,192]{1,0:T(8,128)(2,1)S(1)} %concatenate.75), channel_id=1, source_target_pairs={{0,4},{4,0},{8,12},{12,8},{16,20},{20,16},{24,28},{28,24},{32,36},... | collective-permute-start | bytes 154376 | tf_op jit(solution)/shard_map/ppermute | solution.py:211
  49.0 29.2 %copy-start.6 = (bf16[8,128]{1,0:T(8,128)(2,1)}, bf16[8,128]{1,0:T(8,128)(2,1)S(1)}, u32[]{:S(2)}) copy-start(bf16[8,128]{1,0:T(8,128)(2,1)S(1)} %convert_element_type.160) | copy-start | bytes 6148
  50.3 4.4 %collective-permute-start.10 = (bf16[134,192]{1,0:T(8,128)(2,1)S(1)}, bf16[134,192]{1,0:T(8,128)(2,1)S(1)}, u32[]{:S(2)}, u32[]{:S(2)}) collective-permute-start(bf16[134,192]{1,0:T(8,128)(2,1)S(1)} %concatenate.76), channel_id=1, source_target_pairs={{0,8},{4,12},{8,0},{12,4},{16,24},{20,28},{24,16},{28,20},{32,40},... | collective-permute-start | bytes 154376 | tf_op jit(solution)/shard_map/ppermute | solution.py:211
  54.8 5.3 %collective-permute-start.11 = (bf16[134,192]{1,0:T(8,128)(2,1)S(1)}, bf16[134,192]{1,0:T(8,128)(2,1)S(1)}, u32[]{:S(2)}, u32[]{:S(2)}) collective-permute-start(bf16[134,192]{1,0:T(8,128)(2,1)S(1)} %concatenate.77), channel_id=1, source_target_pairs={{0,16},{4,20},{8,24},{12,28},{16,0},{20,4},{24,8},{28,12},{32,48},... | collective-permute-start | bytes 154376 | tf_op jit(solution)/shard_map/ppermute | solution.py:211
  60.2 7.3 %collective-permute-start.12 = (bf16[134,192]{1,0:T(8,128)(2,1)S(1)}, bf16[134,192]{1,0:T(8,128)(2,1)S(1)}, u32[]{:S(2)}, u32[]{:S(2)}) collective-permute-start(bf16[134,192]{1,0:T(8,128)(2,1)S(1)} %concatenate.78), channel_id=1, source_target_pairs={{0,48},{4,52},{8,56},{12,60},{16,32},{20,36},{24,40},{28,44},{32,1... | collective-permute-start | bytes 154376 | tf_op jit(solution)/shard_map/ppermute | solution.py:211
  64.9 14.1 %copy-start.3 = (bf16[8,128]{1,0:T(8,128)(2,1)}, bf16[8,128]{1,0:T(8,128)(2,1)S(1)}, u32[]{:S(2)}) copy-start(bf16[8,128]{1,0:T(8,128)(2,1)S(1)} %convert_element_type.161) | copy-start | bytes 6148
  67.6 4.6 %collective-permute-start.13 = (bf16[134,192]{1,0:T(8,128)(2,1)S(1)}, bf16[134,192]{1,0:T(8,128)(2,1)S(1)}, u32[]{:S(2)}, u32[]{:S(2)}) collective-permute-start(bf16[134,192]{1,0:T(8,128)(2,1)S(1)} %concatenate.79), channel_id=1, source_target_pairs={{0,64},{4,68},{8,72},{12,76},{16,80},{20,84},{24,88},{28,92},{32,9... | collective-permute-start | bytes 154376 | tf_op jit(solution)/shard_map/ppermute | solution.py:211
  72.3 5.6 %collective-permute-start.14 = (bf16[134,192]{1,0:T(8,128)(2,1)S(1)}, bf16[134,192]{1,0:T(8,128)(2,1)S(1)}, u32[]{:S(2)}, u32[]{:S(2)}) collective-permute-start(bf16[134,192]{1,0:T(8,128)(2,1)S(1)} %concatenate.80), channel_id=1, source_target_pairs={{0,192},{4,196},{8,200},{12,204},{16,208},{20,212},{24,216},{28,22... | collective-permute-start | bytes 154376 | tf_op jit(solution)/shard_map/ppermute | solution.py:211
  79.1 13.9 %copy-start.1 = (bf16[4,2,640]{2,1,0:T(2,128)(2,1)S(1)}, bf16[4,2,640]{2,1,0:T(2,128)(2,1)}, u32[]{:S(2)}) copy-start(bf16[4,2,640]{2,1,0:T(2,128)(2,1)} %param.14) | copy-start | bytes 30724
  83.7 5.0 %collective-permute-start.15 = (f32[8,640]{1,0:T(8,128)S(1)}, f32[8,640]{1,0:T(8,128)S(1)}, u32[]{:S(2)}, u32[]{:S(2)}) collective-permute-start(f32[8,640]{1,0:T(8,128)S(1)} %get-tuple-element.73), channel_id=1, source_target_pairs={{0,1},{1,2},{2,3},{3,0},{4,5},{5,6},{6,7},{7,4},{8,9},{9,10},{10,1... | collective-permute-start | bytes 61448 | tf_op jit(solution)/shard_map/ppermute | solution.py:159
  84.3 4.4 %collective-permute-start.17 = (f32[8,640]{1,0:T(8,128)S(1)}, f32[8,640]{1,0:T(8,128)S(1)}, u32[]{:S(2)}, u32[]{:S(2)}) collective-permute-start(f32[8,640]{1,0:T(8,128)S(1)} %get-tuple-element.74), channel_id=1, source_target_pairs={{0,3},{1,0},{2,1},{3,2},{4,7},{5,4},{6,5},{7,6},{8,11},{9,8},{10,9... | collective-permute-start | bytes 61448 | tf_op jit(solution)/shard_map/ppermute | solution.py:159
  86.9 5.3 %collective-permute-start.16 = (f32[8,640]{1,0:T(8,128)S(1)}, f32[8,640]{1,0:T(8,128)S(1)}, u32[]{:S(2)}, u32[]{:S(2)}) collective-permute-start(f32[8,640]{1,0:T(8,128)S(1)} %get-tuple-element.75), channel_id=1, source_target_pairs={{0,2},{1,3},{2,0},{3,1},{4,6},{5,7},{6,4},{7,5},{8,10},{9,11},{10,... | collective-permute-start | bytes 61448 | tf_op jit(solution)/shard_map/ppermute | solution.py:159

commit v12 on v10

--- a/solution.py
+++ b/solution.py
@@ -54,8 +54,8 @@
         for h in range(product.shape[1] // HEAD_SIZE):
             o_ref[:, h * HEAD_SIZE : (h + 1) * HEAD_SIZE] = norm_rotate(
                 product[:, h * HEAD_SIZE : (h + 1) * HEAD_SIZE], gain
-            )
-    v_ref[...] = jnp.dot(normed, wv_ref[...], preferred_element_type=jnp.float32)
+            ).astype(o_ref.dtype)
+    v_ref[...] = jnp.dot(normed, wv_ref[...], preferred_element_type=jnp.float32).astype(v_ref.dtype)
 
 
 def project_rows(x, gain, query_gain, key_gain, positions, w_query, key_matrix, value_matrix):
@@ -71,10 +71,10 @@
     widths = [w.shape[1] for w in weights]
     return pl.pallas_call(
         _project_kernel,
-        out_shape=[jax.ShapeDtypeStruct((m, n), jnp.float32) for n in widths],
+        out_shape=[jax.ShapeDtypeStruct((m, n), jnp.bfloat16) for n in widths],
         cost_estimate=pl.CostEstimate(
             flops=2 * m * k * sum(widths),
-            bytes_accessed=2 * (m * k + k * sum(widths)) + 4 * m * sum(widths),
+            bytes_accessed=2 * (m * k + k * sum(widths)) + 2 * m * sum(widths),
             transcendentals=m,
         ),
     )(
@@ -249,9 +249,8 @@
     query, keys, values = project_rows(
         wide, norm_gain, query_gain, key_gain, positions, w_query, key_matrix, value_matrix
     )
-    query = query.reshape(rows, q_heads, HEAD_SIZE).astype(jnp.bfloat16)
-    keys = keys.reshape(rows, kv_heads, HEAD_SIZE).astype(jnp.bfloat16)
-    values = values.astype(jnp.bfloat16)
+    query = query.reshape(rows, q_heads, HEAD_SIZE)
+    keys = keys.reshape(rows, kv_heads, HEAD_SIZE)
     new_keys = keys.reshape(steps, own_rows, kv_heads * HEAD_SIZE)
     new_values = values.reshape(steps, own_rows, kv_heads * HEAD_SIZE)
     own_query = query.reshape(steps, own_rows, q_heads, HEAD_SIZE).transpose(1, 0, 2, 3)

time: 93 us -> 92.9 us (level)
  no operation moved by 1% of the time
where the time goes in v12:
time: 92.9 us; the launch traced here: 92.5 us
  waiting for transfers between devices  39.3 us (42%)
  starting transfers between devices  27.4 us (29%)
  local copies, waits for them, and re-layouts  8.79 us (9%)
  other arithmetic  7.86 us (8%)
  Pallas kernels  6.45 us (7%)
  matrix products  1.61 us (2%)
  between operations  1.08 us (1%)
    ppermute x6, waiting for transfers between devices, stats_butterfly(): arrived = lax.ppermute(packed, 'seq', pairs)  19.3 us
    ppermute x6, waiting for transfers between devices, butterfly(): lax.ppermute(value, 'seq', [(i, i ^ stride) for i in range(n_seq)])  17.1 us
    ppermute x6, starting transfers between devices, butterfly(): lax.ppermute(value, 'seq', [(i, i ^ stride) for i in range(n_seq)])  10.4 us
    ppermute x6, starting transfers between devices, stats_butterfly(): arrived = lax.ppermute(packed, 'seq', pairs)  7.65 us
    ppermute x3, starting transfers between devices, gather_mp(): lax.ppermute(block, 'mp', [(i, (i + s) % n_mp) for i in range(n_mp)])  4.69 us
    ppermute x3, starting transfers between devices, reduce_scatter_mp(): lax.ppermute(outgoing, 'mp', [(i, (i + s) % n_mp) for i in range(n_mp)])  4.65 us
    pallas_call x1, Pallas kernels, project_rows(): pl.pallas_call(_project_kernel, out_shape=[jax.ShapeDtypeStruct((m, n), j...  3.62 us
    ppermute x3, waiting for transfers between devices, reduce_scatter_mp(): lax.ppermute(outgoing, 'mp', [(i, (i + s) % n_mp) for i in range(n_mp)])  2.86 us
  transfers between devices with their start and end apart: 18, of which 15 were waited for; matrix products, arithmetic and copies ran while one was open for 7% of the time, Pallas kernels for 0%

profile of v12, /device:TPU:38, one launch (start us, length us, event | category | flops | bytes accessed | tf_op | source)
XLA Modules:
  0.0 92.5 jit_solution(2566417228208486586)
XLA Ops:
  0.7 3.1 %collective-permute-start = (bf16[4,2,640]{2,1,0:T(2,128)(2,1)}, bf16[4,2,640]{2,1,0:T(2,128)(2,1)S(1)}, u32[]{:S(2)}, u32[]{:S(2)}) collective-permute-start(bf16[4,2,640]{2,1,0:T(2,128)(2,1)} %param.14), channel_id=1, source_target_pairs={{0,3},{1,0},{2,1},{3,2},{4,7},{5,4},{6,5},{7,6},{8,11},{9,8},{10,9... | collective-permute-start | bytes 30728 | tf_op jit(solution)/shard_map/ppermute | solution.py:135
  3.8 0.6 collective-permute-start.1
  4.4 1.0 %collective-permute-start.2 = (bf16[4,2,640]{2,1,0:T(2,128)(2,1)}, bf16[4,2,640]{2,1,0:T(2,128)(2,1)S(1)}, u32[]{:S(2)}, u32[]{:S(2)}) collective-permute-start(bf16[4,2,640]{2,1,0:T(2,128)(2,1)} %param.14), channel_id=1, source_target_pairs={{0,1},{1,2},{2,3},{3,0},{4,5},{5,6},{6,7},{7,4},{8,9},{9,10},{10,1... | collective-permute-start | bytes 30728 | tf_op jit(solution)/shard_map/ppermute | solution.py:135
  5.4 0.7 broadcast_compare_fusion.2
  6.1 0.7 dynamic_slice.24
  7.0 0.7 pad_maximum_fusion.3.cos_ref
  8.1 0.7 pad_maximum_fusion.4.sin_ref
  8.8 1.3 %reshape.368.g_ref = f32[1,2560]{1,0:T(1,128)} reshape(f32[2560]{0:T(1024)} %param.15) | data formatting | bytes 20480 | tf_op jit(solution)/shard_map/reshape | solution.py:82
  10.1 0.7 broadcast_select_fusion.11
  10.9 0.6 reshape.367.x_ref
  11.5 3.6 %shard_map.157 = (bf16[8,512]{1,0:T(8,128)(2,1)}, bf16[8,128]{1,0:T(8,128)(2,1)}, bf16[8,128]{1,0:T(8,128)(2,1)}) custom-call(bf16[8,2560]{1,0:T(8,128)(2,1)} %reshape.367.x_ref, f32[1,2560]{1,0:T(1,128)} %reshape.368.g_ref, f32[1,128]{1,0:T(1,128)} %bitcast.220, f32[1,128]{1,0:T(1,128)} %bitcast.221, f32[8,128]{1,0:T(8,128)} %pad_maximum_fusion.3.cos_ref, ...), custom_call_target="tpu_custom_call" | custom-call | flops 31457280 | bytes 3985408 | tf_op jit(solution)/shard_map/pallas_call | solution.py:72
  15.1 0.7 reshape_reshape.9
  16.2 1.1 %collective-permute-done.3 = bf16[12,4,4,128]{3,2,1,0:T(4,128)(2,1)S(1)} collective-permute-done((bf16[12,4,4,128]{3,2,1,0:T(4,128)(2,1)S(1)}, bf16[12,4,4,128]{3,2,1,0:T(4,128)(2,1)S(1)}, u32[]{:S(2)}, u32[]{:S(2)}) %collective-permute-start.3) | collective-permute-done | bytes 49184 | tf_op jit(solution)/shard_map/ppermute | solution.py:164
  17.3 0.2 collective-permute-start.4
  17.5 0.2 fusion.30
  17.7 0.2 select_reduce_fusion.7
  17.9 3.6 %collective-permute-done.4 = bf16[12,4,4,128]{3,2,1,0:T(4,128)(2,1)S(1)} collective-permute-done((bf16[12,4,4,128]{3,2,1,0:T(4,128)(2,1)S(1)}, bf16[12,4,4,128]{3,2,1,0:T(4,128)(2,1)S(1)}, u32[]{:S(2)}, u32[]{:S(2)}) %collective-permute-start.4) | collective-permute-done | bytes 49184 | tf_op jit(solution)/shard_map/ppermute | solution.py:164
  21.5 3.4 %collective-permute-start.5 = (bf16[12,4,4,128]{3,2,1,0:T(4,128)(2,1)S(1)}, bf16[12,4,4,128]{3,2,1,0:T(4,128)(2,1)S(1)}, u32[]{:S(2)}, u32[]{:S(2)}) collective-permute-start(bf16[12,4,4,128]{3,2,1,0:T(4,128)(2,1)S(1)} %add.268), channel_id=1, source_target_pairs={{0,16},{4,20},{8,24},{12,28},{16,0},{20,4},{24,8},{28,12},{32,48},... | collective-permute-start | bytes 147464 | tf_op jit(solution)/shard_map/ppermute | solution.py:164
  25.0 2.0 %collective-permute-done.5 = bf16[12,4,4,128]{3,2,1,0:T(4,128)(2,1)S(1)} collective-permute-done((bf16[12,4,4,128]{3,2,1,0:T(4,128)(2,1)S(1)}, bf16[12,4,4,128]{3,2,1,0:T(4,128)(2,1)S(1)}, u32[]{:S(2)}, u32[]{:S(2)}) %collective-permute-start.5) | collective-permute-done | bytes 49184 | tf_op jit(solution)/shard_map/ppermute | solution.py:164
  27.0 5.2 %collective-permute-start.6 = (bf16[12,4,4,128]{3,2,1,0:T(4,128)(2,1)S(1)}, bf16[12,4,4,128]{3,2,1,0:T(4,128)(2,1)S(1)}, u32[]{:S(2)}, u32[]{:S(2)}) collective-permute-start(bf16[12,4,4,128]{3,2,1,0:T(4,128)(2,1)S(1)} %add.269), channel_id=1, source_target_pairs={{0,48},{4,52},{8,56},{12,60},{16,32},{20,36},{24,40},{28,44},{32,1... | collective-permute-start | bytes 147464 | tf_op jit(solution)/shard_map/ppermute | solution.py:164
  32.3 2.5 %collective-permute-done.6 = bf16[12,4,4,128]{3,2,1,0:T(4,128)(2,1)S(1)} collective-permute-done((bf16[12,4,4,128]{3,2,1,0:T(4,128)(2,1)S(1)}, bf16[12,4,4,128]{3,2,1,0:T(4,128)(2,1)S(1)}, u32[]{:S(2)}, u32[]{:S(2)}) %collective-permute-start.6) | collective-permute-done | bytes 49184 | tf_op jit(solution)/shard_map/ppermute | solution.py:164
  34.9 0.9 collective-permute-start.7
  35.9 3.2 %collective-permute-done.7 = bf16[12,4,4,128]{3,2,1,0:T(4,128)(2,1)S(1)} collective-permute-done((bf16[12,4,4,128]{3,2,1,0:T(4,128)(2,1)S(1)}, bf16[12,4,4,128]{3,2,1,0:T(4,128)(2,1)S(1)}, u32[]{:S(2)}, u32[]{:S(2)}) %collective-permute-start.7) | collective-permute-done | bytes 49184 | tf_op jit(solution)/shard_map/ppermute | solution.py:164
  39.1 0.6 collective-permute-start.8
  39.7 4.8 %collective-permute-done.8 = bf16[12,4,4,128]{3,2,1,0:T(4,128)(2,1)S(1)} collective-permute-done((bf16[12,4,4,128]{3,2,1,0:T(4,128)(2,1)S(1)}, bf16[12,4,4,128]{3,2,1,0:T(4,128)(2,1)S(1)}, u32[]{:S(2)}, u32[]{:S(2)}) %collective-permute-start.8) | collective-permute-done | bytes 49184 | tf_op jit(solution)/shard_map/ppermute | solution.py:164
  44.6 0.6 gather_fusion
  45.2 0.5 select_reduce_fusion.1
  46.1 0.3 bitcast_reduce_fusion
  46.5 0.4 fusion.1
  46.8 0.3 convolution_bitcast_fusion
  47.2 0.2 fusion.74
  47.4 0.2 copy.151
  47.7 0.2 select_reduce_fusion.3
  47.8 0.5 copy.152
  48.9 1.2 %collective-permute-done.9 = bf16[134,192]{1,0:T(8,128)(2,1)S(1)} collective-permute-done((bf16[134,192]{1,0:T(8,128)(2,1)S(1)}, bf16[134,192]{1,0:T(8,128)(2,1)S(1)}, u32[]{:S(2)}, u32[]{:S(2)}) %collective-permute-start.9) | collective-permute-done | bytes 51488 | tf_op jit(solution)/shard_map/ppermute | solution.py:204
  50.2 0.6 collective-permute-start.10
  50.8 0.2 convolution_multiply_fusion.1
  51.0 3.6 %collective-permute-done.10 = bf16[134,192]{1,0:T(8,128)(2,1)S(1)} collective-permute-done((bf16[134,192]{1,0:T(8,128)(2,1)S(1)}, bf16[134,192]{1,0:T(8,128)(2,1)S(1)}, u32[]{:S(2)}, u32[]{:S(2)}) %collective-permute-start.10) | collective-permute-done | bytes 51488 | tf_op jit(solution)/shard_map/ppermute | solution.py:204
  54.7 1.5 %collective-permute-start.11 = (bf16[134,192]{1,0:T(8,128)(2,1)S(1)}, bf16[134,192]{1,0:T(8,128)(2,1)S(1)}, u32[]{:S(2)}, u32[]{:S(2)}) collective-permute-start(bf16[134,192]{1,0:T(8,128)(2,1)S(1)} %concatenate.77), channel_id=1, source_target_pairs={{0,16},{4,20},{8,24},{12,28},{16,0},{20,4},{24,8},{28,12},{32,48},... | collective-permute-start | bytes 154376 | tf_op jit(solution)/shard_map/ppermute | solution.py:204
  56.3 3.7 %collective-permute-done.11 = bf16[134,192]{1,0:T(8,128)(2,1)S(1)} collective-permute-done((bf16[134,192]{1,0:T(8,128)(2,1)S(1)}, bf16[134,192]{1,0:T(8,128)(2,1)S(1)}, u32[]{:S(2)}, u32[]{:S(2)}) %collective-permute-start.11) | collective-permute-done | bytes 51488 | tf_op jit(solution)/shard_map/ppermute | solution.py:204
  60.2 4.6 %collective-permute-start.12 = (bf16[134,192]{1,0:T(8,128)(2,1)S(1)}, bf16[134,192]{1,0:T(8,128)(2,1)S(1)}, u32[]{:S(2)}, u32[]{:S(2)}) collective-permute-start(bf16[134,192]{1,0:T(8,128)(2,1)S(1)} %concatenate.78), channel_id=1, source_target_pairs={{0,48},{4,52},{8,56},{12,60},{16,32},{20,36},{24,40},{28,44},{32,1... | collective-permute-start | bytes 154376 | tf_op jit(solution)/shard_map/ppermute | solution.py:204
  65.0 2.4 %collective-permute-done.12 = bf16[134,192]{1,0:T(8,128)(2,1)S(1)} collective-permute-done((bf16[134,192]{1,0:T(8,128)(2,1)S(1)}, bf16[134,192]{1,0:T(8,128)(2,1)S(1)}, u32[]{:S(2)}, u32[]{:S(2)}) %collective-permute-start.12) | collective-permute-done | bytes 51488 | tf_op jit(solution)/shard_map/ppermute | solution.py:204
  67.6 0.3 collective-permute-start.13
  68.0 0.3 copy.162
  68.2 3.9 %collective-permute-done.13 = bf16[134,192]{1,0:T(8,128)(2,1)S(1)} collective-permute-done((bf16[134,192]{1,0:T(8,128)(2,1)S(1)}, bf16[134,192]{1,0:T(8,128)(2,1)S(1)}, u32[]{:S(2)}, u32[]{:S(2)}) %collective-permute-start.13) | collective-permute-done | bytes 51488 | tf_op jit(solution)/shard_map/ppermute | solution.py:204
  72.3 0.6 collective-permute-start.14
  72.9 0.4 copy.156
  73.3 4.5 %collective-permute-done.14 = bf16[134,192]{1,0:T(8,128)(2,1)S(1)} collective-permute-done((bf16[134,192]{1,0:T(8,128)(2,1)S(1)}, bf16[134,192]{1,0:T(8,128)(2,1)S(1)}, u32[]{:S(2)}, u32[]{:S(2)}) %collective-permute-start.14) | collective-permute-done | bytes 51488 | tf_op jit(solution)/shard_map/ppermute | solution.py:204
  78.2 0.2 select_reduce_fusion
  78.4 0.4 copy.155
  78.8 0.2 bitcast_select_fusion
  79.0 0.2 fusion.7
  79.2 0.2 copy.165
  79.4 0.6 copy.193
  80.0 2.8 %shard_map.158 = f32[4,8,640]{2,1,0:T(8,128)} custom-call(bf16[8,512]{1,0:T(8,128)(2,1)} %bitcast.187, bf16[512,2560]{1,0:T(8,128)(2,1)} %w_ref.1), custom_call_target="tpu_custom_call" | custom-call | flops 20971520 | bytes 2711552 | tf_op jit(solution)/shard_map/pallas_call | solution.py:121
  82.8 0.8 dynamic-slice_bitcast_fusion.2
  83.6 1.9 %collective-permute-start.15 = (f32[8,640]{1,0:T(8,128)S(1)}, f32[8,640]{1,0:T(8,128)S(1)}, u32[]{:S(2)}, u32[]{:S(2)}) collective-permute-start(f32[8,640]{1,0:T(8,128)S(1)} %get-tuple-element.73), channel_id=1, source_target_pairs={{0,1},{1,2},{2,3},{3,0},{4,5},{5,6},{6,7},{7,4},{8,9},{9,10},{10,1... | collective-permute-start | bytes 61448 | tf_op jit(solution)/shard_map/ppermute | solution.py:152
  85.5 1.8 %collective-permute-start.16 = (f32[8,640]{1,0:T(8,128)S(1)}, f32[8,640]{1,0:T(8,128)S(1)}, u32[]{:S(2)}, u32[]{:S(2)}) collective-permute-start(f32[8,640]{1,0:T(8,128)S(1)} %get-tuple-element.75), channel_id=1, source_target_pairs={{0,2},{1,3},{2,0},{3,1},{4,6},{5,7},{6,4},{7,5},{8,10},{9,11},{10,... | collective-permute-start | bytes 61448 | tf_op jit(solution)/shard_map/ppermute | solution.py:152
  87.3 0.9 collective-permute-start.17
  88.2 0.3 collective-permute-done.15
  88.6 2.2 %collective-permute-done.16 = f32[8,640]{1,0:T(8,128)S(1)} collective-permute-done((f32[8,640]{1,0:T(8,128)S(1)}, f32[8,640]{1,0:T(8,128)S(1)}, u32[]{:S(2)}, u32[]{:S(2)}) %collective-permute-start.16) | collective-permute-done | bytes 20512 | tf_op jit(solution)/shard_map/ppermute | solution.py:152
  90.8 0.3 collective-permute-done.17
  91.1 0.7 fusion.20
  91.9 0.6 add_convert_fusion
  (108 shorter events, 4.2 us)
Async XLA Ops:
  0.6 44.6 %copy-start = (bf16[16,256,128]{2,1,0:T(8,128)(2,1)S(1)}, bf16[16,256,128]{2,1,0:T(8,128)(2,1)}, u32[]{:S(2)}) copy-start(bf16[16,256,128]{2,1,0:T(8,128)(2,1)} %param.22) | copy-start | bytes 3145732
  0.6 17.1 %copy-start.4 = (s32[128]{0:T(128)S(1)}, s32[128]{0:T(128)}, u32[]{:S(2)}) copy-start(s32[128]{0:T(128)} %param.24) | copy-start | bytes 1540
  0.7 16.9 %copy-start.2 = (s32[16]{0:T(128)S(1)}, s32[16]{0:T(128)}, u32[]{:S(2)}) copy-start(s32[16]{0:T(128)} %param.25) | copy-start | bytes 196
  0.7 17.3 %copy-start.8 = (s32[16]{0:T(128)S(1)}, s32[16]{0:T(128)}, u32[]{:S(2)}) copy-start(s32[16]{0:T(128)} %param.26) | copy-start | bytes 196
  0.7 17.2 %copy-start.5 = (s32[16]{0:T(128)S(1)}, s32[16]{0:T(128)}, u32[]{:S(2)}) copy-start(s32[16]{0:T(128)} %param.27) | copy-start | bytes 196
  0.7 9.4 %collective-permute-start = (bf16[4,2,640]{2,1,0:T(2,128)(2,1)}, bf16[4,2,640]{2,1,0:T(2,128)(2,1)S(1)}, u32[]{:S(2)}, u32[]{:S(2)}) collective-permute-start(bf16[4,2,640]{2,1,0:T(2,128)(2,1)} %param.14), channel_id=1, source_target_pairs={{0,3},{1,0},{2,1},{3,2},{4,7},{5,4},{6,5},{7,6},{8,11},{9,8},{10,9... | collective-permute-start | bytes 30728 | tf_op jit(solution)/shard_map/ppermute | solution.py:135
  3.8 6.3 %collective-permute-start.1 = (bf16[4,2,640]{2,1,0:T(2,128)(2,1)}, bf16[4,2,640]{2,1,0:T(2,128)(2,1)S(1)}, u32[]{:S(2)}, u32[]{:S(2)}) collective-permute-start(bf16[4,2,640]{2,1,0:T(2,128)(2,1)} %param.14), channel_id=1, source_target_pairs={{0,2},{1,3},{2,0},{3,1},{4,6},{5,7},{6,4},{7,5},{8,10},{9,11},{10,... | collective-permute-start | bytes 30728 | tf_op jit(solution)/shard_map/ppermute | solution.py:135
  4.4 5.7 %collective-permute-start.2 = (bf16[4,2,640]{2,1,0:T(2,128)(2,1)}, bf16[4,2,640]{2,1,0:T(2,128)(2,1)S(1)}, u32[]{:S(2)}, u32[]{:S(2)}) collective-permute-start(bf16[4,2,640]{2,1,0:T(2,128)(2,1)} %param.14), channel_id=1, source_target_pairs={{0,1},{1,2},{2,3},{3,0},{4,5},{5,6},{6,7},{7,4},{8,9},{9,10},{10,1... | collective-permute-start | bytes 30728 | tf_op jit(solution)/shard_map/ppermute | solution.py:135
  11.5 34.9 %copy-start.6 = (bf16[16,256,128]{2,1,0:T(8,128)(2,1)S(1)}, bf16[16,256,128]{2,1,0:T(8,128)(2,1)}, u32[]{:S(2)}) copy-start(bf16[16,256,128]{2,1,0:T(8,128)(2,1)} %param.23) | copy-start | bytes 3145732
  16.0 1.3 %collective-permute-start.3 = (bf16[12,4,4,128]{3,2,1,0:T(4,128)(2,1)S(1)}, bf16[12,4,4,128]{3,2,1,0:T(4,128)(2,1)S(1)}, u32[]{:S(2)}, u32[]{:S(2)}) collective-permute-start(bf16[12,4,4,128]{3,2,1,0:T(4,128)(2,1)S(1)} %select_reduce_fusion.4), channel_id=1, source_target_pairs={{0,4},{4,0},{8,12},{12,8},{16,20},{20,16},{24,28},{28,24},{32,36},... | collective-permute-start | bytes 147464 | tf_op jit(solution)/shard_map/ppermute | solution.py:164
  17.3 4.2 %collective-permute-start.4 = (bf16[12,4,4,128]{3,2,1,0:T(4,128)(2,1)S(1)}, bf16[12,4,4,128]{3,2,1,0:T(4,128)(2,1)S(1)}, u32[]{:S(2)}, u32[]{:S(2)}) collective-permute-start(bf16[12,4,4,128]{3,2,1,0:T(4,128)(2,1)S(1)} %add.262), channel_id=1, source_target_pairs={{0,8},{4,12},{8,0},{12,4},{16,24},{20,28},{24,16},{28,20},{32,40},... | collective-permute-start | bytes 147464 | tf_op jit(solution)/shard_map/ppermute | solution.py:164
  21.5 5.4 %collective-permute-start.5 = (bf16[12,4,4,128]{3,2,1,0:T(4,128)(2,1)S(1)}, bf16[12,4,4,128]{3,2,1,0:T(4,128)(2,1)S(1)}, u32[]{:S(2)}, u32[]{:S(2)}) collective-permute-start(bf16[12,4,4,128]{3,2,1,0:T(4,128)(2,1)S(1)} %add.268), channel_id=1, source_target_pairs={{0,16},{4,20},{8,24},{12,28},{16,0},{20,4},{24,8},{28,12},{32,48},... | collective-permute-start | bytes 147464 | tf_op jit(solution)/shard_map/ppermute | solution.py:164
  27.0 7.8 %collective-permute-start.6 = (bf16[12,4,4,128]{3,2,1,0:T(4,128)(2,1)S(1)}, bf16[12,4,4,128]{3,2,1,0:T(4,128)(2,1)S(1)}, u32[]{:S(2)}, u32[]{:S(2)}) collective-permute-start(bf16[12,4,4,128]{3,2,1,0:T(4,128)(2,1)S(1)} %add.269), channel_id=1, source_target_pairs={{0,48},{4,52},{8,56},{12,60},{16,32},{20,36},{24,40},{28,44},{32,1... | collective-permute-start | bytes 147464 | tf_op jit(solution)/shard_map/ppermute | solution.py:164
  34.9 4.2 %collective-permute-start.7 = (bf16[12,4,4,128]{3,2,1,0:T(4,128)(2,1)S(1)}, bf16[12,4,4,128]{3,2,1,0:T(4,128)(2,1)S(1)}, u32[]{:S(2)}, u32[]{:S(2)}) collective-permute-start(bf16[12,4,4,128]{3,2,1,0:T(4,128)(2,1)S(1)} %add.270), channel_id=1, source_target_pairs={{0,64},{4,68},{8,72},{12,76},{16,80},{20,84},{24,88},{28,92},{32,9... | collective-permute-start | bytes 147464 | tf_op jit(solution)/shard_map/ppermute | solution.py:164
  39.1 5.4 %collective-permute-start.8 = (bf16[12,4,4,128]{3,2,1,0:T(4,128)(2,1)S(1)}, bf16[12,4,4,128]{3,2,1,0:T(4,128)(2,1)S(1)}, u32[]{:S(2)}, u32[]{:S(2)}) collective-permute-start(bf16[12,4,4,128]{3,2,1,0:T(4,128)(2,1)S(1)} %add.271), channel_id=1, source_target_pairs={{0,192},{4,196},{8,200},{12,204},{16,208},{20,212},{24,216},{28,22... | collective-permute-start | bytes 147464 | tf_op jit(solution)/shard_map/ppermute | solution.py:164
  46.4 4.4 %copy-start.7 = (bf16[8,128]{1,0:T(8,128)(2,1)S(1)}, bf16[8,128]{1,0:T(8,128)(2,1)}, u32[]{:S(2)}) copy-start(bf16[8,128]{1,0:T(8,128)(2,1)} %get-tuple-element.17) | copy-start | bytes 6148
  46.8 21.0 %copy-start.3 = (bf16[8,128]{1,0:T(8,128)(2,1)S(1)}, bf16[8,128]{1,0:T(8,128)(2,1)}, u32[]{:S(2)}) copy-start(bf16[8,128]{1,0:T(8,128)(2,1)} %get-tuple-element.18) | copy-start | bytes 6148
  48.7 1.3 %collective-permute-start.9 = (bf16[134,192]{1,0:T(8,128)(2,1)S(1)}, bf16[134,192]{1,0:T(8,128)(2,1)S(1)}, u32[]{:S(2)}, u32[]{:S(2)}) collective-permute-start(bf16[134,192]{1,0:T(8,128)(2,1)S(1)} %concatenate.75), channel_id=1, source_target_pairs={{0,4},{4,0},{8,12},{12,8},{16,20},{20,16},{24,28},{28,24},{32,36},... | collective-permute-start | bytes 154376 | tf_op jit(solution)/shard_map/ppermute | solution.py:204
  50.2 4.4 %collective-permute-start.10 = (bf16[134,192]{1,0:T(8,128)(2,1)S(1)}, bf16[134,192]{1,0:T(8,128)(2,1)S(1)}, u32[]{:S(2)}, u32[]{:S(2)}) collective-permute-start(bf16[134,192]{1,0:T(8,128)(2,1)S(1)} %concatenate.76), channel_id=1, source_target_pairs={{0,8},{4,12},{8,0},{12,4},{16,24},{20,28},{24,16},{28,20},{32,40},... | collective-permute-start | bytes 154376 | tf_op jit(solution)/shard_map/ppermute | solution.py:204
  54.7 5.3 %collective-permute-start.11 = (bf16[134,192]{1,0:T(8,128)(2,1)S(1)}, bf16[134,192]{1,0:T(8,128)(2,1)S(1)}, u32[]{:S(2)}, u32[]{:S(2)}) collective-permute-start(bf16[134,192]{1,0:T(8,128)(2,1)S(1)} %concatenate.77), channel_id=1, source_target_pairs={{0,16},{4,20},{8,24},{12,28},{16,0},{20,4},{24,8},{28,12},{32,48},... | collective-permute-start | bytes 154376 | tf_op jit(solution)/shard_map/ppermute | solution.py:204
  60.2 7.3 %collective-permute-start.12 = (bf16[134,192]{1,0:T(8,128)(2,1)S(1)}, bf16[134,192]{1,0:T(8,128)(2,1)S(1)}, u32[]{:S(2)}, u32[]{:S(2)}) collective-permute-start(bf16[134,192]{1,0:T(8,128)(2,1)S(1)} %concatenate.78), channel_id=1, source_target_pairs={{0,48},{4,52},{8,56},{12,60},{16,32},{20,36},{24,40},{28,44},{32,1... | collective-permute-start | bytes 154376 | tf_op jit(solution)/shard_map/ppermute | solution.py:204
  67.6 4.6 %collective-permute-start.13 = (bf16[134,192]{1,0:T(8,128)(2,1)S(1)}, bf16[134,192]{1,0:T(8,128)(2,1)S(1)}, u32[]{:S(2)}, u32[]{:S(2)}) collective-permute-start(bf16[134,192]{1,0:T(8,128)(2,1)S(1)} %concatenate.79), channel_id=1, source_target_pairs={{0,64},{4,68},{8,72},{12,76},{16,80},{20,84},{24,88},{28,92},{32,9... | collective-permute-start | bytes 154376 | tf_op jit(solution)/shard_map/ppermute | solution.py:204
  72.3 5.6 %collective-permute-start.14 = (bf16[134,192]{1,0:T(8,128)(2,1)S(1)}, bf16[134,192]{1,0:T(8,128)(2,1)S(1)}, u32[]{:S(2)}, u32[]{:S(2)}) collective-permute-start(bf16[134,192]{1,0:T(8,128)(2,1)S(1)} %concatenate.80), channel_id=1, source_target_pairs={{0,192},{4,196},{8,200},{12,204},{16,208},{20,212},{24,216},{28,22... | collective-permute-start | bytes 154376 | tf_op jit(solution)/shard_map/ppermute | solution.py:204
  79.0 12.9 %copy-start.1 = (bf16[4,2,640]{2,1,0:T(2,128)(2,1)S(1)}, bf16[4,2,640]{2,1,0:T(2,128)(2,1)}, u32[]{:S(2)}) copy-start(bf16[4,2,640]{2,1,0:T(2,128)(2,1)} %param.14) | copy-start | bytes 30724
  83.6 5.0 %collective-permute-start.15 = (f32[8,640]{1,0:T(8,128)S(1)}, f32[8,640]{1,0:T(8,128)S(1)}, u32[]{:S(2)}, u32[]{:S(2)}) collective-permute-start(f32[8,640]{1,0:T(8,128)S(1)} %get-tuple-element.73), channel_id=1, source_target_pairs={{0,1},{1,2},{2,3},{3,0},{4,5},{5,6},{6,7},{7,4},{8,9},{9,10},{10,1... | collective-permute-start | bytes 61448 | tf_op jit(solution)/shard_map/ppermute | solution.py:152
  85.5 5.3 %collective-permute-start.16 = (f32[8,640]{1,0:T(8,128)S(1)}, f32[8,640]{1,0:T(8,128)S(1)}, u32[]{:S(2)}, u32[]{:S(2)}) collective-permute-start(f32[8,640]{1,0:T(8,128)S(1)} %get-tuple-element.75), channel_id=1, source_target_pairs={{0,2},{1,3},{2,0},{3,1},{4,6},{5,7},{6,4},{7,5},{8,10},{9,11},{10,... | collective-permute-start | bytes 61448 | tf_op jit(solution)/shard_map/ppermute | solution.py:152
  87.3 3.8 %collective-permute-start.17 = (f32[8,640]{1,0:T(8,128)S(1)}, f32[8,640]{1,0:T(8,128)S(1)}, u32[]{:S(2)}, u32[]{:S(2)}) collective-permute-start(f32[8,640]{1,0:T(8,128)S(1)} %get-tuple-element.74), channel_id=1, source_target_pairs={{0,3},{1,0},{2,1},{3,2},{4,7},{5,4},{6,5},{7,6},{8,11},{9,8},{10,9... | collective-permute-start | bytes 61448 | tf_op jit(solution)/shard_map/ppermute | solution.py:152

commit v13 on v12

--- a/solution.py
+++ b/solution.py
@@ -79,7 +79,7 @@
         ),
     )(
         x,
-        gain.reshape(1, k),
+        jnp.broadcast_to(gain[None, :], (m, k)),
         query_gain.reshape(1, HEAD_SIZE),
         key_gain.reshape(1, HEAD_SIZE),
         cos_both,

time: 92.9 us -> 92.9 us (level)
    broadcast_in_dim x0 -> x1, local copies, waits for them, and re-layouts: none -> 1.34 us  [project_rows(): jnp.broadcast_to(gain[None, :], (m, k))]
    reshape x1 -> x0, local copies, waits for them, and re-layouts: 1.31 us -> none  [project_rows(): gain.reshape(1, k)]
  transfers between devices with their start and end apart: 18 -> 18, of which waited for: 15 -> 17; matrix products, arithmetic and copies ran while one was open for 7% -> 6% of each run, Pallas kernels for 0% -> 0%
where the time goes in v13:
time: 92.9 us; the launch traced here: 92.5 us
  waiting for transfers between devices  39.7 us (43%)
  starting transfers between devices  27 us (29%)
  local copies, waits for them, and re-layouts  8.82 us (9%)
  other arithmetic  7.85 us (8%)
  Pallas kernels  6.47 us (7%)
  matrix products  1.61 us (2%)
  between operations  1.08 us (1%)
    ppermute x6, waiting for transfers between devices, stats_butterfly(): arrived = lax.ppermute(packed, 'seq', pairs)  19.3 us
    ppermute x6, waiting for transfers between devices, butterfly(): lax.ppermute(value, 'seq', [(i, i ^ stride) for i in range(n_seq)])  17.1 us
    ppermute x6, starting transfers between devices, butterfly(): lax.ppermute(value, 'seq', [(i, i ^ stride) for i in range(n_seq)])  10.4 us
    ppermute x6, starting transfers between devices, stats_butterfly(): arrived = lax.ppermute(packed, 'seq', pairs)  7.64 us
    ppermute x3, starting transfers between devices, gather_mp(): lax.ppermute(block, 'mp', [(i, (i + s) % n_mp) for i in range(n_mp)])  4.69 us
    ppermute x3, starting transfers between devices, reduce_scatter_mp(): lax.ppermute(outgoing, 'mp', [(i, (i + s) % n_mp) for i in range(n_mp)])  4.32 us
    pallas_call x1, Pallas kernels, project_rows(): pl.pallas_call(_project_kernel, out_shape=[jax.ShapeDtypeStruct((m, n), j...  3.64 us
    pallas_call x1, Pallas kernels, chunked_matmul(): pl.pallas_call(_chunked_kernel, out_shape=jax.ShapeDtypeStruct((chunks, m...  2.83 us
  transfers between devices with their start and end apart: 18, of which 17 were waited for; matrix products, arithmetic and copies ran while one was open for 6% of the time, Pallas kernels for 0%

profile of v13, /device:TPU:38, one launch (start us, length us, event | category | flops | bytes accessed | tf_op | source)
XLA Modules:
  0.0 92.5 jit_solution(2621530225335696242)
XLA Ops:
  0.7 3.1 %collective-permute-start = (bf16[4,2,640]{2,1,0:T(2,128)(2,1)}, bf16[4,2,640]{2,1,0:T(2,128)(2,1)S(1)}, u32[]{:S(2)}, u32[]{:S(2)}) collective-permute-start(bf16[4,2,640]{2,1,0:T(2,128)(2,1)} %param.14), channel_id=1, source_target_pairs={{0,3},{1,0},{2,1},{3,2},{4,7},{5,4},{6,5},{7,6},{8,11},{9,8},{10,9... | collective-permute-start | bytes 30728 | tf_op jit(solution)/shard_map/ppermute | solution.py:135
  3.8 0.6 collective-permute-start.1
  4.4 1.0 %collective-permute-start.2 = (bf16[4,2,640]{2,1,0:T(2,128)(2,1)}, bf16[4,2,640]{2,1,0:T(2,128)(2,1)S(1)}, u32[]{:S(2)}, u32[]{:S(2)}) collective-permute-start(bf16[4,2,640]{2,1,0:T(2,128)(2,1)} %param.14), channel_id=1, source_target_pairs={{0,1},{1,2},{2,3},{3,0},{4,5},{5,6},{6,7},{7,4},{8,9},{9,10},{10,1... | collective-permute-start | bytes 30728 | tf_op jit(solution)/shard_map/ppermute | solution.py:135
  5.4 0.7 broadcast_compare_fusion.2
  6.1 0.7 dynamic_slice.24
  7.0 0.7 pad_maximum_fusion.3.cos_ref
  8.1 0.7 pad_maximum_fusion.4.sin_ref
  8.8 0.4 collective-permute-done.1
  9.2 0.3 collective-permute-done.2
  9.5 0.7 broadcast_select_fusion.11
  10.3 0.6 reshape.365.x_ref
  10.9 1.3 %broadcast_in_dim.269.g_ref = f32[8,2560]{1,0:T(8,128)} broadcast(f32[2560]{0:T(1024)} %param.15), dimensions={1} | broadcast | bytes 92160 | tf_op jit(solution)/shard_map/broadcast_in_dim | solution.py:82
  12.2 3.6 %shard_map.157 = (bf16[8,512]{1,0:T(8,128)(2,1)}, bf16[8,128]{1,0:T(8,128)(2,1)}, bf16[8,128]{1,0:T(8,128)(2,1)}) custom-call(bf16[8,2560]{1,0:T(8,128)(2,1)} %reshape.365.x_ref, f32[8,2560]{1,0:T(8,128)} %broadcast_in_dim.269.g_ref, f32[1,128]{1,0:T(1,128)} %bitcast.220, f32[1,128]{1,0:T(1,128)} %bitcast.221, f32[8,128]{1,0:T(8,128)} %pad_maximum_fusion.3.cos_ref, ...), custom_call_target="tpu_custom_call" | custom-call | flops 31457280 | bytes 3985408 | tf_op jit(solution)/shard_map/pallas_call | solution.py:72
  15.9 0.7 reshape_reshape.9
  17.0 1.1 %collective-permute-done.3 = bf16[12,4,4,128]{3,2,1,0:T(4,128)(2,1)S(1)} collective-permute-done((bf16[12,4,4,128]{3,2,1,0:T(4,128)(2,1)S(1)}, bf16[12,4,4,128]{3,2,1,0:T(4,128)(2,1)S(1)}, u32[]{:S(2)}, u32[]{:S(2)}) %collective-permute-start.3) | collective-permute-done | bytes 49184 | tf_op jit(solution)/shard_map/ppermute | solution.py:164
  18.1 0.2 collective-permute-start.4
  18.3 0.2 fusion.30
  18.5 0.2 select_reduce_fusion.7
  18.7 3.6 %collective-permute-done.4 = bf16[12,4,4,128]{3,2,1,0:T(4,128)(2,1)S(1)} collective-permute-done((bf16[12,4,4,128]{3,2,1,0:T(4,128)(2,1)S(1)}, bf16[12,4,4,128]{3,2,1,0:T(4,128)(2,1)S(1)}, u32[]{:S(2)}, u32[]{:S(2)}) %collective-permute-start.4) | collective-permute-done | bytes 49184 | tf_op jit(solution)/shard_map/ppermute | solution.py:164
  22.3 3.4 %collective-permute-start.5 = (bf16[12,4,4,128]{3,2,1,0:T(4,128)(2,1)S(1)}, bf16[12,4,4,128]{3,2,1,0:T(4,128)(2,1)S(1)}, u32[]{:S(2)}, u32[]{:S(2)}) collective-permute-start(bf16[12,4,4,128]{3,2,1,0:T(4,128)(2,1)S(1)} %add.268), channel_id=1, source_target_pairs={{0,16},{4,20},{8,24},{12,28},{16,0},{20,4},{24,8},{28,12},{32,48},... | collective-permute-start | bytes 147464 | tf_op jit(solution)/shard_map/ppermute | solution.py:164
  25.7 2.0 %collective-permute-done.5 = bf16[12,4,4,128]{3,2,1,0:T(4,128)(2,1)S(1)} collective-permute-done((bf16[12,4,4,128]{3,2,1,0:T(4,128)(2,1)S(1)}, bf16[12,4,4,128]{3,2,1,0:T(4,128)(2,1)S(1)}, u32[]{:S(2)}, u32[]{:S(2)}) %collective-permute-start.5) | collective-permute-done | bytes 49184 | tf_op jit(solution)/shard_map/ppermute | solution.py:164
  27.7 5.2 %collective-permute-start.6 = (bf16[12,4,4,128]{3,2,1,0:T(4,128)(2,1)S(1)}, bf16[12,4,4,128]{3,2,1,0:T(4,128)(2,1)S(1)}, u32[]{:S(2)}, u32[]{:S(2)}) collective-permute-start(bf16[12,4,4,128]{3,2,1,0:T(4,128)(2,1)S(1)} %add.269), channel_id=1, source_target_pairs={{0,48},{4,52},{8,56},{12,60},{16,32},{20,36},{24,40},{28,44},{32,1... | collective-permute-start | bytes 147464 | tf_op jit(solution)/shard_map/ppermute | solution.py:164
  33.1 2.5 %collective-permute-done.6 = bf16[12,4,4,128]{3,2,1,0:T(4,128)(2,1)S(1)} collective-permute-done((bf16[12,4,4,128]{3,2,1,0:T(4,128)(2,1)S(1)}, bf16[12,4,4,128]{3,2,1,0:T(4,128)(2,1)S(1)}, u32[]{:S(2)}, u32[]{:S(2)}) %collective-permute-start.6) | collective-permute-done | bytes 49184 | tf_op jit(solution)/shard_map/ppermute | solution.py:164
  35.6 0.9 collective-permute-start.7
  36.6 3.2 %collective-permute-done.7 = bf16[12,4,4,128]{3,2,1,0:T(4,128)(2,1)S(1)} collective-permute-done((bf16[12,4,4,128]{3,2,1,0:T(4,128)(2,1)S(1)}, bf16[12,4,4,128]{3,2,1,0:T(4,128)(2,1)S(1)}, u32[]{:S(2)}, u32[]{:S(2)}) %collective-permute-start.7) | collective-permute-done | bytes 49184 | tf_op jit(solution)/shard_map/ppermute | solution.py:164
  39.8 0.6 collective-permute-start.8
  40.4 4.8 %collective-permute-done.8 = bf16[12,4,4,128]{3,2,1,0:T(4,128)(2,1)S(1)} collective-permute-done((bf16[12,4,4,128]{3,2,1,0:T(4,128)(2,1)S(1)}, bf16[12,4,4,128]{3,2,1,0:T(4,128)(2,1)S(1)}, u32[]{:S(2)}, u32[]{:S(2)}) %collective-permute-start.8) | collective-permute-done | bytes 49184 | tf_op jit(solution)/shard_map/ppermute | solution.py:164
  45.4 0.6 gather_fusion
  46.0 0.5 select_reduce_fusion.1
  46.8 0.3 bitcast_reduce_fusion
  47.2 0.4 fusion.1
  47.6 0.3 convolution_bitcast_fusion
  48.0 0.2 fusion.74
  48.2 0.2 copy.151
  48.6 0.5 copy.152
  49.7 1.2 %collective-permute-done.9 = bf16[134,192]{1,0:T(8,128)(2,1)S(1)} collective-permute-done((bf16[134,192]{1,0:T(8,128)(2,1)S(1)}, bf16[134,192]{1,0:T(8,128)(2,1)S(1)}, u32[]{:S(2)}, u32[]{:S(2)}) %collective-permute-start.9) | collective-permute-done | bytes 51488 | tf_op jit(solution)/shard_map/ppermute | solution.py:204
  50.9 0.6 collective-permute-start.10
  51.7 3.6 %collective-permute-done.10 = bf16[134,192]{1,0:T(8,128)(2,1)S(1)} collective-permute-done((bf16[134,192]{1,0:T(8,128)(2,1)S(1)}, bf16[134,192]{1,0:T(8,128)(2,1)S(1)}, u32[]{:S(2)}, u32[]{:S(2)}) %collective-permute-start.10) | collective-permute-done | bytes 51488 | tf_op jit(solution)/shard_map/ppermute | solution.py:204
  55.5 1.5 %collective-permute-start.11 = (bf16[134,192]{1,0:T(8,128)(2,1)S(1)}, bf16[134,192]{1,0:T(8,128)(2,1)S(1)}, u32[]{:S(2)}, u32[]{:S(2)}) collective-permute-start(bf16[134,192]{1,0:T(8,128)(2,1)S(1)} %concatenate.77), channel_id=1, source_target_pairs={{0,16},{4,20},{8,24},{12,28},{16,0},{20,4},{24,8},{28,12},{32,48},... | collective-permute-start | bytes 154376 | tf_op jit(solution)/shard_map/ppermute | solution.py:204
  57.1 3.7 %collective-permute-done.11 = bf16[134,192]{1,0:T(8,128)(2,1)S(1)} collective-permute-done((bf16[134,192]{1,0:T(8,128)(2,1)S(1)}, bf16[134,192]{1,0:T(8,128)(2,1)S(1)}, u32[]{:S(2)}, u32[]{:S(2)}) %collective-permute-start.11) | collective-permute-done | bytes 51488 | tf_op jit(solution)/shard_map/ppermute | solution.py:204
  60.9 4.6 %collective-permute-start.12 = (bf16[134,192]{1,0:T(8,128)(2,1)S(1)}, bf16[134,192]{1,0:T(8,128)(2,1)S(1)}, u32[]{:S(2)}, u32[]{:S(2)}) collective-permute-start(bf16[134,192]{1,0:T(8,128)(2,1)S(1)} %concatenate.78), channel_id=1, source_target_pairs={{0,48},{4,52},{8,56},{12,60},{16,32},{20,36},{24,40},{28,44},{32,1... | collective-permute-start | bytes 154376 | tf_op jit(solution)/shard_map/ppermute | solution.py:204
  65.7 2.4 %collective-permute-done.12 = bf16[134,192]{1,0:T(8,128)(2,1)S(1)} collective-permute-done((bf16[134,192]{1,0:T(8,128)(2,1)S(1)}, bf16[134,192]{1,0:T(8,128)(2,1)S(1)}, u32[]{:S(2)}, u32[]{:S(2)}) %collective-permute-start.12) | collective-permute-done | bytes 51488 | tf_op jit(solution)/shard_map/ppermute | solution.py:204
  68.3 0.3 collective-permute-start.13
  68.7 0.3 copy.162
  69.0 3.9 %collective-permute-done.13 = bf16[134,192]{1,0:T(8,128)(2,1)S(1)} collective-permute-done((bf16[134,192]{1,0:T(8,128)(2,1)S(1)}, bf16[134,192]{1,0:T(8,128)(2,1)S(1)}, u32[]{:S(2)}, u32[]{:S(2)}) %collective-permute-start.13) | collective-permute-done | bytes 51488 | tf_op jit(solution)/shard_map/ppermute | solution.py:204
  73.0 0.6 collective-permute-start.14
  73.7 0.4 copy.156
  74.1 4.5 %collective-permute-done.14 = bf16[134,192]{1,0:T(8,128)(2,1)S(1)} collective-permute-done((bf16[134,192]{1,0:T(8,128)(2,1)S(1)}, bf16[134,192]{1,0:T(8,128)(2,1)S(1)}, u32[]{:S(2)}, u32[]{:S(2)}) %collective-permute-start.14) | collective-permute-done | bytes 51488 | tf_op jit(solution)/shard_map/ppermute | solution.py:204
  78.9 0.2 select_reduce_fusion
  79.1 0.4 copy.155
  79.5 0.2 bitcast_select_fusion
  79.8 0.2 fusion.7
  79.9 0.2 copy.165
  80.1 0.6 copy.193
  80.7 2.8 %shard_map.158 = f32[4,8,640]{2,1,0:T(8,128)} custom-call(bf16[8,512]{1,0:T(8,128)(2,1)} %bitcast.187, bf16[512,2560]{1,0:T(8,128)(2,1)} %w_ref.1), custom_call_target="tpu_custom_call" | custom-call | flops 20971520 | bytes 2711552 | tf_op jit(solution)/shard_map/pallas_call | solution.py:121
  83.6 0.8 dynamic-slice_bitcast_fusion.2
  84.3 1.2 %collective-permute-start.15 = (f32[8,640]{1,0:T(8,128)S(1)}, f32[8,640]{1,0:T(8,128)S(1)}, u32[]{:S(2)}, u32[]{:S(2)}) collective-permute-start(f32[8,640]{1,0:T(8,128)S(1)} %get-tuple-element.73), channel_id=1, source_target_pairs={{0,1},{1,2},{2,3},{3,0},{4,5},{5,6},{6,7},{7,4},{8,9},{9,10},{10,1... | collective-permute-start | bytes 61448 | tf_op jit(solution)/shard_map/ppermute | solution.py:152
  85.5 1.8 %collective-permute-start.16 = (f32[8,640]{1,0:T(8,128)S(1)}, f32[8,640]{1,0:T(8,128)S(1)}, u32[]{:S(2)}, u32[]{:S(2)}) collective-permute-start(f32[8,640]{1,0:T(8,128)S(1)} %get-tuple-element.75), channel_id=1, source_target_pairs={{0,2},{1,3},{2,0},{3,1},{4,6},{5,7},{6,4},{7,5},{8,10},{9,11},{10,... | collective-permute-start | bytes 61448 | tf_op jit(solution)/shard_map/ppermute | solution.py:152
  87.4 1.3 %collective-permute-start.17 = (f32[8,640]{1,0:T(8,128)S(1)}, f32[8,640]{1,0:T(8,128)S(1)}, u32[]{:S(2)}, u32[]{:S(2)}) collective-permute-start(f32[8,640]{1,0:T(8,128)S(1)} %get-tuple-element.74), channel_id=1, source_target_pairs={{0,3},{1,0},{2,1},{3,2},{4,7},{5,4},{6,5},{7,6},{8,11},{9,8},{10,9... | collective-permute-start | bytes 61448 | tf_op jit(solution)/shard_map/ppermute | solution.py:152
  88.7 0.7 collective-permute-done.15
  89.3 1.5 %collective-permute-done.16 = f32[8,640]{1,0:T(8,128)S(1)} collective-permute-done((f32[8,640]{1,0:T(8,128)S(1)}, f32[8,640]{1,0:T(8,128)S(1)}, u32[]{:S(2)}, u32[]{:S(2)}) %collective-permute-start.16) | collective-permute-done | bytes 20512 | tf_op jit(solution)/shard_map/ppermute | solution.py:152
  90.8 0.3 collective-permute-done.17
  91.2 0.7 fusion.20
  91.9 0.6 add_convert_fusion
  (108 shorter events, 4.5 us)
Async XLA Ops:
  0.6 45.3 %copy-start = (bf16[16,256,128]{2,1,0:T(8,128)(2,1)S(1)}, bf16[16,256,128]{2,1,0:T(8,128)(2,1)}, u32[]{:S(2)}) copy-start(bf16[16,256,128]{2,1,0:T(8,128)(2,1)} %param.22) | copy-start | bytes 3145732
  0.6 17.8 %copy-start.4 = (s32[128]{0:T(128)S(1)}, s32[128]{0:T(128)}, u32[]{:S(2)}) copy-start(s32[128]{0:T(128)} %param.24) | copy-start | bytes 1540
  0.7 17.6 %copy-start.2 = (s32[16]{0:T(128)S(1)}, s32[16]{0:T(128)}, u32[]{:S(2)}) copy-start(s32[16]{0:T(128)} %param.25) | copy-start | bytes 196
  0.7 18.0 %copy-start.8 = (s32[16]{0:T(128)S(1)}, s32[16]{0:T(128)}, u32[]{:S(2)}) copy-start(s32[16]{0:T(128)} %param.26) | copy-start | bytes 196
  0.7 18.0 %copy-start.5 = (s32[16]{0:T(128)S(1)}, s32[16]{0:T(128)}, u32[]{:S(2)}) copy-start(s32[16]{0:T(128)} %param.27) | copy-start | bytes 196
  0.7 8.1 %collective-permute-start = (bf16[4,2,640]{2,1,0:T(2,128)(2,1)}, bf16[4,2,640]{2,1,0:T(2,128)(2,1)S(1)}, u32[]{:S(2)}, u32[]{:S(2)}) collective-permute-start(bf16[4,2,640]{2,1,0:T(2,128)(2,1)} %param.14), channel_id=1, source_target_pairs={{0,3},{1,0},{2,1},{3,2},{4,7},{5,4},{6,5},{7,6},{8,11},{9,8},{10,9... | collective-permute-start | bytes 30728 | tf_op jit(solution)/shard_map/ppermute | solution.py:135
  3.8 5.4 %collective-permute-start.1 = (bf16[4,2,640]{2,1,0:T(2,128)(2,1)}, bf16[4,2,640]{2,1,0:T(2,128)(2,1)S(1)}, u32[]{:S(2)}, u32[]{:S(2)}) collective-permute-start(bf16[4,2,640]{2,1,0:T(2,128)(2,1)} %param.14), channel_id=1, source_target_pairs={{0,2},{1,3},{2,0},{3,1},{4,6},{5,7},{6,4},{7,5},{8,10},{9,11},{10,... | collective-permute-start | bytes 30728 | tf_op jit(solution)/shard_map/ppermute | solution.py:135
  4.4 5.1 %collective-permute-start.2 = (bf16[4,2,640]{2,1,0:T(2,128)(2,1)}, bf16[4,2,640]{2,1,0:T(2,128)(2,1)S(1)}, u32[]{:S(2)}, u32[]{:S(2)}) collective-permute-start(bf16[4,2,640]{2,1,0:T(2,128)(2,1)} %param.14), channel_id=1, source_target_pairs={{0,1},{1,2},{2,3},{3,0},{4,5},{5,6},{6,7},{7,4},{8,9},{9,10},{10,1... | collective-permute-start | bytes 30728 | tf_op jit(solution)/shard_map/ppermute | solution.py:135
  12.2 34.9 %copy-start.6 = (bf16[16,256,128]{2,1,0:T(8,128)(2,1)S(1)}, bf16[16,256,128]{2,1,0:T(8,128)(2,1)}, u32[]{:S(2)}) copy-start(bf16[16,256,128]{2,1,0:T(8,128)(2,1)} %param.23) | copy-start | bytes 3145732
  16.7 1.3 %collective-permute-start.3 = (bf16[12,4,4,128]{3,2,1,0:T(4,128)(2,1)S(1)}, bf16[12,4,4,128]{3,2,1,0:T(4,128)(2,1)S(1)}, u32[]{:S(2)}, u32[]{:S(2)}) collective-permute-start(bf16[12,4,4,128]{3,2,1,0:T(4,128)(2,1)S(1)} %select_reduce_fusion.4), channel_id=1, source_target_pairs={{0,4},{4,0},{8,12},{12,8},{16,20},{20,16},{24,28},{28,24},{32,36},... | collective-permute-start | bytes 147464 | tf_op jit(solution)/shard_map/ppermute | solution.py:164
  18.1 4.2 %collective-permute-start.4 = (bf16[12,4,4,128]{3,2,1,0:T(4,128)(2,1)S(1)}, bf16[12,4,4,128]{3,2,1,0:T(4,128)(2,1)S(1)}, u32[]{:S(2)}, u32[]{:S(2)}) collective-permute-start(bf16[12,4,4,128]{3,2,1,0:T(4,128)(2,1)S(1)} %add.262), channel_id=1, source_target_pairs={{0,8},{4,12},{8,0},{12,4},{16,24},{20,28},{24,16},{28,20},{32,40},... | collective-permute-start | bytes 147464 | tf_op jit(solution)/shard_map/ppermute | solution.py:164
  22.3 5.4 %collective-permute-start.5 = (bf16[12,4,4,128]{3,2,1,0:T(4,128)(2,1)S(1)}, bf16[12,4,4,128]{3,2,1,0:T(4,128)(2,1)S(1)}, u32[]{:S(2)}, u32[]{:S(2)}) collective-permute-start(bf16[12,4,4,128]{3,2,1,0:T(4,128)(2,1)S(1)} %add.268), channel_id=1, source_target_pairs={{0,16},{4,20},{8,24},{12,28},{16,0},{20,4},{24,8},{28,12},{32,48},... | collective-permute-start | bytes 147464 | tf_op jit(solution)/shard_map/ppermute | solution.py:164
  27.7 7.8 %collective-permute-start.6 = (bf16[12,4,4,128]{3,2,1,0:T(4,128)(2,1)S(1)}, bf16[12,4,4,128]{3,2,1,0:T(4,128)(2,1)S(1)}, u32[]{:S(2)}, u32[]{:S(2)}) collective-permute-start(bf16[12,4,4,128]{3,2,1,0:T(4,128)(2,1)S(1)} %add.269), channel_id=1, source_target_pairs={{0,48},{4,52},{8,56},{12,60},{16,32},{20,36},{24,40},{28,44},{32,1... | collective-permute-start | bytes 147464 | tf_op jit(solution)/shard_map/ppermute | solution.py:164
  35.6 4.2 %collective-permute-start.7 = (bf16[12,4,4,128]{3,2,1,0:T(4,128)(2,1)S(1)}, bf16[12,4,4,128]{3,2,1,0:T(4,128)(2,1)S(1)}, u32[]{:S(2)}, u32[]{:S(2)}) collective-permute-start(bf16[12,4,4,128]{3,2,1,0:T(4,128)(2,1)S(1)} %add.270), channel_id=1, source_target_pairs={{0,64},{4,68},{8,72},{12,76},{16,80},{20,84},{24,88},{28,92},{32,9... | collective-permute-start | bytes 147464 | tf_op jit(solution)/shard_map/ppermute | solution.py:164
  39.8 5.4 %collective-permute-start.8 = (bf16[12,4,4,128]{3,2,1,0:T(4,128)(2,1)S(1)}, bf16[12,4,4,128]{3,2,1,0:T(4,128)(2,1)S(1)}, u32[]{:S(2)}, u32[]{:S(2)}) collective-permute-start(bf16[12,4,4,128]{3,2,1,0:T(4,128)(2,1)S(1)} %add.271), channel_id=1, source_target_pairs={{0,192},{4,196},{8,200},{12,204},{16,208},{20,212},{24,216},{28,22... | collective-permute-start | bytes 147464 | tf_op jit(solution)/shard_map/ppermute | solution.py:164
  47.2 4.4 %copy-start.7 = (bf16[8,128]{1,0:T(8,128)(2,1)S(1)}, bf16[8,128]{1,0:T(8,128)(2,1)}, u32[]{:S(2)}) copy-start(bf16[8,128]{1,0:T(8,128)(2,1)} %get-tuple-element.17) | copy-start | bytes 6148
  47.6 21.0 %copy-start.3 = (bf16[8,128]{1,0:T(8,128)(2,1)S(1)}, bf16[8,128]{1,0:T(8,128)(2,1)}, u32[]{:S(2)}) copy-start(bf16[8,128]{1,0:T(8,128)(2,1)} %get-tuple-element.18) | copy-start | bytes 6148
  49.5 1.3 %collective-permute-start.9 = (bf16[134,192]{1,0:T(8,128)(2,1)S(1)}, bf16[134,192]{1,0:T(8,128)(2,1)S(1)}, u32[]{:S(2)}, u32[]{:S(2)}) collective-permute-start(bf16[134,192]{1,0:T(8,128)(2,1)S(1)} %concatenate.75), channel_id=1, source_target_pairs={{0,4},{4,0},{8,12},{12,8},{16,20},{20,16},{24,28},{28,24},{32,36},... | collective-permute-start | bytes 154376 | tf_op jit(solution)/shard_map/ppermute | solution.py:204
  50.9 4.4 %collective-permute-start.10 = (bf16[134,192]{1,0:T(8,128)(2,1)S(1)}, bf16[134,192]{1,0:T(8,128)(2,1)S(1)}, u32[]{:S(2)}, u32[]{:S(2)}) collective-permute-start(bf16[134,192]{1,0:T(8,128)(2,1)S(1)} %concatenate.76), channel_id=1, source_target_pairs={{0,8},{4,12},{8,0},{12,4},{16,24},{20,28},{24,16},{28,20},{32,40},... | collective-permute-start | bytes 154376 | tf_op jit(solution)/shard_map/ppermute | solution.py:204
  55.5 5.3 %collective-permute-start.11 = (bf16[134,192]{1,0:T(8,128)(2,1)S(1)}, bf16[134,192]{1,0:T(8,128)(2,1)S(1)}, u32[]{:S(2)}, u32[]{:S(2)}) collective-permute-start(bf16[134,192]{1,0:T(8,128)(2,1)S(1)} %concatenate.77), channel_id=1, source_target_pairs={{0,16},{4,20},{8,24},{12,28},{16,0},{20,4},{24,8},{28,12},{32,48},... | collective-permute-start | bytes 154376 | tf_op jit(solution)/shard_map/ppermute | solution.py:204
  60.9 7.3 %collective-permute-start.12 = (bf16[134,192]{1,0:T(8,128)(2,1)S(1)}, bf16[134,192]{1,0:T(8,128)(2,1)S(1)}, u32[]{:S(2)}, u32[]{:S(2)}) collective-permute-start(bf16[134,192]{1,0:T(8,128)(2,1)S(1)} %concatenate.78), channel_id=1, source_target_pairs={{0,48},{4,52},{8,56},{12,60},{16,32},{20,36},{24,40},{28,44},{32,1... | collective-permute-start | bytes 154376 | tf_op jit(solution)/shard_map/ppermute | solution.py:204
  68.3 4.6 %collective-permute-start.13 = (bf16[134,192]{1,0:T(8,128)(2,1)S(1)}, bf16[134,192]{1,0:T(8,128)(2,1)S(1)}, u32[]{:S(2)}, u32[]{:S(2)}) collective-permute-start(bf16[134,192]{1,0:T(8,128)(2,1)S(1)} %concatenate.79), channel_id=1, source_target_pairs={{0,64},{4,68},{8,72},{12,76},{16,80},{20,84},{24,88},{28,92},{32,9... | collective-permute-start | bytes 154376 | tf_op jit(solution)/shard_map/ppermute | solution.py:204
  73.0 5.6 %collective-permute-start.14 = (bf16[134,192]{1,0:T(8,128)(2,1)S(1)}, bf16[134,192]{1,0:T(8,128)(2,1)S(1)}, u32[]{:S(2)}, u32[]{:S(2)}) collective-permute-start(bf16[134,192]{1,0:T(8,128)(2,1)S(1)} %concatenate.80), channel_id=1, source_target_pairs={{0,192},{4,196},{8,200},{12,204},{16,208},{20,212},{24,216},{28,22... | collective-permute-start | bytes 154376 | tf_op jit(solution)/shard_map/ppermute | solution.py:204
  79.7 12.2 %copy-start.1 = (bf16[4,2,640]{2,1,0:T(2,128)(2,1)S(1)}, bf16[4,2,640]{2,1,0:T(2,128)(2,1)}, u32[]{:S(2)}) copy-start(bf16[4,2,640]{2,1,0:T(2,128)(2,1)} %param.14) | copy-start | bytes 30724
  84.3 5.0 %collective-permute-start.15 = (f32[8,640]{1,0:T(8,128)S(1)}, f32[8,640]{1,0:T(8,128)S(1)}, u32[]{:S(2)}, u32[]{:S(2)}) collective-permute-start(f32[8,640]{1,0:T(8,128)S(1)} %get-tuple-element.73), channel_id=1, source_target_pairs={{0,1},{1,2},{2,3},{3,0},{4,5},{5,6},{6,7},{7,4},{8,9},{9,10},{10,1... | collective-permute-start | bytes 61448 | tf_op jit(solution)/shard_map/ppermute | solution.py:152
  85.5 5.3 %collective-permute-start.16 = (f32[8,640]{1,0:T(8,128)S(1)}, f32[8,640]{1,0:T(8,128)S(1)}, u32[]{:S(2)}, u32[]{:S(2)}) collective-permute-start(f32[8,640]{1,0:T(8,128)S(1)} %get-tuple-element.75), channel_id=1, source_target_pairs={{0,2},{1,3},{2,0},{3,1},{4,6},{5,7},{6,4},{7,5},{8,10},{9,11},{10,... | collective-permute-start | bytes 61448 | tf_op jit(solution)/shard_map/ppermute | solution.py:152
  87.4 3.8 %collective-permute-start.17 = (f32[8,640]{1,0:T(8,128)S(1)}, f32[8,640]{1,0:T(8,128)S(1)}, u32[]{:S(2)}, u32[]{:S(2)}) collective-permute-start(f32[8,640]{1,0:T(8,128)S(1)} %get-tuple-element.74), channel_id=1, source_target_pairs={{0,3},{1,0},{2,1},{3,2},{4,7},{5,4},{6,5},{7,6},{8,11},{9,8},{10,9... | collective-permute-start | bytes 61448 | tf_op jit(solution)/shard_map/ppermute | solution.py:152

commit v14 on v13

--- a/solution.py
+++ b/solution.py
@@ -144,9 +144,9 @@
     return jnp.concatenate(ordered, axis=-1)
 
 
-def reduce_scatter_mp(chunks, n_mp):
+def reduce_scatter_mp(chunks, n_mp, start):
     me = lax.axis_index("mp")
-    total = lax.dynamic_index_in_dim(chunks, me, axis=0, keepdims=False)
+    total = lax.dynamic_index_in_dim(chunks, me, axis=0, keepdims=False) + start
     for s in range(1, n_mp):
         outgoing = lax.dynamic_index_in_dim(chunks, (me + s) % n_mp, axis=0, keepdims=False)
         total = total + lax.ppermute(outgoing, "mp", [(i, (i + s) % n_mp) for i in range(n_mp)])
@@ -368,8 +368,9 @@
     attended = (mixture / denominator[..., None]).astype(jnp.bfloat16)
     attended = attended.transpose(1, 0, 2, 3, 4).reshape(steps * own_rows, q_heads * HEAD_SIZE)
     projected = chunked_matmul(attended, w_out, n_mp)
-    summed = reduce_scatter_mp(projected, n_mp).reshape(steps, own_rows, -1)
-    hidden = (states.astype(jnp.float32) + summed).astype(jnp.bfloat16)
+    own_states = states.astype(jnp.float32).reshape(steps * own_rows, -1)
+    summed = reduce_scatter_mp(projected, n_mp, own_states)
+    hidden = summed.astype(jnp.bfloat16).reshape(states.shape)
     return hidden, new_keys, new_values
 
 

time: 92.9 us -> 92.9 us (level)
  no operation moved by 1% of the time
where the time goes in v14:
time: 92.9 us; the launch traced here: 92.5 us
  waiting for transfers between devices  39.7 us (43%)
  starting transfers between devices  27 us (29%)
  local copies, waits for them, and re-layouts  9.41 us (10%)
  other arithmetic  7.25 us (8%)
  Pallas kernels  6.47 us (7%)
  matrix products  1.61 us (2%)
  between operations  1.07 us (1%)
    ppermute x6, waiting for transfers between devices, stats_butterfly(): arrived = lax.ppermute(packed, 'seq', pairs)  19.3 us
    ppermute x6, waiting for transfers between devices, butterfly(): lax.ppermute(value, 'seq', [(i, i ^ stride) for i in range(n_seq)])  17.1 us
    ppermute x6, starting transfers between devices, butterfly(): lax.ppermute(value, 'seq', [(i, i ^ stride) for i in range(n_seq)])  10.4 us
    ppermute x6, starting transfers between devices, stats_butterfly(): arrived = lax.ppermute(packed, 'seq', pairs)  7.65 us
    ppermute x3, starting transfers between devices, gather_mp(): lax.ppermute(block, 'mp', [(i, (i + s) % n_mp) for i in range(n_mp)])  4.69 us
    ppermute x3, starting transfers between devices, reduce_scatter_mp(): lax.ppermute(outgoing, 'mp', [(i, (i + s) % n_mp) for i in range(n_mp)])  4.32 us
    pallas_call x1, Pallas kernels, project_rows(): pl.pallas_call(_project_kernel, out_shape=[jax.ShapeDtypeStruct((m, n), j...  3.64 us
    pallas_call x1, Pallas kernels, chunked_matmul(): pl.pallas_call(_chunked_kernel, out_shape=jax.ShapeDtypeStruct((chunks, m...  2.83 us
  transfers between devices with their start and end apart: 18, of which 17 were waited for; matrix products, arithmetic and copies ran while one was open for 6% of the time, Pallas kernels for 0%

profile of v14, /device:TPU:38, one launch (start us, length us, event | category | flops | bytes accessed | tf_op | source)
XLA Modules:
  0.0 92.5 jit_solution(12032538699320657113)
XLA Ops:
  0.7 3.1 %collective-permute-start = (bf16[4,2,640]{2,1,0:T(2,128)(2,1)}, bf16[4,2,640]{2,1,0:T(2,128)(2,1)S(1)}, u32[]{:S(2)}, u32[]{:S(2)}) collective-permute-start(bf16[4,2,640]{2,1,0:T(2,128)(2,1)} %param.14), channel_id=1, source_target_pairs={{0,3},{1,0},{2,1},{3,2},{4,7},{5,4},{6,5},{7,6},{8,11},{9,8},{10,9... | collective-permute-start | bytes 30728 | tf_op jit(solution)/shard_map/ppermute | solution.py:135
  3.8 0.6 collective-permute-start.1
  4.4 1.0 %collective-permute-start.2 = (bf16[4,2,640]{2,1,0:T(2,128)(2,1)}, bf16[4,2,640]{2,1,0:T(2,128)(2,1)S(1)}, u32[]{:S(2)}, u32[]{:S(2)}) collective-permute-start(bf16[4,2,640]{2,1,0:T(2,128)(2,1)} %param.14), channel_id=1, source_target_pairs={{0,1},{1,2},{2,3},{3,0},{4,5},{5,6},{6,7},{7,4},{8,9},{9,10},{10,1... | collective-permute-start | bytes 30728 | tf_op jit(solution)/shard_map/ppermute | solution.py:135
  5.4 0.7 broadcast_compare_fusion.2
  6.1 0.7 dynamic_slice.24
  7.0 0.7 pad_maximum_fusion.3.cos_ref
  8.1 0.7 pad_maximum_fusion.4.sin_ref
  8.8 0.4 collective-permute-done.1
  9.2 0.3 collective-permute-done.2
  9.5 0.7 broadcast_select_fusion.11
  10.3 0.6 reshape.371.x_ref
  10.9 1.3 %broadcast_in_dim.269.g_ref = f32[8,2560]{1,0:T(8,128)} broadcast(f32[2560]{0:T(1024)} %param.15), dimensions={1} | broadcast | bytes 92160 | tf_op jit(solution)/shard_map/broadcast_in_dim | solution.py:82
  12.2 3.6 %shard_map.157 = (bf16[8,512]{1,0:T(8,128)(2,1)}, bf16[8,128]{1,0:T(8,128)(2,1)}, bf16[8,128]{1,0:T(8,128)(2,1)}) custom-call(bf16[8,2560]{1,0:T(8,128)(2,1)} %reshape.371.x_ref, f32[8,2560]{1,0:T(8,128)} %broadcast_in_dim.269.g_ref, f32[1,128]{1,0:T(1,128)} %bitcast.224, f32[1,128]{1,0:T(1,128)} %bitcast.225, f32[8,128]{1,0:T(8,128)} %pad_maximum_fusion.3.cos_ref, ...), custom_call_target="tpu_custom_call" | custom-call | flops 31457280 | bytes 3985408 | tf_op jit(solution)/shard_map/pallas_call | solution.py:72
  15.9 0.7 reshape_reshape.9
  17.0 1.1 %collective-permute-done.3 = bf16[12,4,4,128]{3,2,1,0:T(4,128)(2,1)S(1)} collective-permute-done((bf16[12,4,4,128]{3,2,1,0:T(4,128)(2,1)S(1)}, bf16[12,4,4,128]{3,2,1,0:T(4,128)(2,1)S(1)}, u32[]{:S(2)}, u32[]{:S(2)}) %collective-permute-start.3) | collective-permute-done | bytes 49184 | tf_op jit(solution)/shard_map/ppermute | solution.py:164
  18.1 0.2 collective-permute-start.4
  18.3 0.2 fusion.32
  18.5 0.2 select_reduce_fusion.7
  18.7 3.6 %collective-permute-done.4 = bf16[12,4,4,128]{3,2,1,0:T(4,128)(2,1)S(1)} collective-permute-done((bf16[12,4,4,128]{3,2,1,0:T(4,128)(2,1)S(1)}, bf16[12,4,4,128]{3,2,1,0:T(4,128)(2,1)S(1)}, u32[]{:S(2)}, u32[]{:S(2)}) %collective-permute-start.4) | collective-permute-done | bytes 49184 | tf_op jit(solution)/shard_map/ppermute | solution.py:164
  22.3 3.4 %collective-permute-start.5 = (bf16[12,4,4,128]{3,2,1,0:T(4,128)(2,1)S(1)}, bf16[12,4,4,128]{3,2,1,0:T(4,128)(2,1)S(1)}, u32[]{:S(2)}, u32[]{:S(2)}) collective-permute-start(bf16[12,4,4,128]{3,2,1,0:T(4,128)(2,1)S(1)} %add.268), channel_id=1, source_target_pairs={{0,16},{4,20},{8,24},{12,28},{16,0},{20,4},{24,8},{28,12},{32,48},... | collective-permute-start | bytes 147464 | tf_op jit(solution)/shard_map/ppermute | solution.py:164
  25.7 2.0 %collective-permute-done.5 = bf16[12,4,4,128]{3,2,1,0:T(4,128)(2,1)S(1)} collective-permute-done((bf16[12,4,4,128]{3,2,1,0:T(4,128)(2,1)S(1)}, bf16[12,4,4,128]{3,2,1,0:T(4,128)(2,1)S(1)}, u32[]{:S(2)}, u32[]{:S(2)}) %collective-permute-start.5) | collective-permute-done | bytes 49184 | tf_op jit(solution)/shard_map/ppermute | solution.py:164
  27.7 5.2 %collective-permute-start.6 = (bf16[12,4,4,128]{3,2,1,0:T(4,128)(2,1)S(1)}, bf16[12,4,4,128]{3,2,1,0:T(4,128)(2,1)S(1)}, u32[]{:S(2)}, u32[]{:S(2)}) collective-permute-start(bf16[12,4,4,128]{3,2,1,0:T(4,128)(2,1)S(1)} %add.269), channel_id=1, source_target_pairs={{0,48},{4,52},{8,56},{12,60},{16,32},{20,36},{24,40},{28,44},{32,1... | collective-permute-start | bytes 147464 | tf_op jit(solution)/shard_map/ppermute | solution.py:164
  33.1 2.5 %collective-permute-done.6 = bf16[12,4,4,128]{3,2,1,0:T(4,128)(2,1)S(1)} collective-permute-done((bf16[12,4,4,128]{3,2,1,0:T(4,128)(2,1)S(1)}, bf16[12,4,4,128]{3,2,1,0:T(4,128)(2,1)S(1)}, u32[]{:S(2)}, u32[]{:S(2)}) %collective-permute-start.6) | collective-permute-done | bytes 49184 | tf_op jit(solution)/shard_map/ppermute | solution.py:164
  35.6 0.9 collective-permute-start.7
  36.6 3.2 %collective-permute-done.7 = bf16[12,4,4,128]{3,2,1,0:T(4,128)(2,1)S(1)} collective-permute-done((bf16[12,4,4,128]{3,2,1,0:T(4,128)(2,1)S(1)}, bf16[12,4,4,128]{3,2,1,0:T(4,128)(2,1)S(1)}, u32[]{:S(2)}, u32[]{:S(2)}) %collective-permute-start.7) | collective-permute-done | bytes 49184 | tf_op jit(solution)/shard_map/ppermute | solution.py:164
  39.8 0.6 collective-permute-start.8
  40.4 4.8 %collective-permute-done.8 = bf16[12,4,4,128]{3,2,1,0:T(4,128)(2,1)S(1)} collective-permute-done((bf16[12,4,4,128]{3,2,1,0:T(4,128)(2,1)S(1)}, bf16[12,4,4,128]{3,2,1,0:T(4,128)(2,1)S(1)}, u32[]{:S(2)}, u32[]{:S(2)}) %collective-permute-start.8) | collective-permute-done | bytes 49184 | tf_op jit(solution)/shard_map/ppermute | solution.py:164
  45.4 0.6 gather_fusion
  46.0 0.5 select_reduce_fusion.1
  46.8 0.3 bitcast_reduce_fusion
  47.2 0.4 fusion.1
  47.6 0.3 convolution_bitcast_fusion
  48.0 0.2 fusion.76
  48.2 0.2 copy.151
  48.6 0.5 copy.152
  49.7 1.2 %collective-permute-done.9 = bf16[134,192]{1,0:T(8,128)(2,1)S(1)} collective-permute-done((bf16[134,192]{1,0:T(8,128)(2,1)S(1)}, bf16[134,192]{1,0:T(8,128)(2,1)S(1)}, u32[]{:S(2)}, u32[]{:S(2)}) %collective-permute-start.9) | collective-permute-done | bytes 51488 | tf_op jit(solution)/shard_map/ppermute | solution.py:204
  50.9 0.6 collective-permute-start.10
  51.7 3.6 %collective-permute-done.10 = bf16[134,192]{1,0:T(8,128)(2,1)S(1)} collective-permute-done((bf16[134,192]{1,0:T(8,128)(2,1)S(1)}, bf16[134,192]{1,0:T(8,128)(2,1)S(1)}, u32[]{:S(2)}, u32[]{:S(2)}) %collective-permute-start.10) | collective-permute-done | bytes 51488 | tf_op jit(solution)/shard_map/ppermute | solution.py:204
  55.5 1.5 %collective-permute-start.11 = (bf16[134,192]{1,0:T(8,128)(2,1)S(1)}, bf16[134,192]{1,0:T(8,128)(2,1)S(1)}, u32[]{:S(2)}, u32[]{:S(2)}) collective-permute-start(bf16[134,192]{1,0:T(8,128)(2,1)S(1)} %concatenate.77), channel_id=1, source_target_pairs={{0,16},{4,20},{8,24},{12,28},{16,0},{20,4},{24,8},{28,12},{32,48},... | collective-permute-start | bytes 154376 | tf_op jit(solution)/shard_map/ppermute | solution.py:204
  57.1 3.7 %collective-permute-done.11 = bf16[134,192]{1,0:T(8,128)(2,1)S(1)} collective-permute-done((bf16[134,192]{1,0:T(8,128)(2,1)S(1)}, bf16[134,192]{1,0:T(8,128)(2,1)S(1)}, u32[]{:S(2)}, u32[]{:S(2)}) %collective-permute-start.11) | collective-permute-done | bytes 51488 | tf_op jit(solution)/shard_map/ppermute | solution.py:204
  60.9 4.6 %collective-permute-start.12 = (bf16[134,192]{1,0:T(8,128)(2,1)S(1)}, bf16[134,192]{1,0:T(8,128)(2,1)S(1)}, u32[]{:S(2)}, u32[]{:S(2)}) collective-permute-start(bf16[134,192]{1,0:T(8,128)(2,1)S(1)} %concatenate.78), channel_id=1, source_target_pairs={{0,48},{4,52},{8,56},{12,60},{16,32},{20,36},{24,40},{28,44},{32,1... | collective-permute-start | bytes 154376 | tf_op jit(solution)/shard_map/ppermute | solution.py:204
  65.7 2.4 %collective-permute-done.12 = bf16[134,192]{1,0:T(8,128)(2,1)S(1)} collective-permute-done((bf16[134,192]{1,0:T(8,128)(2,1)S(1)}, bf16[134,192]{1,0:T(8,128)(2,1)S(1)}, u32[]{:S(2)}, u32[]{:S(2)}) %collective-permute-start.12) | collective-permute-done | bytes 51488 | tf_op jit(solution)/shard_map/ppermute | solution.py:204
  68.3 0.3 collective-permute-start.13
  68.7 0.3 copy.162
  69.0 3.9 %collective-permute-done.13 = bf16[134,192]{1,0:T(8,128)(2,1)S(1)} collective-permute-done((bf16[134,192]{1,0:T(8,128)(2,1)S(1)}, bf16[134,192]{1,0:T(8,128)(2,1)S(1)}, u32[]{:S(2)}, u32[]{:S(2)}) %collective-permute-start.13) | collective-permute-done | bytes 51488 | tf_op jit(solution)/shard_map/ppermute | solution.py:204
  73.0 0.6 collective-permute-start.14
  73.7 0.4 copy.156
  74.1 4.5 %collective-permute-done.14 = bf16[134,192]{1,0:T(8,128)(2,1)S(1)} collective-permute-done((bf16[134,192]{1,0:T(8,128)(2,1)S(1)}, bf16[134,192]{1,0:T(8,128)(2,1)S(1)}, u32[]{:S(2)}, u32[]{:S(2)}) %collective-permute-start.14) | collective-permute-done | bytes 51488 | tf_op jit(solution)/shard_map/ppermute | solution.py:204
  78.9 0.2 select_reduce_fusion
  79.1 0.4 copy.155
  79.5 0.2 bitcast_select_fusion
  79.8 0.2 fusion.7
  79.9 0.2 copy.165
  80.1 0.6 copy.193
  80.7 2.8 %shard_map.158 = f32[4,8,640]{2,1,0:T(8,128)} custom-call(bf16[8,512]{1,0:T(8,128)(2,1)} %bitcast.191, bf16[512,2560]{1,0:T(8,128)(2,1)} %w_ref.1), custom_call_target="tpu_custom_call" | custom-call | flops 20971520 | bytes 2711552 | tf_op jit(solution)/shard_map/pallas_call | solution.py:121
  83.6 0.8 dynamic-slice_bitcast_fusion.2
  84.3 1.2 %collective-permute-start.15 = (f32[8,640]{1,0:T(8,128)S(1)}, f32[8,640]{1,0:T(8,128)S(1)}, u32[]{:S(2)}, u32[]{:S(2)}) collective-permute-start(f32[8,640]{1,0:T(8,128)S(1)} %get-tuple-element.73), channel_id=1, source_target_pairs={{0,1},{1,2},{2,3},{3,0},{4,5},{5,6},{6,7},{7,4},{8,9},{9,10},{10,1... | collective-permute-start | bytes 61448 | tf_op jit(solution)/shard_map/ppermute | solution.py:152
  85.5 1.8 %collective-permute-start.16 = (f32[8,640]{1,0:T(8,128)S(1)}, f32[8,640]{1,0:T(8,128)S(1)}, u32[]{:S(2)}, u32[]{:S(2)}) collective-permute-start(f32[8,640]{1,0:T(8,128)S(1)} %get-tuple-element.75), channel_id=1, source_target_pairs={{0,2},{1,3},{2,0},{3,1},{4,6},{5,7},{6,4},{7,5},{8,10},{9,11},{10,... | collective-permute-start | bytes 61448 | tf_op jit(solution)/shard_map/ppermute | solution.py:152
  87.4 1.3 %collective-permute-start.17 = (f32[8,640]{1,0:T(8,128)S(1)}, f32[8,640]{1,0:T(8,128)S(1)}, u32[]{:S(2)}, u32[]{:S(2)}) collective-permute-start(f32[8,640]{1,0:T(8,128)S(1)} %get-tuple-element.74), channel_id=1, source_target_pairs={{0,3},{1,0},{2,1},{3,2},{4,7},{5,4},{6,5},{7,6},{8,11},{9,8},{10,9... | collective-permute-start | bytes 61448 | tf_op jit(solution)/shard_map/ppermute | solution.py:152
  88.7 0.7 collective-permute-done.15
  89.3 1.5 %collective-permute-done.16 = f32[8,640]{1,0:T(8,128)S(1)} collective-permute-done((f32[8,640]{1,0:T(8,128)S(1)}, f32[8,640]{1,0:T(8,128)S(1)}, u32[]{:S(2)}, u32[]{:S(2)}) %collective-permute-start.16) | collective-permute-done | bytes 20512 | tf_op jit(solution)/shard_map/ppermute | solution.py:152
  90.8 0.3 collective-permute-done.17
  91.2 0.7 fusion.22
  91.9 0.6 reshape.383
  (108 shorter events, 4.5 us)
Async XLA Ops:
  0.6 45.3 %copy-start = (bf16[16,256,128]{2,1,0:T(8,128)(2,1)S(1)}, bf16[16,256,128]{2,1,0:T(8,128)(2,1)}, u32[]{:S(2)}) copy-start(bf16[16,256,128]{2,1,0:T(8,128)(2,1)} %param.22) | copy-start | bytes 3145732
  0.6 17.8 %copy-start.4 = (s32[128]{0:T(128)S(1)}, s32[128]{0:T(128)}, u32[]{:S(2)}) copy-start(s32[128]{0:T(128)} %param.24) | copy-start | bytes 1540
  0.7 17.6 %copy-start.2 = (s32[16]{0:T(128)S(1)}, s32[16]{0:T(128)}, u32[]{:S(2)}) copy-start(s32[16]{0:T(128)} %param.25) | copy-start | bytes 196
  0.7 18.0 %copy-start.8 = (s32[16]{0:T(128)S(1)}, s32[16]{0:T(128)}, u32[]{:S(2)}) copy-start(s32[16]{0:T(128)} %param.26) | copy-start | bytes 196
  0.7 18.0 %copy-start.5 = (s32[16]{0:T(128)S(1)}, s32[16]{0:T(128)}, u32[]{:S(2)}) copy-start(s32[16]{0:T(128)} %param.27) | copy-start | bytes 196
  0.7 8.1 %collective-permute-start = (bf16[4,2,640]{2,1,0:T(2,128)(2,1)}, bf16[4,2,640]{2,1,0:T(2,128)(2,1)S(1)}, u32[]{:S(2)}, u32[]{:S(2)}) collective-permute-start(bf16[4,2,640]{2,1,0:T(2,128)(2,1)} %param.14), channel_id=1, source_target_pairs={{0,3},{1,0},{2,1},{3,2},{4,7},{5,4},{6,5},{7,6},{8,11},{9,8},{10,9... | collective-permute-start | bytes 30728 | tf_op jit(solution)/shard_map/ppermute | solution.py:135
  3.8 5.4 %collective-permute-start.1 = (bf16[4,2,640]{2,1,0:T(2,128)(2,1)}, bf16[4,2,640]{2,1,0:T(2,128)(2,1)S(1)}, u32[]{:S(2)}, u32[]{:S(2)}) collective-permute-start(bf16[4,2,640]{2,1,0:T(2,128)(2,1)} %param.14), channel_id=1, source_target_pairs={{0,2},{1,3},{2,0},{3,1},{4,6},{5,7},{6,4},{7,5},{8,10},{9,11},{10,... | collective-permute-start | bytes 30728 | tf_op jit(solution)/shard_map/ppermute | solution.py:135
  4.4 5.1 %collective-permute-start.2 = (bf16[4,2,640]{2,1,0:T(2,128)(2,1)}, bf16[4,2,640]{2,1,0:T(2,128)(2,1)S(1)}, u32[]{:S(2)}, u32[]{:S(2)}) collective-permute-start(bf16[4,2,640]{2,1,0:T(2,128)(2,1)} %param.14), channel_id=1, source_target_pairs={{0,1},{1,2},{2,3},{3,0},{4,5},{5,6},{6,7},{7,4},{8,9},{9,10},{10,1... | collective-permute-start | bytes 30728 | tf_op jit(solution)/shard_map/ppermute | solution.py:135
  12.2 34.9 %copy-start.6 = (bf16[16,256,128]{2,1,0:T(8,128)(2,1)S(1)}, bf16[16,256,128]{2,1,0:T(8,128)(2,1)}, u32[]{:S(2)}) copy-start(bf16[16,256,128]{2,1,0:T(8,128)(2,1)} %param.23) | copy-start | bytes 3145732
  16.7 1.3 %collective-permute-start.3 = (bf16[12,4,4,128]{3,2,1,0:T(4,128)(2,1)S(1)}, bf16[12,4,4,128]{3,2,1,0:T(4,128)(2,1)S(1)}, u32[]{:S(2)}, u32[]{:S(2)}) collective-permute-start(bf16[12,4,4,128]{3,2,1,0:T(4,128)(2,1)S(1)} %select_reduce_fusion.4), channel_id=1, source_target_pairs={{0,4},{4,0},{8,12},{12,8},{16,20},{20,16},{24,28},{28,24},{32,36},... | collective-permute-start | bytes 147464 | tf_op jit(solution)/shard_map/ppermute | solution.py:164
  18.1 4.2 %collective-permute-start.4 = (bf16[12,4,4,128]{3,2,1,0:T(4,128)(2,1)S(1)}, bf16[12,4,4,128]{3,2,1,0:T(4,128)(2,1)S(1)}, u32[]{:S(2)}, u32[]{:S(2)}) collective-permute-start(bf16[12,4,4,128]{3,2,1,0:T(4,128)(2,1)S(1)} %add.262), channel_id=1, source_target_pairs={{0,8},{4,12},{8,0},{12,4},{16,24},{20,28},{24,16},{28,20},{32,40},... | collective-permute-start | bytes 147464 | tf_op jit(solution)/shard_map/ppermute | solution.py:164
  22.3 5.4 %collective-permute-start.5 = (bf16[12,4,4,128]{3,2,1,0:T(4,128)(2,1)S(1)}, bf16[12,4,4,128]{3,2,1,0:T(4,128)(2,1)S(1)}, u32[]{:S(2)}, u32[]{:S(2)}) collective-permute-start(bf16[12,4,4,128]{3,2,1,0:T(4,128)(2,1)S(1)} %add.268), channel_id=1, source_target_pairs={{0,16},{4,20},{8,24},{12,28},{16,0},{20,4},{24,8},{28,12},{32,48},... | collective-permute-start | bytes 147464 | tf_op jit(solution)/shard_map/ppermute | solution.py:164
  27.7 7.8 %collective-permute-start.6 = (bf16[12,4,4,128]{3,2,1,0:T(4,128)(2,1)S(1)}, bf16[12,4,4,128]{3,2,1,0:T(4,128)(2,1)S(1)}, u32[]{:S(2)}, u32[]{:S(2)}) collective-permute-start(bf16[12,4,4,128]{3,2,1,0:T(4,128)(2,1)S(1)} %add.269), channel_id=1, source_target_pairs={{0,48},{4,52},{8,56},{12,60},{16,32},{20,36},{24,40},{28,44},{32,1... | collective-permute-start | bytes 147464 | tf_op jit(solution)/shard_map/ppermute | solution.py:164
  35.6 4.2 %collective-permute-start.7 = (bf16[12,4,4,128]{3,2,1,0:T(4,128)(2,1)S(1)}, bf16[12,4,4,128]{3,2,1,0:T(4,128)(2,1)S(1)}, u32[]{:S(2)}, u32[]{:S(2)}) collective-permute-start(bf16[12,4,4,128]{3,2,1,0:T(4,128)(2,1)S(1)} %add.270), channel_id=1, source_target_pairs={{0,64},{4,68},{8,72},{12,76},{16,80},{20,84},{24,88},{28,92},{32,9... | collective-permute-start | bytes 147464 | tf_op jit(solution)/shard_map/ppermute | solution.py:164
  39.8 5.4 %collective-permute-start.8 = (bf16[12,4,4,128]{3,2,1,0:T(4,128)(2,1)S(1)}, bf16[12,4,4,128]{3,2,1,0:T(4,128)(2,1)S(1)}, u32[]{:S(2)}, u32[]{:S(2)}) collective-permute-start(bf16[12,4,4,128]{3,2,1,0:T(4,128)(2,1)S(1)} %add.271), channel_id=1, source_target_pairs={{0,192},{4,196},{8,200},{12,204},{16,208},{20,212},{24,216},{28,22... | collective-permute-start | bytes 147464 | tf_op jit(solution)/shard_map/ppermute | solution.py:164
  47.2 4.4 %copy-start.7 = (bf16[8,128]{1,0:T(8,128)(2,1)S(1)}, bf16[8,128]{1,0:T(8,128)(2,1)}, u32[]{:S(2)}) copy-start(bf16[8,128]{1,0:T(8,128)(2,1)} %get-tuple-element.17) | copy-start | bytes 6148
  47.6 21.0 %copy-start.3 = (bf16[8,128]{1,0:T(8,128)(2,1)S(1)}, bf16[8,128]{1,0:T(8,128)(2,1)}, u32[]{:S(2)}) copy-start(bf16[8,128]{1,0:T(8,128)(2,1)} %get-tuple-element.18) | copy-start | bytes 6148
  49.5 1.3 %collective-permute-start.9 = (bf16[134,192]{1,0:T(8,128)(2,1)S(1)}, bf16[134,192]{1,0:T(8,128)(2,1)S(1)}, u32[]{:S(2)}, u32[]{:S(2)}) collective-permute-start(bf16[134,192]{1,0:T(8,128)(2,1)S(1)} %concatenate.75), channel_id=1, source_target_pairs={{0,4},{4,0},{8,12},{12,8},{16,20},{20,16},{24,28},{28,24},{32,36},... | collective-permute-start | bytes 154376 | tf_op jit(solution)/shard_map/ppermute | solution.py:204
  50.9 4.4 %collective-permute-start.10 = (bf16[134,192]{1,0:T(8,128)(2,1)S(1)}, bf16[134,192]{1,0:T(8,128)(2,1)S(1)}, u32[]{:S(2)}, u32[]{:S(2)}) collective-permute-start(bf16[134,192]{1,0:T(8,128)(2,1)S(1)} %concatenate.76), channel_id=1, source_target_pairs={{0,8},{4,12},{8,0},{12,4},{16,24},{20,28},{24,16},{28,20},{32,40},... | collective-permute-start | bytes 154376 | tf_op jit(solution)/shard_map/ppermute | solution.py:204
  55.5 5.3 %collective-permute-start.11 = (bf16[134,192]{1,0:T(8,128)(2,1)S(1)}, bf16[134,192]{1,0:T(8,128)(2,1)S(1)}, u32[]{:S(2)}, u32[]{:S(2)}) collective-permute-start(bf16[134,192]{1,0:T(8,128)(2,1)S(1)} %concatenate.77), channel_id=1, source_target_pairs={{0,16},{4,20},{8,24},{12,28},{16,0},{20,4},{24,8},{28,12},{32,48},... | collective-permute-start | bytes 154376 | tf_op jit(solution)/shard_map/ppermute | solution.py:204
  60.9 7.3 %collective-permute-start.12 = (bf16[134,192]{1,0:T(8,128)(2,1)S(1)}, bf16[134,192]{1,0:T(8,128)(2,1)S(1)}, u32[]{:S(2)}, u32[]{:S(2)}) collective-permute-start(bf16[134,192]{1,0:T(8,128)(2,1)S(1)} %concatenate.78), channel_id=1, source_target_pairs={{0,48},{4,52},{8,56},{12,60},{16,32},{20,36},{24,40},{28,44},{32,1... | collective-permute-start | bytes 154376 | tf_op jit(solution)/shard_map/ppermute | solution.py:204
  68.3 4.6 %collective-permute-start.13 = (bf16[134,192]{1,0:T(8,128)(2,1)S(1)}, bf16[134,192]{1,0:T(8,128)(2,1)S(1)}, u32[]{:S(2)}, u32[]{:S(2)}) collective-permute-start(bf16[134,192]{1,0:T(8,128)(2,1)S(1)} %concatenate.79), channel_id=1, source_target_pairs={{0,64},{4,68},{8,72},{12,76},{16,80},{20,84},{24,88},{28,92},{32,9... | collective-permute-start | bytes 154376 | tf_op jit(solution)/shard_map/ppermute | solution.py:204
  73.0 5.6 %collective-permute-start.14 = (bf16[134,192]{1,0:T(8,128)(2,1)S(1)}, bf16[134,192]{1,0:T(8,128)(2,1)S(1)}, u32[]{:S(2)}, u32[]{:S(2)}) collective-permute-start(bf16[134,192]{1,0:T(8,128)(2,1)S(1)} %concatenate.80), channel_id=1, source_target_pairs={{0,192},{4,196},{8,200},{12,204},{16,208},{20,212},{24,216},{28,22... | collective-permute-start | bytes 154376 | tf_op jit(solution)/shard_map/ppermute | solution.py:204
  79.7 8.9 %copy-start.1 = (bf16[4,2,640]{2,1,0:T(2,128)(2,1)S(1)}, bf16[4,2,640]{2,1,0:T(2,128)(2,1)}, u32[]{:S(2)}) copy-start(bf16[4,2,640]{2,1,0:T(2,128)(2,1)} %param.14) | copy-start | bytes 30724
  84.3 5.0 %collective-permute-start.15 = (f32[8,640]{1,0:T(8,128)S(1)}, f32[8,640]{1,0:T(8,128)S(1)}, u32[]{:S(2)}, u32[]{:S(2)}) collective-permute-start(f32[8,640]{1,0:T(8,128)S(1)} %get-tuple-element.73), channel_id=1, source_target_pairs={{0,1},{1,2},{2,3},{3,0},{4,5},{5,6},{6,7},{7,4},{8,9},{9,10},{10,1... | collective-permute-start | bytes 61448 | tf_op jit(solution)/shard_map/ppermute | solution.py:152
  85.5 5.3 %collective-permute-start.16 = (f32[8,640]{1,0:T(8,128)S(1)}, f32[8,640]{1,0:T(8,128)S(1)}, u32[]{:S(2)}, u32[]{:S(2)}) collective-permute-start(f32[8,640]{1,0:T(8,128)S(1)} %get-tuple-element.75), channel_id=1, source_target_pairs={{0,2},{1,3},{2,0},{3,1},{4,6},{5,7},{6,4},{7,5},{8,10},{9,11},{10,... | collective-permute-start | bytes 61448 | tf_op jit(solution)/shard_map/ppermute | solution.py:152
  87.4 3.8 %collective-permute-start.17 = (f32[8,640]{1,0:T(8,128)S(1)}, f32[8,640]{1,0:T(8,128)S(1)}, u32[]{:S(2)}, u32[]{:S(2)}) collective-permute-start(f32[8,640]{1,0:T(8,128)S(1)} %get-tuple-element.74), channel_id=1, source_target_pairs={{0,3},{1,0},{2,1},{3,2},{4,7},{5,4},{6,5},{7,6},{8,11},{9,8},{10,9... | collective-permute-start | bytes 61448 | tf_op jit(solution)/shard_map/ppermute | solution.py:152

commit v15 on v14

--- a/solution.py
+++ b/solution.py
@@ -110,9 +110,18 @@
 
 def _chunked_kernel(x_ref, w_ref, o_ref):
     chunks, _, width = o_ref.shape
+    me = lax.axis_index("mp")
     x = x_ref[...]
-    for c in range(chunks):
-        o_ref[c] = jnp.dot(x, w_ref[:, c * width : (c + 1) * width], preferred_element_type=jnp.float32)
+    products = [
+        jnp.dot(x, w_ref[:, c * width : (c + 1) * width], preferred_element_type=jnp.float32)
+        for c in range(chunks)
+    ]
+    for s in range(chunks):
+        index = (me + s) % chunks
+        chosen = products[0]
+        for c in range(1, chunks):
+            chosen = jnp.where(index == c, products[c], chosen)
+        o_ref[s] = chosen
 
 
 def chunked_matmul(x, w, chunks):
@@ -145,11 +154,9 @@
 
 
 def reduce_scatter_mp(chunks, n_mp, start):
-    me = lax.axis_index("mp")
-    total = lax.dynamic_index_in_dim(chunks, me, axis=0, keepdims=False) + start
+    total = chunks[0] + start
     for s in range(1, n_mp):
-        outgoing = lax.dynamic_index_in_dim(chunks, (me + s) % n_mp, axis=0, keepdims=False)
-        total = total + lax.ppermute(outgoing, "mp", [(i, (i + s) % n_mp) for i in range(n_mp)])
+        total = total + lax.ppermute(chunks[s], "mp", [(i, (i + s) % n_mp) for i in range(n_mp)])
     return total
 
 

time: 92.9 us -> 92.4 us (level)
  transfers between devices with their start and end apart: 18 -> 18, of which waited for: 17 -> 17; matrix products, arithmetic and copies ran while one was open for 6% -> 5% of each run, Pallas kernels for 0% -> 0%
where the time goes in v15:
time: 92.4 us; the launch traced here: 91.9 us
  waiting for transfers between devices  39.6 us (43%)
  starting transfers between devices  27 us (29%)
  local copies, waits for them, and re-layouts  9.43 us (10%)
  other arithmetic  6.58 us (7%)
  Pallas kernels  6.48 us (7%)
  matrix products  1.59 us (2%)
  between operations  1.08 us (1%)
    ppermute x6, waiting for transfers between devices, stats_butterfly(): arrived = lax.ppermute(packed, 'seq', pairs)  19.3 us
    ppermute x6, waiting for transfers between devices, butterfly(): lax.ppermute(value, 'seq', [(i, i ^ stride) for i in range(n_seq)])  17.1 us
    ppermute x6, starting transfers between devices, butterfly(): lax.ppermute(value, 'seq', [(i, i ^ stride) for i in range(n_seq)])  10.4 us
    ppermute x6, starting transfers between devices, stats_butterfly(): arrived = lax.ppermute(packed, 'seq', pairs)  7.66 us
    ppermute x3, starting transfers between devices, gather_mp(): lax.ppermute(block, 'mp', [(i, (i + s) % n_mp) for i in range(n_mp)])  4.69 us
    ppermute x3, starting transfers between devices, reduce_scatter_mp(): lax.ppermute(chunks[s], 'mp', [(i, (i + s) % n_mp) for i in range(n_mp)])  4.32 us
    pallas_call x1, Pallas kernels, project_rows(): pl.pallas_call(_project_kernel, out_shape=[jax.ShapeDtypeStruct((m, n), j...  3.64 us
    pallas_call x1, Pallas kernels, chunked_matmul(): pl.pallas_call(_chunked_kernel, out_shape=jax.ShapeDtypeStruct((chunks, m...  2.85 us
  transfers between devices with their start and end apart: 18, of which 17 were waited for; matrix products, arithmetic and copies ran while one was open for 5% of the time, Pallas kernels for 0%

profile of v15, /device:TPU:38, one launch (start us, length us, event | category | flops | bytes accessed | tf_op | source)
XLA Modules:
  0.0 91.9 jit_solution(14490166372563255848)
XLA Ops:
  0.7 3.1 %collective-permute-start = (bf16[4,2,640]{2,1,0:T(2,128)(2,1)}, bf16[4,2,640]{2,1,0:T(2,128)(2,1)S(1)}, u32[]{:S(2)}, u32[]{:S(2)}) collective-permute-start(bf16[4,2,640]{2,1,0:T(2,128)(2,1)} %param.14), channel_id=1, source_target_pairs={{0,3},{1,0},{2,1},{3,2},{4,7},{5,4},{6,5},{7,6},{8,11},{9,8},{10,9... | collective-permute-start | bytes 30728 | tf_op jit(solution)/shard_map/ppermute | solution.py:144
  3.8 0.6 collective-permute-start.1
  4.4 1.0 %collective-permute-start.2 = (bf16[4,2,640]{2,1,0:T(2,128)(2,1)}, bf16[4,2,640]{2,1,0:T(2,128)(2,1)S(1)}, u32[]{:S(2)}, u32[]{:S(2)}) collective-permute-start(bf16[4,2,640]{2,1,0:T(2,128)(2,1)} %param.14), channel_id=1, source_target_pairs={{0,1},{1,2},{2,3},{3,0},{4,5},{5,6},{6,7},{7,4},{8,9},{9,10},{10,1... | collective-permute-start | bytes 30728 | tf_op jit(solution)/shard_map/ppermute | solution.py:144
  5.4 0.7 broadcast_compare_fusion.2
  6.1 0.7 dynamic_slice.11
  7.5 0.7 pad_maximum_fusion.3
  8.1 1.0 %collective-permute-done.1 = bf16[4,2,640]{2,1,0:T(2,128)(2,1)S(1)} collective-permute-done((bf16[4,2,640]{2,1,0:T(2,128)(2,1)}, bf16[4,2,640]{2,1,0:T(2,128)(2,1)S(1)}, u32[]{:S(2)}, u32[]{:S(2)}) %collective-permute-start.1) | collective-permute-done | bytes 10272 | tf_op jit(solution)/shard_map/ppermute | solution.py:144
  9.2 0.3 collective-permute-done.2
  9.5 0.7 broadcast_select_fusion.11
  10.3 0.6 reshape.371.x_ref
  10.9 1.3 %broadcast_in_dim.269.g_ref = f32[8,2560]{1,0:T(8,128)} broadcast(f32[2560]{0:T(1024)} %param.15), dimensions={1} | broadcast | bytes 92160 | tf_op jit(solution)/shard_map/broadcast_in_dim | solution.py:82
  12.3 3.6 %shard_map.157 = (bf16[8,512]{1,0:T(8,128)(2,1)}, bf16[8,128]{1,0:T(8,128)(2,1)}, bf16[8,128]{1,0:T(8,128)(2,1)}) custom-call(bf16[8,2560]{1,0:T(8,128)(2,1)} %reshape.371.x_ref, f32[8,2560]{1,0:T(8,128)} %broadcast_in_dim.269.g_ref, f32[1,128]{1,0:T(1,128)} %bitcast.226, f32[1,128]{1,0:T(1,128)} %bitcast.227, f32[8,128]{1,0:T(8,128)} %get-tuple-element.141.cos_ref, ...), custom_call_target="tpu_custom_call" | custom-call | flops 31457280 | bytes 3985408 | tf_op jit(solution)/shard_map/pallas_call | solution.py:72
  15.9 0.7 reshape_reshape.9
  17.0 1.1 %collective-permute-done.3 = bf16[12,4,4,128]{3,2,1,0:T(4,128)(2,1)S(1)} collective-permute-done((bf16[12,4,4,128]{3,2,1,0:T(4,128)(2,1)S(1)}, bf16[12,4,4,128]{3,2,1,0:T(4,128)(2,1)S(1)}, u32[]{:S(2)}, u32[]{:S(2)}) %collective-permute-start.3) | collective-permute-done | bytes 49184 | tf_op jit(solution)/shard_map/ppermute | solution.py:171
  18.1 0.2 collective-permute-start.4
  18.3 0.2 select_reduce_fusion.7
  18.7 3.6 %collective-permute-done.4 = bf16[12,4,4,128]{3,2,1,0:T(4,128)(2,1)S(1)} collective-permute-done((bf16[12,4,4,128]{3,2,1,0:T(4,128)(2,1)S(1)}, bf16[12,4,4,128]{3,2,1,0:T(4,128)(2,1)S(1)}, u32[]{:S(2)}, u32[]{:S(2)}) %collective-permute-start.4) | collective-permute-done | bytes 49184 | tf_op jit(solution)/shard_map/ppermute | solution.py:171
  22.3 3.4 %collective-permute-start.5 = (bf16[12,4,4,128]{3,2,1,0:T(4,128)(2,1)S(1)}, bf16[12,4,4,128]{3,2,1,0:T(4,128)(2,1)S(1)}, u32[]{:S(2)}, u32[]{:S(2)}) collective-permute-start(bf16[12,4,4,128]{3,2,1,0:T(4,128)(2,1)S(1)} %add.237), channel_id=1, source_target_pairs={{0,16},{4,20},{8,24},{12,28},{16,0},{20,4},{24,8},{28,12},{32,48},... | collective-permute-start | bytes 147464 | tf_op jit(solution)/shard_map/ppermute | solution.py:171
  25.7 2.0 %collective-permute-done.5 = bf16[12,4,4,128]{3,2,1,0:T(4,128)(2,1)S(1)} collective-permute-done((bf16[12,4,4,128]{3,2,1,0:T(4,128)(2,1)S(1)}, bf16[12,4,4,128]{3,2,1,0:T(4,128)(2,1)S(1)}, u32[]{:S(2)}, u32[]{:S(2)}) %collective-permute-start.5) | collective-permute-done | bytes 49184 | tf_op jit(solution)/shard_map/ppermute | solution.py:171
  27.8 5.2 %collective-permute-start.6 = (bf16[12,4,4,128]{3,2,1,0:T(4,128)(2,1)S(1)}, bf16[12,4,4,128]{3,2,1,0:T(4,128)(2,1)S(1)}, u32[]{:S(2)}, u32[]{:S(2)}) collective-permute-start(bf16[12,4,4,128]{3,2,1,0:T(4,128)(2,1)S(1)} %add.238), channel_id=1, source_target_pairs={{0,48},{4,52},{8,56},{12,60},{16,32},{20,36},{24,40},{28,44},{32,1... | collective-permute-start | bytes 147464 | tf_op jit(solution)/shard_map/ppermute | solution.py:171
  33.0 0.2 fusion.33
  33.2 2.4 %collective-permute-done.6 = bf16[12,4,4,128]{3,2,1,0:T(4,128)(2,1)S(1)} collective-permute-done((bf16[12,4,4,128]{3,2,1,0:T(4,128)(2,1)S(1)}, bf16[12,4,4,128]{3,2,1,0:T(4,128)(2,1)S(1)}, u32[]{:S(2)}, u32[]{:S(2)}) %collective-permute-start.6) | collective-permute-done | bytes 49184 | tf_op jit(solution)/shard_map/ppermute | solution.py:171
  35.6 0.9 collective-permute-start.7
  36.6 3.2 %collective-permute-done.7 = bf16[12,4,4,128]{3,2,1,0:T(4,128)(2,1)S(1)} collective-permute-done((bf16[12,4,4,128]{3,2,1,0:T(4,128)(2,1)S(1)}, bf16[12,4,4,128]{3,2,1,0:T(4,128)(2,1)S(1)}, u32[]{:S(2)}, u32[]{:S(2)}) %collective-permute-start.7) | collective-permute-done | bytes 49184 | tf_op jit(solution)/shard_map/ppermute | solution.py:171
  39.8 0.6 collective-permute-start.8
  40.4 4.8 %collective-permute-done.8 = bf16[12,4,4,128]{3,2,1,0:T(4,128)(2,1)S(1)} collective-permute-done((bf16[12,4,4,128]{3,2,1,0:T(4,128)(2,1)S(1)}, bf16[12,4,4,128]{3,2,1,0:T(4,128)(2,1)S(1)}, u32[]{:S(2)}, u32[]{:S(2)}) %collective-permute-start.8) | collective-permute-done | bytes 49184 | tf_op jit(solution)/shard_map/ppermute | solution.py:171
  45.4 0.6 gather_fusion
  46.0 0.5 select_reduce_fusion.1
  46.9 0.3 bitcast_reduce_fusion
  47.2 0.3 fusion.1
  47.6 0.3 convolution_bitcast_fusion
  48.0 0.2 fusion.77
  48.2 0.2 copy.151
  48.4 0.2 select_reduce_fusion.3
  48.6 0.5 copy.152
  49.7 1.2 %collective-permute-done.9 = bf16[134,192]{1,0:T(8,128)(2,1)S(1)} collective-permute-done((bf16[134,192]{1,0:T(8,128)(2,1)S(1)}, bf16[134,192]{1,0:T(8,128)(2,1)S(1)}, u32[]{:S(2)}, u32[]{:S(2)}) %collective-permute-start.9) | collective-permute-done | bytes 51488 | tf_op jit(solution)/shard_map/ppermute | solution.py:211
  50.9 0.6 collective-permute-start.10
  51.7 3.6 %collective-permute-done.10 = bf16[134,192]{1,0:T(8,128)(2,1)S(1)} collective-permute-done((bf16[134,192]{1,0:T(8,128)(2,1)S(1)}, bf16[134,192]{1,0:T(8,128)(2,1)S(1)}, u32[]{:S(2)}, u32[]{:S(2)}) %collective-permute-start.10) | collective-permute-done | bytes 51488 | tf_op jit(solution)/shard_map/ppermute | solution.py:211
  55.5 1.5 %collective-permute-start.11 = (bf16[134,192]{1,0:T(8,128)(2,1)S(1)}, bf16[134,192]{1,0:T(8,128)(2,1)S(1)}, u32[]{:S(2)}, u32[]{:S(2)}) collective-permute-start(bf16[134,192]{1,0:T(8,128)(2,1)S(1)} %concatenate.77), channel_id=1, source_target_pairs={{0,16},{4,20},{8,24},{12,28},{16,0},{20,4},{24,8},{28,12},{32,48},... | collective-permute-start | bytes 154376 | tf_op jit(solution)/shard_map/ppermute | solution.py:211
  57.1 3.7 %collective-permute-done.11 = bf16[134,192]{1,0:T(8,128)(2,1)S(1)} collective-permute-done((bf16[134,192]{1,0:T(8,128)(2,1)S(1)}, bf16[134,192]{1,0:T(8,128)(2,1)S(1)}, u32[]{:S(2)}, u32[]{:S(2)}) %collective-permute-start.11) | collective-permute-done | bytes 51488 | tf_op jit(solution)/shard_map/ppermute | solution.py:211
  60.9 4.6 %collective-permute-start.12 = (bf16[134,192]{1,0:T(8,128)(2,1)S(1)}, bf16[134,192]{1,0:T(8,128)(2,1)S(1)}, u32[]{:S(2)}, u32[]{:S(2)}) collective-permute-start(bf16[134,192]{1,0:T(8,128)(2,1)S(1)} %concatenate.78), channel_id=1, source_target_pairs={{0,48},{4,52},{8,56},{12,60},{16,32},{20,36},{24,40},{28,44},{32,1... | collective-permute-start | bytes 154376 | tf_op jit(solution)/shard_map/ppermute | solution.py:211
  65.7 2.4 %collective-permute-done.12 = bf16[134,192]{1,0:T(8,128)(2,1)S(1)} collective-permute-done((bf16[134,192]{1,0:T(8,128)(2,1)S(1)}, bf16[134,192]{1,0:T(8,128)(2,1)S(1)}, u32[]{:S(2)}, u32[]{:S(2)}) %collective-permute-start.12) | collective-permute-done | bytes 51488 | tf_op jit(solution)/shard_map/ppermute | solution.py:211
  68.3 0.3 collective-permute-start.13
  68.7 0.3 copy.162
  69.0 3.9 %collective-permute-done.13 = bf16[134,192]{1,0:T(8,128)(2,1)S(1)} collective-permute-done((bf16[134,192]{1,0:T(8,128)(2,1)S(1)}, bf16[134,192]{1,0:T(8,128)(2,1)S(1)}, u32[]{:S(2)}, u32[]{:S(2)}) %collective-permute-start.13) | collective-permute-done | bytes 51488 | tf_op jit(solution)/shard_map/ppermute | solution.py:211
  73.0 0.6 collective-permute-start.14
  73.7 0.4 copy.156
  74.1 4.5 %collective-permute-done.14 = bf16[134,192]{1,0:T(8,128)(2,1)S(1)} collective-permute-done((bf16[134,192]{1,0:T(8,128)(2,1)S(1)}, bf16[134,192]{1,0:T(8,128)(2,1)S(1)}, u32[]{:S(2)}, u32[]{:S(2)}) %collective-permute-start.14) | collective-permute-done | bytes 51488 | tf_op jit(solution)/shard_map/ppermute | solution.py:211
  78.9 0.2 select_reduce_fusion
  79.1 0.4 copy.155
  79.5 0.2 bitcast_select_fusion
  79.8 0.2 fusion.7
  79.9 0.2 copy.165
  80.1 0.6 copy.193
  80.7 2.8 %shard_map.158 = f32[4,8,640]{2,1,0:T(8,128)} custom-call(bf16[8,512]{1,0:T(8,128)(2,1)} %bitcast.193, bf16[512,2560]{1,0:T(8,128)(2,1)} %w_ref.1), custom_call_target="tpu_custom_call" | custom-call | flops 20971520 | bytes 2711552 | tf_op jit(solution)/shard_map/pallas_call | solution.py:130
  83.6 0.8 slice_bitcast_fusion.2
  84.3 0.5 collective-permute-start.15
  84.9 1.8 %collective-permute-start.16 = (f32[8,640]{1,0:T(8,128)S(1)}, f32[8,640]{1,0:T(8,128)S(1)}, u32[]{:S(2)}, u32[]{:S(2)}) collective-permute-start(f32[8,640]{1,0:T(8,128)S(1)} %get-tuple-element.75), channel_id=1, source_target_pairs={{0,2},{1,3},{2,0},{3,1},{4,6},{5,7},{6,4},{7,5},{8,10},{9,11},{10,... | collective-permute-start | bytes 61448 | tf_op jit(solution)/shard_map/ppermute | solution.py:159
  86.7 2.0 %collective-permute-start.17 = (f32[8,640]{1,0:T(8,128)S(1)}, f32[8,640]{1,0:T(8,128)S(1)}, u32[]{:S(2)}, u32[]{:S(2)}) collective-permute-start(f32[8,640]{1,0:T(8,128)S(1)} %get-tuple-element.74), channel_id=1, source_target_pairs={{0,3},{1,0},{2,1},{3,2},{4,7},{5,4},{6,5},{7,6},{8,11},{9,8},{10,9... | collective-permute-start | bytes 61448 | tf_op jit(solution)/shard_map/ppermute | solution.py:159
  88.7 0.7 collective-permute-done.15
  89.3 0.8 collective-permute-done.16
  90.2 0.3 collective-permute-done.17
  90.5 0.7 fusion.23
  91.2 0.6 reshape.383
  (108 shorter events, 4.3 us)
Async XLA Ops:
  0.6 45.4 %copy-start = (bf16[16,256,128]{2,1,0:T(8,128)(2,1)S(1)}, bf16[16,256,128]{2,1,0:T(8,128)(2,1)}, u32[]{:S(2)}) copy-start(bf16[16,256,128]{2,1,0:T(8,128)(2,1)} %param.22) | copy-start | bytes 3145732
  0.6 17.7 %copy-start.4 = (s32[128]{0:T(128)S(1)}, s32[128]{0:T(128)}, u32[]{:S(2)}) copy-start(s32[128]{0:T(128)} %param.24) | copy-start | bytes 1540
  0.7 17.7 %copy-start.2 = (s32[16]{0:T(128)S(1)}, s32[16]{0:T(128)}, u32[]{:S(2)}) copy-start(s32[16]{0:T(128)} %param.25) | copy-start | bytes 196
  0.7 17.6 %copy-start.8 = (s32[16]{0:T(128)S(1)}, s32[16]{0:T(128)}, u32[]{:S(2)}) copy-start(s32[16]{0:T(128)} %param.26) | copy-start | bytes 196
  0.7 17.6 %copy-start.7 = (s32[16]{0:T(128)S(1)}, s32[16]{0:T(128)}, u32[]{:S(2)}) copy-start(s32[16]{0:T(128)} %param.27) | copy-start | bytes 196
  0.7 7.4 %collective-permute-start = (bf16[4,2,640]{2,1,0:T(2,128)(2,1)}, bf16[4,2,640]{2,1,0:T(2,128)(2,1)S(1)}, u32[]{:S(2)}, u32[]{:S(2)}) collective-permute-start(bf16[4,2,640]{2,1,0:T(2,128)(2,1)} %param.14), channel_id=1, source_target_pairs={{0,3},{1,0},{2,1},{3,2},{4,7},{5,4},{6,5},{7,6},{8,11},{9,8},{10,9... | collective-permute-start | bytes 30728 | tf_op jit(solution)/shard_map/ppermute | solution.py:144
  3.8 5.4 %collective-permute-start.1 = (bf16[4,2,640]{2,1,0:T(2,128)(2,1)}, bf16[4,2,640]{2,1,0:T(2,128)(2,1)S(1)}, u32[]{:S(2)}, u32[]{:S(2)}) collective-permute-start(bf16[4,2,640]{2,1,0:T(2,128)(2,1)} %param.14), channel_id=1, source_target_pairs={{0,2},{1,3},{2,0},{3,1},{4,6},{5,7},{6,4},{7,5},{8,10},{9,11},{10,... | collective-permute-start | bytes 30728 | tf_op jit(solution)/shard_map/ppermute | solution.py:144
  4.4 5.1 %collective-permute-start.2 = (bf16[4,2,640]{2,1,0:T(2,128)(2,1)}, bf16[4,2,640]{2,1,0:T(2,128)(2,1)S(1)}, u32[]{:S(2)}, u32[]{:S(2)}) collective-permute-start(bf16[4,2,640]{2,1,0:T(2,128)(2,1)} %param.14), channel_id=1, source_target_pairs={{0,1},{1,2},{2,3},{3,0},{4,5},{5,6},{6,7},{7,4},{8,9},{9,10},{10,1... | collective-permute-start | bytes 30728 | tf_op jit(solution)/shard_map/ppermute | solution.py:144
  12.3 34.9 %copy-start.5 = (bf16[16,256,128]{2,1,0:T(8,128)(2,1)S(1)}, bf16[16,256,128]{2,1,0:T(8,128)(2,1)}, u32[]{:S(2)}) copy-start(bf16[16,256,128]{2,1,0:T(8,128)(2,1)} %param.23) | copy-start | bytes 3145732
  16.7 1.3 %collective-permute-start.3 = (bf16[12,4,4,128]{3,2,1,0:T(4,128)(2,1)S(1)}, bf16[12,4,4,128]{3,2,1,0:T(4,128)(2,1)S(1)}, u32[]{:S(2)}, u32[]{:S(2)}) collective-permute-start(bf16[12,4,4,128]{3,2,1,0:T(4,128)(2,1)S(1)} %select_reduce_fusion.4), channel_id=1, source_target_pairs={{0,4},{4,0},{8,12},{12,8},{16,20},{20,16},{24,28},{28,24},{32,36},... | collective-permute-start | bytes 147464 | tf_op jit(solution)/shard_map/ppermute | solution.py:171
  18.1 4.2 %collective-permute-start.4 = (bf16[12,4,4,128]{3,2,1,0:T(4,128)(2,1)S(1)}, bf16[12,4,4,128]{3,2,1,0:T(4,128)(2,1)S(1)}, u32[]{:S(2)}, u32[]{:S(2)}) collective-permute-start(bf16[12,4,4,128]{3,2,1,0:T(4,128)(2,1)S(1)} %add.231), channel_id=1, source_target_pairs={{0,8},{4,12},{8,0},{12,4},{16,24},{20,28},{24,16},{28,20},{32,40},... | collective-permute-start | bytes 147464 | tf_op jit(solution)/shard_map/ppermute | solution.py:171
  22.3 5.4 %collective-permute-start.5 = (bf16[12,4,4,128]{3,2,1,0:T(4,128)(2,1)S(1)}, bf16[12,4,4,128]{3,2,1,0:T(4,128)(2,1)S(1)}, u32[]{:S(2)}, u32[]{:S(2)}) collective-permute-start(bf16[12,4,4,128]{3,2,1,0:T(4,128)(2,1)S(1)} %add.237), channel_id=1, source_target_pairs={{0,16},{4,20},{8,24},{12,28},{16,0},{20,4},{24,8},{28,12},{32,48},... | collective-permute-start | bytes 147464 | tf_op jit(solution)/shard_map/ppermute | solution.py:171
  27.8 7.8 %collective-permute-start.6 = (bf16[12,4,4,128]{3,2,1,0:T(4,128)(2,1)S(1)}, bf16[12,4,4,128]{3,2,1,0:T(4,128)(2,1)S(1)}, u32[]{:S(2)}, u32[]{:S(2)}) collective-permute-start(bf16[12,4,4,128]{3,2,1,0:T(4,128)(2,1)S(1)} %add.238), channel_id=1, source_target_pairs={{0,48},{4,52},{8,56},{12,60},{16,32},{20,36},{24,40},{28,44},{32,1... | collective-permute-start | bytes 147464 | tf_op jit(solution)/shard_map/ppermute | solution.py:171
  35.6 4.2 %collective-permute-start.7 = (bf16[12,4,4,128]{3,2,1,0:T(4,128)(2,1)S(1)}, bf16[12,4,4,128]{3,2,1,0:T(4,128)(2,1)S(1)}, u32[]{:S(2)}, u32[]{:S(2)}) collective-permute-start(bf16[12,4,4,128]{3,2,1,0:T(4,128)(2,1)S(1)} %add.239), channel_id=1, source_target_pairs={{0,64},{4,68},{8,72},{12,76},{16,80},{20,84},{24,88},{28,92},{32,9... | collective-permute-start | bytes 147464 | tf_op jit(solution)/shard_map/ppermute | solution.py:171
  39.8 5.4 %collective-permute-start.8 = (bf16[12,4,4,128]{3,2,1,0:T(4,128)(2,1)S(1)}, bf16[12,4,4,128]{3,2,1,0:T(4,128)(2,1)S(1)}, u32[]{:S(2)}, u32[]{:S(2)}) collective-permute-start(bf16[12,4,4,128]{3,2,1,0:T(4,128)(2,1)S(1)} %add.240), channel_id=1, source_target_pairs={{0,192},{4,196},{8,200},{12,204},{16,208},{20,212},{24,216},{28,22... | collective-permute-start | bytes 147464 | tf_op jit(solution)/shard_map/ppermute | solution.py:171
  47.2 4.4 %copy-start.6 = (bf16[8,128]{1,0:T(8,128)(2,1)S(1)}, bf16[8,128]{1,0:T(8,128)(2,1)}, u32[]{:S(2)}) copy-start(bf16[8,128]{1,0:T(8,128)(2,1)} %get-tuple-element.17) | copy-start | bytes 6148
  47.6 21.0 %copy-start.3 = (bf16[8,128]{1,0:T(8,128)(2,1)S(1)}, bf16[8,128]{1,0:T(8,128)(2,1)}, u32[]{:S(2)}) copy-start(bf16[8,128]{1,0:T(8,128)(2,1)} %get-tuple-element.18) | copy-start | bytes 6148
  49.5 1.3 %collective-permute-start.9 = (bf16[134,192]{1,0:T(8,128)(2,1)S(1)}, bf16[134,192]{1,0:T(8,128)(2,1)S(1)}, u32[]{:S(2)}, u32[]{:S(2)}) collective-permute-start(bf16[134,192]{1,0:T(8,128)(2,1)S(1)} %concatenate.75), channel_id=1, source_target_pairs={{0,4},{4,0},{8,12},{12,8},{16,20},{20,16},{24,28},{28,24},{32,36},... | collective-permute-start | bytes 154376 | tf_op jit(solution)/shard_map/ppermute | solution.py:211
  50.9 4.4 %collective-permute-start.10 = (bf16[134,192]{1,0:T(8,128)(2,1)S(1)}, bf16[134,192]{1,0:T(8,128)(2,1)S(1)}, u32[]{:S(2)}, u32[]{:S(2)}) collective-permute-start(bf16[134,192]{1,0:T(8,128)(2,1)S(1)} %concatenate.76), channel_id=1, source_target_pairs={{0,8},{4,12},{8,0},{12,4},{16,24},{20,28},{24,16},{28,20},{32,40},... | collective-permute-start | bytes 154376 | tf_op jit(solution)/shard_map/ppermute | solution.py:211
  55.5 5.3 %collective-permute-start.11 = (bf16[134,192]{1,0:T(8,128)(2,1)S(1)}, bf16[134,192]{1,0:T(8,128)(2,1)S(1)}, u32[]{:S(2)}, u32[]{:S(2)}) collective-permute-start(bf16[134,192]{1,0:T(8,128)(2,1)S(1)} %concatenate.77), channel_id=1, source_target_pairs={{0,16},{4,20},{8,24},{12,28},{16,0},{20,4},{24,8},{28,12},{32,48},... | collective-permute-start | bytes 154376 | tf_op jit(solution)/shard_map/ppermute | solution.py:211
  60.9 7.3 %collective-permute-start.12 = (bf16[134,192]{1,0:T(8,128)(2,1)S(1)}, bf16[134,192]{1,0:T(8,128)(2,1)S(1)}, u32[]{:S(2)}, u32[]{:S(2)}) collective-permute-start(bf16[134,192]{1,0:T(8,128)(2,1)S(1)} %concatenate.78), channel_id=1, source_target_pairs={{0,48},{4,52},{8,56},{12,60},{16,32},{20,36},{24,40},{28,44},{32,1... | collective-permute-start | bytes 154376 | tf_op jit(solution)/shard_map/ppermute | solution.py:211
  68.3 4.6 %collective-permute-start.13 = (bf16[134,192]{1,0:T(8,128)(2,1)S(1)}, bf16[134,192]{1,0:T(8,128)(2,1)S(1)}, u32[]{:S(2)}, u32[]{:S(2)}) collective-permute-start(bf16[134,192]{1,0:T(8,128)(2,1)S(1)} %concatenate.79), channel_id=1, source_target_pairs={{0,64},{4,68},{8,72},{12,76},{16,80},{20,84},{24,88},{28,92},{32,9... | collective-permute-start | bytes 154376 | tf_op jit(solution)/shard_map/ppermute | solution.py:211
  73.0 5.6 %collective-permute-start.14 = (bf16[134,192]{1,0:T(8,128)(2,1)S(1)}, bf16[134,192]{1,0:T(8,128)(2,1)S(1)}, u32[]{:S(2)}, u32[]{:S(2)}) collective-permute-start(bf16[134,192]{1,0:T(8,128)(2,1)S(1)} %concatenate.80), channel_id=1, source_target_pairs={{0,192},{4,196},{8,200},{12,204},{16,208},{20,212},{24,216},{28,22... | collective-permute-start | bytes 154376 | tf_op jit(solution)/shard_map/ppermute | solution.py:211
  79.7 9.0 %copy-start.1 = (bf16[4,2,640]{2,1,0:T(2,128)(2,1)S(1)}, bf16[4,2,640]{2,1,0:T(2,128)(2,1)}, u32[]{:S(2)}) copy-start(bf16[4,2,640]{2,1,0:T(2,128)(2,1)} %param.14) | copy-start | bytes 30724
  84.3 5.0 %collective-permute-start.15 = (f32[8,640]{1,0:T(8,128)S(1)}, f32[8,640]{1,0:T(8,128)S(1)}, u32[]{:S(2)}, u32[]{:S(2)}) collective-permute-start(f32[8,640]{1,0:T(8,128)S(1)} %get-tuple-element.73), channel_id=1, source_target_pairs={{0,1},{1,2},{2,3},{3,0},{4,5},{5,6},{6,7},{7,4},{8,9},{9,10},{10,1... | collective-permute-start | bytes 61448 | tf_op jit(solution)/shard_map/ppermute | solution.py:159
  84.9 5.3 %collective-permute-start.16 = (f32[8,640]{1,0:T(8,128)S(1)}, f32[8,640]{1,0:T(8,128)S(1)}, u32[]{:S(2)}, u32[]{:S(2)}) collective-permute-start(f32[8,640]{1,0:T(8,128)S(1)} %get-tuple-element.75), channel_id=1, source_target_pairs={{0,2},{1,3},{2,0},{3,1},{4,6},{5,7},{6,4},{7,5},{8,10},{9,11},{10,... | collective-permute-start | bytes 61448 | tf_op jit(solution)/shard_map/ppermute | solution.py:159
  86.7 3.8 %collective-permute-start.17 = (f32[8,640]{1,0:T(8,128)S(1)}, f32[8,640]{1,0:T(8,128)S(1)}, u32[]{:S(2)}, u32[]{:S(2)}) collective-permute-start(f32[8,640]{1,0:T(8,128)S(1)} %get-tuple-element.74), channel_id=1, source_target_pairs={{0,3},{1,0},{2,1},{3,2},{4,7},{5,4},{6,5},{7,6},{8,11},{9,8},{10,9... | collective-permute-start | bytes 61448 | tf_op jit(solution)/shard_map/ppermute | solution.py:159

commit v16 on v15

--- a/solution.py
+++ b/solution.py
@@ -80,8 +80,8 @@
     )(
         x,
         jnp.broadcast_to(gain[None, :], (m, k)),
-        query_gain.reshape(1, HEAD_SIZE),
-        key_gain.reshape(1, HEAD_SIZE),
+        jnp.broadcast_to(query_gain[None, :], (m, HEAD_SIZE)),
+        jnp.broadcast_to(key_gain[None, :], (m, HEAD_SIZE)),
         cos_both,
         sin_signed,
         *weights,

time: 92.4 us -> 94.9 us (1.027)
  local copies, waits for them, and re-layouts: 9.43 us -> 11.9 us
    broadcast_in_dim x0 -> x2, local copies, waits for them, and re-layouts: none -> 2.48 us  [the longest x1 1.25 us: project_rows(): jnp.broadcast_to(query_gain[None, :], (m, HEAD_SIZE))]
where the time goes in v16:
time: 94.9 us; the launch traced here: 94.3 us
  waiting for transfers between devices  39.7 us (42%)
  starting transfers between devices  27 us (28%)
  local copies, waits for them, and re-layouts  11.9 us (13%)
  other arithmetic  6.59 us (7%)
  Pallas kernels  6.46 us (7%)
  matrix products  1.6 us (2%)
  between operations  1.08 us (1%)
    ppermute x6, waiting for transfers between devices, stats_butterfly(): arrived = lax.ppermute(packed, 'seq', pairs)  19.3 us
    ppermute x6, waiting for transfers between devices, butterfly(): lax.ppermute(value, 'seq', [(i, i ^ stride) for i in range(n_seq)])  17.1 us
    ppermute x6, starting transfers between devices, butterfly(): lax.ppermute(value, 'seq', [(i, i ^ stride) for i in range(n_seq)])  10.4 us
    ppermute x6, starting transfers between devices, stats_butterfly(): arrived = lax.ppermute(packed, 'seq', pairs)  7.65 us
    ppermute x3, starting transfers between devices, gather_mp(): lax.ppermute(block, 'mp', [(i, (i + s) % n_mp) for i in range(n_mp)])  4.69 us
    ppermute x3, starting transfers between devices, reduce_scatter_mp(): lax.ppermute(chunks[s], 'mp', [(i, (i + s) % n_mp) for i in range(n_mp)])  4.32 us
    pallas_call x1, Pallas kernels, project_rows(): pl.pallas_call(_project_kernel, out_shape=[jax.ShapeDtypeStruct((m, n), j...  3.61 us
    pallas_call x1, Pallas kernels, chunked_matmul(): pl.pallas_call(_chunked_kernel, out_shape=jax.ShapeDtypeStruct((chunks, m...  2.85 us
  transfers between devices with their start and end apart: 18, of which 17 were waited for; matrix products, arithmetic and copies ran while one was open for 5% of the time, Pallas kernels for 0%

profile of v16, /device:TPU:38, one launch (start us, length us, event | category | flops | bytes accessed | tf_op | source)
XLA Modules:
  0.0 94.3 jit_solution(3717114592569620456)
XLA Ops:
  0.7 3.1 %collective-permute-start = (bf16[4,2,640]{2,1,0:T(2,128)(2,1)}, bf16[4,2,640]{2,1,0:T(2,128)(2,1)S(1)}, u32[]{:S(2)}, u32[]{:S(2)}) collective-permute-start(bf16[4,2,640]{2,1,0:T(2,128)(2,1)} %param.14), channel_id=1, source_target_pairs={{0,3},{1,0},{2,1},{3,2},{4,7},{5,4},{6,5},{7,6},{8,11},{9,8},{10,9... | collective-permute-start | bytes 30728 | tf_op jit(solution)/shard_map/ppermute | solution.py:144
  3.8 0.6 collective-permute-start.1
  4.4 1.0 %collective-permute-start.2 = (bf16[4,2,640]{2,1,0:T(2,128)(2,1)}, bf16[4,2,640]{2,1,0:T(2,128)(2,1)S(1)}, u32[]{:S(2)}, u32[]{:S(2)}) collective-permute-start(bf16[4,2,640]{2,1,0:T(2,128)(2,1)} %param.14), channel_id=1, source_target_pairs={{0,1},{1,2},{2,3},{3,0},{4,5},{5,6},{6,7},{7,4},{8,9},{9,10},{10,1... | collective-permute-start | bytes 30728 | tf_op jit(solution)/shard_map/ppermute | solution.py:144
  5.4 0.7 broadcast_compare_fusion.2
  6.1 0.7 dynamic_slice.11
  7.5 0.7 pad_maximum_fusion.3
  8.1 1.0 %collective-permute-done.1 = bf16[4,2,640]{2,1,0:T(2,128)(2,1)S(1)} collective-permute-done((bf16[4,2,640]{2,1,0:T(2,128)(2,1)}, bf16[4,2,640]{2,1,0:T(2,128)(2,1)S(1)}, u32[]{:S(2)}, u32[]{:S(2)}) %collective-permute-start.1) | collective-permute-done | bytes 10272 | tf_op jit(solution)/shard_map/ppermute | solution.py:144
  9.2 0.3 collective-permute-done.2
  9.5 0.7 broadcast_select_fusion.11
  10.3 0.6 reshape.367.x_ref
  10.9 1.3 %broadcast_in_dim.281.g_ref = f32[8,2560]{1,0:T(8,128)} broadcast(f32[2560]{0:T(1024)} %param.15), dimensions={1} | broadcast | bytes 92160 | tf_op jit(solution)/shard_map/broadcast_in_dim | solution.py:82
  12.3 1.2 %broadcast_in_dim.282.qg_ref = f32[8,128]{1,0:T(8,128)} broadcast(f32[128]{0:T(128)} %param.16), dimensions={1} | broadcast | bytes 4608 | tf_op jit(solution)/shard_map/broadcast_in_dim | solution.py:83
  13.5 1.2 %broadcast_in_dim.283.kg_ref = f32[8,128]{1,0:T(8,128)} broadcast(f32[128]{0:T(128)} %param.17), dimensions={1} | broadcast | bytes 4608 | tf_op jit(solution)/shard_map/broadcast_in_dim | solution.py:84
  14.7 3.6 %shard_map.157 = (bf16[8,512]{1,0:T(8,128)(2,1)}, bf16[8,128]{1,0:T(8,128)(2,1)}, bf16[8,128]{1,0:T(8,128)(2,1)}) custom-call(bf16[8,2560]{1,0:T(8,128)(2,1)} %reshape.367.x_ref, f32[8,2560]{1,0:T(8,128)} %broadcast_in_dim.281.g_ref, f32[8,128]{1,0:T(8,128)} %broadcast_in_dim.282.qg_ref, f32[8,128]{1,0:T(8,128)} %broadcast_in_dim.283.kg_ref, ...), custom_call_target="tpu_custom_call" | custom-call | flops 31457280 | bytes 3985408 | tf_op jit(solution)/shard_map/pallas_call | solution.py:72
  18.4 0.7 reshape_reshape.9
  19.5 1.1 %collective-permute-done.3 = bf16[12,4,4,128]{3,2,1,0:T(4,128)(2,1)S(1)} collective-permute-done((bf16[12,4,4,128]{3,2,1,0:T(4,128)(2,1)S(1)}, bf16[12,4,4,128]{3,2,1,0:T(4,128)(2,1)S(1)}, u32[]{:S(2)}, u32[]{:S(2)}) %collective-permute-start.3) | collective-permute-done | bytes 49184 | tf_op jit(solution)/shard_map/ppermute | solution.py:171
  20.6 0.2 collective-permute-start.4
  20.8 0.2 select_reduce_fusion.7
  21.1 3.6 %collective-permute-done.4 = bf16[12,4,4,128]{3,2,1,0:T(4,128)(2,1)S(1)} collective-permute-done((bf16[12,4,4,128]{3,2,1,0:T(4,128)(2,1)S(1)}, bf16[12,4,4,128]{3,2,1,0:T(4,128)(2,1)S(1)}, u32[]{:S(2)}, u32[]{:S(2)}) %collective-permute-start.4) | collective-permute-done | bytes 49184 | tf_op jit(solution)/shard_map/ppermute | solution.py:171
  24.8 3.4 %collective-permute-start.5 = (bf16[12,4,4,128]{3,2,1,0:T(4,128)(2,1)S(1)}, bf16[12,4,4,128]{3,2,1,0:T(4,128)(2,1)S(1)}, u32[]{:S(2)}, u32[]{:S(2)}) collective-permute-start(bf16[12,4,4,128]{3,2,1,0:T(4,128)(2,1)S(1)} %add.237), channel_id=1, source_target_pairs={{0,16},{4,20},{8,24},{12,28},{16,0},{20,4},{24,8},{28,12},{32,48},... | collective-permute-start | bytes 147464 | tf_op jit(solution)/shard_map/ppermute | solution.py:171
  28.2 2.0 %collective-permute-done.5 = bf16[12,4,4,128]{3,2,1,0:T(4,128)(2,1)S(1)} collective-permute-done((bf16[12,4,4,128]{3,2,1,0:T(4,128)(2,1)S(1)}, bf16[12,4,4,128]{3,2,1,0:T(4,128)(2,1)S(1)}, u32[]{:S(2)}, u32[]{:S(2)}) %collective-permute-start.5) | collective-permute-done | bytes 49184 | tf_op jit(solution)/shard_map/ppermute | solution.py:171
  30.2 5.2 %collective-permute-start.6 = (bf16[12,4,4,128]{3,2,1,0:T(4,128)(2,1)S(1)}, bf16[12,4,4,128]{3,2,1,0:T(4,128)(2,1)S(1)}, u32[]{:S(2)}, u32[]{:S(2)}) collective-permute-start(bf16[12,4,4,128]{3,2,1,0:T(4,128)(2,1)S(1)} %add.238), channel_id=1, source_target_pairs={{0,48},{4,52},{8,56},{12,60},{16,32},{20,36},{24,40},{28,44},{32,1... | collective-permute-start | bytes 147464 | tf_op jit(solution)/shard_map/ppermute | solution.py:171
  35.5 0.2 fusion.33
  35.7 2.4 %collective-permute-done.6 = bf16[12,4,4,128]{3,2,1,0:T(4,128)(2,1)S(1)} collective-permute-done((bf16[12,4,4,128]{3,2,1,0:T(4,128)(2,1)S(1)}, bf16[12,4,4,128]{3,2,1,0:T(4,128)(2,1)S(1)}, u32[]{:S(2)}, u32[]{:S(2)}) %collective-permute-start.6) | collective-permute-done | bytes 49184 | tf_op jit(solution)/shard_map/ppermute | solution.py:171
  38.1 0.9 collective-permute-start.7
  39.0 3.2 %collective-permute-done.7 = bf16[12,4,4,128]{3,2,1,0:T(4,128)(2,1)S(1)} collective-permute-done((bf16[12,4,4,128]{3,2,1,0:T(4,128)(2,1)S(1)}, bf16[12,4,4,128]{3,2,1,0:T(4,128)(2,1)S(1)}, u32[]{:S(2)}, u32[]{:S(2)}) %collective-permute-start.7) | collective-permute-done | bytes 49184 | tf_op jit(solution)/shard_map/ppermute | solution.py:171
  42.3 0.6 collective-permute-start.8
  42.9 4.8 %collective-permute-done.8 = bf16[12,4,4,128]{3,2,1,0:T(4,128)(2,1)S(1)} collective-permute-done((bf16[12,4,4,128]{3,2,1,0:T(4,128)(2,1)S(1)}, bf16[12,4,4,128]{3,2,1,0:T(4,128)(2,1)S(1)}, u32[]{:S(2)}, u32[]{:S(2)}) %collective-permute-start.8) | collective-permute-done | bytes 49184 | tf_op jit(solution)/shard_map/ppermute | solution.py:171
  47.8 0.6 gather_fusion
  48.5 0.5 select_reduce_fusion.1
  49.3 0.3 bitcast_reduce_fusion
  49.7 0.3 fusion.1
  50.0 0.3 convolution_bitcast_fusion
  50.5 0.2 fusion.77
  50.6 0.2 copy.151
  51.0 0.5 copy.152
  52.1 1.2 %collective-permute-done.9 = bf16[134,192]{1,0:T(8,128)(2,1)S(1)} collective-permute-done((bf16[134,192]{1,0:T(8,128)(2,1)S(1)}, bf16[134,192]{1,0:T(8,128)(2,1)S(1)}, u32[]{:S(2)}, u32[]{:S(2)}) %collective-permute-start.9) | collective-permute-done | bytes 51488 | tf_op jit(solution)/shard_map/ppermute | solution.py:211
  53.4 0.6 collective-permute-start.10
  54.2 3.6 %collective-permute-done.10 = bf16[134,192]{1,0:T(8,128)(2,1)S(1)} collective-permute-done((bf16[134,192]{1,0:T(8,128)(2,1)S(1)}, bf16[134,192]{1,0:T(8,128)(2,1)S(1)}, u32[]{:S(2)}, u32[]{:S(2)}) %collective-permute-start.10) | collective-permute-done | bytes 51488 | tf_op jit(solution)/shard_map/ppermute | solution.py:211
  57.9 1.5 %collective-permute-start.11 = (bf16[134,192]{1,0:T(8,128)(2,1)S(1)}, bf16[134,192]{1,0:T(8,128)(2,1)S(1)}, u32[]{:S(2)}, u32[]{:S(2)}) collective-permute-start(bf16[134,192]{1,0:T(8,128)(2,1)S(1)} %concatenate.77), channel_id=1, source_target_pairs={{0,16},{4,20},{8,24},{12,28},{16,0},{20,4},{24,8},{28,12},{32,48},... | collective-permute-start | bytes 154376 | tf_op jit(solution)/shard_map/ppermute | solution.py:211
  59.5 3.7 %collective-permute-done.11 = bf16[134,192]{1,0:T(8,128)(2,1)S(1)} collective-permute-done((bf16[134,192]{1,0:T(8,128)(2,1)S(1)}, bf16[134,192]{1,0:T(8,128)(2,1)S(1)}, u32[]{:S(2)}, u32[]{:S(2)}) %collective-permute-start.11) | collective-permute-done | bytes 51488 | tf_op jit(solution)/shard_map/ppermute | solution.py:211
  63.4 4.6 %collective-permute-start.12 = (bf16[134,192]{1,0:T(8,128)(2,1)S(1)}, bf16[134,192]{1,0:T(8,128)(2,1)S(1)}, u32[]{:S(2)}, u32[]{:S(2)}) collective-permute-start(bf16[134,192]{1,0:T(8,128)(2,1)S(1)} %concatenate.78), channel_id=1, source_target_pairs={{0,48},{4,52},{8,56},{12,60},{16,32},{20,36},{24,40},{28,44},{32,1... | collective-permute-start | bytes 154376 | tf_op jit(solution)/shard_map/ppermute | solution.py:211
  68.2 2.4 %collective-permute-done.12 = bf16[134,192]{1,0:T(8,128)(2,1)S(1)} collective-permute-done((bf16[134,192]{1,0:T(8,128)(2,1)S(1)}, bf16[134,192]{1,0:T(8,128)(2,1)S(1)}, u32[]{:S(2)}, u32[]{:S(2)}) %collective-permute-start.12) | collective-permute-done | bytes 51488 | tf_op jit(solution)/shard_map/ppermute | solution.py:211
  70.8 0.3 collective-permute-start.13
  71.2 0.3 copy.162
  71.4 3.9 %collective-permute-done.13 = bf16[134,192]{1,0:T(8,128)(2,1)S(1)} collective-permute-done((bf16[134,192]{1,0:T(8,128)(2,1)S(1)}, bf16[134,192]{1,0:T(8,128)(2,1)S(1)}, u32[]{:S(2)}, u32[]{:S(2)}) %collective-permute-start.13) | collective-permute-done | bytes 51488 | tf_op jit(solution)/shard_map/ppermute | solution.py:211
  75.5 0.6 collective-permute-start.14
  76.1 0.4 copy.156
  76.5 4.5 %collective-permute-done.14 = bf16[134,192]{1,0:T(8,128)(2,1)S(1)} collective-permute-done((bf16[134,192]{1,0:T(8,128)(2,1)S(1)}, bf16[134,192]{1,0:T(8,128)(2,1)S(1)}, u32[]{:S(2)}, u32[]{:S(2)}) %collective-permute-start.14) | collective-permute-done | bytes 51488 | tf_op jit(solution)/shard_map/ppermute | solution.py:211
  81.6 0.4 copy.155
  82.0 0.2 bitcast_select_fusion
  82.2 0.2 fusion.7
  82.4 0.2 copy.165
  82.6 0.6 copy.193
  83.2 2.8 %shard_map.158 = f32[4,8,640]{2,1,0:T(8,128)} custom-call(bf16[8,512]{1,0:T(8,128)(2,1)} %bitcast.191, bf16[512,2560]{1,0:T(8,128)(2,1)} %w_ref.1), custom_call_target="tpu_custom_call" | custom-call | flops 20971520 | bytes 2711552 | tf_op jit(solution)/shard_map/pallas_call | solution.py:130
  86.0 0.8 slice_bitcast_fusion.2
  86.8 0.5 collective-permute-start.15
  87.3 1.8 %collective-permute-start.16 = (f32[8,640]{1,0:T(8,128)S(1)}, f32[8,640]{1,0:T(8,128)S(1)}, u32[]{:S(2)}, u32[]{:S(2)}) collective-permute-start(f32[8,640]{1,0:T(8,128)S(1)} %get-tuple-element.75), channel_id=1, source_target_pairs={{0,2},{1,3},{2,0},{3,1},{4,6},{5,7},{6,4},{7,5},{8,10},{9,11},{10,... | collective-permute-start | bytes 61448 | tf_op jit(solution)/shard_map/ppermute | solution.py:159
  89.2 2.0 %collective-permute-start.17 = (f32[8,640]{1,0:T(8,128)S(1)}, f32[8,640]{1,0:T(8,128)S(1)}, u32[]{:S(2)}, u32[]{:S(2)}) collective-permute-start(f32[8,640]{1,0:T(8,128)S(1)} %get-tuple-element.74), channel_id=1, source_target_pairs={{0,3},{1,0},{2,1},{3,2},{4,7},{5,4},{6,5},{7,6},{8,11},{9,8},{10,9... | collective-permute-start | bytes 61448 | tf_op jit(solution)/shard_map/ppermute | solution.py:159
  91.1 0.7 collective-permute-done.15
  91.8 0.8 collective-permute-done.16
  92.6 0.3 collective-permute-done.17
  93.0 0.7 fusion.23
  93.7 0.6 reshape.377
  (110 shorter events, 4.6 us)
Async XLA Ops:
  0.6 47.8 %copy-start = (bf16[16,256,128]{2,1,0:T(8,128)(2,1)S(1)}, bf16[16,256,128]{2,1,0:T(8,128)(2,1)}, u32[]{:S(2)}) copy-start(bf16[16,256,128]{2,1,0:T(8,128)(2,1)} %param.22) | copy-start | bytes 3145732
  0.6 20.1 %copy-start.4 = (s32[128]{0:T(128)S(1)}, s32[128]{0:T(128)}, u32[]{:S(2)}) copy-start(s32[128]{0:T(128)} %param.24) | copy-start | bytes 1540
  0.7 20.1 %copy-start.2 = (s32[16]{0:T(128)S(1)}, s32[16]{0:T(128)}, u32[]{:S(2)}) copy-start(s32[16]{0:T(128)} %param.25) | copy-start | bytes 196
  0.7 20.1 %copy-start.8 = (s32[16]{0:T(128)S(1)}, s32[16]{0:T(128)}, u32[]{:S(2)}) copy-start(s32[16]{0:T(128)} %param.26) | copy-start | bytes 196
  0.7 20.1 %copy-start.7 = (s32[16]{0:T(128)S(1)}, s32[16]{0:T(128)}, u32[]{:S(2)}) copy-start(s32[16]{0:T(128)} %param.27) | copy-start | bytes 196
  0.7 7.4 %collective-permute-start = (bf16[4,2,640]{2,1,0:T(2,128)(2,1)}, bf16[4,2,640]{2,1,0:T(2,128)(2,1)S(1)}, u32[]{:S(2)}, u32[]{:S(2)}) collective-permute-start(bf16[4,2,640]{2,1,0:T(2,128)(2,1)} %param.14), channel_id=1, source_target_pairs={{0,3},{1,0},{2,1},{3,2},{4,7},{5,4},{6,5},{7,6},{8,11},{9,8},{10,9... | collective-permute-start | bytes 30728 | tf_op jit(solution)/shard_map/ppermute | solution.py:144
  3.8 5.4 %collective-permute-start.1 = (bf16[4,2,640]{2,1,0:T(2,128)(2,1)}, bf16[4,2,640]{2,1,0:T(2,128)(2,1)S(1)}, u32[]{:S(2)}, u32[]{:S(2)}) collective-permute-start(bf16[4,2,640]{2,1,0:T(2,128)(2,1)} %param.14), channel_id=1, source_target_pairs={{0,2},{1,3},{2,0},{3,1},{4,6},{5,7},{6,4},{7,5},{8,10},{9,11},{10,... | collective-permute-start | bytes 30728 | tf_op jit(solution)/shard_map/ppermute | solution.py:144
  4.4 5.1 %collective-permute-start.2 = (bf16[4,2,640]{2,1,0:T(2,128)(2,1)}, bf16[4,2,640]{2,1,0:T(2,128)(2,1)S(1)}, u32[]{:S(2)}, u32[]{:S(2)}) collective-permute-start(bf16[4,2,640]{2,1,0:T(2,128)(2,1)} %param.14), channel_id=1, source_target_pairs={{0,1},{1,2},{2,3},{3,0},{4,5},{5,6},{6,7},{7,4},{8,9},{9,10},{10,1... | collective-permute-start | bytes 30728 | tf_op jit(solution)/shard_map/ppermute | solution.py:144
  14.7 34.9 %copy-start.5 = (bf16[16,256,128]{2,1,0:T(8,128)(2,1)S(1)}, bf16[16,256,128]{2,1,0:T(8,128)(2,1)}, u32[]{:S(2)}) copy-start(bf16[16,256,128]{2,1,0:T(8,128)(2,1)} %param.23) | copy-start | bytes 3145732
  19.2 1.3 %collective-permute-start.3 = (bf16[12,4,4,128]{3,2,1,0:T(4,128)(2,1)S(1)}, bf16[12,4,4,128]{3,2,1,0:T(4,128)(2,1)S(1)}, u32[]{:S(2)}, u32[]{:S(2)}) collective-permute-start(bf16[12,4,4,128]{3,2,1,0:T(4,128)(2,1)S(1)} %select_reduce_fusion.4), channel_id=1, source_target_pairs={{0,4},{4,0},{8,12},{12,8},{16,20},{20,16},{24,28},{28,24},{32,36},... | collective-permute-start | bytes 147464 | tf_op jit(solution)/shard_map/ppermute | solution.py:171
  20.6 4.2 %collective-permute-start.4 = (bf16[12,4,4,128]{3,2,1,0:T(4,128)(2,1)S(1)}, bf16[12,4,4,128]{3,2,1,0:T(4,128)(2,1)S(1)}, u32[]{:S(2)}, u32[]{:S(2)}) collective-permute-start(bf16[12,4,4,128]{3,2,1,0:T(4,128)(2,1)S(1)} %add.231), channel_id=1, source_target_pairs={{0,8},{4,12},{8,0},{12,4},{16,24},{20,28},{24,16},{28,20},{32,40},... | collective-permute-start | bytes 147464 | tf_op jit(solution)/shard_map/ppermute | solution.py:171
  24.8 5.4 %collective-permute-start.5 = (bf16[12,4,4,128]{3,2,1,0:T(4,128)(2,1)S(1)}, bf16[12,4,4,128]{3,2,1,0:T(4,128)(2,1)S(1)}, u32[]{:S(2)}, u32[]{:S(2)}) collective-permute-start(bf16[12,4,4,128]{3,2,1,0:T(4,128)(2,1)S(1)} %add.237), channel_id=1, source_target_pairs={{0,16},{4,20},{8,24},{12,28},{16,0},{20,4},{24,8},{28,12},{32,48},... | collective-permute-start | bytes 147464 | tf_op jit(solution)/shard_map/ppermute | solution.py:171
  30.2 7.8 %collective-permute-start.6 = (bf16[12,4,4,128]{3,2,1,0:T(4,128)(2,1)S(1)}, bf16[12,4,4,128]{3,2,1,0:T(4,128)(2,1)S(1)}, u32[]{:S(2)}, u32[]{:S(2)}) collective-permute-start(bf16[12,4,4,128]{3,2,1,0:T(4,128)(2,1)S(1)} %add.238), channel_id=1, source_target_pairs={{0,48},{4,52},{8,56},{12,60},{16,32},{20,36},{24,40},{28,44},{32,1... | collective-permute-start | bytes 147464 | tf_op jit(solution)/shard_map/ppermute | solution.py:171
  38.1 4.2 %collective-permute-start.7 = (bf16[12,4,4,128]{3,2,1,0:T(4,128)(2,1)S(1)}, bf16[12,4,4,128]{3,2,1,0:T(4,128)(2,1)S(1)}, u32[]{:S(2)}, u32[]{:S(2)}) collective-permute-start(bf16[12,4,4,128]{3,2,1,0:T(4,128)(2,1)S(1)} %add.239), channel_id=1, source_target_pairs={{0,64},{4,68},{8,72},{12,76},{16,80},{20,84},{24,88},{28,92},{32,9... | collective-permute-start | bytes 147464 | tf_op jit(solution)/shard_map/ppermute | solution.py:171
  42.3 5.4 %collective-permute-start.8 = (bf16[12,4,4,128]{3,2,1,0:T(4,128)(2,1)S(1)}, bf16[12,4,4,128]{3,2,1,0:T(4,128)(2,1)S(1)}, u32[]{:S(2)}, u32[]{:S(2)}) collective-permute-start(bf16[12,4,4,128]{3,2,1,0:T(4,128)(2,1)S(1)} %add.240), channel_id=1, source_target_pairs={{0,192},{4,196},{8,200},{12,204},{16,208},{20,212},{24,216},{28,22... | collective-permute-start | bytes 147464 | tf_op jit(solution)/shard_map/ppermute | solution.py:171
  49.7 4.4 %copy-start.6 = (bf16[8,128]{1,0:T(8,128)(2,1)S(1)}, bf16[8,128]{1,0:T(8,128)(2,1)}, u32[]{:S(2)}) copy-start(bf16[8,128]{1,0:T(8,128)(2,1)} %get-tuple-element.17) | copy-start | bytes 6148
  50.0 21.0 %copy-start.3 = (bf16[8,128]{1,0:T(8,128)(2,1)S(1)}, bf16[8,128]{1,0:T(8,128)(2,1)}, u32[]{:S(2)}) copy-start(bf16[8,128]{1,0:T(8,128)(2,1)} %get-tuple-element.18) | copy-start | bytes 6148
  51.9 1.3 %collective-permute-start.9 = (bf16[134,192]{1,0:T(8,128)(2,1)S(1)}, bf16[134,192]{1,0:T(8,128)(2,1)S(1)}, u32[]{:S(2)}, u32[]{:S(2)}) collective-permute-start(bf16[134,192]{1,0:T(8,128)(2,1)S(1)} %concatenate.75), channel_id=1, source_target_pairs={{0,4},{4,0},{8,12},{12,8},{16,20},{20,16},{24,28},{28,24},{32,36},... | collective-permute-start | bytes 154376 | tf_op jit(solution)/shard_map/ppermute | solution.py:211
  53.4 4.4 %collective-permute-start.10 = (bf16[134,192]{1,0:T(8,128)(2,1)S(1)}, bf16[134,192]{1,0:T(8,128)(2,1)S(1)}, u32[]{:S(2)}, u32[]{:S(2)}) collective-permute-start(bf16[134,192]{1,0:T(8,128)(2,1)S(1)} %concatenate.76), channel_id=1, source_target_pairs={{0,8},{4,12},{8,0},{12,4},{16,24},{20,28},{24,16},{28,20},{32,40},... | collective-permute-start | bytes 154376 | tf_op jit(solution)/shard_map/ppermute | solution.py:211
  57.9 5.3 %collective-permute-start.11 = (bf16[134,192]{1,0:T(8,128)(2,1)S(1)}, bf16[134,192]{1,0:T(8,128)(2,1)S(1)}, u32[]{:S(2)}, u32[]{:S(2)}) collective-permute-start(bf16[134,192]{1,0:T(8,128)(2,1)S(1)} %concatenate.77), channel_id=1, source_target_pairs={{0,16},{4,20},{8,24},{12,28},{16,0},{20,4},{24,8},{28,12},{32,48},... | collective-permute-start | bytes 154376 | tf_op jit(solution)/shard_map/ppermute | solution.py:211
  63.4 7.3 %collective-permute-start.12 = (bf16[134,192]{1,0:T(8,128)(2,1)S(1)}, bf16[134,192]{1,0:T(8,128)(2,1)S(1)}, u32[]{:S(2)}, u32[]{:S(2)}) collective-permute-start(bf16[134,192]{1,0:T(8,128)(2,1)S(1)} %concatenate.78), channel_id=1, source_target_pairs={{0,48},{4,52},{8,56},{12,60},{16,32},{20,36},{24,40},{28,44},{32,1... | collective-permute-start | bytes 154376 | tf_op jit(solution)/shard_map/ppermute | solution.py:211
  70.8 4.6 %collective-permute-start.13 = (bf16[134,192]{1,0:T(8,128)(2,1)S(1)}, bf16[134,192]{1,0:T(8,128)(2,1)S(1)}, u32[]{:S(2)}, u32[]{:S(2)}) collective-permute-start(bf16[134,192]{1,0:T(8,128)(2,1)S(1)} %concatenate.79), channel_id=1, source_target_pairs={{0,64},{4,68},{8,72},{12,76},{16,80},{20,84},{24,88},{28,92},{32,9... | collective-permute-start | bytes 154376 | tf_op jit(solution)/shard_map/ppermute | solution.py:211
  75.5 5.6 %collective-permute-start.14 = (bf16[134,192]{1,0:T(8,128)(2,1)S(1)}, bf16[134,192]{1,0:T(8,128)(2,1)S(1)}, u32[]{:S(2)}, u32[]{:S(2)}) collective-permute-start(bf16[134,192]{1,0:T(8,128)(2,1)S(1)} %concatenate.80), channel_id=1, source_target_pairs={{0,192},{4,196},{8,200},{12,204},{16,208},{20,212},{24,216},{28,22... | collective-permute-start | bytes 154376 | tf_op jit(solution)/shard_map/ppermute | solution.py:211
  82.2 9.0 %copy-start.1 = (bf16[4,2,640]{2,1,0:T(2,128)(2,1)S(1)}, bf16[4,2,640]{2,1,0:T(2,128)(2,1)}, u32[]{:S(2)}) copy-start(bf16[4,2,640]{2,1,0:T(2,128)(2,1)} %param.14) | copy-start | bytes 30724
  86.8 5.0 %collective-permute-start.15 = (f32[8,640]{1,0:T(8,128)S(1)}, f32[8,640]{1,0:T(8,128)S(1)}, u32[]{:S(2)}, u32[]{:S(2)}) collective-permute-start(f32[8,640]{1,0:T(8,128)S(1)} %get-tuple-element.73), channel_id=1, source_target_pairs={{0,1},{1,2},{2,3},{3,0},{4,5},{5,6},{6,7},{7,4},{8,9},{9,10},{10,1... | collective-permute-start | bytes 61448 | tf_op jit(solution)/shard_map/ppermute | solution.py:159
  87.3 5.3 %collective-permute-start.16 = (f32[8,640]{1,0:T(8,128)S(1)}, f32[8,640]{1,0:T(8,128)S(1)}, u32[]{:S(2)}, u32[]{:S(2)}) collective-permute-start(f32[8,640]{1,0:T(8,128)S(1)} %get-tuple-element.75), channel_id=1, source_target_pairs={{0,2},{1,3},{2,0},{3,1},{4,6},{5,7},{6,4},{7,5},{8,10},{9,11},{10,... | collective-permute-start | bytes 61448 | tf_op jit(solution)/shard_map/ppermute | solution.py:159
  89.2 3.8 %collective-permute-start.17 = (f32[8,640]{1,0:T(8,128)S(1)}, f32[8,640]{1,0:T(8,128)S(1)}, u32[]{:S(2)}, u32[]{:S(2)}) collective-permute-start(f32[8,640]{1,0:T(8,128)S(1)} %get-tuple-element.74), channel_id=1, source_target_pairs={{0,3},{1,0},{2,1},{3,2},{4,7},{5,4},{6,5},{7,6},{8,11},{9,8},{10,9... | collective-permute-start | bytes 61448 | tf_op jit(solution)/shard_map/ppermute | solution.py:159
